TPU v7x, 256 devices: a whole 4x4x8 slice. The times are simulated.
256 devices in a mesh: seq: 32 (over z_hi, y, x), wt: 2 (over core), head: 4 (over z_lo).
Axes of the slice: x: 4, y: 4, z: 8 (z_hi: 2, z_lo: 4; z = z_hi * 4 + z_lo), core: 2. Of those that a mesh axis runs over, the one named last changes fastest.
Arguments:
- tokens: bfloat16 [2, 4096, 5120], P('wt', 'seq'), may hold values from -6 to 6
- w_query: bfloat16 [5120, 2560], P('wt', 'head'), may hold values from -0.078125 to 0.078125
- w_key: bfloat16 [5120, 2560], P('wt', 'head'), may hold values from -0.078125 to 0.078125
- w_value: bfloat16 [5120, 2560], P('wt', 'head'), may hold values from -0.078125 to 0.078125
- w_output: bfloat16 [2560, 5120], P('head', 'wt'), may hold values from -0.125 to 0.125
Outputs:
- mixed: bfloat16 [2, 4096, 5120], P('wt', 'seq', 'head')
All inputs are finite; a program needn't handle non-finite values.
Results may differ from a plain program's by a relative error of at most 0.013.
Values may be sent and summed in bfloat16 or wider, within the bound.
No kernel may reach another device: no remote copies, remote signals or barrier semaphores. Data moves between devices by JAX's collectives and lax.ppermute only.
A program may use at most 128 MiB of HBM per device.

v0:
```python
import jax
import jax.numpy as jnp
from jax import lax
from jax.sharding import PartitionSpec as P

HD = 128


def carried_in(x, axis, join, neutral):
    place = lax.axis_index(axis)
    gathered = lax.all_gather(x.astype(jnp.bfloat16), axis)
    state = jnp.zeros_like(x) + jnp.asarray(neutral, x.dtype)

    def one(step, state):
        return join(state, lax.dynamic_index_in_dim(gathered, step, 0, False).astype(x.dtype))

    return lax.fori_loop(0, place, one, state)


def add_rows(left, piece):
    return jnp.dot(left, piece, preferred_element_type=jnp.float32)


def add_states(earlier, later):
    return earlier + later


def shards(tokens, w_query, w_key, w_value, w_output):
    rows_in = tokens.reshape(tokens.shape[1], tokens.shape[2])
    tok_count = rows_in.shape[0]
    width_local = w_query.shape[1]
    head_count = width_local // HD

    def add_single(piece):
        return add_rows(rows_in, piece)

    query_sum = add_single(lax.all_gather(w_query, "wt", axis=0, tiled=True))
    key_sum = add_single(lax.all_gather(w_key, "wt", axis=0, tiled=True))
    value_sum = add_single(lax.all_gather(w_value, "wt", axis=0, tiled=True))
    queries = jax.nn.silu(query_sum).astype(jnp.bfloat16).reshape(tok_count, head_count, HD)
    keys_all = jax.nn.silu(key_sum).astype(jnp.bfloat16).reshape(tok_count, head_count, HD)
    values = value_sum.astype(jnp.bfloat16).reshape(tok_count, head_count, HD)
    local_state = jnp.einsum("thd,the->hde", keys_all, values, preferred_element_type=jnp.float32)
    prefix_state = carried_in(local_state, "seq", add_states, jnp.zeros_like(local_state))
    scores = jnp.einsum("thd,shd->hts", queries, keys_all, preferred_element_type=jnp.float32)
    positions = jnp.arange(tok_count)
    causal = (positions[None, :] <= positions[:, None]).astype(jnp.float32)
    scores = (scores * causal[None, :, :]).astype(jnp.bfloat16)
    local_part = jnp.einsum("hts,shd->thd", scores, values, preferred_element_type=jnp.float32)
    carried = jnp.einsum(
        "thd,hde->the", queries.astype(jnp.float32), prefix_state, precision=lax.Precision.HIGHEST
    )
    attended = local_part + carried
    scale = lax.rsqrt(jnp.mean(attended * attended, axis=2, keepdims=True) + 1e-06)
    normed = (attended * scale).reshape(tok_count, width_local).astype(jnp.bfloat16)
    terms = jnp.dot(
        normed,
        lax.all_gather(w_output, "wt", axis=1, tiled=True),
        preferred_element_type=jnp.float32,
    )
    mixed = lax.psum_scatter(terms.astype(jnp.bfloat16), "head", scatter_dimension=1, tiled=True)
    return mixed.reshape(1, tok_count, mixed.shape[1])


def solution(mesh):
    placed = (
        P("wt", "seq", None),
        P("wt", "head"),
        P("wt", "head"),
        P("wt", "head"),
        P("head", "wt"),
    )
    return jax.shard_map(
        shards, mesh=mesh, in_specs=placed, out_specs=P("wt", "seq", "head"), check_vma=False
    )
```

profile of v0, /device:TPU:10, one launch (start us, length us, event | category | flops | bytes accessed | tf_op | source)
XLA Modules:
  0.0 286.6 jit_solution(9090709857213491844)
XLA Ops:
  6.5 0.0 copy-start
  6.5 0.0 all-gather.7.cloned.1.call-start
  6.5 0.7 all-gather.7.cloned.1.call-update
  7.3 0.0 all-gather.11.cloned.1.call-start
  7.3 0.7 all-gather.11.cloned.1.call-update
  8.0 0.0 all-gather.9.cloned.1.call-start
  8.1 0.7 all-gather.9.cloned.1.call-update
  8.7 0.0 all-gather.15.cloned.1.call-start
  8.8 25.7 %all-gather.7.cloned.1.call-done = bf16[5120,640]{1,0:T(8,128)(2,1)} async-done(((bf16[2560,640]{1,0:T(8,128)(2,1)}), bf16[5120,640]{1,0:T(8,128)(2,1)}) %all-gather.7.cloned.1.call-update) | async-done | bytes 6553616 | tf_op jit(solution)/shard_map/all_gather | solution.py:39
  34.5 0.0 copy-done
  34.5 4.1 %fusion.8 = bf16[128,640]{1,0:T(8,128)(2,1)S(1)} fusion(bf16[5120,640]{1,0:T(8,128)(2,1)} %all-gather.7.cloned.1.call-done, bf16[1,128,5120]{2,1,0:T(8,128)(2,1)S(1)} %copy-done), kind=kOutput, calls=%fused_computation.13 | convolution fusion | flops 838942720 | bytes 8028160 | tf_op jit(solution)/shard_map/dot_general | solution.py:21
  38.6 0.2 copy.17
  38.7 21.4 %all-gather.11.cloned.1.call-done = bf16[5120,640]{1,0:T(8,128)(2,1)} async-done(((bf16[2560,640]{1,0:T(8,128)(2,1)}), bf16[5120,640]{1,0:T(8,128)(2,1)}) %all-gather.11.cloned.1.call-update) | async-done | bytes 6553616 | tf_op jit(solution)/shard_map/all_gather | solution.py:38
  60.1 4.1 %multiply_convert_fusion.1 = bf16[128,640]{1,0:T(8,128)(2,1)S(1)} fusion(bf16[5120,640]{1,0:T(8,128)(2,1)} %all-gather.11.cloned.1.call-done, bf16[1,128,5120]{2,1,0:T(8,128)(2,1)S(1)} %copy-done), kind=kOutput, calls=%fused_computation.17 | convolution fusion | flops 839270400 | bytes 8028160 | tf_op jit(solution)/shard_map/dot_general | solution.py:21
  64.2 0.2 copy.19
  64.3 0.9 convolution_convert_fusion.1
  65.3 0.0 all-gather.15.cloned.1.call-update
  65.3 0.0 all-gather.13.cloned.1.call-start
  65.3 0.5 all-gather.13.cloned.1.call-update
  65.9 0.0 reduce-scatter.2.cloned.1.call-start
  65.9 19.8 %all-gather.9.cloned.1.call-done = bf16[5120,640]{1,0:T(8,128)(2,1)} async-done(((bf16[2560,640]{1,0:T(8,128)(2,1)}), bf16[5120,640]{1,0:T(8,128)(2,1)}) %all-gather.9.cloned.1.call-update) | async-done | bytes 6553616 | tf_op jit(solution)/shard_map/all_gather | solution.py:37
  85.7 4.1 %multiply_convert_fusion.2 = bf16[128,640]{1,0:T(8,128)(2,1)S(1)} fusion(bf16[5120,640]{1,0:T(8,128)(2,1)} %all-gather.9.cloned.1.call-done, bf16[1,128,5120]{2,1,0:T(8,128)(2,1)S(1)} %copy-done), kind=kOutput, calls=%fused_computation.18 | convolution fusion | flops 839270400 | bytes 8028160 | tf_op jit(solution)/shard_map/dot_general | solution.py:21
  89.8 0.2 copy.18
  90.0 0.4 fusion.11
  90.4 119.8 %all-gather.15.cloned.1.call-done = bf16[160,128,128]{2,1,0:T(8,128)(2,1)} async-done(((bf16[5,128,128]{2,1,0:T(8,128)(2,1)}), bf16[160,128,128]{2,1,0:T(8,128)(2,1)}) %all-gather.15.cloned.1.call-update) | async-done | bytes 5242896 | tf_op jit(solution)/shard_map/all_gather | solution.py:11
  210.2 5.1 %while.10 = (s32[]{:T(128)}, f32[5,128,128]{2,1,0:T(8,128)S(1)}, s32[]{:T(128)}, bf16[32,5,128,128]{3,2,1,0:T(8,128)(2,1)}, s32[]{:T(128)}, /*index=5*/s32[]{:T(128)}, s32[]{:T(128)}) while((s32[]{:T(128)}, f32[5,128,128]{2,1,0:T(8,128)S(1)}, s32[]{:T(128)}, bf16[32,5,128,128]{3,2,1,0:T(8,128)(2,1)}, s32[]{:T(128)}, /*index=5*/s32[]{:T(128)}, ...), condition=%wide.region_1.2_spmd, body=%wide.region_0.1_spmd.sunk | while | flops 163845 | bytes 819315 | solution.py:17
  210.2 1.0 convert_add_fusion.2
  211.2 1.0 convert_add_fusion.2
  212.2 1.0 convert_add_fusion.2
  213.3 1.0 convert_add_fusion.2
  214.3 1.0 convert_add_fusion.2
  215.3 0.5 multiply_reduce_fusion
  215.8 14.3 %all-gather.13.cloned.1.call-done = bf16[640,5120]{1,0:T(8,128)(2,1)} async-done(((bf16[640,2560]{1,0:T(8,128)(2,1)}), bf16[640,5120]{1,0:T(8,128)(2,1)}) %all-gather.13.cloned.1.call-update) | async-done | bytes 6553616 | tf_op jit(solution)/shard_map/all_gather | solution.py:58
  230.1 5.1 %convolution_convert_fusion = bf16[128,5120]{1,0:T(8,128)(2,1)} fusion(bf16[128,640]{0,1:T(8,128)(2,1)S(1)} %bitcast.44, bf16[640,5120]{1,0:T(8,128)(2,1)} %all-gather.13.cloned.1.call-done), kind=kOutput, calls=%fused_computation.1 | convolution fusion | flops 839516160 | bytes 8028160 | tf_op jit(solution)/shard_map/dot_general | solution.py:56
  235.3 0.0 reduce-scatter.2.cloned.1.call-update
  235.3 44.4 %reduce-scatter.2.cloned.1.call-done = bf16[128,1280]{1,0:T(8,128)(2,1)} async-done(((bf16[128,5120]{1,0:T(8,128)(2,1)}), bf16[128,1280]{1,0:T(8,128)(2,1)}) %reduce-scatter.2.cloned.1.call-update) | async-done | bytes 327696 | tf_op jit(solution)/shard_map/reduce_scatter | solution.py:61
  (4 shorter events, 0.1 us)
Async XLA Ops:
  6.5 28.0 %copy-start = (bf16[1,128,5120]{2,1,0:T(8,128)(2,1)S(1)}, bf16[1,128,5120]{2,1,0:T(8,128)(2,1)}, u32[]{:S(2)}) copy-start(bf16[1,128,5120]{2,1,0:T(8,128)(2,1)} %param.7) | copy-start | bytes 3932164
  6.5 28.0 %all-gather.7.cloned.1.call-start = ((), (), s32[]{:S(2)}) async-start(), calls=%async_computation.1 | async-start | bytes 9830400 | tf_op jit(solution)/shard_map/all_gather | solution.py:39
  7.3 52.8 %all-gather.11.cloned.1.call-start = ((), (), s32[]{:S(2)}) async-start(), calls=%async_computation.3 | async-start | bytes 9830400 | tf_op jit(solution)/shard_map/all_gather | solution.py:38
  8.0 77.7 %all-gather.9.cloned.1.call-start = ((), (), s32[]{:S(2)}) async-start(), calls=%async_computation.2 | async-start | bytes 9830400 | tf_op jit(solution)/shard_map/all_gather | solution.py:37
  8.7 201.4 %all-gather.15.cloned.1.call-start = ((), (), s32[]{:S(2)}) async-start(), calls=%async_computation.6 | async-start | bytes 5406720 | tf_op jit(solution)/shard_map/all_gather | solution.py:11
  65.3 164.8 %all-gather.13.cloned.1.call-start = ((), (), s32[]{:S(2)}) async-start(), calls=%async_computation.4 | async-start | bytes 9830400 | tf_op jit(solution)/shard_map/all_gather | solution.py:58
  65.9 213.8 %reduce-scatter.2.cloned.1.call-start = ((), (), s32[]{:S(2)}) async-start(), calls=%async_computation.5 | async-start | bytes 1638400 | tf_op jit(solution)/shard_map/reduce_scatter | solution.py:61
Sparse Core Ops, SparseCore 0:
  9.1 25.3 all-gather.6
  36.3 23.7 all-gather.10
  61.9 23.7 all-gather.8
  89.0 121.1 all-gather.14
  211.8 18.2 all-gather.12
  235.4 44.2 reduce-scatter.1
where the time goes:
time: 288 us; the launch traced here: 287 us
  waiting for transfers between devices  248 us (86%)
  matrix products  19.2 us (7%)
  between operations  13.5 us (5%)
  other arithmetic  5.01 us (2%)
    all_gather x1, waiting for transfers between devices, carried_in(): gathered = lax.all_gather(x.astype(jnp.bfloat16), axis)  120 us
    reduce_scatter x1, waiting for transfers between devices, shards(): lax.psum_scatter(terms.astype(jnp.bfloat16), 'head', scatter_dimension=1,...  44.4 us
    all_gather x1, waiting for transfers between devices, shards(): value_sum = add_single(lax.all_gather(w_value, 'wt', axis=0, tiled=True))  25.7 us
    all_gather x1, waiting for transfers between devices, shards(): key_sum = add_single(lax.all_gather(w_key, 'wt', axis=0, tiled=True))  21.4 us
    all_gather x1, waiting for transfers between devices, shards(): query_sum = add_single(lax.all_gather(w_query, 'wt', axis=0, tiled=True))  19.8 us
    all_gather x1, waiting for transfers between devices, shards(): lax.all_gather(w_output, 'wt', axis=1, tiled=True)  14.3 us
    dot_general x3, matrix products, add_rows(): return jnp.dot(left, piece, preferred_element_type=jnp.float32)  12.2 us
  transfers between devices with their start and end apart: 6, of which 6 were waited for; matrix products, arithmetic and copies ran while one was open for 7% of the time, Pallas kernels for 0%

commit v1 on v0

v1 whole, which is shorter than its diff:
```python
import jax
import jax.numpy as jnp
from jax import lax
from jax.sharding import PartitionSpec as P

HD = 128
F32 = jnp.float32
BF16 = jnp.bfloat16


def swap_cores(x):
    return lax.ppermute(x, "wt", [(0, 1), (1, 0)])


def shifted(x, axis, pairs):
    return lax.ppermute(x, axis, pairs)


def prefix_over_seq(state, seq_size):
    nx, ny = 4, 4
    nz = seq_size // (nx * ny)
    i = lax.axis_index("seq")
    x = i % nx
    y = (i // nx) % ny

    def along(value, stride, size, pos):
        sent = value.astype(BF16)
        before = jnp.zeros_like(value)
        total = value
        for d in range(1, size):
            pairs = []
            for j in range(seq_size):
                jp = (j // stride) % size
                pairs.append((j, j + (((jp + d) % size) - jp) * stride))
            got = shifted(sent, "seq", pairs).astype(F32)
            before = before + jnp.where((pos - d) % size < pos, got, 0.0)
            total = total + got
        return before, total

    ex, row_total = along(state, 1, nx, x)
    ey, plane_total = along(row_total, nx, ny, y)
    ez = jnp.zeros_like(state)
    if nz > 1:
        plane = nx * ny
        zpairs = [(j, j + plane) for j in range(seq_size - plane)]
        ez = shifted(plane_total.astype(BF16), "seq", zpairs).astype(F32)
    return ex + ey + ez


def shards(seq_size, tokens, w_query, w_key, w_value, w_output):
    rows_in = tokens.reshape(tokens.shape[1], tokens.shape[2])
    tok_count = rows_in.shape[0]
    half = w_query.shape[0]
    width_local = w_query.shape[1]
    head_count = width_local // HD
    c = lax.axis_index("wt")

    mine_cols = lax.dynamic_slice_in_dim(rows_in, c * half, half, axis=1)
    their_cols = lax.dynamic_slice_in_dim(rows_in, (1 - c) * half, half, axis=1)
    got_cols = swap_cores(their_cols)
    sums = []
    for w in (w_query, w_key, w_value):
        lent = swap_cores(jnp.dot(got_cols, w, preferred_element_type=F32))
        own = jnp.dot(mine_cols, w, preferred_element_type=F32)
        sums.append(own + lent)
    query_sum, key_sum, value_sum = sums

    queries = jax.nn.silu(query_sum).astype(BF16).reshape(tok_count, head_count, HD)
    keys_all = jax.nn.silu(key_sum).astype(BF16).reshape(tok_count, head_count, HD)
    values = value_sum.astype(BF16).reshape(tok_count, head_count, HD)
    local_state = jnp.einsum("thd,the->hde", keys_all, values, preferred_element_type=F32)
    prefix_state = prefix_over_seq(local_state, seq_size)

    scores = jnp.einsum("thd,shd->hts", queries, keys_all, preferred_element_type=F32)
    positions = jnp.arange(tok_count)
    causal = (positions[None, :] <= positions[:, None]).astype(F32)
    scores = (scores * causal[None, :, :]).astype(BF16)
    local_part = jnp.einsum("hts,shd->thd", scores, values, preferred_element_type=F32)
    carried = jnp.einsum(
        "thd,hde->the", queries.astype(F32), prefix_state, precision=lax.Precision.HIGHEST
    )
    attended = local_part + carried
    scale = lax.rsqrt(jnp.mean(attended * attended, axis=2, keepdims=True) + 1e-06)
    normed = (attended * scale).reshape(tok_count, width_local).astype(BF16)

    w_other = swap_cores(w_output)
    y_mine = jnp.dot(normed, w_output, preferred_element_type=F32)
    y_other = jnp.dot(normed, w_other, preferred_element_type=F32)
    quarter = y_mine.shape[1] // 2

    def block(q):
        sub = q % 2
        a = lax.dynamic_slice_in_dim(y_mine, sub * quarter, quarter, axis=1)
        b = lax.dynamic_slice_in_dim(y_other, sub * quarter, quarter, axis=1)
        return jnp.where(q // 2 == c, a, b)

    n = 4
    h = lax.axis_index("head")
    right = jnp.zeros((tok_count, quarter), F32)
    left = jnp.zeros((tok_count, quarter), F32)
    for s in range(1, n):
        qr = jnp.clip(h + n - s, 0, n - 1)
        ql = jnp.clip(h - n + s, 0, n - 1)
        send_r = (block(qr) + right).astype(BF16)
        send_l = (block(ql) + left).astype(BF16)
        rpairs = [(j, j + 1) for j in range(s) if j + 1 < n]
        lpairs = [(j, j - 1) for j in range(n - s, n) if j - 1 >= 0]
        right = lax.ppermute(send_r, "head", rpairs).astype(F32)
        left = lax.ppermute(send_l, "head", lpairs).astype(F32)
    mixed = (block(h) + right + left).astype(BF16)
    return mixed.reshape(1, tok_count, quarter)


def solution(mesh):
    import functools

    placed = (
        P("wt", "seq", None),
        P("wt", "head"),
        P("wt", "head"),
        P("wt", "head"),
        P("head", "wt"),
    )
    return jax.shard_map(
        functools.partial(shards, mesh.shape["seq"]),
        mesh=mesh,
        in_specs=placed,
        out_specs=P("wt", "seq", "head"),
        check_vma=False,
    )
```

time: 288 us -> 122 us (0.42)
  waiting for transfers between devices: 248 us -> 29.8 us
  starting transfers between devices: 0.2 us -> 41.5 us
  between operations: 13.5 us -> 0.19 us
  other arithmetic: 5.01 us -> 17.1 us
  matrix products: 19.2 us -> 25.8 us
  local copies, waits for them, and re-layouts: 0.52 us -> 6.74 us
    all_gather x5 -> x0, waiting for transfers between devices: 201 us -> none  [the longest x1 120 us: carried_in(): gathered = lax.all_gather(x.astype(jnp.bfloat16), axis)]
    reduce_scatter x1 -> x0, waiting for transfers between devices: 44.4 us -> none  [shards(): lax.psum_scatter(terms.astype(jnp.bfloat16), 'head', scatter_dimension=1,...]
    ppermute x0 -> x18, starting transfers between devices: none -> 41.5 us  [the longest x7 18.9 us: shifted(): return lax.ppermute(x, axis, pairs)]
    ppermute x0 -> x18, waiting for transfers between devices: none -> 29.8 us  [the longest x3 10.6 us: shards(): left = lax.ppermute(send_l, 'head', lpairs).astype(F32)]
    convert_element_type x2 -> x11, other arithmetic: 0.04 us -> 14.7 us  [the longest x3 6.28 us: shards(): send_r = (block(qr) + right).astype(BF16)]
    dot_general x7 -> x11, matrix products: 19.2 us -> 25.8 us  [the longest x3 6.9 us: shards(): lent = swap_cores(jnp.dot(got_cols, w, preferred_element_type=F32))]
    add x5 -> x0, other arithmetic: 4.96 us -> none  [add_states(): return earlier + later]
    convert_element_type x3, local copies, waits for them, and re-layouts: 0.5 us -> 4.49 us  [the longest x1 1.71 us: shards(): jax.nn.silu(key_sum).astype(BF16).reshape(tok_count, head_count, HD)]
  transfers between devices with their start and end apart: 6 -> 18, of which waited for: 6 -> 9; matrix products, arithmetic and copies ran while one was open for 7% -> 31% of each run, Pallas kernels for 0% -> 0%
where the time goes in v1:
time: 122 us; the launch traced here: 121 us
  starting transfers between devices  41.5 us (34%)
  waiting for transfers between devices  29.8 us (24%)
  matrix products  25.8 us (21%)
  other arithmetic  17.1 us (14%)
  local copies, waits for them, and re-layouts  6.74 us (6%)
    ppermute x7, starting transfers between devices, shifted(): return lax.ppermute(x, axis, pairs)  18.9 us
    ppermute x3, starting transfers between devices, shards(): right = lax.ppermute(send_r, 'head', rpairs).astype(F32)  17.5 us
    ppermute x3, waiting for transfers between devices, shards(): left = lax.ppermute(send_l, 'head', lpairs).astype(F32)  10.6 us
    ppermute x3, waiting for transfers between devices, shards(): right = lax.ppermute(send_r, 'head', rpairs).astype(F32)  10 us
    ppermute x7, waiting for transfers between devices, shifted(): return lax.ppermute(x, axis, pairs)  9.13 us
    dot_general x3, matrix products, shards(): lent = swap_cores(jnp.dot(got_cols, w, preferred_element_type=F32))  6.9 us
    dot_general x3, matrix products, shards(): own = jnp.dot(mine_cols, w, preferred_element_type=F32)  6.87 us
    convert_element_type x3, other arithmetic, shards(): send_r = (block(qr) + right).astype(BF16)  6.28 us
  transfers between devices with their start and end apart: 18, of which 9 were waited for; matrix products, arithmetic and copies ran while one was open for 31% of the time, Pallas kernels for 0%

profile of v1, /device:TPU:10, one launch (start us, length us, event | category | flops | bytes accessed | tf_op | source)
XLA Modules:
  0.0 121.0 jit_solution(7370744177044125870)
XLA Ops:
  0.0 0.0 copy-start
  0.0 2.1 %dynamic-slice_bitcast_fusion = bf16[128,2560]{1,0:T(8,128)(2,1)} fusion(bf16[1,128,5120]{2,1,0:T(8,128)(2,1)} %param.5, s32[]{:T(128)S(6)} %select_n.207), kind=kLoop, calls=%fused_computation.17 | loop fusion | bytes 1310724 | tf_op jit(solution)/shard_map/dynamic_slice | solution.py:59
  2.1 0.0 collective-permute-start
  2.1 0.5 collective-permute-start.11
  2.6 2.6 %fusion.6 = f32[128,640]{1,0:T(8,128)} fusion(bf16[2560,640]{1,0:T(8,128)(2,1)S(1)} %copy-done, bf16[1,128,5120]{2,1,0:T(8,128)(2,1)} %param.5, s32[]{:T(128)S(6)} %select_n.206), kind=kOutput, calls=%fused_computation.8 | convolution fusion | flops 419430400 | bytes 4259844 | tf_op jit(solution)/shard_map/dot_general | solution.py:64
  5.3 0.0 collective-permute-done
  5.3 2.6 %fusion.38 = f32[128,640]{1,0:T(8,128)} fusion(bf16[128,2560]{1,0:T(8,128)(2,1)} %collective-permute-done, bf16[2560,640]{1,0:T(8,128)(2,1)S(1)} %copy-done), kind=kOutput, calls=%fused_computation.65 | convolution fusion | flops 419430400 | bytes 4259840 | tf_op jit(solution)/shard_map/dot_general | solution.py:63
  7.9 0.0 collective-permute-start.1
  7.9 2.5 %fusion.40 = f32[128,640]{1,0:T(8,128)} fusion(bf16[128,2560]{1,0:T(8,128)(2,1)} %collective-permute-done, bf16[2560,640]{1,0:T(8,128)(2,1)S(1)} %copy-done.3), kind=kOutput, calls=%fused_computation.67 | convolution fusion | flops 419430400 | bytes 4259840 | tf_op jit(solution)/shard_map/dot_general | solution.py:63
  10.4 0.5 collective-permute-start.3
  10.9 1.4 %fusion.2 = f32[128,640]{1,0:T(8,128)} fusion(bf16[2560,640]{1,0:T(8,128)(2,1)S(1)} %copy-done.3, bf16[1,128,5120]{2,1,0:T(8,128)(2,1)S(1)} %copy-done.5, s32[]{:T(128)S(6)} %select_n.206), kind=kOutput, calls=%fused_computation.4 | convolution fusion | flops 419430400 | bytes 4259844 | tf_op jit(solution)/shard_map/dot_general | solution.py:64
  12.4 0.0 collective-permute-done.1
  12.4 1.8 %add_convert_fusion.5 = bf16[128,640]{1,0:T(8,128)(2,1)} fusion(f32[128,640]{1,0:T(8,128)} %fusion.6, f32[128,640]{1,0:T(8,128)} %collective-permute-done.1), kind=kLoop, calls=%fused_computation.47 | loop fusion | flops 163840 | bytes 819200 | tf_op jit(solution)/shard_map/convert_element_type | solution.py:70
  14.1 1.1 copy.11
  15.2 0.0 collective-permute-done.3
  15.2 1.8 %multiply_convert_fusion.1 = bf16[128,640]{1,0:T(8,128)(2,1)} fusion(f32[128,640]{1,0:T(8,128)} %fusion.2, f32[128,640]{1,0:T(8,128)} %collective-permute-done.3), kind=kLoop, calls=%fused_computation.45 | loop fusion | flops 491520 | bytes 819200 | tf_op jit(solution)/shard_map/convert_element_type | solution.py:69
  17.0 1.7 %copy.13 = bf16[128,640]{0,1:T(8,128)(2,1)} copy(bf16[128,640]{1,0:T(8,128)(2,1)} %multiply_convert_fusion.1) | data formatting | bytes 327680 | tf_op jit(solution)/shard_map/convert_element_type | solution.py:69
  18.8 1.3 %fusion.37 = (bf16[5,128,128]{2,1,0:T(8,128)(2,1)S(1)}, f32[5,128,128]{2,1,0:T(8,128)S(1)}) fusion(bf16[128,5,128]{0,2,1:T(8,128)(2,1)} %bitcast.40, bf16[128,5,128]{0,2,1:T(8,128)(2,1)S(1)} %bitcast.38), kind=kOutput, calls=%fused_computation.64 | convolution fusion | flops 21053440 | bytes 819200 | tf_op jit(solution)/shard_map/thd,the->hde/dot_general | solution.py:71
  20.1 1.5 %collective-permute-start.4 = (bf16[5,128,128]{2,1,0:T(8,128)(2,1)S(1)}, bf16[5,128,128]{2,1,0:T(8,128)(2,1)S(1)}, u32[]{:S(2)}, u32[]{:S(2)}) collective-permute-start(bf16[5,128,128]{2,1,0:T(8,128)(2,1)S(1)} %get-tuple-element.9), channel_id=1, source_target_pairs={{0,8},{8,16},{16,24},{24,0},{32,40},{40,48},{48,56},{56,32},{64,72... | collective-permute-start | bytes 491528 | tf_op jit(solution)/shard_map/ppermute | solution.py:16
  21.6 1.1 collective-permute-start.5
  22.7 2.2 %collective-permute-start.6 = (bf16[5,128,128]{2,1,0:T(8,128)(2,1)S(1)}, bf16[5,128,128]{2,1,0:T(8,128)(2,1)S(1)}, u32[]{:S(2)}, u32[]{:S(2)}) collective-permute-start(bf16[5,128,128]{2,1,0:T(8,128)(2,1)S(1)} %get-tuple-element.9), channel_id=1, source_target_pairs={{0,24},{8,0},{16,8},{24,16},{32,56},{40,32},{48,40},{56,48},{64,88... | collective-permute-start | bytes 491528 | tf_op jit(solution)/shard_map/ppermute | solution.py:16
  24.9 2.8 %fusion.4 = f32[128,640]{1,0:T(8,128)S(1)} fusion(bf16[2560,640]{1,0:T(8,128)(2,1)} %param.6, bf16[1,128,5120]{2,1,0:T(8,128)(2,1)} %param.5, s32[]{:T(128)S(6)} %select_n.206), kind=kOutput, calls=%fused_computation.6 | convolution fusion | flops 419430400 | bytes 4259844 | tf_op jit(solution)/shard_map/dot_general | solution.py:64
  27.7 0.0 collective-permute-done.4
  27.7 2.5 %collective-permute-done.5 = bf16[5,128,128]{2,1,0:T(8,128)(2,1)S(1)} collective-permute-done((bf16[5,128,128]{2,1,0:T(8,128)(2,1)S(1)}, bf16[5,128,128]{2,1,0:T(8,128)(2,1)S(1)}, u32[]{:S(2)}, u32[]{:S(2)}) %collective-permute-start.5) | collective-permute-done | bytes 163872 | tf_op jit(solution)/shard_map/ppermute | solution.py:16
  30.2 1.6 %collective-permute-done.6 = bf16[5,128,128]{2,1,0:T(8,128)(2,1)S(1)} collective-permute-done((bf16[5,128,128]{2,1,0:T(8,128)(2,1)S(1)}, bf16[5,128,128]{2,1,0:T(8,128)(2,1)S(1)}, u32[]{:S(2)}, u32[]{:S(2)}) %collective-permute-start.6) | collective-permute-done | bytes 163872 | tf_op jit(solution)/shard_map/ppermute | solution.py:16
  31.8 0.1 fusion.32
  31.9 1.7 %collective-permute-start.7 = (bf16[5,128,128]{2,1,0:T(8,128)(2,1)S(1)}, bf16[5,128,128]{2,1,0:T(8,128)(2,1)S(1)}, u32[]{:S(2)}, u32[]{:S(2)}) collective-permute-start(bf16[5,128,128]{2,1,0:T(8,128)(2,1)S(1)} %fusion.32), channel_id=1, source_target_pairs={{0,32},{8,40},{16,48},{24,56},{32,64},{40,72},{48,80},{56,88},{64,... | collective-permute-start | bytes 491528 | tf_op jit(solution)/shard_map/ppermute | solution.py:16
  33.6 1.6 %collective-permute-start.8 = (bf16[5,128,128]{2,1,0:T(8,128)(2,1)S(1)}, bf16[5,128,128]{2,1,0:T(8,128)(2,1)S(1)}, u32[]{:S(2)}, u32[]{:S(2)}) collective-permute-start(bf16[5,128,128]{2,1,0:T(8,128)(2,1)S(1)} %fusion.32), channel_id=1, source_target_pairs={{0,64},{8,72},{16,80},{24,88},{32,96},{40,104},{48,112},{56,120},{... | collective-permute-start | bytes 491528 | tf_op jit(solution)/shard_map/ppermute | solution.py:16
  35.1 1.8 %collective-permute-start.9 = (bf16[5,128,128]{2,1,0:T(8,128)(2,1)S(1)}, bf16[5,128,128]{2,1,0:T(8,128)(2,1)S(1)}, u32[]{:S(2)}, u32[]{:S(2)}) collective-permute-start(bf16[5,128,128]{2,1,0:T(8,128)(2,1)S(1)} %fusion.32), channel_id=1, source_target_pairs={{0,96},{8,104},{16,112},{24,120},{32,0},{40,8},{48,16},{56,24},{64... | collective-permute-start | bytes 491528 | tf_op jit(solution)/shard_map/ppermute | solution.py:16
  36.9 1.8 %fusion.39 = f32[128,640]{1,0:T(8,128)S(1)} fusion(bf16[128,2560]{1,0:T(8,128)(2,1)} %collective-permute-done, bf16[2560,640]{1,0:T(8,128)(2,1)S(1)} %copy-done.4), kind=kOutput, calls=%fused_computation.66 | convolution fusion | flops 419430400 | bytes 4259840 | tf_op jit(solution)/shard_map/dot_general | solution.py:63
  38.7 0.1 collective-permute-start.2
  38.8 0.0 collective-permute-done.7
  38.8 3.2 %collective-permute-done.8 = bf16[5,128,128]{2,1,0:T(8,128)(2,1)S(1)} collective-permute-done((bf16[5,128,128]{2,1,0:T(8,128)(2,1)S(1)}, bf16[5,128,128]{2,1,0:T(8,128)(2,1)S(1)}, u32[]{:S(2)}, u32[]{:S(2)}) %collective-permute-start.8) | collective-permute-done | bytes 163872 | tf_op jit(solution)/shard_map/ppermute | solution.py:16
  42.0 1.8 %collective-permute-done.9 = bf16[5,128,128]{2,1,0:T(8,128)(2,1)S(1)} collective-permute-done((bf16[5,128,128]{2,1,0:T(8,128)(2,1)S(1)}, bf16[5,128,128]{2,1,0:T(8,128)(2,1)S(1)}, u32[]{:S(2)}, u32[]{:S(2)}) %collective-permute-start.9) | collective-permute-done | bytes 163872 | tf_op jit(solution)/shard_map/ppermute | solution.py:16
  43.8 0.8 fusion.20
  44.6 9.0 %collective-permute-start.10 = (bf16[5,128,128]{2,1,0:T(8,128)(2,1)}, bf16[5,128,128]{2,1,0:T(8,128)(2,1)}, u32[]{:S(2)}, u32[]{:S(2)}) collective-permute-start(bf16[5,128,128]{2,1,0:T(8,128)(2,1)} %fusion.20), channel_id=1, source_target_pairs={{0,128},{8,136},{16,144},{24,152},{32,160},{40,168},{48,176},{56,1... | collective-permute-start | bytes 491528 | tf_op jit(solution)/shard_map/ppermute | solution.py:16
  53.6 0.0 collective-permute-done.2
  53.6 0.8 multiply_convert_fusion.2
  54.4 1.7 %copy.12 = bf16[128,640]{0,1:T(8,128)(2,1)} copy(bf16[128,640]{1,0:T(8,128)(2,1)} %multiply_convert_fusion.2) | data formatting | bytes 327680 | tf_op jit(solution)/shard_map/convert_element_type | solution.py:68
  56.1 0.1 collective-permute-done.10
  56.2 2.7 %fusion.15 = f32[5,128,128]{2,1,0:T(8,128)} fusion(bf16[128,5,128]{0,2,1:T(8,128)(2,1)} %bitcast.42, bf16[5,128,128]{2,1,0:T(8,128)(2,1)} %copy-done.6, bf16[5,128,128]{2,1,0:T(8,128)(2,1)} %copy-done.7, bf16[5,128,128]{2,1,0:T(8,128)(2,1)} %copy-done.8, bf16[5,128,128]{2,1,0:T(8,128)(2,1)} %copy-done.9, bf16[5,128,128]{2,1,0:T(8,128)(2,1)} %copy-done.10, ...), kind=kOutput, calls=%fused_computation.37 | convolution fusion | flops 127385600 | bytes 1638406 | tf_op jit(solution)/shard_map/thd,hde->the/dot_general | solution.py:79
  58.9 2.3 %multiply_reduce_fusion = (f32[128,5]{0,1:T(8,128)S(1)}, f32[128,5,128]{0,2,1:T(8,128)}) fusion(f32[5,128,128]{2,1,0:T(8,128)} %fusion.15, bf16[128,5,128]{0,2,1:T(8,128)(2,1)S(1)} %bitcast.39, bf16[128,5,128]{0,2,1:T(8,128)(2,1)} %bitcast.43, bf16[128,5,128]{0,2,1:T(8,128)(2,1)} %bitcast.41, f32[128,128]{1,0:T(8,128)S(1)} %fusion.31), kind=kOutput, calls=%fused_computation.43 | convolution fusion | flops 42352000 | bytes 1214976 | tf_op jit(solution)/shard_map/hts,shd->thd/dot_general | solution.py:78
  61.2 1.0 multiply_convert_fusion
  62.2 2.6 %fusion.41 = f32[128,2560]{1,0:T(8,128)S(1)} fusion(bf16[128,640]{0,1:T(8,128)(2,1)S(1)} %bitcast.36, bf16[640,2560]{1,0:T(8,128)(2,1)} %param.9), kind=kOutput, calls=%fused_computation.68 | convolution fusion | flops 419430400 | bytes 4751360 | tf_op jit(solution)/shard_map/dot_general | solution.py:87
  64.9 0.0 collective-permute-done.11
  64.9 3.1 %fusion.42 = f32[128,2560]{1,0:T(8,128)S(1)} fusion(bf16[128,640]{0,1:T(8,128)(2,1)S(1)} %bitcast.37, bf16[640,2560]{1,0:T(8,128)(2,1)} %collective-permute-done.11), kind=kOutput, calls=%fused_computation.69 | convolution fusion | flops 419430400 | bytes 4751360 | tf_op jit(solution)/shard_map/dot_general | solution.py:88
  68.0 1.2 select_convert_fusion.1
  69.2 0.1 copy-done.2
  69.3 7.2 %collective-permute-start.12 = (bf16[128,1280]{1,0:T(8,128)(2,1)}, bf16[128,1280]{1,0:T(8,128)(2,1)}, u32[]{:S(2)}, u32[]{:S(2)}) collective-permute-start(bf16[128,1280]{1,0:T(8,128)(2,1)} %get-tuple-element.7), channel_id=1, source_target_pairs={{0,1},{4,5},{8,9},{12,13},{16,17},{20,21},{24,25},{28,29},{32,33},... | collective-permute-start | bytes 983048 | tf_op jit(solution)/shard_map/ppermute | solution.py:108
  76.4 1.4 %collective-permute-start.15 = (bf16[128,1280]{1,0:T(8,128)(2,1)}, bf16[128,1280]{1,0:T(8,128)(2,1)}, u32[]{:S(2)}, u32[]{:S(2)}) collective-permute-start(bf16[128,1280]{1,0:T(8,128)(2,1)} %get-tuple-element.8), channel_id=1, source_target_pairs={{3,2},{7,6},{11,10},{15,14},{19,18},{23,22},{27,26},{31,30},{35,34... | collective-permute-start | bytes 983048 | tf_op jit(solution)/shard_map/ppermute | solution.py:109
  77.8 4.4 %collective-permute-done.12 = bf16[128,1280]{1,0:T(8,128)(2,1)} collective-permute-done((bf16[128,1280]{1,0:T(8,128)(2,1)}, bf16[128,1280]{1,0:T(8,128)(2,1)}, u32[]{:S(2)}, u32[]{:S(2)}) %collective-permute-start.12) | collective-permute-done | bytes 327712 | tf_op jit(solution)/shard_map/ppermute | solution.py:108
  82.2 2.2 %add_convert_fusion.4 = bf16[128,1280]{1,0:T(8,128)(2,1)} fusion(bf16[128,1280]{1,0:T(8,128)(2,1)} %collective-permute-done.12, f32[128,2560]{1,0:T(8,128)} %copy-done.2, s32[]{:T(128)S(6)} %select_n.240, f32[128,2560]{1,0:T(8,128)} %copy-done.1, pred[]{:T(512)S(6)} %eq.39), kind=kLoop, calls=%fused_computation.15 | loop fusion | flops 655360 | bytes 1966085 | tf_op jit(solution)/shard_map/convert_element_type | solution.py:104
  84.4 5.1 %collective-permute-start.13 = (bf16[128,1280]{1,0:T(8,128)(2,1)}, bf16[128,1280]{1,0:T(8,128)(2,1)}, u32[]{:S(2)}, u32[]{:S(2)}) collective-permute-start(bf16[128,1280]{1,0:T(8,128)(2,1)} %add_convert_fusion.4), channel_id=1, source_target_pairs={{0,1},{1,2},{4,5},{5,6},{8,9},{9,10},{12,13},{13,14},{16,17},{17,1... | collective-permute-start | bytes 983048 | tf_op jit(solution)/shard_map/ppermute | solution.py:108
  89.6 0.0 collective-permute-done.15
  89.6 4.9 %collective-permute-done.13 = bf16[128,1280]{1,0:T(8,128)(2,1)} collective-permute-done((bf16[128,1280]{1,0:T(8,128)(2,1)}, bf16[128,1280]{1,0:T(8,128)(2,1)}, u32[]{:S(2)}, u32[]{:S(2)}) %collective-permute-start.13) | collective-permute-done | bytes 327712 | tf_op jit(solution)/shard_map/ppermute | solution.py:108
  94.5 2.9 %add_convert_fusion.3 = (bf16[128,1280]{1,0:T(8,128)(2,1)}, bf16[128,1280]{1,0:T(8,128)(2,1)}) fusion(bf16[128,1280]{1,0:T(8,128)(2,1)} %collective-permute-done.13, f32[128,2560]{1,0:T(8,128)} %copy-done.2, s32[]{:T(128)S(6)} %select_n.235, f32[128,2560]{1,0:T(8,128)} %copy-done.1, pred[]{:T(512)S(6)} %eq.38, bf16[128,1280]{1,0:T(8,128)(2,1)} %collective-permute-done.15, ...), kind=kLoop, calls=%fused_computation.14 | loop fusion | flops 1310720 | bytes 3932170 | tf_op jit(solution)/shard_map/convert_element_type | solution.py:104
  97.4 1.4 %collective-permute-start.16 = (bf16[128,1280]{1,0:T(8,128)(2,1)}, bf16[128,1280]{1,0:T(8,128)(2,1)}, u32[]{:S(2)}, u32[]{:S(2)}) collective-permute-start(bf16[128,1280]{1,0:T(8,128)(2,1)} %get-tuple-element.6), channel_id=1, source_target_pairs={{2,1},{3,2},{6,5},{7,6},{10,9},{11,10},{14,13},{15,14},{18,17},{19... | collective-permute-start | bytes 983048 | tf_op jit(solution)/shard_map/ppermute | solution.py:109
  98.8 5.2 %collective-permute-start.14 = (bf16[128,1280]{1,0:T(8,128)(2,1)}, bf16[128,1280]{1,0:T(8,128)(2,1)}, u32[]{:S(2)}, u32[]{:S(2)}) collective-permute-start(bf16[128,1280]{1,0:T(8,128)(2,1)} %get-tuple-element.5), channel_id=1, source_target_pairs={{0,1},{1,2},{2,3},{4,5},{5,6},{6,7},{8,9},{9,10},{10,11},{12,13},{... | collective-permute-start | bytes 983048 | tf_op jit(solution)/shard_map/ppermute | solution.py:108
  103.9 0.0 collective-permute-done.16
  103.9 2.2 %add_convert_fusion.1 = bf16[128,1280]{1,0:T(8,128)(2,1)} fusion(bf16[128,1280]{1,0:T(8,128)(2,1)} %collective-permute-done.16, f32[128,2560]{1,0:T(8,128)} %copy-done.2, s32[]{:T(128)S(6)} %select_n.250, f32[128,2560]{1,0:T(8,128)} %copy-done.1, pred[]{:T(512)S(6)} %eq.41), kind=kLoop, calls=%fused_computation.11 | loop fusion | flops 655360 | bytes 1966085 | tf_op jit(solution)/shard_map/convert_element_type | solution.py:105
  106.1 1.3 %collective-permute-start.17 = (bf16[128,1280]{1,0:T(8,128)(2,1)}, bf16[128,1280]{1,0:T(8,128)(2,1)}, u32[]{:S(2)}, u32[]{:S(2)}) collective-permute-start(bf16[128,1280]{1,0:T(8,128)(2,1)} %add_convert_fusion.1), channel_id=1, source_target_pairs={{1,0},{2,1},{3,2},{5,4},{6,5},{7,6},{9,8},{10,9},{11,10},{13,12},{... | collective-permute-start | bytes 983048 | tf_op jit(solution)/shard_map/ppermute | solution.py:109
  107.4 0.7 collective-permute-done.14
  108.1 10.6 %collective-permute-done.17 = bf16[128,1280]{1,0:T(8,128)(2,1)} collective-permute-done((bf16[128,1280]{1,0:T(8,128)(2,1)}, bf16[128,1280]{1,0:T(8,128)(2,1)}, u32[]{:S(2)}, u32[]{:S(2)}) %collective-permute-start.17) | collective-permute-done | bytes 327712 | tf_op jit(solution)/shard_map/ppermute | solution.py:109
  118.7 2.3 %fusion.21 = bf16[1,128,1280]{2,1,0:T(8,128)(2,1)} fusion(bf16[128,1280]{1,0:T(8,128)(2,1)} %collective-permute-done.17, bf16[128,1280]{1,0:T(8,128)(2,1)} %collective-permute-done.14, f32[128,2560]{1,0:T(8,128)} %copy-done.2, s32[]{:T(128)S(6)} %select_n.230, f32[128,2560]{1,0:T(8,128)} %copy-done.1, pred[]{:T(512)S(6)} %eq.37), kind=kLoop, calls=%fused_computation.41 | loop fusion | flops 983040 | bytes 2293765 | tf_op jit(solution)/shard_map/reshape | solution.py:111
  (24 shorter events, 0.1 us)
Async XLA Ops:
  0.0 2.6 %copy-start = (bf16[2560,640]{1,0:T(8,128)(2,1)S(1)}, bf16[2560,640]{1,0:T(8,128)(2,1)}, u32[]{:S(2)}) copy-start(bf16[2560,640]{1,0:T(8,128)(2,1)} %param.8) | copy-start | bytes 9830404
  2.1 3.2 %collective-permute-start = (bf16[128,2560]{1,0:T(8,128)(2,1)}, bf16[128,2560]{1,0:T(8,128)(2,1)}, u32[]{:S(2)}, u32[]{:S(2)}) collective-permute-start(bf16[128,2560]{1,0:T(8,128)(2,1)} %dynamic-slice_bitcast_fusion), channel_id=1, source_target_pairs={{0,4},{4,0},{1,5},{5,1},{2,6},{6,2},{3,7},{7,3},{8,12},{12,8},{9,1... | collective-permute-start | bytes 1966088 | tf_op jit(solution)/shard_map/ppermute | solution.py:12
  2.1 62.7 %collective-permute-start.11 = (bf16[640,2560]{1,0:T(8,128)(2,1)}, bf16[640,2560]{1,0:T(8,128)(2,1)}, u32[]{:S(2)}, u32[]{:S(2)}) collective-permute-start(bf16[640,2560]{1,0:T(8,128)(2,1)} %param.9), channel_id=1, source_target_pairs={{0,4},{4,0},{1,5},{5,1},{2,6},{6,2},{3,7},{7,3},{8,12},{12,8},{9,1... | collective-permute-start | bytes 9830408 | tf_op jit(solution)/shard_map/ppermute | solution.py:12
  2.6 5.3 %copy-start.3 = (bf16[2560,640]{1,0:T(8,128)(2,1)S(1)}, bf16[2560,640]{1,0:T(8,128)(2,1)}, u32[]{:S(2)}) copy-start(bf16[2560,640]{1,0:T(8,128)(2,1)} %param.7) | copy-start | bytes 9830404
  5.3 5.7 %copy-start.5 = (bf16[1,128,5120]{2,1,0:T(8,128)(2,1)S(1)}, bf16[1,128,5120]{2,1,0:T(8,128)(2,1)}, u32[]{:S(2)}) copy-start(bf16[1,128,5120]{2,1,0:T(8,128)(2,1)} %param.5) | copy-start | bytes 3932164
  7.9 4.5 %collective-permute-start.1 = (f32[128,640]{1,0:T(8,128)}, f32[128,640]{1,0:T(8,128)}, u32[]{:S(2)}, u32[]{:S(2)}) collective-permute-start(f32[128,640]{1,0:T(8,128)} %fusion.38), channel_id=1, source_target_pairs={{0,4},{4,0},{1,5},{5,1},{2,6},{6,2},{3,7},{7,3},{8,12},{12,8},{9,1... | collective-permute-start | bytes 983048 | tf_op jit(solution)/shard_map/ppermute | solution.py:12
  10.4 4.8 %collective-permute-start.3 = (f32[128,640]{1,0:T(8,128)}, f32[128,640]{1,0:T(8,128)}, u32[]{:S(2)}, u32[]{:S(2)}) collective-permute-start(f32[128,640]{1,0:T(8,128)} %fusion.40), channel_id=1, source_target_pairs={{0,4},{4,0},{1,5},{5,1},{2,6},{6,2},{3,7},{7,3},{8,12},{12,8},{9,1... | collective-permute-start | bytes 983048 | tf_op jit(solution)/shard_map/ppermute | solution.py:12
  18.7 18.2 %copy-start.4 = (bf16[2560,640]{1,0:T(8,128)(2,1)S(1)}, bf16[2560,640]{1,0:T(8,128)(2,1)}, u32[]{:S(2)}) copy-start(bf16[2560,640]{1,0:T(8,128)(2,1)} %param.6) | copy-start | bytes 9830404
  20.1 7.6 %collective-permute-start.4 = (bf16[5,128,128]{2,1,0:T(8,128)(2,1)S(1)}, bf16[5,128,128]{2,1,0:T(8,128)(2,1)S(1)}, u32[]{:S(2)}, u32[]{:S(2)}) collective-permute-start(bf16[5,128,128]{2,1,0:T(8,128)(2,1)S(1)} %get-tuple-element.9), channel_id=1, source_target_pairs={{0,8},{8,16},{16,24},{24,0},{32,40},{40,48},{48,56},{56,32},{64,72... | collective-permute-start | bytes 491528 | tf_op jit(solution)/shard_map/ppermute | solution.py:16
  21.6 8.6 %collective-permute-start.5 = (bf16[5,128,128]{2,1,0:T(8,128)(2,1)S(1)}, bf16[5,128,128]{2,1,0:T(8,128)(2,1)S(1)}, u32[]{:S(2)}, u32[]{:S(2)}) collective-permute-start(bf16[5,128,128]{2,1,0:T(8,128)(2,1)S(1)} %get-tuple-element.9), channel_id=1, source_target_pairs={{0,16},{8,24},{16,0},{24,8},{32,48},{40,56},{48,32},{56,40},{64,80... | collective-permute-start | bytes 491528 | tf_op jit(solution)/shard_map/ppermute | solution.py:16
  22.7 9.1 %collective-permute-start.6 = (bf16[5,128,128]{2,1,0:T(8,128)(2,1)S(1)}, bf16[5,128,128]{2,1,0:T(8,128)(2,1)S(1)}, u32[]{:S(2)}, u32[]{:S(2)}) collective-permute-start(bf16[5,128,128]{2,1,0:T(8,128)(2,1)S(1)} %get-tuple-element.9), channel_id=1, source_target_pairs={{0,24},{8,0},{16,8},{24,16},{32,56},{40,32},{48,40},{56,48},{64,88... | collective-permute-start | bytes 491528 | tf_op jit(solution)/shard_map/ppermute | solution.py:16
  27.7 16.9 %copy-start.6 = (bf16[5,128,128]{2,1,0:T(8,128)(2,1)}, bf16[5,128,128]{2,1,0:T(8,128)(2,1)S(1)}, u32[]{:S(2)}) copy-start(bf16[5,128,128]{2,1,0:T(8,128)(2,1)S(1)} %collective-permute-done.4) | copy-start | bytes 491524
  30.2 14.4 %copy-start.7 = (bf16[5,128,128]{2,1,0:T(8,128)(2,1)}, bf16[5,128,128]{2,1,0:T(8,128)(2,1)S(1)}, u32[]{:S(2)}) copy-start(bf16[5,128,128]{2,1,0:T(8,128)(2,1)S(1)} %collective-permute-done.5) | copy-start | bytes 491524
  31.8 12.8 %copy-start.8 = (bf16[5,128,128]{2,1,0:T(8,128)(2,1)}, bf16[5,128,128]{2,1,0:T(8,128)(2,1)S(1)}, u32[]{:S(2)}) copy-start(bf16[5,128,128]{2,1,0:T(8,128)(2,1)S(1)} %collective-permute-done.6) | copy-start | bytes 491524
  31.9 6.9 %collective-permute-start.7 = (bf16[5,128,128]{2,1,0:T(8,128)(2,1)S(1)}, bf16[5,128,128]{2,1,0:T(8,128)(2,1)S(1)}, u32[]{:S(2)}, u32[]{:S(2)}) collective-permute-start(bf16[5,128,128]{2,1,0:T(8,128)(2,1)S(1)} %fusion.32), channel_id=1, source_target_pairs={{0,32},{8,40},{16,48},{24,56},{32,64},{40,72},{48,80},{56,88},{64,... | collective-permute-start | bytes 491528 | tf_op jit(solution)/shard_map/ppermute | solution.py:16
  33.6 8.4 %collective-permute-start.8 = (bf16[5,128,128]{2,1,0:T(8,128)(2,1)S(1)}, bf16[5,128,128]{2,1,0:T(8,128)(2,1)S(1)}, u32[]{:S(2)}, u32[]{:S(2)}) collective-permute-start(bf16[5,128,128]{2,1,0:T(8,128)(2,1)S(1)} %fusion.32), channel_id=1, source_target_pairs={{0,64},{8,72},{16,80},{24,88},{32,96},{40,104},{48,112},{56,120},{... | collective-permute-start | bytes 491528 | tf_op jit(solution)/shard_map/ppermute | solution.py:16
  35.1 8.6 %collective-permute-start.9 = (bf16[5,128,128]{2,1,0:T(8,128)(2,1)S(1)}, bf16[5,128,128]{2,1,0:T(8,128)(2,1)S(1)}, u32[]{:S(2)}, u32[]{:S(2)}) collective-permute-start(bf16[5,128,128]{2,1,0:T(8,128)(2,1)S(1)} %fusion.32), channel_id=1, source_target_pairs={{0,96},{8,104},{16,112},{24,120},{32,0},{40,8},{48,16},{56,24},{64... | collective-permute-start | bytes 491528 | tf_op jit(solution)/shard_map/ppermute | solution.py:16
  38.7 14.9 %collective-permute-start.2 = (f32[128,640]{1,0:T(8,128)S(1)}, f32[128,640]{1,0:T(8,128)S(1)}, u32[]{:S(2)}, u32[]{:S(2)}) collective-permute-start(f32[128,640]{1,0:T(8,128)S(1)} %fusion.39), channel_id=1, source_target_pairs={{0,4},{4,0},{1,5},{5,1},{2,6},{6,2},{3,7},{7,3},{8,12},{12,8},{9,1... | collective-permute-start | bytes 983048 | tf_op jit(solution)/shard_map/ppermute | solution.py:12
  38.8 14.8 %copy-start.9 = (bf16[5,128,128]{2,1,0:T(8,128)(2,1)}, bf16[5,128,128]{2,1,0:T(8,128)(2,1)S(1)}, u32[]{:S(2)}) copy-start(bf16[5,128,128]{2,1,0:T(8,128)(2,1)S(1)} %collective-permute-done.7) | copy-start | bytes 491524
  42.0 11.6 %copy-start.10 = (bf16[5,128,128]{2,1,0:T(8,128)(2,1)}, bf16[5,128,128]{2,1,0:T(8,128)(2,1)S(1)}, u32[]{:S(2)}) copy-start(bf16[5,128,128]{2,1,0:T(8,128)(2,1)S(1)} %collective-permute-done.8) | copy-start | bytes 491524
  43.8 9.9 %copy-start.11 = (bf16[5,128,128]{2,1,0:T(8,128)(2,1)}, bf16[5,128,128]{2,1,0:T(8,128)(2,1)S(1)}, u32[]{:S(2)}) copy-start(bf16[5,128,128]{2,1,0:T(8,128)(2,1)S(1)} %collective-permute-done.9) | copy-start | bytes 491524
  44.6 11.6 %collective-permute-start.10 = (bf16[5,128,128]{2,1,0:T(8,128)(2,1)}, bf16[5,128,128]{2,1,0:T(8,128)(2,1)}, u32[]{:S(2)}, u32[]{:S(2)}) collective-permute-start(bf16[5,128,128]{2,1,0:T(8,128)(2,1)} %fusion.20), channel_id=1, source_target_pairs={{0,128},{8,136},{16,144},{24,152},{32,160},{40,168},{48,176},{56,1... | collective-permute-start | bytes 491528 | tf_op jit(solution)/shard_map/ppermute | solution.py:16
  64.8 4.3 %copy-start.1 = (f32[128,2560]{1,0:T(8,128)}, f32[128,2560]{1,0:T(8,128)S(1)}, u32[]{:S(2)}) copy-start(f32[128,2560]{1,0:T(8,128)S(1)} %fusion.41) | copy-start | bytes 3932164
  68.0 1.3 %copy-start.2 = (f32[128,2560]{1,0:T(8,128)}, f32[128,2560]{1,0:T(8,128)S(1)}, u32[]{:S(2)}) copy-start(f32[128,2560]{1,0:T(8,128)S(1)} %fusion.42) | copy-start | bytes 3932164
  69.3 13.0 %collective-permute-start.12 = (bf16[128,1280]{1,0:T(8,128)(2,1)}, bf16[128,1280]{1,0:T(8,128)(2,1)}, u32[]{:S(2)}, u32[]{:S(2)}) collective-permute-start(bf16[128,1280]{1,0:T(8,128)(2,1)} %get-tuple-element.7), channel_id=1, source_target_pairs={{0,1},{4,5},{8,9},{12,13},{16,17},{20,21},{24,25},{28,29},{32,33},... | collective-permute-start | bytes 983048 | tf_op jit(solution)/shard_map/ppermute | solution.py:108
  76.4 13.1 %collective-permute-start.15 = (bf16[128,1280]{1,0:T(8,128)(2,1)}, bf16[128,1280]{1,0:T(8,128)(2,1)}, u32[]{:S(2)}, u32[]{:S(2)}) collective-permute-start(bf16[128,1280]{1,0:T(8,128)(2,1)} %get-tuple-element.8), channel_id=1, source_target_pairs={{3,2},{7,6},{11,10},{15,14},{19,18},{23,22},{27,26},{31,30},{35,34... | collective-permute-start | bytes 983048 | tf_op jit(solution)/shard_map/ppermute | solution.py:109
  84.4 10.1 %collective-permute-start.13 = (bf16[128,1280]{1,0:T(8,128)(2,1)}, bf16[128,1280]{1,0:T(8,128)(2,1)}, u32[]{:S(2)}, u32[]{:S(2)}) collective-permute-start(bf16[128,1280]{1,0:T(8,128)(2,1)} %add_convert_fusion.4), channel_id=1, source_target_pairs={{0,1},{1,2},{4,5},{5,6},{8,9},{9,10},{12,13},{13,14},{16,17},{17,1... | collective-permute-start | bytes 983048 | tf_op jit(solution)/shard_map/ppermute | solution.py:108
  97.4 6.5 %collective-permute-start.16 = (bf16[128,1280]{1,0:T(8,128)(2,1)}, bf16[128,1280]{1,0:T(8,128)(2,1)}, u32[]{:S(2)}, u32[]{:S(2)}) collective-permute-start(bf16[128,1280]{1,0:T(8,128)(2,1)} %get-tuple-element.6), channel_id=1, source_target_pairs={{2,1},{3,2},{6,5},{7,6},{10,9},{11,10},{14,13},{15,14},{18,17},{19... | collective-permute-start | bytes 983048 | tf_op jit(solution)/shard_map/ppermute | solution.py:109
  98.8 9.3 %collective-permute-start.14 = (bf16[128,1280]{1,0:T(8,128)(2,1)}, bf16[128,1280]{1,0:T(8,128)(2,1)}, u32[]{:S(2)}, u32[]{:S(2)}) collective-permute-start(bf16[128,1280]{1,0:T(8,128)(2,1)} %get-tuple-element.5), channel_id=1, source_target_pairs={{0,1},{1,2},{2,3},{4,5},{5,6},{6,7},{8,9},{9,10},{10,11},{12,13},{... | collective-permute-start | bytes 983048 | tf_op jit(solution)/shard_map/ppermute | solution.py:108
  106.1 12.6 %collective-permute-start.17 = (bf16[128,1280]{1,0:T(8,128)(2,1)}, bf16[128,1280]{1,0:T(8,128)(2,1)}, u32[]{:S(2)}, u32[]{:S(2)}) collective-permute-start(bf16[128,1280]{1,0:T(8,128)(2,1)} %add_convert_fusion.1), channel_id=1, source_target_pairs={{1,0},{2,1},{3,2},{5,4},{6,5},{7,6},{9,8},{10,9},{11,10},{13,12},{... | collective-permute-start | bytes 983048 | tf_op jit(solution)/shard_map/ppermute | solution.py:109

commit v2 on v1

--- a/solution.py
+++ b/solution.py
@@ -17,13 +17,11 @@
 
 
 def prefix_over_seq(state, seq_size):
-    nx, ny = 4, 4
-    nz = seq_size // (nx * ny)
+    nx = 4
+    rows = seq_size // nx
     i = lax.axis_index("seq")
-    x = i % nx
-    y = (i // nx) % ny
 
-    def along(value, stride, size, pos):
+    def gather(value, stride, size, pos):
         sent = value.astype(BF16)
         before = jnp.zeros_like(value)
         total = value
@@ -37,14 +35,9 @@
             total = total + got
         return before, total
 
-    ex, row_total = along(state, 1, nx, x)
-    ey, plane_total = along(row_total, nx, ny, y)
-    ez = jnp.zeros_like(state)
-    if nz > 1:
-        plane = nx * ny
-        zpairs = [(j, j + plane) for j in range(seq_size - plane)]
-        ez = shifted(plane_total.astype(BF16), "seq", zpairs).astype(F32)
-    return ex + ey + ez
+    ex, row_total = gather(state, 1, nx, i % nx)
+    erow, _ = gather(row_total, nx, rows, i // nx)
+    return ex + erow
 
 
 def shards(seq_size, tokens, w_query, w_key, w_value, w_output):
@@ -84,30 +77,35 @@
     normed = (attended * scale).reshape(tok_count, width_local).astype(BF16)
 
     w_other = swap_cores(w_output)
-    y_mine = jnp.dot(normed, w_output, preferred_element_type=F32)
-    y_other = jnp.dot(normed, w_other, preferred_element_type=F32)
-    quarter = y_mine.shape[1] // 2
+    quarter = w_output.shape[1] // 2
+    n = 4
+    h = lax.axis_index("head")
 
-    def block(q):
+    def weight_for(q):
         sub = q % 2
-        a = lax.dynamic_slice_in_dim(y_mine, sub * quarter, quarter, axis=1)
-        b = lax.dynamic_slice_in_dim(y_other, sub * quarter, quarter, axis=1)
+        a = lax.dynamic_slice_in_dim(w_output, sub * quarter, quarter, axis=1)
+        b = lax.dynamic_slice_in_dim(w_other, sub * quarter, quarter, axis=1)
         return jnp.where(q // 2 == c, a, b)
 
-    n = 4
-    h = lax.axis_index("head")
+    targets = [jnp.clip(h + n - s, 0, n - 1) for s in range(1, n)]
+    targets += [jnp.clip(h - n + s, 0, n - 1) for s in range(1, n)]
+    targets.append(h)
+    picked = lax.optimization_barrier([weight_for(q) for q in targets])
+    w_right, w_left, w_own = picked[: n - 1], picked[n - 1 : 2 * n - 2], picked[-1]
+
+    def block(wq):
+        return jnp.dot(normed, wq, preferred_element_type=F32)
+
     right = jnp.zeros((tok_count, quarter), F32)
     left = jnp.zeros((tok_count, quarter), F32)
     for s in range(1, n):
-        qr = jnp.clip(h + n - s, 0, n - 1)
-        ql = jnp.clip(h - n + s, 0, n - 1)
-        send_r = (block(qr) + right).astype(BF16)
-        send_l = (block(ql) + left).astype(BF16)
+        send_r = (block(w_right[s - 1]) + right).astype(BF16)
+        send_l = (block(w_left[s - 1]) + left).astype(BF16)
         rpairs = [(j, j + 1) for j in range(s) if j + 1 < n]
         lpairs = [(j, j - 1) for j in range(n - s, n) if j - 1 >= 0]
         right = lax.ppermute(send_r, "head", rpairs).astype(F32)
         left = lax.ppermute(send_l, "head", lpairs).astype(F32)
-    mixed = (block(h) + right + left).astype(BF16)
+    mixed = (block(w_own) + right + left).astype(BF16)
     return mixed.reshape(1, tok_count, quarter)
 
 

time: 122 us -> 127 us (1.041)
  waiting for transfers between devices: 29.8 us -> 35.2 us
  matrix products: 25.8 us -> 22.3 us
  starting transfers between devices: 41.5 us -> 43 us
    ppermute x7 -> x10, waiting for transfers between devices: 9.13 us -> 20.8 us  [shifted(): return lax.ppermute(x, axis, pairs)]
    select_n x0 -> x1, other arithmetic: none -> 10.6 us  [weight_for(): return jnp.where(q // 2 == c, a, b)]
    ppermute x7 -> x10, starting transfers between devices: 18.9 us -> 28.1 us  [shifted(): return lax.ppermute(x, axis, pairs)]
    convert_element_type x6 -> x3, other arithmetic: 9.35 us -> 0.86 us  [the longest x1 0.75 us: gather(): sent = value.astype(BF16)]
    ppermute x3, starting transfers between devices: 17.5 us -> 11.2 us  [shards(): right = lax.ppermute(send_r, 'head', rpairs).astype(F32)]
    ppermute x3, waiting for transfers between devices: 10.6 us -> 4.49 us  [shards(): left = lax.ppermute(send_l, 'head', lpairs).astype(F32)]
    dot_general x2 -> x7, matrix products: 5.72 us -> 3.21 us  [block(): return jnp.dot(normed, wq, preferred_element_type=F32)]
    dot_general x3, matrix products: 6.87 us -> 4.59 us  [shards(): own = jnp.dot(mine_cols, w, preferred_element_type=F32)]
  transfers between devices with their start and end apart: 18 -> 21, of which waited for: 9 -> 10; matrix products, arithmetic and copies ran while one was open for 31% -> 26% of each run, Pallas kernels for 0% -> 0%
where the time goes in v2:
time: 127 us; the launch traced here: 125 us
  starting transfers between devices  43 us (34%)
  waiting for transfers between devices  35.2 us (28%)
  matrix products  22.3 us (18%)
  other arithmetic  17.7 us (14%)
  local copies, waits for them, and re-layouts  6.66 us (5%)
    ppermute x10, starting transfers between devices, shifted(): return lax.ppermute(x, axis, pairs)  28.1 us
    ppermute x10, waiting for transfers between devices, shifted(): return lax.ppermute(x, axis, pairs)  20.8 us
    ppermute x3, starting transfers between devices, shards(): right = lax.ppermute(send_r, 'head', rpairs).astype(F32)  11.2 us
    select_n x1, other arithmetic, weight_for(): return jnp.where(q // 2 == c, a, b)  10.6 us
    ppermute x3, waiting for transfers between devices, shards(): right = lax.ppermute(send_r, 'head', rpairs).astype(F32)  9.74 us
    dot_general x3, matrix products, shards(): lent = swap_cores(jnp.dot(got_cols, w, preferred_element_type=F32))  8.09 us
    dot_general x3, matrix products, shards(): own = jnp.dot(mine_cols, w, preferred_element_type=F32)  4.59 us
    ppermute x3, waiting for transfers between devices, shards(): left = lax.ppermute(send_l, 'head', lpairs).astype(F32)  4.49 us
  transfers between devices with their start and end apart: 21, of which 10 were waited for; matrix products, arithmetic and copies ran while one was open for 26% of the time, Pallas kernels for 0%

profile of v2, /device:TPU:10, one launch (start us, length us, event | category | flops | bytes accessed | tf_op | source)
XLA Modules:
  0.0 125.0 jit_solution(1417083382605443615)
XLA Ops:
  0.0 2.1 %dynamic-slice_bitcast_fusion = bf16[128,2560]{1,0:T(8,128)(2,1)} fusion(bf16[1,128,5120]{2,1,0:T(8,128)(2,1)} %param.5, s32[]{:T(128)S(6)} %select_n.241), kind=kLoop, calls=%fused_computation.24 | loop fusion | bytes 1310724 | tf_op jit(solution)/shard_map/dynamic_slice | solution.py:52
  2.1 0.0 collective-permute-start
  2.1 0.5 collective-permute-start.14
  2.6 1.8 %fusion.6 = f32[128,640]{1,0:T(8,128)S(1)} fusion(bf16[2560,640]{1,0:T(8,128)(2,1)S(1)} %copy-done, bf16[1,128,5120]{2,1,0:T(8,128)(2,1)} %param.5, s32[]{:T(128)S(6)} %select_n.240), kind=kOutput, calls=%fused_computation.17 | convolution fusion | flops 419430400 | bytes 4259844 | tf_op jit(solution)/shard_map/dot_general | solution.py:57
  4.4 0.0 copy-start.1
  4.4 0.1 collective-permute-done
  4.6 1.9 %fusion.56 = f32[128,640]{1,0:T(8,128)S(1)} fusion(bf16[128,2560]{1,0:T(8,128)(2,1)} %collective-permute-done, bf16[2560,640]{1,0:T(8,128)(2,1)S(1)} %copy-done), kind=kOutput, calls=%fused_computation.85 | convolution fusion | flops 419430400 | bytes 4259840 | tf_op jit(solution)/shard_map/dot_general | solution.py:56
  6.5 0.0 copy-start.3
  6.5 0.2 collective-permute-start.1
  6.7 2.6 %fusion.58 = f32[128,640]{1,0:T(8,128)} fusion(bf16[128,2560]{1,0:T(8,128)(2,1)} %collective-permute-done, bf16[2560,640]{1,0:T(8,128)(2,1)S(1)} %copy-done.1), kind=kOutput, calls=%fused_computation.87 | convolution fusion | flops 419430400 | bytes 4259840 | tf_op jit(solution)/shard_map/dot_general | solution.py:56
  9.4 0.3 collective-permute-start.3
  9.6 1.4 %fusion.2 = f32[128,640]{1,0:T(8,128)} fusion(bf16[2560,640]{1,0:T(8,128)(2,1)S(1)} %copy-done.1, bf16[1,128,5120]{2,1,0:T(8,128)(2,1)S(1)} %copy-done.3, s32[]{:T(128)S(6)} %select_n.240), kind=kOutput, calls=%fused_computation.13 | convolution fusion | flops 419430400 | bytes 4259844 | tf_op jit(solution)/shard_map/dot_general | solution.py:57
  11.0 0.0 collective-permute-done.1
  11.0 0.7 add_convert_fusion.5
  11.7 1.1 copy.11
  12.8 1.8 %multiply_convert_fusion.1 = bf16[128,640]{1,0:T(8,128)(2,1)} fusion(f32[128,640]{1,0:T(8,128)} %fusion.2, f32[128,640]{1,0:T(8,128)} %collective-permute-done.3), kind=kLoop, calls=%fused_computation.62 | loop fusion | flops 491520 | bytes 819200 | tf_op jit(solution)/shard_map/convert_element_type | solution.py:62
  14.7 1.7 %copy.13 = bf16[128,640]{0,1:T(8,128)(2,1)} copy(bf16[128,640]{1,0:T(8,128)(2,1)} %multiply_convert_fusion.1) | data formatting | bytes 327680 | tf_op jit(solution)/shard_map/convert_element_type | solution.py:62
  16.4 1.2 fusion.55
  17.5 0.0 copy-start.2
  17.5 0.0 copy-start.4
  17.5 1.6 %collective-permute-start.4 = (bf16[5,128,128]{2,1,0:T(8,128)(2,1)S(1)}, bf16[5,128,128]{2,1,0:T(8,128)(2,1)S(1)}, u32[]{:S(2)}, u32[]{:S(2)}) collective-permute-start(bf16[5,128,128]{2,1,0:T(8,128)(2,1)S(1)} %get-tuple-element.26), channel_id=1, source_target_pairs={{0,8},{8,16},{16,24},{24,0},{32,40},{40,48},{48,56},{56,32},{64,72... | collective-permute-start | bytes 491528 | tf_op jit(solution)/shard_map/ppermute | solution.py:16
  19.1 1.1 collective-permute-start.5
  20.2 2.2 %collective-permute-start.6 = (bf16[5,128,128]{2,1,0:T(8,128)(2,1)S(1)}, bf16[5,128,128]{2,1,0:T(8,128)(2,1)S(1)}, u32[]{:S(2)}, u32[]{:S(2)}) collective-permute-start(bf16[5,128,128]{2,1,0:T(8,128)(2,1)S(1)} %get-tuple-element.26), channel_id=1, source_target_pairs={{0,24},{8,0},{16,8},{24,16},{32,56},{40,32},{48,40},{56,48},{64,88... | collective-permute-start | bytes 491528 | tf_op jit(solution)/shard_map/ppermute | solution.py:16
  22.4 3.5 %fusion.57 = f32[128,640]{1,0:T(8,128)} fusion(bf16[128,2560]{1,0:T(8,128)(2,1)} %collective-permute-done, bf16[2560,640]{1,0:T(8,128)(2,1)} %param.6), kind=kOutput, calls=%fused_computation.86 | convolution fusion | flops 419430400 | bytes 4259840 | tf_op jit(solution)/shard_map/dot_general | solution.py:56
  25.9 0.0 collective-permute-start.2
  25.9 1.8 %collective-permute-done.5 = bf16[5,128,128]{2,1,0:T(8,128)(2,1)S(1)} collective-permute-done((bf16[5,128,128]{2,1,0:T(8,128)(2,1)S(1)}, bf16[5,128,128]{2,1,0:T(8,128)(2,1)S(1)}, u32[]{:S(2)}, u32[]{:S(2)}) %collective-permute-start.5) | collective-permute-done | bytes 163872 | tf_op jit(solution)/shard_map/ppermute | solution.py:16
  27.7 1.8 %collective-permute-done.6 = bf16[5,128,128]{2,1,0:T(8,128)(2,1)S(1)} collective-permute-done((bf16[5,128,128]{2,1,0:T(8,128)(2,1)S(1)}, bf16[5,128,128]{2,1,0:T(8,128)(2,1)S(1)}, u32[]{:S(2)}, u32[]{:S(2)}) %collective-permute-start.6) | collective-permute-done | bytes 163872 | tf_op jit(solution)/shard_map/ppermute | solution.py:16
  29.6 0.8 fusion.16
  30.3 7.2 %collective-permute-start.10 = (bf16[5,128,128]{2,1,0:T(8,128)(2,1)}, bf16[5,128,128]{2,1,0:T(8,128)(2,1)}, u32[]{:S(2)}, u32[]{:S(2)}) collective-permute-start(bf16[5,128,128]{2,1,0:T(8,128)(2,1)} %fusion.16), channel_id=1, source_target_pairs={{0,128},{8,136},{16,144},{24,152},{32,160},{40,168},{48,176},{56,1... | collective-permute-start | bytes 491528 | tf_op jit(solution)/shard_map/ppermute | solution.py:16
  37.5 1.1 collective-permute-start.11
  38.6 0.9 collective-permute-start.12
  39.5 1.4 %fusion.4 = f32[128,640]{1,0:T(8,128)} fusion(bf16[2560,640]{1,0:T(8,128)(2,1)S(1)} %copy-done.2, bf16[1,128,5120]{2,1,0:T(8,128)(2,1)S(1)} %copy-done.4, s32[]{:T(128)S(6)} %select_n.240), kind=kOutput, calls=%fused_computation.15 | convolution fusion | flops 419430400 | bytes 4259844 | tf_op jit(solution)/shard_map/dot_general | solution.py:57
  41.0 8.0 %collective-permute-start.13 = (bf16[5,128,128]{2,1,0:T(8,128)(2,1)}, bf16[5,128,128]{2,1,0:T(8,128)(2,1)}, u32[]{:S(2)}, u32[]{:S(2)}) collective-permute-start(bf16[5,128,128]{2,1,0:T(8,128)(2,1)} %fusion.16), channel_id=1, source_target_pairs={{0,224},{8,232},{16,240},{24,248},{32,0},{40,8},{48,16},{56,24},{6... | collective-permute-start | bytes 491528 | tf_op jit(solution)/shard_map/ppermute | solution.py:16
  48.9 0.0 collective-permute-done.10
  48.9 6.7 %collective-permute-done.11 = bf16[5,128,128]{2,1,0:T(8,128)(2,1)} collective-permute-done((bf16[5,128,128]{2,1,0:T(8,128)(2,1)}, bf16[5,128,128]{2,1,0:T(8,128)(2,1)}, u32[]{:S(2)}, u32[]{:S(2)}) %collective-permute-start.11) | collective-permute-done | bytes 163872 | tf_op jit(solution)/shard_map/ppermute | solution.py:16
  55.7 2.8 %collective-permute-done.12 = bf16[5,128,128]{2,1,0:T(8,128)(2,1)} collective-permute-done((bf16[5,128,128]{2,1,0:T(8,128)(2,1)}, bf16[5,128,128]{2,1,0:T(8,128)(2,1)}, u32[]{:S(2)}, u32[]{:S(2)}) %collective-permute-start.12) | collective-permute-done | bytes 163872 | tf_op jit(solution)/shard_map/ppermute | solution.py:16
  58.4 6.1 %collective-permute-start.9 = (bf16[5,128,128]{2,1,0:T(8,128)(2,1)}, bf16[5,128,128]{2,1,0:T(8,128)(2,1)}, u32[]{:S(2)}, u32[]{:S(2)}) collective-permute-start(bf16[5,128,128]{2,1,0:T(8,128)(2,1)} %fusion.16), channel_id=1, source_target_pairs={{0,96},{8,104},{16,112},{24,120},{32,128},{40,136},{48,144},{56,15... | collective-permute-start | bytes 491528 | tf_op jit(solution)/shard_map/ppermute | solution.py:16
  64.6 1.9 %multiply_convert_fusion.2 = bf16[128,640]{1,0:T(8,128)(2,1)} fusion(f32[128,640]{1,0:T(8,128)} %fusion.4, f32[128,640]{1,0:T(8,128)} %collective-permute-done.2), kind=kLoop, calls=%fused_computation.63 | loop fusion | flops 491520 | bytes 819200 | tf_op jit(solution)/shard_map/convert_element_type | solution.py:61
  66.4 1.7 %copy.12 = bf16[128,640]{0,1:T(8,128)(2,1)} copy(bf16[128,640]{1,0:T(8,128)(2,1)} %multiply_convert_fusion.2) | data formatting | bytes 327680 | tf_op jit(solution)/shard_map/convert_element_type | solution.py:61
  68.1 7.7 %collective-permute-done.8 = bf16[5,128,128]{2,1,0:T(8,128)(2,1)} collective-permute-done((bf16[5,128,128]{2,1,0:T(8,128)(2,1)}, bf16[5,128,128]{2,1,0:T(8,128)(2,1)}, u32[]{:S(2)}, u32[]{:S(2)}) %collective-permute-start.8) | collective-permute-done | bytes 163872 | tf_op jit(solution)/shard_map/ppermute | solution.py:16
  75.8 3.0 %fusion.14 = f32[5,128,128]{2,1,0:T(8,128)} fusion(bf16[128,5,128]{0,2,1:T(8,128)(2,1)} %bitcast.57, bf16[5,128,128]{2,1,0:T(8,128)(2,1)} %copy-done.5, bf16[5,128,128]{2,1,0:T(8,128)(2,1)} %copy-done.6, bf16[5,128,128]{2,1,0:T(8,128)(2,1)} %copy-done.7, bf16[5,128,128]{2,1,0:T(8,128)(2,1)} %collective-permute-done.13, ...), kind=kOutput, calls=%fused_computation.37 | convolution fusion | flops 128204800 | bytes 2129930 | tf_op jit(solution)/shard_map/thd,hde->the/dot_general | solution.py:72
  78.8 2.3 %multiply_reduce_fusion = (f32[128,5]{0,1:T(8,128)S(1)}, f32[128,5,128]{0,2,1:T(8,128)}) fusion(f32[5,128,128]{2,1,0:T(8,128)} %fusion.14, bf16[128,5,128]{0,2,1:T(8,128)(2,1)S(1)} %bitcast.54, bf16[128,5,128]{0,2,1:T(8,128)(2,1)} %bitcast.58, bf16[128,5,128]{0,2,1:T(8,128)(2,1)} %bitcast.56, f32[128,128]{1,0:T(8,128)S(1)} %fusion.50), kind=kOutput, calls=%fused_computation.41 | convolution fusion | flops 42352000 | bytes 1214976 | tf_op jit(solution)/shard_map/hts,shd->thd/dot_general | solution.py:71
  81.1 1.0 multiply_convert_fusion
  82.1 10.6 %dynamic-slice_select_fusion = (bf16[640,1280]{1,0:T(8,128)(2,1)S(1)}, bf16[640,1280]{1,0:T(8,128)(2,1)S(1)}, bf16[640,1280]{1,0:T(8,128)(2,1)S(1)}, bf16[640,12...) fusion(bf16[640,2560]{1,0:T(8,128)(2,1)} %collective-permute-do, ...), kind=kLoop, calls=%fused_computation.2 | loop fusion | flops 5734400 | bytes 34406436 | tf_op jit(solution)/shard_map/jit(_where)/select_n | solution.py:88
  92.7 0.5 convolution_convert_fusion.1
  93.1 2.4 %collective-permute-start.15 = (bf16[128,1280]{1,0:T(8,128)(2,1)S(1)}, bf16[128,1280]{1,0:T(8,128)(2,1)S(1)}, u32[]{:S(2)}, u32[]{:S(2)}) collective-permute-start(bf16[128,1280]{1,0:T(8,128)(2,1)S(1)} %convolution_convert_fusion.1), channel_id=1, source_target_pairs={{0,1},{4,5},{8,9},{12,13},{16,17},{20,21},{24,25},{28,29},{32,33},... | collective-permute-start | bytes 983048 | tf_op jit(solution)/shard_map/ppermute | solution.py:106
  95.5 0.5 convolution_convert_fusion
  95.9 0.7 collective-permute-start.18
  96.6 0.5 fusion.60
  97.1 2.9 %collective-permute-done.15 = bf16[128,1280]{1,0:T(8,128)(2,1)S(1)} collective-permute-done((bf16[128,1280]{1,0:T(8,128)(2,1)S(1)}, bf16[128,1280]{1,0:T(8,128)(2,1)S(1)}, u32[]{:S(2)}, u32[]{:S(2)}) %collective-permute-start.15) | collective-permute-done | bytes 327712 | tf_op jit(solution)/shard_map/ppermute | solution.py:106
  100.0 0.5 add_convert_fusion.4
  100.5 4.4 %collective-permute-start.16 = (bf16[128,1280]{1,0:T(8,128)(2,1)S(1)}, bf16[128,1280]{1,0:T(8,128)(2,1)S(1)}, u32[]{:S(2)}, u32[]{:S(2)}) collective-permute-start(bf16[128,1280]{1,0:T(8,128)(2,1)S(1)} %add_convert_fusion.4), channel_id=1, source_target_pairs={{0,1},{1,2},{4,5},{5,6},{8,9},{9,10},{12,13},{13,14},{16,17},{17,1... | collective-permute-start | bytes 983048 | tf_op jit(solution)/shard_map/ppermute | solution.py:106
  104.9 0.5 fusion.61
  105.4 0.5 add_convert_fusion.2
  105.9 0.7 collective-permute-start.19
  106.6 4.1 %collective-permute-done.16 = bf16[128,1280]{1,0:T(8,128)(2,1)S(1)} collective-permute-done((bf16[128,1280]{1,0:T(8,128)(2,1)S(1)}, bf16[128,1280]{1,0:T(8,128)(2,1)S(1)}, u32[]{:S(2)}, u32[]{:S(2)}) %collective-permute-start.16) | collective-permute-done | bytes 327712 | tf_op jit(solution)/shard_map/ppermute | solution.py:106
  110.6 0.1 add_convert_fusion.3
  110.7 4.4 %collective-permute-start.17 = (bf16[128,1280]{1,0:T(8,128)(2,1)S(1)}, bf16[128,1280]{1,0:T(8,128)(2,1)S(1)}, u32[]{:S(2)}, u32[]{:S(2)}) collective-permute-start(bf16[128,1280]{1,0:T(8,128)(2,1)S(1)} %add_convert_fusion.3), channel_id=1, source_target_pairs={{0,1},{1,2},{2,3},{4,5},{5,6},{6,7},{8,9},{9,10},{10,11},{12,13},{... | collective-permute-start | bytes 983048 | tf_op jit(solution)/shard_map/ppermute | solution.py:106
  115.1 0.1 add_convert_fusion.1
  115.2 1.3 %collective-permute-start.20 = (bf16[128,1280]{1,0:T(8,128)(2,1)S(1)}, bf16[128,1280]{1,0:T(8,128)(2,1)S(1)}, u32[]{:S(2)}, u32[]{:S(2)}) collective-permute-start(bf16[128,1280]{1,0:T(8,128)(2,1)S(1)} %add_convert_fusion.1), channel_id=1, source_target_pairs={{1,0},{2,1},{3,2},{5,4},{6,5},{7,6},{9,8},{10,9},{11,10},{13,12},{... | collective-permute-start | bytes 983048 | tf_op jit(solution)/shard_map/ppermute | solution.py:107
  116.5 0.5 fusion.59
  117.0 2.7 %collective-permute-done.17 = bf16[128,1280]{1,0:T(8,128)(2,1)S(1)} collective-permute-done((bf16[128,1280]{1,0:T(8,128)(2,1)S(1)}, bf16[128,1280]{1,0:T(8,128)(2,1)S(1)}, u32[]{:S(2)}, u32[]{:S(2)}) %collective-permute-start.17) | collective-permute-done | bytes 327712 | tf_op jit(solution)/shard_map/ppermute | solution.py:106
  119.7 4.5 %collective-permute-done.20 = bf16[128,1280]{1,0:T(8,128)(2,1)S(1)} collective-permute-done((bf16[128,1280]{1,0:T(8,128)(2,1)S(1)}, bf16[128,1280]{1,0:T(8,128)(2,1)S(1)}, u32[]{:S(2)}, u32[]{:S(2)}) %collective-permute-start.20) | collective-permute-done | bytes 327712 | tf_op jit(solution)/shard_map/ppermute | solution.py:107
  124.2 0.8 fusion.17
  (25 shorter events, 0.1 us)
Async XLA Ops:
  0.0 2.6 %copy-start = (bf16[2560,640]{1,0:T(8,128)(2,1)S(1)}, bf16[2560,640]{1,0:T(8,128)(2,1)}, u32[]{:S(2)}) copy-start(bf16[2560,640]{1,0:T(8,128)(2,1)} %param.8) | copy-start | bytes 9830404
  2.1 2.4 %collective-permute-start = (bf16[128,2560]{1,0:T(8,128)(2,1)}, bf16[128,2560]{1,0:T(8,128)(2,1)}, u32[]{:S(2)}, u32[]{:S(2)}) collective-permute-start(bf16[128,2560]{1,0:T(8,128)(2,1)} %dynamic-slice_bitcast_fusion), channel_id=1, source_target_pairs={{0,4},{4,0},{1,5},{5,1},{2,6},{6,2},{3,7},{7,3},{8,12},{12,8},{9,1... | collective-permute-start | bytes 1966088 | tf_op jit(solution)/shard_map/ppermute | solution.py:12
  2.1 80.0 %collective-permute-start.14 = (bf16[640,2560]{1,0:T(8,128)(2,1)}, bf16[640,2560]{1,0:T(8,128)(2,1)}, u32[]{:S(2)}, u32[]{:S(2)}) collective-permute-start(bf16[640,2560]{1,0:T(8,128)(2,1)} %param.9), channel_id=1, source_target_pairs={{0,4},{4,0},{1,5},{5,1},{2,6},{6,2},{3,7},{7,3},{8,12},{12,8},{9,1... | collective-permute-start | bytes 9830408 | tf_op jit(solution)/shard_map/ppermute | solution.py:12
  4.4 2.3 %copy-start.1 = (bf16[2560,640]{1,0:T(8,128)(2,1)S(1)}, bf16[2560,640]{1,0:T(8,128)(2,1)}, u32[]{:S(2)}) copy-start(bf16[2560,640]{1,0:T(8,128)(2,1)} %param.7) | copy-start | bytes 9830404
  6.5 3.1 %copy-start.3 = (bf16[1,128,5120]{2,1,0:T(8,128)(2,1)S(1)}, bf16[1,128,5120]{2,1,0:T(8,128)(2,1)}, u32[]{:S(2)}) copy-start(bf16[1,128,5120]{2,1,0:T(8,128)(2,1)} %param.5) | copy-start | bytes 3932164
  6.5 4.5 %collective-permute-start.1 = (f32[128,640]{1,0:T(8,128)S(1)}, f32[128,640]{1,0:T(8,128)S(1)}, u32[]{:S(2)}, u32[]{:S(2)}) collective-permute-start(f32[128,640]{1,0:T(8,128)S(1)} %fusion.56), channel_id=1, source_target_pairs={{0,4},{4,0},{1,5},{5,1},{2,6},{6,2},{3,7},{7,3},{8,12},{12,8},{9,1... | collective-permute-start | bytes 983048 | tf_op jit(solution)/shard_map/ppermute | solution.py:12
  9.4 3.4 %collective-permute-start.3 = (f32[128,640]{1,0:T(8,128)}, f32[128,640]{1,0:T(8,128)}, u32[]{:S(2)}, u32[]{:S(2)}) collective-permute-start(f32[128,640]{1,0:T(8,128)} %fusion.58), channel_id=1, source_target_pairs={{0,4},{4,0},{1,5},{5,1},{2,6},{6,2},{3,7},{7,3},{8,12},{12,8},{9,1... | collective-permute-start | bytes 983048 | tf_op jit(solution)/shard_map/ppermute | solution.py:12
  17.5 22.0 %copy-start.2 = (bf16[2560,640]{1,0:T(8,128)(2,1)S(1)}, bf16[2560,640]{1,0:T(8,128)(2,1)}, u32[]{:S(2)}) copy-start(bf16[2560,640]{1,0:T(8,128)(2,1)} %param.6) | copy-start | bytes 9830404
  17.5 22.0 %copy-start.4 = (bf16[1,128,5120]{2,1,0:T(8,128)(2,1)S(1)}, bf16[1,128,5120]{2,1,0:T(8,128)(2,1)}, u32[]{:S(2)}) copy-start(bf16[1,128,5120]{2,1,0:T(8,128)(2,1)} %param.5) | copy-start | bytes 3932164
  17.5 8.4 %collective-permute-start.4 = (bf16[5,128,128]{2,1,0:T(8,128)(2,1)S(1)}, bf16[5,128,128]{2,1,0:T(8,128)(2,1)S(1)}, u32[]{:S(2)}, u32[]{:S(2)}) collective-permute-start(bf16[5,128,128]{2,1,0:T(8,128)(2,1)S(1)} %get-tuple-element.26), channel_id=1, source_target_pairs={{0,8},{8,16},{16,24},{24,0},{32,40},{40,48},{48,56},{56,32},{64,72... | collective-permute-start | bytes 491528 | tf_op jit(solution)/shard_map/ppermute | solution.py:16
  19.1 8.6 %collective-permute-start.5 = (bf16[5,128,128]{2,1,0:T(8,128)(2,1)S(1)}, bf16[5,128,128]{2,1,0:T(8,128)(2,1)S(1)}, u32[]{:S(2)}, u32[]{:S(2)}) collective-permute-start(bf16[5,128,128]{2,1,0:T(8,128)(2,1)S(1)} %get-tuple-element.26), channel_id=1, source_target_pairs={{0,16},{8,24},{16,0},{24,8},{32,48},{40,56},{48,32},{56,40},{64,80... | collective-permute-start | bytes 491528 | tf_op jit(solution)/shard_map/ppermute | solution.py:16
  20.2 9.3 %collective-permute-start.6 = (bf16[5,128,128]{2,1,0:T(8,128)(2,1)S(1)}, bf16[5,128,128]{2,1,0:T(8,128)(2,1)S(1)}, u32[]{:S(2)}, u32[]{:S(2)}) collective-permute-start(bf16[5,128,128]{2,1,0:T(8,128)(2,1)S(1)} %get-tuple-element.26), channel_id=1, source_target_pairs={{0,24},{8,0},{16,8},{24,16},{32,56},{40,32},{48,40},{56,48},{64,88... | collective-permute-start | bytes 491528 | tf_op jit(solution)/shard_map/ppermute | solution.py:16
  25.9 15.0 %collective-permute-start.2 = (f32[128,640]{1,0:T(8,128)}, f32[128,640]{1,0:T(8,128)}, u32[]{:S(2)}, u32[]{:S(2)}) collective-permute-start(f32[128,640]{1,0:T(8,128)} %fusion.57), channel_id=1, source_target_pairs={{0,4},{4,0},{1,5},{5,1},{2,6},{6,2},{3,7},{7,3},{8,12},{12,8},{9,1... | collective-permute-start | bytes 983048 | tf_op jit(solution)/shard_map/ppermute | solution.py:12
  25.9 4.4 %copy-start.5 = (bf16[5,128,128]{2,1,0:T(8,128)(2,1)}, bf16[5,128,128]{2,1,0:T(8,128)(2,1)S(1)}, u32[]{:S(2)}) copy-start(bf16[5,128,128]{2,1,0:T(8,128)(2,1)S(1)} %collective-permute-done.4) | copy-start | bytes 491524
  27.7 9.8 %copy-start.6 = (bf16[5,128,128]{2,1,0:T(8,128)(2,1)}, bf16[5,128,128]{2,1,0:T(8,128)(2,1)S(1)}, u32[]{:S(2)}) copy-start(bf16[5,128,128]{2,1,0:T(8,128)(2,1)S(1)} %collective-permute-done.5) | copy-start | bytes 491524
  29.6 9.0 %copy-start.7 = (bf16[5,128,128]{2,1,0:T(8,128)(2,1)}, bf16[5,128,128]{2,1,0:T(8,128)(2,1)S(1)}, u32[]{:S(2)}) copy-start(bf16[5,128,128]{2,1,0:T(8,128)(2,1)S(1)} %collective-permute-done.6) | copy-start | bytes 491524
  30.3 18.6 %collective-permute-start.10 = (bf16[5,128,128]{2,1,0:T(8,128)(2,1)}, bf16[5,128,128]{2,1,0:T(8,128)(2,1)}, u32[]{:S(2)}, u32[]{:S(2)}) collective-permute-start(bf16[5,128,128]{2,1,0:T(8,128)(2,1)} %fusion.16), channel_id=1, source_target_pairs={{0,128},{8,136},{16,144},{24,152},{32,160},{40,168},{48,176},{56,1... | collective-permute-start | bytes 491528 | tf_op jit(solution)/shard_map/ppermute | solution.py:16
  37.5 18.1 %collective-permute-start.11 = (bf16[5,128,128]{2,1,0:T(8,128)(2,1)}, bf16[5,128,128]{2,1,0:T(8,128)(2,1)}, u32[]{:S(2)}, u32[]{:S(2)}) collective-permute-start(bf16[5,128,128]{2,1,0:T(8,128)(2,1)} %fusion.16), channel_id=1, source_target_pairs={{0,160},{8,168},{16,176},{24,184},{32,192},{40,200},{48,208},{56,2... | collective-permute-start | bytes 491528 | tf_op jit(solution)/shard_map/ppermute | solution.py:16
  38.6 19.8 %collective-permute-start.12 = (bf16[5,128,128]{2,1,0:T(8,128)(2,1)}, bf16[5,128,128]{2,1,0:T(8,128)(2,1)}, u32[]{:S(2)}, u32[]{:S(2)}) collective-permute-start(bf16[5,128,128]{2,1,0:T(8,128)(2,1)} %fusion.16), channel_id=1, source_target_pairs={{0,192},{8,200},{16,208},{24,216},{32,224},{40,232},{48,240},{56,2... | collective-permute-start | bytes 491528 | tf_op jit(solution)/shard_map/ppermute | solution.py:16
  41.0 27.2 %collective-permute-start.13 = (bf16[5,128,128]{2,1,0:T(8,128)(2,1)}, bf16[5,128,128]{2,1,0:T(8,128)(2,1)}, u32[]{:S(2)}, u32[]{:S(2)}) collective-permute-start(bf16[5,128,128]{2,1,0:T(8,128)(2,1)} %fusion.16), channel_id=1, source_target_pairs={{0,224},{8,232},{16,240},{24,248},{32,0},{40,8},{48,16},{56,24},{6... | collective-permute-start | bytes 491528 | tf_op jit(solution)/shard_map/ppermute | solution.py:16
  48.9 19.2 %collective-permute-start.7 = (bf16[5,128,128]{2,1,0:T(8,128)(2,1)}, bf16[5,128,128]{2,1,0:T(8,128)(2,1)}, u32[]{:S(2)}, u32[]{:S(2)}) collective-permute-start(bf16[5,128,128]{2,1,0:T(8,128)(2,1)} %fusion.16), channel_id=1, source_target_pairs={{0,32},{8,40},{16,48},{24,56},{32,64},{40,72},{48,80},{56,88},{64,... | collective-permute-start | bytes 491528 | tf_op jit(solution)/shard_map/ppermute | solution.py:16
  55.7 20.1 %collective-permute-start.8 = (bf16[5,128,128]{2,1,0:T(8,128)(2,1)}, bf16[5,128,128]{2,1,0:T(8,128)(2,1)}, u32[]{:S(2)}, u32[]{:S(2)}) collective-permute-start(bf16[5,128,128]{2,1,0:T(8,128)(2,1)} %fusion.16), channel_id=1, source_target_pairs={{0,64},{8,72},{16,80},{24,88},{32,96},{40,104},{48,112},{56,120},{... | collective-permute-start | bytes 491528 | tf_op jit(solution)/shard_map/ppermute | solution.py:16
  58.4 17.4 %collective-permute-start.9 = (bf16[5,128,128]{2,1,0:T(8,128)(2,1)}, bf16[5,128,128]{2,1,0:T(8,128)(2,1)}, u32[]{:S(2)}, u32[]{:S(2)}) collective-permute-start(bf16[5,128,128]{2,1,0:T(8,128)(2,1)} %fusion.16), channel_id=1, source_target_pairs={{0,96},{8,104},{16,112},{24,120},{32,128},{40,136},{48,144},{56,15... | collective-permute-start | bytes 491528 | tf_op jit(solution)/shard_map/ppermute | solution.py:16
  93.1 6.9 %collective-permute-start.15 = (bf16[128,1280]{1,0:T(8,128)(2,1)S(1)}, bf16[128,1280]{1,0:T(8,128)(2,1)S(1)}, u32[]{:S(2)}, u32[]{:S(2)}) collective-permute-start(bf16[128,1280]{1,0:T(8,128)(2,1)S(1)} %convolution_convert_fusion.1), channel_id=1, source_target_pairs={{0,1},{4,5},{8,9},{12,13},{16,17},{20,21},{24,25},{28,29},{32,33},... | collective-permute-start | bytes 983048 | tf_op jit(solution)/shard_map/ppermute | solution.py:106
  95.9 9.4 %collective-permute-start.18 = (bf16[128,1280]{1,0:T(8,128)(2,1)S(1)}, bf16[128,1280]{1,0:T(8,128)(2,1)S(1)}, u32[]{:S(2)}, u32[]{:S(2)}) collective-permute-start(bf16[128,1280]{1,0:T(8,128)(2,1)S(1)} %convolution_convert_fusion), channel_id=1, source_target_pairs={{3,2},{7,6},{11,10},{15,14},{19,18},{23,22},{27,26},{31,30},{35,34... | collective-permute-start | bytes 983048 | tf_op jit(solution)/shard_map/ppermute | solution.py:107
  100.5 10.1 %collective-permute-start.16 = (bf16[128,1280]{1,0:T(8,128)(2,1)S(1)}, bf16[128,1280]{1,0:T(8,128)(2,1)S(1)}, u32[]{:S(2)}, u32[]{:S(2)}) collective-permute-start(bf16[128,1280]{1,0:T(8,128)(2,1)S(1)} %add_convert_fusion.4), channel_id=1, source_target_pairs={{0,1},{1,2},{4,5},{5,6},{8,9},{9,10},{12,13},{13,14},{16,17},{17,1... | collective-permute-start | bytes 983048 | tf_op jit(solution)/shard_map/ppermute | solution.py:106
  105.9 9.3 %collective-permute-start.19 = (bf16[128,1280]{1,0:T(8,128)(2,1)S(1)}, bf16[128,1280]{1,0:T(8,128)(2,1)S(1)}, u32[]{:S(2)}, u32[]{:S(2)}) collective-permute-start(bf16[128,1280]{1,0:T(8,128)(2,1)S(1)} %add_convert_fusion.2), channel_id=1, source_target_pairs={{2,1},{3,2},{6,5},{7,6},{10,9},{11,10},{14,13},{15,14},{18,17},{19... | collective-permute-start | bytes 983048 | tf_op jit(solution)/shard_map/ppermute | solution.py:107
  110.7 9.0 %collective-permute-start.17 = (bf16[128,1280]{1,0:T(8,128)(2,1)S(1)}, bf16[128,1280]{1,0:T(8,128)(2,1)S(1)}, u32[]{:S(2)}, u32[]{:S(2)}) collective-permute-start(bf16[128,1280]{1,0:T(8,128)(2,1)S(1)} %add_convert_fusion.3), channel_id=1, source_target_pairs={{0,1},{1,2},{2,3},{4,5},{5,6},{6,7},{8,9},{9,10},{10,11},{12,13},{... | collective-permute-start | bytes 983048 | tf_op jit(solution)/shard_map/ppermute | solution.py:106
  115.2 9.0 %collective-permute-start.20 = (bf16[128,1280]{1,0:T(8,128)(2,1)S(1)}, bf16[128,1280]{1,0:T(8,128)(2,1)S(1)}, u32[]{:S(2)}, u32[]{:S(2)}) collective-permute-start(bf16[128,1280]{1,0:T(8,128)(2,1)S(1)} %add_convert_fusion.1), channel_id=1, source_target_pairs={{1,0},{2,1},{3,2},{5,4},{6,5},{7,6},{9,8},{10,9},{11,10},{13,12},{... | collective-permute-start | bytes 983048 | tf_op jit(solution)/shard_map/ppermute | solution.py:107

commit v3 on v1

--- a/solution.py
+++ b/solution.py
@@ -84,18 +84,22 @@
     normed = (attended * scale).reshape(tok_count, width_local).astype(BF16)
 
     w_other = swap_cores(w_output)
-    y_mine = jnp.dot(normed, w_output, preferred_element_type=F32)
-    y_other = jnp.dot(normed, w_other, preferred_element_type=F32)
-    quarter = y_mine.shape[1] // 2
+    quarter = w_output.shape[1] // 2
+    n = 4
+    h = lax.axis_index("head")
+
+    products = jnp.stack(
+        [
+            jnp.dot(normed, w[:, k * quarter : (k + 1) * quarter], preferred_element_type=F32)
+            for w in (w_output, w_other)
+            for k in range(2)
+        ]
+    )
 
     def block(q):
-        sub = q % 2
-        a = lax.dynamic_slice_in_dim(y_mine, sub * quarter, quarter, axis=1)
-        b = lax.dynamic_slice_in_dim(y_other, sub * quarter, quarter, axis=1)
-        return jnp.where(q // 2 == c, a, b)
+        k = jnp.where(q // 2 == c, 0, 2) + q % 2
+        return lax.dynamic_index_in_dim(products, k, 0, keepdims=False)
 
-    n = 4
-    h = lax.axis_index("head")
     right = jnp.zeros((tok_count, quarter), F32)
     left = jnp.zeros((tok_count, quarter), F32)
     for s in range(1, n):

time: 122 us -> 124 us (1.016)
  local copies, waits for them, and re-layouts: 6.74 us -> 9.1 us
  other arithmetic: 17.1 us -> 15 us
  matrix products: 25.8 us -> 27.6 us
    convert_element_type x3 -> x2, other arithmetic: 6.28 us -> 4.4 us  [shards(): send_r = (block(qr) + right).astype(BF16)]
    dot_general x2 -> x4, matrix products: 5.72 us -> 7.53 us  [shards(): jnp.dot(normed, w[:, k * quarter:(k + 1) * quarter], preferred_element_ty...]
    unnamed x24 -> x22, local copies, waits for them, and re-layouts: 0.13 us -> 1.55 us
where the time goes in v3:
time: 124 us; the launch traced here: 123 us
  starting transfers between devices  41.4 us (33%)
  waiting for transfers between devices  29.7 us (24%)
  matrix products  27.6 us (22%)
  other arithmetic  15 us (12%)
  local copies, waits for them, and re-layouts  9.1 us (7%)
    ppermute x7, starting transfers between devices, shifted(): return lax.ppermute(x, axis, pairs)  18.9 us
    ppermute x3, starting transfers between devices, shards(): right = lax.ppermute(send_r, 'head', rpairs).astype(F32)  17.3 us
    ppermute x3, waiting for transfers between devices, shards(): left = lax.ppermute(send_l, 'head', lpairs).astype(F32)  10.4 us
    ppermute x3, waiting for transfers between devices, shards(): right = lax.ppermute(send_r, 'head', rpairs).astype(F32)  10.2 us
    ppermute x7, waiting for transfers between devices, shifted(): return lax.ppermute(x, axis, pairs)  9.08 us
    dot_general x4, matrix products, shards(): jnp.dot(normed, w[:, k * quarter:(k + 1) * quarter], preferred_element_ty...  7.53 us
    dot_general x3, matrix products, shards(): lent = swap_cores(jnp.dot(got_cols, w, preferred_element_type=F32))  6.88 us
    dot_general x3, matrix products, shards(): own = jnp.dot(mine_cols, w, preferred_element_type=F32)  6.88 us
  transfers between devices with their start and end apart: 18, of which 9 were waited for; matrix products, arithmetic and copies ran while one was open for 31% of the time, Pallas kernels for 0%

profile of v3, /device:TPU:10, one launch (start us, length us, event | category | flops | bytes accessed | tf_op | source)
XLA Modules:
  0.0 123.0 jit_solution(9970129077890349773)
XLA Ops:
  0.0 2.1 %dynamic-slice_bitcast_fusion = bf16[128,2560]{1,0:T(8,128)(2,1)} fusion(bf16[1,128,5120]{2,1,0:T(8,128)(2,1)} %param.5, s32[]{:T(128)S(6)} %select_n.177), kind=kLoop, calls=%fused_computation.32 | loop fusion | bytes 1310724 | tf_op jit(solution)/shard_map/dynamic_slice | solution.py:59
  2.1 0.0 collective-permute-start
  2.1 0.5 collective-permute-start.11
  2.6 2.7 %fusion.16 = f32[128,640]{1,0:T(8,128)} fusion(bf16[2560,640]{1,0:T(8,128)(2,1)S(1)} %copy-done, bf16[1,128,5120]{2,1,0:T(8,128)(2,1)} %param.5, s32[]{:T(128)S(6)} %select_n.176), kind=kOutput, calls=%fused_computation.28 | convolution fusion | flops 419430400 | bytes 4259844 | tf_op jit(solution)/shard_map/dot_general | solution.py:64
  5.3 0.0 collective-permute-done
  5.3 2.6 %fusion.50 = f32[128,640]{1,0:T(8,128)} fusion(bf16[128,2560]{1,0:T(8,128)(2,1)} %collective-permute-done, bf16[2560,640]{1,0:T(8,128)(2,1)S(1)} %copy-done), kind=kOutput, calls=%fused_computation.82 | convolution fusion | flops 419430400 | bytes 4259840 | tf_op jit(solution)/shard_map/dot_general | solution.py:63
  7.9 0.0 collective-permute-start.1
  7.9 2.5 %fusion.52 = f32[128,640]{1,0:T(8,128)} fusion(bf16[128,2560]{1,0:T(8,128)(2,1)} %collective-permute-done, bf16[2560,640]{1,0:T(8,128)(2,1)S(1)} %copy-done.2), kind=kOutput, calls=%fused_computation.84 | convolution fusion | flops 419430400 | bytes 4259840 | tf_op jit(solution)/shard_map/dot_general | solution.py:63
  10.4 0.5 collective-permute-start.3
  10.9 1.4 %fusion.12 = f32[128,640]{1,0:T(8,128)} fusion(bf16[2560,640]{1,0:T(8,128)(2,1)S(1)} %copy-done.2, bf16[1,128,5120]{2,1,0:T(8,128)(2,1)S(1)} %copy-done.4, s32[]{:T(128)S(6)} %select_n.176), kind=kOutput, calls=%fused_computation.24 | convolution fusion | flops 419430400 | bytes 4259844 | tf_op jit(solution)/shard_map/dot_general | solution.py:64
  12.4 0.0 collective-permute-done.1
  12.4 1.8 %add_convert_fusion = bf16[128,640]{1,0:T(8,128)(2,1)} fusion(f32[128,640]{1,0:T(8,128)} %fusion.16, f32[128,640]{1,0:T(8,128)} %collective-permute-done.1), kind=kLoop, calls=%fused_computation.64 | loop fusion | flops 163840 | bytes 819200 | tf_op jit(solution)/shard_map/convert_element_type | solution.py:70
  14.1 1.1 copy.11
  15.2 0.0 collective-permute-done.3
  15.2 1.8 %multiply_convert_fusion.1 = bf16[128,640]{1,0:T(8,128)(2,1)} fusion(f32[128,640]{1,0:T(8,128)} %fusion.12, f32[128,640]{1,0:T(8,128)} %collective-permute-done.3), kind=kLoop, calls=%fused_computation.62 | loop fusion | flops 491520 | bytes 819200 | tf_op jit(solution)/shard_map/convert_element_type | solution.py:69
  17.0 1.7 %copy.13 = bf16[128,640]{0,1:T(8,128)(2,1)} copy(bf16[128,640]{1,0:T(8,128)(2,1)} %multiply_convert_fusion.1) | data formatting | bytes 327680 | tf_op jit(solution)/shard_map/convert_element_type | solution.py:69
  18.8 1.3 %fusion.49 = (bf16[5,128,128]{2,1,0:T(8,128)(2,1)S(1)}, f32[5,128,128]{2,1,0:T(8,128)S(1)}) fusion(bf16[128,5,128]{0,2,1:T(8,128)(2,1)} %bitcast.78, bf16[128,5,128]{0,2,1:T(8,128)(2,1)S(1)} %bitcast.76), kind=kOutput, calls=%fused_computation.81 | convolution fusion | flops 21053440 | bytes 819200 | tf_op jit(solution)/shard_map/thd,the->hde/dot_general | solution.py:71
  20.1 1.6 %collective-permute-start.4 = (bf16[5,128,128]{2,1,0:T(8,128)(2,1)S(1)}, bf16[5,128,128]{2,1,0:T(8,128)(2,1)S(1)}, u32[]{:S(2)}, u32[]{:S(2)}) collective-permute-start(bf16[5,128,128]{2,1,0:T(8,128)(2,1)S(1)} %get-tuple-element.9), channel_id=1, source_target_pairs={{0,8},{8,16},{16,24},{24,0},{32,40},{40,48},{48,56},{56,32},{64,72... | collective-permute-start | bytes 491528 | tf_op jit(solution)/shard_map/ppermute | solution.py:16
  21.7 1.1 collective-permute-start.5
  22.8 2.1 %collective-permute-start.6 = (bf16[5,128,128]{2,1,0:T(8,128)(2,1)S(1)}, bf16[5,128,128]{2,1,0:T(8,128)(2,1)S(1)}, u32[]{:S(2)}, u32[]{:S(2)}) collective-permute-start(bf16[5,128,128]{2,1,0:T(8,128)(2,1)S(1)} %get-tuple-element.9), channel_id=1, source_target_pairs={{0,24},{8,0},{16,8},{24,16},{32,56},{40,32},{48,40},{56,48},{64,88... | collective-permute-start | bytes 491528 | tf_op jit(solution)/shard_map/ppermute | solution.py:16
  24.9 2.8 %fusion.14 = f32[128,640]{1,0:T(8,128)S(1)} fusion(bf16[2560,640]{1,0:T(8,128)(2,1)} %param.6, bf16[1,128,5120]{2,1,0:T(8,128)(2,1)} %param.5, s32[]{:T(128)S(6)} %select_n.176), kind=kOutput, calls=%fused_computation.26 | convolution fusion | flops 419430400 | bytes 4259844 | tf_op jit(solution)/shard_map/dot_general | solution.py:64
  27.7 0.0 collective-permute-done.4
  27.8 2.5 %collective-permute-done.5 = bf16[5,128,128]{2,1,0:T(8,128)(2,1)S(1)} collective-permute-done((bf16[5,128,128]{2,1,0:T(8,128)(2,1)S(1)}, bf16[5,128,128]{2,1,0:T(8,128)(2,1)S(1)}, u32[]{:S(2)}, u32[]{:S(2)}) %collective-permute-start.5) | collective-permute-done | bytes 163872 | tf_op jit(solution)/shard_map/ppermute | solution.py:16
  30.2 1.6 %collective-permute-done.6 = bf16[5,128,128]{2,1,0:T(8,128)(2,1)S(1)} collective-permute-done((bf16[5,128,128]{2,1,0:T(8,128)(2,1)S(1)}, bf16[5,128,128]{2,1,0:T(8,128)(2,1)S(1)}, u32[]{:S(2)}, u32[]{:S(2)}) %collective-permute-start.6) | collective-permute-done | bytes 163872 | tf_op jit(solution)/shard_map/ppermute | solution.py:16
  31.9 0.1 fusion.44
  31.9 1.6 %collective-permute-start.7 = (bf16[5,128,128]{2,1,0:T(8,128)(2,1)S(1)}, bf16[5,128,128]{2,1,0:T(8,128)(2,1)S(1)}, u32[]{:S(2)}, u32[]{:S(2)}) collective-permute-start(bf16[5,128,128]{2,1,0:T(8,128)(2,1)S(1)} %fusion.44), channel_id=1, source_target_pairs={{0,32},{8,40},{16,48},{24,56},{32,64},{40,72},{48,80},{56,88},{64,... | collective-permute-start | bytes 491528 | tf_op jit(solution)/shard_map/ppermute | solution.py:16
  33.6 1.6 %collective-permute-start.8 = (bf16[5,128,128]{2,1,0:T(8,128)(2,1)S(1)}, bf16[5,128,128]{2,1,0:T(8,128)(2,1)S(1)}, u32[]{:S(2)}, u32[]{:S(2)}) collective-permute-start(bf16[5,128,128]{2,1,0:T(8,128)(2,1)S(1)} %fusion.44), channel_id=1, source_target_pairs={{0,64},{8,72},{16,80},{24,88},{32,96},{40,104},{48,112},{56,120},{... | collective-permute-start | bytes 491528 | tf_op jit(solution)/shard_map/ppermute | solution.py:16
  35.2 1.7 %collective-permute-start.9 = (bf16[5,128,128]{2,1,0:T(8,128)(2,1)S(1)}, bf16[5,128,128]{2,1,0:T(8,128)(2,1)S(1)}, u32[]{:S(2)}, u32[]{:S(2)}) collective-permute-start(bf16[5,128,128]{2,1,0:T(8,128)(2,1)S(1)} %fusion.44), channel_id=1, source_target_pairs={{0,96},{8,104},{16,112},{24,120},{32,0},{40,8},{48,16},{56,24},{64... | collective-permute-start | bytes 491528 | tf_op jit(solution)/shard_map/ppermute | solution.py:16
  36.9 1.8 %fusion.51 = f32[128,640]{1,0:T(8,128)S(1)} fusion(bf16[128,2560]{1,0:T(8,128)(2,1)} %collective-permute-done, bf16[2560,640]{1,0:T(8,128)(2,1)S(1)} %copy-done.3), kind=kOutput, calls=%fused_computation.83 | convolution fusion | flops 419430400 | bytes 4259840 | tf_op jit(solution)/shard_map/dot_general | solution.py:63
  38.7 0.1 collective-permute-start.2
  38.8 0.0 collective-permute-done.7
  38.8 3.2 %collective-permute-done.8 = bf16[5,128,128]{2,1,0:T(8,128)(2,1)S(1)} collective-permute-done((bf16[5,128,128]{2,1,0:T(8,128)(2,1)S(1)}, bf16[5,128,128]{2,1,0:T(8,128)(2,1)S(1)}, u32[]{:S(2)}, u32[]{:S(2)}) %collective-permute-start.8) | collective-permute-done | bytes 163872 | tf_op jit(solution)/shard_map/ppermute | solution.py:16
  42.0 1.8 %collective-permute-done.9 = bf16[5,128,128]{2,1,0:T(8,128)(2,1)S(1)} collective-permute-done((bf16[5,128,128]{2,1,0:T(8,128)(2,1)S(1)}, bf16[5,128,128]{2,1,0:T(8,128)(2,1)S(1)}, u32[]{:S(2)}, u32[]{:S(2)}) %collective-permute-start.9) | collective-permute-done | bytes 163872 | tf_op jit(solution)/shard_map/ppermute | solution.py:16
  43.8 0.8 fusion.30
  44.6 9.1 %collective-permute-start.10 = (bf16[5,128,128]{2,1,0:T(8,128)(2,1)}, bf16[5,128,128]{2,1,0:T(8,128)(2,1)}, u32[]{:S(2)}, u32[]{:S(2)}) collective-permute-start(bf16[5,128,128]{2,1,0:T(8,128)(2,1)} %fusion.30), channel_id=1, source_target_pairs={{0,128},{8,136},{16,144},{24,152},{32,160},{40,168},{48,176},{56,1... | collective-permute-start | bytes 491528 | tf_op jit(solution)/shard_map/ppermute | solution.py:16
  53.7 0.0 collective-permute-done.2
  53.7 0.8 multiply_convert_fusion.2
  54.5 1.7 %copy.12 = bf16[128,640]{0,1:T(8,128)(2,1)} copy(bf16[128,640]{1,0:T(8,128)(2,1)} %multiply_convert_fusion.2) | data formatting | bytes 327680 | tf_op jit(solution)/shard_map/convert_element_type | solution.py:68
  56.2 0.1 collective-permute-done.10
  56.2 2.7 %fusion.25 = f32[5,128,128]{2,1,0:T(8,128)} fusion(bf16[128,5,128]{0,2,1:T(8,128)(2,1)} %bitcast.80, bf16[5,128,128]{2,1,0:T(8,128)(2,1)} %copy-done.5, bf16[5,128,128]{2,1,0:T(8,128)(2,1)} %copy-done.6, bf16[5,128,128]{2,1,0:T(8,128)(2,1)} %copy-done.7, bf16[5,128,128]{2,1,0:T(8,128)(2,1)} %copy-done.8, bf16[5,128,128]{2,1,0:T(8,128)(2,1)} %copy-done.9, ...), kind=kOutput, calls=%fused_computation.52 | convolution fusion | flops 127385600 | bytes 1638406 | tf_op jit(solution)/shard_map/thd,hde->the/dot_general | solution.py:79
  58.9 2.3 %multiply_reduce_fusion = (f32[128,5]{0,1:T(8,128)S(1)}, f32[128,5,128]{0,2,1:T(8,128)}) fusion(f32[5,128,128]{2,1,0:T(8,128)} %fusion.25, bf16[128,5,128]{0,2,1:T(8,128)(2,1)S(1)} %bitcast.77, bf16[128,5,128]{0,2,1:T(8,128)(2,1)} %bitcast.81, bf16[128,5,128]{0,2,1:T(8,128)(2,1)} %bitcast.79, f32[128,128]{1,0:T(8,128)S(1)} %fusion.43), kind=kOutput, calls=%fused_computation.60 | convolution fusion | flops 42352000 | bytes 1214976 | tf_op jit(solution)/shard_map/hts,shd->thd/dot_general | solution.py:78
  61.2 1.0 multiply_convert_fusion
  62.2 1.9 %convolution_bitcast_fusion.2 = f32[1,128,1280]{2,1,0:T(8,128)S(1)} fusion(bf16[128,640]{0,1:T(8,128)(2,1)S(1)} %bitcast.72, bf16[640,2560]{1,0:T(8,128)(2,1)} %param.9), kind=kOutput, calls=%fused_computation.3 | convolution fusion | flops 209715200 | bytes 2457600 | tf_op jit(solution)/shard_map/dot_general | solution.py:93
  64.1 1.9 %convolution_bitcast_fusion.3 = f32[1,128,1280]{2,1,0:T(8,128)S(1)} fusion(bf16[128,640]{0,1:T(8,128)(2,1)S(1)} %bitcast.73, bf16[640,2560]{1,0:T(8,128)(2,1)} %param.9), kind=kOutput, calls=%fused_computation.4 | convolution fusion | flops 209715200 | bytes 2457600 | tf_op jit(solution)/shard_map/dot_general | solution.py:93
  66.0 1.9 %convolution_bitcast_fusion = f32[1,128,1280]{2,1,0:T(8,128)S(1)} fusion(bf16[128,640]{0,1:T(8,128)(2,1)S(1)} %bitcast.74, bf16[640,2560]{1,0:T(8,128)(2,1)} %collective-permute-done.11), kind=kOutput, calls=%fused_computation.1 | convolution fusion | flops 209715200 | bytes 2457600 | tf_op jit(solution)/shard_map/dot_general | solution.py:93
  67.9 1.9 %convolution_bitcast_fusion.1 = f32[1,128,1280]{2,1,0:T(8,128)S(1)} fusion(bf16[128,640]{0,1:T(8,128)(2,1)S(1)} %bitcast.75, bf16[640,2560]{1,0:T(8,128)(2,1)} %collective-permute-done.11), kind=kOutput, calls=%fused_computation.2 | convolution fusion | flops 209715200 | bytes 2457600 | tf_op jit(solution)/shard_map/dot_general | solution.py:93
  69.8 0.2 pad_maximum_fusion
  70.1 1.5 %copy-done.1 = f32[4,128,1280]{2,1,0:T(8,128)} copy-done((f32[4,128,1280]{2,1,0:T(8,128)}, f32[4,128,1280]{2,1,0:T(8,128)S(1)}, u32[]{:S(2)}) %copy-start.1) | copy-done | bytes 2621464
  71.6 0.9 fusion.31
  72.5 7.2 %collective-permute-start.12 = (bf16[128,1280]{1,0:T(8,128)(2,1)}, bf16[128,1280]{1,0:T(8,128)(2,1)}, u32[]{:S(2)}, u32[]{:S(2)}) collective-permute-start(bf16[128,1280]{1,0:T(8,128)(2,1)} %get-tuple-element.7), channel_id=1, source_target_pairs={{0,1},{4,5},{8,9},{12,13},{16,17},{20,21},{24,25},{28,29},{32,33},... | collective-permute-start | bytes 983048 | tf_op jit(solution)/shard_map/ppermute | solution.py:112
  79.7 1.4 %collective-permute-start.15 = (bf16[128,1280]{1,0:T(8,128)(2,1)}, bf16[128,1280]{1,0:T(8,128)(2,1)}, u32[]{:S(2)}, u32[]{:S(2)}) collective-permute-start(bf16[128,1280]{1,0:T(8,128)(2,1)} %get-tuple-element.8), channel_id=1, source_target_pairs={{3,2},{7,6},{11,10},{15,14},{19,18},{23,22},{27,26},{31,30},{35,34... | collective-permute-start | bytes 983048 | tf_op jit(solution)/shard_map/ppermute | solution.py:113
  81.1 4.4 %collective-permute-done.12 = bf16[128,1280]{1,0:T(8,128)(2,1)} collective-permute-done((bf16[128,1280]{1,0:T(8,128)(2,1)}, bf16[128,1280]{1,0:T(8,128)(2,1)}, u32[]{:S(2)}, u32[]{:S(2)}) %collective-permute-start.12) | collective-permute-done | bytes 327712 | tf_op jit(solution)/shard_map/ppermute | solution.py:112
  85.5 2.0 %fusion.8 = bf16[128,1280]{1,0:T(8,128)(2,1)} fusion(bf16[128,1280]{1,0:T(8,128)(2,1)} %collective-permute-done.12, f32[4,128,1280]{2,1,0:T(8,128)} %copy-done.1, s32[]{:T(128)S(6)} %select_n.210), kind=kLoop, calls=%fused_computation.18 | loop fusion | flops 491520 | bytes 1310724 | tf_op jit(solution)/shard_map/convert_element_type | solution.py:108
  87.4 5.1 %collective-permute-start.13 = (bf16[128,1280]{1,0:T(8,128)(2,1)}, bf16[128,1280]{1,0:T(8,128)(2,1)}, u32[]{:S(2)}, u32[]{:S(2)}) collective-permute-start(bf16[128,1280]{1,0:T(8,128)(2,1)} %fusion.8), channel_id=1, source_target_pairs={{0,1},{1,2},{4,5},{5,6},{8,9},{9,10},{12,13},{13,14},{16,17},{17,1... | collective-permute-start | bytes 983048 | tf_op jit(solution)/shard_map/ppermute | solution.py:112
  92.5 0.0 collective-permute-done.15
  92.5 5.0 %collective-permute-done.13 = bf16[128,1280]{1,0:T(8,128)(2,1)} collective-permute-done((bf16[128,1280]{1,0:T(8,128)(2,1)}, bf16[128,1280]{1,0:T(8,128)(2,1)}, u32[]{:S(2)}, u32[]{:S(2)}) %collective-permute-start.13) | collective-permute-done | bytes 327712 | tf_op jit(solution)/shard_map/ppermute | solution.py:112
  97.5 2.4 %fusion.9 = (bf16[128,1280]{1,0:T(8,128)(2,1)}, bf16[128,1280]{1,0:T(8,128)(2,1)}) fusion(bf16[128,1280]{1,0:T(8,128)(2,1)} %collective-permute-done.13, f32[4,128,1280]{2,1,0:T(8,128)} %copy-done.1, s32[]{:T(128)S(6)} %select_n.206, bf16[128,1280]{1,0:T(8,128)(2,1)} %collective-permute-done.15, s32[]{:T(128)S(6)} %select_n.222), kind=kLoop, calls=%fused_computation.20 | loop fusion | flops 983040 | bytes 2621448 | tf_op jit(solution)/shard_map/convert_element_type | solution.py:108
  99.9 1.4 %collective-permute-start.16 = (bf16[128,1280]{1,0:T(8,128)(2,1)}, bf16[128,1280]{1,0:T(8,128)(2,1)}, u32[]{:S(2)}, u32[]{:S(2)}) collective-permute-start(bf16[128,1280]{1,0:T(8,128)(2,1)} %get-tuple-element.6), channel_id=1, source_target_pairs={{2,1},{3,2},{6,5},{7,6},{10,9},{11,10},{14,13},{15,14},{18,17},{19... | collective-permute-start | bytes 983048 | tf_op jit(solution)/shard_map/ppermute | solution.py:113
  101.3 5.0 %collective-permute-start.14 = (bf16[128,1280]{1,0:T(8,128)(2,1)}, bf16[128,1280]{1,0:T(8,128)(2,1)}, u32[]{:S(2)}, u32[]{:S(2)}) collective-permute-start(bf16[128,1280]{1,0:T(8,128)(2,1)} %get-tuple-element.5), channel_id=1, source_target_pairs={{0,1},{1,2},{2,3},{4,5},{5,6},{6,7},{8,9},{9,10},{10,11},{12,13},{... | collective-permute-start | bytes 983048 | tf_op jit(solution)/shard_map/ppermute | solution.py:112
  106.3 2.0 %fusion.7 = bf16[128,1280]{1,0:T(8,128)(2,1)} fusion(bf16[128,1280]{1,0:T(8,128)(2,1)} %collective-permute-done.16, f32[4,128,1280]{2,1,0:T(8,128)} %copy-done.1, s32[]{:T(128)S(6)} %select_n.218), kind=kLoop, calls=%fused_computation.16 | loop fusion | flops 491520 | bytes 1310724 | tf_op jit(solution)/shard_map/convert_element_type | solution.py:109
  108.3 1.3 %collective-permute-start.17 = (bf16[128,1280]{1,0:T(8,128)(2,1)}, bf16[128,1280]{1,0:T(8,128)(2,1)}, u32[]{:S(2)}, u32[]{:S(2)}) collective-permute-start(bf16[128,1280]{1,0:T(8,128)(2,1)} %fusion.7), channel_id=1, source_target_pairs={{1,0},{2,1},{3,2},{5,4},{6,5},{7,6},{9,8},{10,9},{11,10},{13,12},{... | collective-permute-start | bytes 983048 | tf_op jit(solution)/shard_map/ppermute | solution.py:113
  109.7 0.8 collective-permute-done.14
  110.5 10.4 %collective-permute-done.17 = bf16[128,1280]{1,0:T(8,128)(2,1)} collective-permute-done((bf16[128,1280]{1,0:T(8,128)(2,1)}, bf16[128,1280]{1,0:T(8,128)(2,1)}, u32[]{:S(2)}, u32[]{:S(2)}) %collective-permute-start.17) | collective-permute-done | bytes 327712 | tf_op jit(solution)/shard_map/ppermute | solution.py:113
  120.9 2.1 %fusion.33 = bf16[1,128,1280]{2,1,0:T(8,128)(2,1)} fusion(bf16[128,1280]{1,0:T(8,128)(2,1)} %collective-permute-done.17, bf16[128,1280]{1,0:T(8,128)(2,1)} %collective-permute-done.14, f32[4,128,1280]{2,1,0:T(8,128)} %copy-done.1, s32[]{:T(128)S(6)} %select_n.202), kind=kLoop, calls=%fused_computation.58 | loop fusion | flops 819200 | bytes 1638404 | tf_op jit(solution)/shard_map/reshape | solution.py:115
  (25 shorter events, 0.1 us)
Async XLA Ops:
  0.0 2.6 %copy-start = (bf16[2560,640]{1,0:T(8,128)(2,1)S(1)}, bf16[2560,640]{1,0:T(8,128)(2,1)}, u32[]{:S(2)}) copy-start(bf16[2560,640]{1,0:T(8,128)(2,1)} %param.8) | copy-start | bytes 9830404
  2.1 3.2 %collective-permute-start = (bf16[128,2560]{1,0:T(8,128)(2,1)}, bf16[128,2560]{1,0:T(8,128)(2,1)}, u32[]{:S(2)}, u32[]{:S(2)}) collective-permute-start(bf16[128,2560]{1,0:T(8,128)(2,1)} %dynamic-slice_bitcast_fusion), channel_id=1, source_target_pairs={{0,4},{4,0},{1,5},{5,1},{2,6},{6,2},{3,7},{7,3},{8,12},{12,8},{9,1... | collective-permute-start | bytes 1966088 | tf_op jit(solution)/shard_map/ppermute | solution.py:12
  2.1 63.9 %collective-permute-start.11 = (bf16[640,2560]{1,0:T(8,128)(2,1)}, bf16[640,2560]{1,0:T(8,128)(2,1)}, u32[]{:S(2)}, u32[]{:S(2)}) collective-permute-start(bf16[640,2560]{1,0:T(8,128)(2,1)} %param.9), channel_id=1, source_target_pairs={{0,4},{4,0},{1,5},{5,1},{2,6},{6,2},{3,7},{7,3},{8,12},{12,8},{9,1... | collective-permute-start | bytes 9830408 | tf_op jit(solution)/shard_map/ppermute | solution.py:12
  2.6 5.3 %copy-start.2 = (bf16[2560,640]{1,0:T(8,128)(2,1)S(1)}, bf16[2560,640]{1,0:T(8,128)(2,1)}, u32[]{:S(2)}) copy-start(bf16[2560,640]{1,0:T(8,128)(2,1)} %param.7) | copy-start | bytes 9830404
  5.3 5.6 %copy-start.4 = (bf16[1,128,5120]{2,1,0:T(8,128)(2,1)S(1)}, bf16[1,128,5120]{2,1,0:T(8,128)(2,1)}, u32[]{:S(2)}) copy-start(bf16[1,128,5120]{2,1,0:T(8,128)(2,1)} %param.5) | copy-start | bytes 3932164
  7.9 4.4 %collective-permute-start.1 = (f32[128,640]{1,0:T(8,128)}, f32[128,640]{1,0:T(8,128)}, u32[]{:S(2)}, u32[]{:S(2)}) collective-permute-start(f32[128,640]{1,0:T(8,128)} %fusion.50), channel_id=1, source_target_pairs={{0,4},{4,0},{1,5},{5,1},{2,6},{6,2},{3,7},{7,3},{8,12},{12,8},{9,1... | collective-permute-start | bytes 983048 | tf_op jit(solution)/shard_map/ppermute | solution.py:12
  10.4 4.8 %collective-permute-start.3 = (f32[128,640]{1,0:T(8,128)}, f32[128,640]{1,0:T(8,128)}, u32[]{:S(2)}, u32[]{:S(2)}) collective-permute-start(f32[128,640]{1,0:T(8,128)} %fusion.52), channel_id=1, source_target_pairs={{0,4},{4,0},{1,5},{5,1},{2,6},{6,2},{3,7},{7,3},{8,12},{12,8},{9,1... | collective-permute-start | bytes 983048 | tf_op jit(solution)/shard_map/ppermute | solution.py:12
  18.8 18.2 %copy-start.3 = (bf16[2560,640]{1,0:T(8,128)(2,1)S(1)}, bf16[2560,640]{1,0:T(8,128)(2,1)}, u32[]{:S(2)}) copy-start(bf16[2560,640]{1,0:T(8,128)(2,1)} %param.6) | copy-start | bytes 9830404
  20.1 7.7 %collective-permute-start.4 = (bf16[5,128,128]{2,1,0:T(8,128)(2,1)S(1)}, bf16[5,128,128]{2,1,0:T(8,128)(2,1)S(1)}, u32[]{:S(2)}, u32[]{:S(2)}) collective-permute-start(bf16[5,128,128]{2,1,0:T(8,128)(2,1)S(1)} %get-tuple-element.9), channel_id=1, source_target_pairs={{0,8},{8,16},{16,24},{24,0},{32,40},{40,48},{48,56},{56,32},{64,72... | collective-permute-start | bytes 491528 | tf_op jit(solution)/shard_map/ppermute | solution.py:16
  21.7 8.6 %collective-permute-start.5 = (bf16[5,128,128]{2,1,0:T(8,128)(2,1)S(1)}, bf16[5,128,128]{2,1,0:T(8,128)(2,1)S(1)}, u32[]{:S(2)}, u32[]{:S(2)}) collective-permute-start(bf16[5,128,128]{2,1,0:T(8,128)(2,1)S(1)} %get-tuple-element.9), channel_id=1, source_target_pairs={{0,16},{8,24},{16,0},{24,8},{32,48},{40,56},{48,32},{56,40},{64,80... | collective-permute-start | bytes 491528 | tf_op jit(solution)/shard_map/ppermute | solution.py:16
  22.8 9.1 %collective-permute-start.6 = (bf16[5,128,128]{2,1,0:T(8,128)(2,1)S(1)}, bf16[5,128,128]{2,1,0:T(8,128)(2,1)S(1)}, u32[]{:S(2)}, u32[]{:S(2)}) collective-permute-start(bf16[5,128,128]{2,1,0:T(8,128)(2,1)S(1)} %get-tuple-element.9), channel_id=1, source_target_pairs={{0,24},{8,0},{16,8},{24,16},{32,56},{40,32},{48,40},{56,48},{64,88... | collective-permute-start | bytes 491528 | tf_op jit(solution)/shard_map/ppermute | solution.py:16
  27.7 16.8 %copy-start.5 = (bf16[5,128,128]{2,1,0:T(8,128)(2,1)}, bf16[5,128,128]{2,1,0:T(8,128)(2,1)S(1)}, u32[]{:S(2)}) copy-start(bf16[5,128,128]{2,1,0:T(8,128)(2,1)S(1)} %collective-permute-done.4) | copy-start | bytes 491524
  30.2 14.3 %copy-start.6 = (bf16[5,128,128]{2,1,0:T(8,128)(2,1)}, bf16[5,128,128]{2,1,0:T(8,128)(2,1)S(1)}, u32[]{:S(2)}) copy-start(bf16[5,128,128]{2,1,0:T(8,128)(2,1)S(1)} %collective-permute-done.5) | copy-start | bytes 491524
  31.9 12.7 %copy-start.7 = (bf16[5,128,128]{2,1,0:T(8,128)(2,1)}, bf16[5,128,128]{2,1,0:T(8,128)(2,1)S(1)}, u32[]{:S(2)}) copy-start(bf16[5,128,128]{2,1,0:T(8,128)(2,1)S(1)} %collective-permute-done.6) | copy-start | bytes 491524
  31.9 6.9 %collective-permute-start.7 = (bf16[5,128,128]{2,1,0:T(8,128)(2,1)S(1)}, bf16[5,128,128]{2,1,0:T(8,128)(2,1)S(1)}, u32[]{:S(2)}, u32[]{:S(2)}) collective-permute-start(bf16[5,128,128]{2,1,0:T(8,128)(2,1)S(1)} %fusion.44), channel_id=1, source_target_pairs={{0,32},{8,40},{16,48},{24,56},{32,64},{40,72},{48,80},{56,88},{64,... | collective-permute-start | bytes 491528 | tf_op jit(solution)/shard_map/ppermute | solution.py:16
  33.6 8.4 %collective-permute-start.8 = (bf16[5,128,128]{2,1,0:T(8,128)(2,1)S(1)}, bf16[5,128,128]{2,1,0:T(8,128)(2,1)S(1)}, u32[]{:S(2)}, u32[]{:S(2)}) collective-permute-start(bf16[5,128,128]{2,1,0:T(8,128)(2,1)S(1)} %fusion.44), channel_id=1, source_target_pairs={{0,64},{8,72},{16,80},{24,88},{32,96},{40,104},{48,112},{56,120},{... | collective-permute-start | bytes 491528 | tf_op jit(solution)/shard_map/ppermute | solution.py:16
  35.2 8.5 %collective-permute-start.9 = (bf16[5,128,128]{2,1,0:T(8,128)(2,1)S(1)}, bf16[5,128,128]{2,1,0:T(8,128)(2,1)S(1)}, u32[]{:S(2)}, u32[]{:S(2)}) collective-permute-start(bf16[5,128,128]{2,1,0:T(8,128)(2,1)S(1)} %fusion.44), channel_id=1, source_target_pairs={{0,96},{8,104},{16,112},{24,120},{32,0},{40,8},{48,16},{56,24},{64... | collective-permute-start | bytes 491528 | tf_op jit(solution)/shard_map/ppermute | solution.py:16
  38.7 15.0 %collective-permute-start.2 = (f32[128,640]{1,0:T(8,128)S(1)}, f32[128,640]{1,0:T(8,128)S(1)}, u32[]{:S(2)}, u32[]{:S(2)}) collective-permute-start(f32[128,640]{1,0:T(8,128)S(1)} %fusion.51), channel_id=1, source_target_pairs={{0,4},{4,0},{1,5},{5,1},{2,6},{6,2},{3,7},{7,3},{8,12},{12,8},{9,1... | collective-permute-start | bytes 983048 | tf_op jit(solution)/shard_map/ppermute | solution.py:12
  38.8 14.8 %copy-start.8 = (bf16[5,128,128]{2,1,0:T(8,128)(2,1)}, bf16[5,128,128]{2,1,0:T(8,128)(2,1)S(1)}, u32[]{:S(2)}) copy-start(bf16[5,128,128]{2,1,0:T(8,128)(2,1)S(1)} %collective-permute-done.7) | copy-start | bytes 491524
  42.0 11.7 %copy-start.9 = (bf16[5,128,128]{2,1,0:T(8,128)(2,1)}, bf16[5,128,128]{2,1,0:T(8,128)(2,1)S(1)}, u32[]{:S(2)}) copy-start(bf16[5,128,128]{2,1,0:T(8,128)(2,1)S(1)} %collective-permute-done.8) | copy-start | bytes 491524
  43.8 9.9 %copy-start.10 = (bf16[5,128,128]{2,1,0:T(8,128)(2,1)}, bf16[5,128,128]{2,1,0:T(8,128)(2,1)S(1)}, u32[]{:S(2)}) copy-start(bf16[5,128,128]{2,1,0:T(8,128)(2,1)S(1)} %collective-permute-done.9) | copy-start | bytes 491524
  44.6 11.7 %collective-permute-start.10 = (bf16[5,128,128]{2,1,0:T(8,128)(2,1)}, bf16[5,128,128]{2,1,0:T(8,128)(2,1)}, u32[]{:S(2)}, u32[]{:S(2)}) collective-permute-start(bf16[5,128,128]{2,1,0:T(8,128)(2,1)} %fusion.30), channel_id=1, source_target_pairs={{0,128},{8,136},{16,144},{24,152},{32,160},{40,168},{48,176},{56,1... | collective-permute-start | bytes 491528 | tf_op jit(solution)/shard_map/ppermute | solution.py:16
  70.1 1.5 %copy-start.1 = (f32[4,128,1280]{2,1,0:T(8,128)}, f32[4,128,1280]{2,1,0:T(8,128)S(1)}, u32[]{:S(2)}) copy-start(f32[4,128,1280]{2,1,0:T(8,128)S(1)} %pad_maximum_fusion) | copy-start | bytes 7864324
  72.5 13.0 %collective-permute-start.12 = (bf16[128,1280]{1,0:T(8,128)(2,1)}, bf16[128,1280]{1,0:T(8,128)(2,1)}, u32[]{:S(2)}, u32[]{:S(2)}) collective-permute-start(bf16[128,1280]{1,0:T(8,128)(2,1)} %get-tuple-element.7), channel_id=1, source_target_pairs={{0,1},{4,5},{8,9},{12,13},{16,17},{20,21},{24,25},{28,29},{32,33},... | collective-permute-start | bytes 983048 | tf_op jit(solution)/shard_map/ppermute | solution.py:112
  79.7 12.8 %collective-permute-start.15 = (bf16[128,1280]{1,0:T(8,128)(2,1)}, bf16[128,1280]{1,0:T(8,128)(2,1)}, u32[]{:S(2)}, u32[]{:S(2)}) collective-permute-start(bf16[128,1280]{1,0:T(8,128)(2,1)} %get-tuple-element.8), channel_id=1, source_target_pairs={{3,2},{7,6},{11,10},{15,14},{19,18},{23,22},{27,26},{31,30},{35,34... | collective-permute-start | bytes 983048 | tf_op jit(solution)/shard_map/ppermute | solution.py:113
  87.4 10.0 %collective-permute-start.13 = (bf16[128,1280]{1,0:T(8,128)(2,1)}, bf16[128,1280]{1,0:T(8,128)(2,1)}, u32[]{:S(2)}, u32[]{:S(2)}) collective-permute-start(bf16[128,1280]{1,0:T(8,128)(2,1)} %fusion.8), channel_id=1, source_target_pairs={{0,1},{1,2},{4,5},{5,6},{8,9},{9,10},{12,13},{13,14},{16,17},{17,1... | collective-permute-start | bytes 983048 | tf_op jit(solution)/shard_map/ppermute | solution.py:112
  99.9 6.4 %collective-permute-start.16 = (bf16[128,1280]{1,0:T(8,128)(2,1)}, bf16[128,1280]{1,0:T(8,128)(2,1)}, u32[]{:S(2)}, u32[]{:S(2)}) collective-permute-start(bf16[128,1280]{1,0:T(8,128)(2,1)} %get-tuple-element.6), channel_id=1, source_target_pairs={{2,1},{3,2},{6,5},{7,6},{10,9},{11,10},{14,13},{15,14},{18,17},{19... | collective-permute-start | bytes 983048 | tf_op jit(solution)/shard_map/ppermute | solution.py:113
  101.3 9.2 %collective-permute-start.14 = (bf16[128,1280]{1,0:T(8,128)(2,1)}, bf16[128,1280]{1,0:T(8,128)(2,1)}, u32[]{:S(2)}, u32[]{:S(2)}) collective-permute-start(bf16[128,1280]{1,0:T(8,128)(2,1)} %get-tuple-element.5), channel_id=1, source_target_pairs={{0,1},{1,2},{2,3},{4,5},{5,6},{6,7},{8,9},{9,10},{10,11},{12,13},{... | collective-permute-start | bytes 983048 | tf_op jit(solution)/shard_map/ppermute | solution.py:112
  108.3 12.6 %collective-permute-start.17 = (bf16[128,1280]{1,0:T(8,128)(2,1)}, bf16[128,1280]{1,0:T(8,128)(2,1)}, u32[]{:S(2)}, u32[]{:S(2)}) collective-permute-start(bf16[128,1280]{1,0:T(8,128)(2,1)} %fusion.7), channel_id=1, source_target_pairs={{1,0},{2,1},{3,2},{5,4},{6,5},{7,6},{9,8},{10,9},{11,10},{13,12},{... | collective-permute-start | bytes 983048 | tf_op jit(solution)/shard_map/ppermute | solution.py:113

commit v4 on v3

--- a/solution.py
+++ b/solution.py
@@ -88,17 +88,12 @@
     n = 4
     h = lax.axis_index("head")
 
-    products = jnp.stack(
-        [
-            jnp.dot(normed, w[:, k * quarter : (k + 1) * quarter], preferred_element_type=F32)
-            for w in (w_output, w_other)
-            for k in range(2)
-        ]
-    )
+    halves = jnp.stack([w_output, w_other])
 
     def block(q):
-        k = jnp.where(q // 2 == c, 0, 2) + q % 2
-        return lax.dynamic_index_in_dim(products, k, 0, keepdims=False)
+        k = jnp.where(q // 2 == c, 0, 1)
+        wq = lax.dynamic_slice(halves, (k, 0, (q % 2) * quarter), (1, halves.shape[1], quarter))[0]
+        return jnp.dot(normed, wq, preferred_element_type=F32)
 
     right = jnp.zeros((tok_count, quarter), F32)
     left = jnp.zeros((tok_count, quarter), F32)
@@ -107,6 +102,7 @@
         ql = jnp.clip(h - n + s, 0, n - 1)
         send_r = (block(qr) + right).astype(BF16)
         send_l = (block(ql) + left).astype(BF16)
+        send_r, send_l = lax.optimization_barrier((send_r, send_l))
         rpairs = [(j, j + 1) for j in range(s) if j + 1 < n]
         lpairs = [(j, j - 1) for j in range(n - s, n) if j - 1 >= 0]
         right = lax.ppermute(send_r, "head", rpairs).astype(F32)

time: 124 us -> 119 us (0.960)
  matrix products: 27.6 us -> 41.4 us
  waiting for transfers between devices: 29.7 us -> 19.3 us
  other arithmetic: 15 us -> 6.29 us
  starting transfers between devices: 41.4 us -> 44.2 us
  local copies, waits for them, and re-layouts: 9.1 us -> 6.69 us
    dot_general x4 -> x7, matrix products: 7.53 us -> 21.3 us  [block(): return jnp.dot(normed, wq, preferred_element_type=F32)]
    convert_element_type x3 -> x0, other arithmetic: 6.38 us -> none  [the longest x2 4.4 us: shards(): send_r = (block(qr) + right).astype(BF16)]
    ppermute x3, waiting for transfers between devices: 10.4 us -> 5.1 us  [shards(): left = lax.ppermute(send_l, 'head', lpairs).astype(F32)]
    ppermute x3, waiting for transfers between devices: 10.2 us -> 5.07 us  [shards(): right = lax.ppermute(send_r, 'head', rpairs).astype(F32)]
    ppermute x3, starting transfers between devices: 17.3 us -> 20.2 us  [shards(): right = lax.ppermute(send_r, 'head', rpairs).astype(F32)]
    reshape x1 -> x0, other arithmetic: 2.11 us -> none  [shards(): return mixed.reshape(1, tok_count, quarter)]
    unnamed x22 -> x26, local copies, waits for them, and re-layouts: 1.55 us -> 0.05 us
  transfers between devices with their start and end apart: 18 -> 18, of which waited for: 9 -> 9; matrix products, arithmetic and copies ran while one was open for 31% -> 32% of each run, Pallas kernels for 0% -> 0%
where the time goes in v4:
time: 119 us; the launch traced here: 118 us
  starting transfers between devices  44.2 us (37%)
  matrix products  41.4 us (35%)
  waiting for transfers between devices  19.3 us (16%)
  local copies, waits for them, and re-layouts  6.69 us (6%)
  other arithmetic  6.29 us (5%)
    dot_general x7, matrix products, block(): return jnp.dot(normed, wq, preferred_element_type=F32)  21.3 us
    ppermute x3, starting transfers between devices, shards(): right = lax.ppermute(send_r, 'head', rpairs).astype(F32)  20.2 us
    ppermute x7, starting transfers between devices, shifted(): return lax.ppermute(x, axis, pairs)  18.9 us
    ppermute x7, waiting for transfers between devices, shifted(): return lax.ppermute(x, axis, pairs)  9.08 us
    dot_general x3, matrix products, shards(): lent = swap_cores(jnp.dot(got_cols, w, preferred_element_type=F32))  6.88 us
    dot_general x3, matrix products, shards(): own = jnp.dot(mine_cols, w, preferred_element_type=F32)  6.88 us
    ppermute x3, waiting for transfers between devices, shards(): left = lax.ppermute(send_l, 'head', lpairs).astype(F32)  5.1 us
    ppermute x3, waiting for transfers between devices, shards(): right = lax.ppermute(send_r, 'head', rpairs).astype(F32)  5.07 us
  transfers between devices with their start and end apart: 18, of which 9 were waited for; matrix products, arithmetic and copies ran while one was open for 32% of the time, Pallas kernels for 0%

profile of v4, /device:TPU:10, one launch (start us, length us, event | category | flops | bytes accessed | tf_op | source)
XLA Modules:
  0.0 118.0 jit_solution(12166363798009156219)
XLA Ops:
  0.0 2.1 %dynamic-slice_bitcast_fusion = bf16[128,2560]{1,0:T(8,128)(2,1)} fusion(bf16[1,128,5120]{2,1,0:T(8,128)(2,1)} %param.5, s32[]{:T(128)S(6)} %select_n.183), kind=kLoop, calls=%fused_computation.57 | loop fusion | bytes 1310724 | tf_op jit(solution)/shard_map/dynamic_slice | solution.py:59
  2.1 0.0 collective-permute-start
  2.1 0.5 collective-permute-start.11
  2.6 2.7 %fusion.68 = f32[128,640]{1,0:T(8,128)} fusion(bf16[2560,640]{1,0:T(8,128)(2,1)S(1)} %copy-done, bf16[1,128,5120]{2,1,0:T(8,128)(2,1)} %param.5, s32[]{:T(128)S(6)} %select_n.182), kind=kOutput, calls=%fused_computation.55 | convolution fusion | flops 419430400 | bytes 4259844 | tf_op jit(solution)/shard_map/dot_general | solution.py:64
  5.3 0.0 collective-permute-done
  5.3 2.6 %fusion.113 = f32[128,640]{1,0:T(8,128)} fusion(bf16[128,2560]{1,0:T(8,128)(2,1)} %collective-permute-done, bf16[2560,640]{1,0:T(8,128)(2,1)S(1)} %copy-done), kind=kOutput, calls=%fused_computation.118 | convolution fusion | flops 419430400 | bytes 4259840 | tf_op jit(solution)/shard_map/dot_general | solution.py:63
  7.9 0.0 collective-permute-start.1
  7.9 0.0 copy-done.4
  7.9 2.5 %fusion.115 = f32[128,640]{1,0:T(8,128)} fusion(bf16[128,2560]{1,0:T(8,128)(2,1)} %collective-permute-done, bf16[2560,640]{1,0:T(8,128)(2,1)S(1)} %copy-done.4), kind=kOutput, calls=%fused_computation.120 | convolution fusion | flops 419430400 | bytes 4259840 | tf_op jit(solution)/shard_map/dot_general | solution.py:63
  10.4 0.5 collective-permute-start.3
  10.9 1.4 %fusion.64 = f32[128,640]{1,0:T(8,128)} fusion(bf16[2560,640]{1,0:T(8,128)(2,1)S(1)} %copy-done.4, bf16[1,128,5120]{2,1,0:T(8,128)(2,1)S(1)} %copy-done.6, s32[]{:T(128)S(6)} %select_n.182), kind=kOutput, calls=%fused_computation.51 | convolution fusion | flops 419430400 | bytes 4259844 | tf_op jit(solution)/shard_map/dot_general | solution.py:64
  12.4 0.0 collective-permute-done.1
  12.4 1.8 %add_convert_fusion = bf16[128,640]{1,0:T(8,128)(2,1)} fusion(f32[128,640]{1,0:T(8,128)} %fusion.68, f32[128,640]{1,0:T(8,128)} %collective-permute-done.1), kind=kLoop, calls=%fused_computation.86 | loop fusion | flops 163840 | bytes 819200 | tf_op jit(solution)/shard_map/convert_element_type | solution.py:70
  14.1 1.1 copy.11
  15.2 0.0 collective-permute-done.3
  15.2 1.8 %multiply_convert_fusion.1 = bf16[128,640]{1,0:T(8,128)(2,1)} fusion(f32[128,640]{1,0:T(8,128)} %fusion.64, f32[128,640]{1,0:T(8,128)} %collective-permute-done.3), kind=kLoop, calls=%fused_computation.84 | loop fusion | flops 491520 | bytes 819200 | tf_op jit(solution)/shard_map/convert_element_type | solution.py:69
  17.0 1.7 %copy.13 = bf16[128,640]{0,1:T(8,128)(2,1)} copy(bf16[128,640]{1,0:T(8,128)(2,1)} %multiply_convert_fusion.1) | data formatting | bytes 327680 | tf_op jit(solution)/shard_map/convert_element_type | solution.py:69
  18.8 1.3 %fusion.112 = (bf16[5,128,128]{2,1,0:T(8,128)(2,1)S(1)}, f32[5,128,128]{2,1,0:T(8,128)S(1)}) fusion(bf16[128,5,128]{0,2,1:T(8,128)(2,1)} %bitcast.102, bf16[128,5,128]{0,2,1:T(8,128)(2,1)S(1)} %bitcast.100), kind=kOutput, calls=%fused_computation.117 | convolution fusion | flops 21053440 | bytes 819200 | tf_op jit(solution)/shard_map/thd,the->hde/dot_general | solution.py:71
  20.1 1.6 %collective-permute-start.4 = (bf16[5,128,128]{2,1,0:T(8,128)(2,1)S(1)}, bf16[5,128,128]{2,1,0:T(8,128)(2,1)S(1)}, u32[]{:S(2)}, u32[]{:S(2)}) collective-permute-start(bf16[5,128,128]{2,1,0:T(8,128)(2,1)S(1)} %get-tuple-element.17), channel_id=1, source_target_pairs={{0,8},{8,16},{16,24},{24,0},{32,40},{40,48},{48,56},{56,32},{64,72... | collective-permute-start | bytes 491528 | tf_op jit(solution)/shard_map/ppermute | solution.py:16
  21.7 1.1 collective-permute-start.5
  22.8 2.1 %collective-permute-start.6 = (bf16[5,128,128]{2,1,0:T(8,128)(2,1)S(1)}, bf16[5,128,128]{2,1,0:T(8,128)(2,1)S(1)}, u32[]{:S(2)}, u32[]{:S(2)}) collective-permute-start(bf16[5,128,128]{2,1,0:T(8,128)(2,1)S(1)} %get-tuple-element.17), channel_id=1, source_target_pairs={{0,24},{8,0},{16,8},{24,16},{32,56},{40,32},{48,40},{56,48},{64,88... | collective-permute-start | bytes 491528 | tf_op jit(solution)/shard_map/ppermute | solution.py:16
  24.9 2.8 %fusion.66 = f32[128,640]{1,0:T(8,128)S(1)} fusion(bf16[2560,640]{1,0:T(8,128)(2,1)} %param.6, bf16[1,128,5120]{2,1,0:T(8,128)(2,1)} %param.5, s32[]{:T(128)S(6)} %select_n.182), kind=kOutput, calls=%fused_computation.53 | convolution fusion | flops 419430400 | bytes 4259844 | tf_op jit(solution)/shard_map/dot_general | solution.py:64
  27.7 0.0 collective-permute-done.4
  27.8 2.5 %collective-permute-done.5 = bf16[5,128,128]{2,1,0:T(8,128)(2,1)S(1)} collective-permute-done((bf16[5,128,128]{2,1,0:T(8,128)(2,1)S(1)}, bf16[5,128,128]{2,1,0:T(8,128)(2,1)S(1)}, u32[]{:S(2)}, u32[]{:S(2)}) %collective-permute-start.5) | collective-permute-done | bytes 163872 | tf_op jit(solution)/shard_map/ppermute | solution.py:16
  30.2 1.6 %collective-permute-done.6 = bf16[5,128,128]{2,1,0:T(8,128)(2,1)S(1)} collective-permute-done((bf16[5,128,128]{2,1,0:T(8,128)(2,1)S(1)}, bf16[5,128,128]{2,1,0:T(8,128)(2,1)S(1)}, u32[]{:S(2)}, u32[]{:S(2)}) %collective-permute-start.6) | collective-permute-done | bytes 163872 | tf_op jit(solution)/shard_map/ppermute | solution.py:16
  31.9 0.1 fusion.93
  31.9 1.6 %collective-permute-start.7 = (bf16[5,128,128]{2,1,0:T(8,128)(2,1)S(1)}, bf16[5,128,128]{2,1,0:T(8,128)(2,1)S(1)}, u32[]{:S(2)}, u32[]{:S(2)}) collective-permute-start(bf16[5,128,128]{2,1,0:T(8,128)(2,1)S(1)} %fusion.93), channel_id=1, source_target_pairs={{0,32},{8,40},{16,48},{24,56},{32,64},{40,72},{48,80},{56,88},{64,... | collective-permute-start | bytes 491528 | tf_op jit(solution)/shard_map/ppermute | solution.py:16
  33.6 1.6 %collective-permute-start.8 = (bf16[5,128,128]{2,1,0:T(8,128)(2,1)S(1)}, bf16[5,128,128]{2,1,0:T(8,128)(2,1)S(1)}, u32[]{:S(2)}, u32[]{:S(2)}) collective-permute-start(bf16[5,128,128]{2,1,0:T(8,128)(2,1)S(1)} %fusion.93), channel_id=1, source_target_pairs={{0,64},{8,72},{16,80},{24,88},{32,96},{40,104},{48,112},{56,120},{... | collective-permute-start | bytes 491528 | tf_op jit(solution)/shard_map/ppermute | solution.py:16
  35.2 1.7 %collective-permute-start.9 = (bf16[5,128,128]{2,1,0:T(8,128)(2,1)S(1)}, bf16[5,128,128]{2,1,0:T(8,128)(2,1)S(1)}, u32[]{:S(2)}, u32[]{:S(2)}) collective-permute-start(bf16[5,128,128]{2,1,0:T(8,128)(2,1)S(1)} %fusion.93), channel_id=1, source_target_pairs={{0,96},{8,104},{16,112},{24,120},{32,0},{40,8},{48,16},{56,24},{64... | collective-permute-start | bytes 491528 | tf_op jit(solution)/shard_map/ppermute | solution.py:16
  36.9 1.8 %fusion.114 = f32[128,640]{1,0:T(8,128)S(1)} fusion(bf16[128,2560]{1,0:T(8,128)(2,1)} %collective-permute-done, bf16[2560,640]{1,0:T(8,128)(2,1)S(1)} %copy-done.5), kind=kOutput, calls=%fused_computation.119 | convolution fusion | flops 419430400 | bytes 4259840 | tf_op jit(solution)/shard_map/dot_general | solution.py:63
  38.7 0.1 collective-permute-start.2
  38.8 0.0 collective-permute-done.7
  38.8 3.2 %collective-permute-done.8 = bf16[5,128,128]{2,1,0:T(8,128)(2,1)S(1)} collective-permute-done((bf16[5,128,128]{2,1,0:T(8,128)(2,1)S(1)}, bf16[5,128,128]{2,1,0:T(8,128)(2,1)S(1)}, u32[]{:S(2)}, u32[]{:S(2)}) %collective-permute-start.8) | collective-permute-done | bytes 163872 | tf_op jit(solution)/shard_map/ppermute | solution.py:16
  42.0 1.8 %collective-permute-done.9 = bf16[5,128,128]{2,1,0:T(8,128)(2,1)S(1)} collective-permute-done((bf16[5,128,128]{2,1,0:T(8,128)(2,1)S(1)}, bf16[5,128,128]{2,1,0:T(8,128)(2,1)S(1)}, u32[]{:S(2)}, u32[]{:S(2)}) %collective-permute-start.9) | collective-permute-done | bytes 163872 | tf_op jit(solution)/shard_map/ppermute | solution.py:16
  43.8 0.8 fusion.82
  44.6 9.1 %collective-permute-start.10 = (bf16[5,128,128]{2,1,0:T(8,128)(2,1)}, bf16[5,128,128]{2,1,0:T(8,128)(2,1)}, u32[]{:S(2)}, u32[]{:S(2)}) collective-permute-start(bf16[5,128,128]{2,1,0:T(8,128)(2,1)} %fusion.82), channel_id=1, source_target_pairs={{0,128},{8,136},{16,144},{24,152},{32,160},{40,168},{48,176},{56,1... | collective-permute-start | bytes 491528 | tf_op jit(solution)/shard_map/ppermute | solution.py:16
  53.7 0.0 collective-permute-done.2
  53.7 0.8 multiply_convert_fusion.2
  54.5 1.7 %copy.12 = bf16[128,640]{0,1:T(8,128)(2,1)} copy(bf16[128,640]{1,0:T(8,128)(2,1)} %multiply_convert_fusion.2) | data formatting | bytes 327680 | tf_op jit(solution)/shard_map/convert_element_type | solution.py:68
  56.2 0.1 collective-permute-done.10
  56.2 2.7 %fusion.77 = f32[5,128,128]{2,1,0:T(8,128)} fusion(bf16[128,5,128]{0,2,1:T(8,128)(2,1)} %bitcast.104, bf16[5,128,128]{2,1,0:T(8,128)(2,1)} %copy-done.7, bf16[5,128,128]{2,1,0:T(8,128)(2,1)} %copy-done.8, bf16[5,128,128]{2,1,0:T(8,128)(2,1)} %copy-done.9, bf16[5,128,128]{2,1,0:T(8,128)(2,1)} %copy-done.10, bf16[5,128,128]{2,1,0:T(8,128)(2,1)} %copy-done.11, ...), kind=kOutput, calls=%fused_computation.77 | convolution fusion | flops 127385600 | bytes 1638406 | tf_op jit(solution)/shard_map/thd,hde->the/dot_general | solution.py:79
  58.9 2.3 %multiply_reduce_fusion = (f32[128,5]{0,1:T(8,128)S(1)}, f32[128,5,128]{0,2,1:T(8,128)}) fusion(f32[5,128,128]{2,1,0:T(8,128)} %fusion.77, bf16[128,5,128]{0,2,1:T(8,128)(2,1)S(1)} %bitcast.101, bf16[128,5,128]{0,2,1:T(8,128)(2,1)} %bitcast.105, bf16[128,5,128]{0,2,1:T(8,128)(2,1)} %bitcast.103, f32[128,128]{1,0:T(8,128)S(1)} %fusion.92), kind=kOutput, calls=%fused_computation.82 | convolution fusion | flops 42352000 | bytes 1214976 | tf_op jit(solution)/shard_map/hts,shd->thd/dot_general | solution.py:78
  61.2 1.0 multiply_convert_fusion
  62.2 0.0 collective-permute-done.11
  62.3 0.0 copy-start.1
  62.3 3.2 %convolution_convert_fusion = bf16[128,1280]{1,0:T(8,128)(2,1)} fusion(bf16[128,640]{0,1:T(8,128)(2,1)S(1)} %bitcast.93, s32[]{:T(128)S(6)} %select_n.222, s32[]{:T(128)S(6)} %select_n.224, bf16[1,640,2560]{2,1,0:T(8,128)(2,1)} %bitcast.86, bf16[1,640,2560]{2,1,0:T(8,128)(2,1)} %bitcast.8), kind=kOutput, calls=%fused_computation.14 | convolution fusion | flops 213155840 | bytes 7045128 | tf_op jit(solution)/shard_map/dot_general | solution.py:96
  65.4 3.0 %convolution_convert_fusion.1 = bf16[128,1280]{1,0:T(8,128)(2,1)} fusion(bf16[128,640]{0,1:T(8,128)(2,1)S(1)} %bitcast.94, s32[]{:T(128)S(6)} %select_n.218, s32[]{:T(128)S(6)} %select_n.220, bf16[1,640,2560]{2,1,0:T(8,128)(2,1)S(1)} %bitcast.90, bf16[1,640,2560]{2,1,0:T(8,128)(2,1)} %bitcast.8), kind=kOutput, calls=%fused_computation.15 | convolution fusion | flops 213155840 | bytes 7045128 | tf_op jit(solution)/shard_map/dot_general | solution.py:96
  68.5 1.4 %collective-permute-start.13 = (bf16[128,1280]{1,0:T(8,128)(2,1)}, bf16[128,1280]{1,0:T(8,128)(2,1)}, u32[]{:S(2)}, u32[]{:S(2)}) collective-permute-start(bf16[128,1280]{1,0:T(8,128)(2,1)} %convolution_convert_fusion), channel_id=1, source_target_pairs={{3,2},{7,6},{11,10},{15,14},{19,18},{23,22},{27,26},{31,30},{35,34... | collective-permute-start | bytes 983048 | tf_op jit(solution)/shard_map/ppermute | solution.py:109
  69.8 7.1 %collective-permute-start.12 = (bf16[128,1280]{1,0:T(8,128)(2,1)}, bf16[128,1280]{1,0:T(8,128)(2,1)}, u32[]{:S(2)}, u32[]{:S(2)}) collective-permute-start(bf16[128,1280]{1,0:T(8,128)(2,1)} %convolution_convert_fusion.1), channel_id=1, source_target_pairs={{0,1},{4,5},{8,9},{12,13},{16,17},{20,21},{24,25},{28,29},{32,33},... | collective-permute-start | bytes 983048 | tf_op jit(solution)/shard_map/ppermute | solution.py:108
  77.0 0.0 collective-permute-done.13
  77.0 3.2 %fusion.21 = bf16[128,1280]{1,0:T(8,128)(2,1)} fusion(bf16[128,640]{0,1:T(8,128)(2,1)S(1)} %bitcast.95, s32[]{:T(128)S(6)} %select_n.226, s32[]{:T(128)S(6)} %select_n.228, bf16[1,640,2560]{2,1,0:T(8,128)(2,1)} %bitcast.87, bf16[1,640,2560]{2,1,0:T(8,128)(2,1)} %bitcast.8, bf16[128,1280]{1,0:T(8,128)(2,1)} %collective-permute-done.13), kind=kOutput, calls=%fused_computation.32 | convolution fusion | flops 213483520 | bytes 7372808 | tf_op jit(solution)/shard_map/dot_general | solution.py:96
  80.2 1.2 %collective-permute-done.12 = bf16[128,1280]{1,0:T(8,128)(2,1)} collective-permute-done((bf16[128,1280]{1,0:T(8,128)(2,1)}, bf16[128,1280]{1,0:T(8,128)(2,1)}, u32[]{:S(2)}, u32[]{:S(2)}) %collective-permute-start.12) | collective-permute-done | bytes 327712 | tf_op jit(solution)/shard_map/ppermute | solution.py:108
  81.4 3.1 %fusion.29 = bf16[128,1280]{1,0:T(8,128)(2,1)} fusion(bf16[128,640]{0,1:T(8,128)(2,1)S(1)} %bitcast.96, s32[]{:T(128)S(6)} %select_n.214, s32[]{:T(128)S(6)} %select_n.216, bf16[1,640,2560]{2,1,0:T(8,128)(2,1)S(1)} %bitcast.91, bf16[1,640,2560]{2,1,0:T(8,128)(2,1)} %bitcast.8, bf16[128,1280]{1,0:T(8,128)(2,1)} %collective-permute-done.12), kind=kOutput, calls=%fused_computation.35 | convolution fusion | flops 213483520 | bytes 7372808 | tf_op jit(solution)/shard_map/dot_general | solution.py:96
  84.4 1.4 %collective-permute-start.15 = (bf16[128,1280]{1,0:T(8,128)(2,1)}, bf16[128,1280]{1,0:T(8,128)(2,1)}, u32[]{:S(2)}, u32[]{:S(2)}) collective-permute-start(bf16[128,1280]{1,0:T(8,128)(2,1)} %fusion.21), channel_id=1, source_target_pairs={{2,1},{3,2},{6,5},{7,6},{10,9},{11,10},{14,13},{15,14},{18,17},{19... | collective-permute-start | bytes 983048 | tf_op jit(solution)/shard_map/ppermute | solution.py:109
  85.8 5.0 %collective-permute-start.14 = (bf16[128,1280]{1,0:T(8,128)(2,1)}, bf16[128,1280]{1,0:T(8,128)(2,1)}, u32[]{:S(2)}, u32[]{:S(2)}) collective-permute-start(bf16[128,1280]{1,0:T(8,128)(2,1)} %fusion.29), channel_id=1, source_target_pairs={{0,1},{1,2},{4,5},{5,6},{8,9},{9,10},{12,13},{13,14},{16,17},{17,1... | collective-permute-start | bytes 983048 | tf_op jit(solution)/shard_map/ppermute | solution.py:108
  90.8 0.0 collective-permute-done.15
  90.8 3.2 %fusion.59 = bf16[128,1280]{1,0:T(8,128)(2,1)} fusion(bf16[128,640]{0,1:T(8,128)(2,1)S(1)} %bitcast.97, s32[]{:T(128)S(6)} %select_n.230, s32[]{:T(128)S(6)} %select_n.232, bf16[1,640,2560]{2,1,0:T(8,128)(2,1)} %bitcast.88, bf16[1,640,2560]{2,1,0:T(8,128)(2,1)} %bitcast.8, bf16[128,1280]{1,0:T(8,128)(2,1)} %collective-permute-done.15), kind=kOutput, calls=%fused_computation.46 | convolution fusion | flops 213483520 | bytes 7372808 | tf_op jit(solution)/shard_map/dot_general | solution.py:96
  94.0 1.0 collective-permute-done.14
  95.0 2.5 %fusion.37 = bf16[128,1280]{1,0:T(8,128)(2,1)} fusion(bf16[128,640]{0,1:T(8,128)(2,1)S(1)} %bitcast.98, s32[]{:T(128)S(6)} %select_n.210, s32[]{:T(128)S(6)} %select_n.212, bf16[1,640,2560]{2,1,0:T(8,128)(2,1)S(1)} %bitcast.92, bf16[1,640,2560]{2,1,0:T(8,128)(2,1)} %bitcast.8, bf16[128,1280]{1,0:T(8,128)(2,1)} %collective-permute-done.14), kind=kOutput, calls=%fused_computation.38 | convolution fusion | flops 213483520 | bytes 7372808 | tf_op jit(solution)/shard_map/dot_general | solution.py:96
  97.6 8.0 %collective-permute-start.16 = (bf16[128,1280]{1,0:T(8,128)(2,1)}, bf16[128,1280]{1,0:T(8,128)(2,1)}, u32[]{:S(2)}, u32[]{:S(2)}) collective-permute-start(bf16[128,1280]{1,0:T(8,128)(2,1)} %fusion.37), channel_id=1, source_target_pairs={{0,1},{1,2},{2,3},{4,5},{5,6},{6,7},{8,9},{9,10},{10,11},{12,13},{... | collective-permute-start | bytes 983048 | tf_op jit(solution)/shard_map/ppermute | solution.py:108
  105.6 1.3 %collective-permute-start.17 = (bf16[128,1280]{1,0:T(8,128)(2,1)}, bf16[128,1280]{1,0:T(8,128)(2,1)}, u32[]{:S(2)}, u32[]{:S(2)}) collective-permute-start(bf16[128,1280]{1,0:T(8,128)(2,1)} %fusion.59), channel_id=1, source_target_pairs={{1,0},{2,1},{3,2},{5,4},{6,5},{7,6},{9,8},{10,9},{11,10},{13,12},{... | collective-permute-start | bytes 983048 | tf_op jit(solution)/shard_map/ppermute | solution.py:109
  106.9 2.9 %collective-permute-done.16 = bf16[128,1280]{1,0:T(8,128)(2,1)} collective-permute-done((bf16[128,1280]{1,0:T(8,128)(2,1)}, bf16[128,1280]{1,0:T(8,128)(2,1)}, u32[]{:S(2)}, u32[]{:S(2)}) %collective-permute-start.16) | collective-permute-done | bytes 327712 | tf_op jit(solution)/shard_map/ppermute | solution.py:108
  109.8 5.1 %collective-permute-done.17 = bf16[128,1280]{1,0:T(8,128)(2,1)} collective-permute-done((bf16[128,1280]{1,0:T(8,128)(2,1)}, bf16[128,1280]{1,0:T(8,128)(2,1)}, u32[]{:S(2)}, u32[]{:S(2)}) %collective-permute-start.17) | collective-permute-done | bytes 327712 | tf_op jit(solution)/shard_map/ppermute | solution.py:109
  114.9 3.1 %fusion.51 = bf16[1,128,1280]{2,1,0:T(8,128)(2,1)} fusion(bf16[128,640]{0,1:T(8,128)(2,1)S(1)} %bitcast.99, s32[]{:T(128)S(6)} %select_n.206, s32[]{:T(128)S(6)} %select_n.208, bf16[1,640,2560]{2,1,0:T(8,128)(2,1)} %bitcast.89, bf16[1,640,2560]{2,1,0:T(8,128)(2,1)} %bitcast.8, bf16[128,1280]{1,0:T(8,128)(2,1)} %collective-permute-done.17, ...), kind=kOutput, calls=%fused_computation.43 | convolution fusion | flops 213811200 | bytes 7700488 | tf_op jit(solution)/shard_map/dot_general | solution.py:96
  (26 shorter events, 0.1 us)
Async XLA Ops:
  0.0 2.6 %copy-start = (bf16[2560,640]{1,0:T(8,128)(2,1)S(1)}, bf16[2560,640]{1,0:T(8,128)(2,1)}, u32[]{:S(2)}) copy-start(bf16[2560,640]{1,0:T(8,128)(2,1)} %param.8) | copy-start | bytes 9830404
  2.1 3.2 %collective-permute-start = (bf16[128,2560]{1,0:T(8,128)(2,1)}, bf16[128,2560]{1,0:T(8,128)(2,1)}, u32[]{:S(2)}, u32[]{:S(2)}) collective-permute-start(bf16[128,2560]{1,0:T(8,128)(2,1)} %dynamic-slice_bitcast_fusion), channel_id=1, source_target_pairs={{0,4},{4,0},{1,5},{5,1},{2,6},{6,2},{3,7},{7,3},{8,12},{12,8},{9,1... | collective-permute-start | bytes 1966088 | tf_op jit(solution)/shard_map/ppermute | solution.py:12
  2.1 60.1 %collective-permute-start.11 = (bf16[640,2560]{1,0:T(8,128)(2,1)}, bf16[640,2560]{1,0:T(8,128)(2,1)}, u32[]{:S(2)}, u32[]{:S(2)}) collective-permute-start(bf16[640,2560]{1,0:T(8,128)(2,1)} %param.9), channel_id=1, source_target_pairs={{0,4},{4,0},{1,5},{5,1},{2,6},{6,2},{3,7},{7,3},{8,12},{12,8},{9,1... | collective-permute-start | bytes 9830408 | tf_op jit(solution)/shard_map/ppermute | solution.py:12
  2.6 5.3 %copy-start.4 = (bf16[2560,640]{1,0:T(8,128)(2,1)S(1)}, bf16[2560,640]{1,0:T(8,128)(2,1)}, u32[]{:S(2)}) copy-start(bf16[2560,640]{1,0:T(8,128)(2,1)} %param.7) | copy-start | bytes 9830404
  5.3 5.6 %copy-start.6 = (bf16[1,128,5120]{2,1,0:T(8,128)(2,1)S(1)}, bf16[1,128,5120]{2,1,0:T(8,128)(2,1)}, u32[]{:S(2)}) copy-start(bf16[1,128,5120]{2,1,0:T(8,128)(2,1)} %param.5) | copy-start | bytes 3932164
  7.9 4.4 %collective-permute-start.1 = (f32[128,640]{1,0:T(8,128)}, f32[128,640]{1,0:T(8,128)}, u32[]{:S(2)}, u32[]{:S(2)}) collective-permute-start(f32[128,640]{1,0:T(8,128)} %fusion.113), channel_id=1, source_target_pairs={{0,4},{4,0},{1,5},{5,1},{2,6},{6,2},{3,7},{7,3},{8,12},{12,8},{9,1... | collective-permute-start | bytes 983048 | tf_op jit(solution)/shard_map/ppermute | solution.py:12
  10.4 4.8 %collective-permute-start.3 = (f32[128,640]{1,0:T(8,128)}, f32[128,640]{1,0:T(8,128)}, u32[]{:S(2)}, u32[]{:S(2)}) collective-permute-start(f32[128,640]{1,0:T(8,128)} %fusion.115), channel_id=1, source_target_pairs={{0,4},{4,0},{1,5},{5,1},{2,6},{6,2},{3,7},{7,3},{8,12},{12,8},{9,1... | collective-permute-start | bytes 983048 | tf_op jit(solution)/shard_map/ppermute | solution.py:12
  18.8 18.2 %copy-start.5 = (bf16[2560,640]{1,0:T(8,128)(2,1)S(1)}, bf16[2560,640]{1,0:T(8,128)(2,1)}, u32[]{:S(2)}) copy-start(bf16[2560,640]{1,0:T(8,128)(2,1)} %param.6) | copy-start | bytes 9830404
  20.1 7.7 %collective-permute-start.4 = (bf16[5,128,128]{2,1,0:T(8,128)(2,1)S(1)}, bf16[5,128,128]{2,1,0:T(8,128)(2,1)S(1)}, u32[]{:S(2)}, u32[]{:S(2)}) collective-permute-start(bf16[5,128,128]{2,1,0:T(8,128)(2,1)S(1)} %get-tuple-element.17), channel_id=1, source_target_pairs={{0,8},{8,16},{16,24},{24,0},{32,40},{40,48},{48,56},{56,32},{64,72... | collective-permute-start | bytes 491528 | tf_op jit(solution)/shard_map/ppermute | solution.py:16
  21.7 8.6 %collective-permute-start.5 = (bf16[5,128,128]{2,1,0:T(8,128)(2,1)S(1)}, bf16[5,128,128]{2,1,0:T(8,128)(2,1)S(1)}, u32[]{:S(2)}, u32[]{:S(2)}) collective-permute-start(bf16[5,128,128]{2,1,0:T(8,128)(2,1)S(1)} %get-tuple-element.17), channel_id=1, source_target_pairs={{0,16},{8,24},{16,0},{24,8},{32,48},{40,56},{48,32},{56,40},{64,80... | collective-permute-start | bytes 491528 | tf_op jit(solution)/shard_map/ppermute | solution.py:16
  22.8 9.1 %collective-permute-start.6 = (bf16[5,128,128]{2,1,0:T(8,128)(2,1)S(1)}, bf16[5,128,128]{2,1,0:T(8,128)(2,1)S(1)}, u32[]{:S(2)}, u32[]{:S(2)}) collective-permute-start(bf16[5,128,128]{2,1,0:T(8,128)(2,1)S(1)} %get-tuple-element.17), channel_id=1, source_target_pairs={{0,24},{8,0},{16,8},{24,16},{32,56},{40,32},{48,40},{56,48},{64,88... | collective-permute-start | bytes 491528 | tf_op jit(solution)/shard_map/ppermute | solution.py:16
  27.7 16.8 %copy-start.7 = (bf16[5,128,128]{2,1,0:T(8,128)(2,1)}, bf16[5,128,128]{2,1,0:T(8,128)(2,1)S(1)}, u32[]{:S(2)}) copy-start(bf16[5,128,128]{2,1,0:T(8,128)(2,1)S(1)} %collective-permute-done.4) | copy-start | bytes 491524
  30.2 14.3 %copy-start.8 = (bf16[5,128,128]{2,1,0:T(8,128)(2,1)}, bf16[5,128,128]{2,1,0:T(8,128)(2,1)S(1)}, u32[]{:S(2)}) copy-start(bf16[5,128,128]{2,1,0:T(8,128)(2,1)S(1)} %collective-permute-done.5) | copy-start | bytes 491524
  31.9 12.7 %copy-start.9 = (bf16[5,128,128]{2,1,0:T(8,128)(2,1)}, bf16[5,128,128]{2,1,0:T(8,128)(2,1)S(1)}, u32[]{:S(2)}) copy-start(bf16[5,128,128]{2,1,0:T(8,128)(2,1)S(1)} %collective-permute-done.6) | copy-start | bytes 491524
  31.9 6.9 %collective-permute-start.7 = (bf16[5,128,128]{2,1,0:T(8,128)(2,1)S(1)}, bf16[5,128,128]{2,1,0:T(8,128)(2,1)S(1)}, u32[]{:S(2)}, u32[]{:S(2)}) collective-permute-start(bf16[5,128,128]{2,1,0:T(8,128)(2,1)S(1)} %fusion.93), channel_id=1, source_target_pairs={{0,32},{8,40},{16,48},{24,56},{32,64},{40,72},{48,80},{56,88},{64,... | collective-permute-start | bytes 491528 | tf_op jit(solution)/shard_map/ppermute | solution.py:16
  33.6 8.4 %collective-permute-start.8 = (bf16[5,128,128]{2,1,0:T(8,128)(2,1)S(1)}, bf16[5,128,128]{2,1,0:T(8,128)(2,1)S(1)}, u32[]{:S(2)}, u32[]{:S(2)}) collective-permute-start(bf16[5,128,128]{2,1,0:T(8,128)(2,1)S(1)} %fusion.93), channel_id=1, source_target_pairs={{0,64},{8,72},{16,80},{24,88},{32,96},{40,104},{48,112},{56,120},{... | collective-permute-start | bytes 491528 | tf_op jit(solution)/shard_map/ppermute | solution.py:16
  35.2 8.5 %collective-permute-start.9 = (bf16[5,128,128]{2,1,0:T(8,128)(2,1)S(1)}, bf16[5,128,128]{2,1,0:T(8,128)(2,1)S(1)}, u32[]{:S(2)}, u32[]{:S(2)}) collective-permute-start(bf16[5,128,128]{2,1,0:T(8,128)(2,1)S(1)} %fusion.93), channel_id=1, source_target_pairs={{0,96},{8,104},{16,112},{24,120},{32,0},{40,8},{48,16},{56,24},{64... | collective-permute-start | bytes 491528 | tf_op jit(solution)/shard_map/ppermute | solution.py:16
  38.7 15.0 %collective-permute-start.2 = (f32[128,640]{1,0:T(8,128)S(1)}, f32[128,640]{1,0:T(8,128)S(1)}, u32[]{:S(2)}, u32[]{:S(2)}) collective-permute-start(f32[128,640]{1,0:T(8,128)S(1)} %fusion.114), channel_id=1, source_target_pairs={{0,4},{4,0},{1,5},{5,1},{2,6},{6,2},{3,7},{7,3},{8,12},{12,8},{9,1... | collective-permute-start | bytes 983048 | tf_op jit(solution)/shard_map/ppermute | solution.py:12
  38.8 14.8 %copy-start.10 = (bf16[5,128,128]{2,1,0:T(8,128)(2,1)}, bf16[5,128,128]{2,1,0:T(8,128)(2,1)S(1)}, u32[]{:S(2)}) copy-start(bf16[5,128,128]{2,1,0:T(8,128)(2,1)S(1)} %collective-permute-done.7) | copy-start | bytes 491524
  42.0 11.7 %copy-start.11 = (bf16[5,128,128]{2,1,0:T(8,128)(2,1)}, bf16[5,128,128]{2,1,0:T(8,128)(2,1)S(1)}, u32[]{:S(2)}) copy-start(bf16[5,128,128]{2,1,0:T(8,128)(2,1)S(1)} %collective-permute-done.8) | copy-start | bytes 491524
  43.8 9.9 %copy-start.12 = (bf16[5,128,128]{2,1,0:T(8,128)(2,1)}, bf16[5,128,128]{2,1,0:T(8,128)(2,1)S(1)}, u32[]{:S(2)}) copy-start(bf16[5,128,128]{2,1,0:T(8,128)(2,1)S(1)} %collective-permute-done.9) | copy-start | bytes 491524
  44.6 11.7 %collective-permute-start.10 = (bf16[5,128,128]{2,1,0:T(8,128)(2,1)}, bf16[5,128,128]{2,1,0:T(8,128)(2,1)}, u32[]{:S(2)}, u32[]{:S(2)}) collective-permute-start(bf16[5,128,128]{2,1,0:T(8,128)(2,1)} %fusion.82), channel_id=1, source_target_pairs={{0,128},{8,136},{16,144},{24,152},{32,160},{40,168},{48,176},{56,1... | collective-permute-start | bytes 491528 | tf_op jit(solution)/shard_map/ppermute | solution.py:16
  62.3 3.2 %copy-start.1 = (bf16[640,2560]{1,0:T(8,128)(2,1)S(1)}, bf16[640,2560]{1,0:T(8,128)(2,1)}, u32[]{:S(2)}) copy-start(bf16[640,2560]{1,0:T(8,128)(2,1)} %param.9) | copy-start | bytes 9830404
  68.5 8.5 %collective-permute-start.13 = (bf16[128,1280]{1,0:T(8,128)(2,1)}, bf16[128,1280]{1,0:T(8,128)(2,1)}, u32[]{:S(2)}, u32[]{:S(2)}) collective-permute-start(bf16[128,1280]{1,0:T(8,128)(2,1)} %convolution_convert_fusion), channel_id=1, source_target_pairs={{3,2},{7,6},{11,10},{15,14},{19,18},{23,22},{27,26},{31,30},{35,34... | collective-permute-start | bytes 983048 | tf_op jit(solution)/shard_map/ppermute | solution.py:109
  69.8 11.5 %collective-permute-start.12 = (bf16[128,1280]{1,0:T(8,128)(2,1)}, bf16[128,1280]{1,0:T(8,128)(2,1)}, u32[]{:S(2)}, u32[]{:S(2)}) collective-permute-start(bf16[128,1280]{1,0:T(8,128)(2,1)} %convolution_convert_fusion.1), channel_id=1, source_target_pairs={{0,1},{4,5},{8,9},{12,13},{16,17},{20,21},{24,25},{28,29},{32,33},... | collective-permute-start | bytes 983048 | tf_op jit(solution)/shard_map/ppermute | solution.py:108
  77.0 4.4 %copy-start.2 = (bf16[640,2560]{1,0:T(8,128)(2,1)S(1)}, bf16[640,2560]{1,0:T(8,128)(2,1)}, u32[]{:S(2)}) copy-start(bf16[640,2560]{1,0:T(8,128)(2,1)} %param.9) | copy-start | bytes 9830404
  84.4 6.4 %collective-permute-start.15 = (bf16[128,1280]{1,0:T(8,128)(2,1)}, bf16[128,1280]{1,0:T(8,128)(2,1)}, u32[]{:S(2)}, u32[]{:S(2)}) collective-permute-start(bf16[128,1280]{1,0:T(8,128)(2,1)} %fusion.21), channel_id=1, source_target_pairs={{2,1},{3,2},{6,5},{7,6},{10,9},{11,10},{14,13},{15,14},{18,17},{19... | collective-permute-start | bytes 983048 | tf_op jit(solution)/shard_map/ppermute | solution.py:109
  85.8 9.2 %collective-permute-start.14 = (bf16[128,1280]{1,0:T(8,128)(2,1)}, bf16[128,1280]{1,0:T(8,128)(2,1)}, u32[]{:S(2)}, u32[]{:S(2)}) collective-permute-start(bf16[128,1280]{1,0:T(8,128)(2,1)} %fusion.29), channel_id=1, source_target_pairs={{0,1},{1,2},{4,5},{5,6},{8,9},{9,10},{12,13},{13,14},{16,17},{17,1... | collective-permute-start | bytes 983048 | tf_op jit(solution)/shard_map/ppermute | solution.py:108
  90.8 4.2 %copy-start.3 = (bf16[640,2560]{1,0:T(8,128)(2,1)S(1)}, bf16[640,2560]{1,0:T(8,128)(2,1)}, u32[]{:S(2)}) copy-start(bf16[640,2560]{1,0:T(8,128)(2,1)} %param.9) | copy-start | bytes 9830404
  97.6 12.2 %collective-permute-start.16 = (bf16[128,1280]{1,0:T(8,128)(2,1)}, bf16[128,1280]{1,0:T(8,128)(2,1)}, u32[]{:S(2)}, u32[]{:S(2)}) collective-permute-start(bf16[128,1280]{1,0:T(8,128)(2,1)} %fusion.37), channel_id=1, source_target_pairs={{0,1},{1,2},{2,3},{4,5},{5,6},{6,7},{8,9},{9,10},{10,11},{12,13},{... | collective-permute-start | bytes 983048 | tf_op jit(solution)/shard_map/ppermute | solution.py:108
  105.6 9.3 %collective-permute-start.17 = (bf16[128,1280]{1,0:T(8,128)(2,1)}, bf16[128,1280]{1,0:T(8,128)(2,1)}, u32[]{:S(2)}, u32[]{:S(2)}) collective-permute-start(bf16[128,1280]{1,0:T(8,128)(2,1)} %fusion.59), channel_id=1, source_target_pairs={{1,0},{2,1},{3,2},{5,4},{6,5},{7,6},{9,8},{10,9},{11,10},{13,12},{... | collective-permute-start | bytes 983048 | tf_op jit(solution)/shard_map/ppermute | solution.py:109

commit v5 on v4

--- a/solution.py
+++ b/solution.py
@@ -89,25 +89,29 @@
     h = lax.axis_index("head")
 
     halves = jnp.stack([w_output, w_other])
+    pieces = []
+    for o in range(n):
+        q = (h + o) % n
+        k = jnp.where(q // 2 == c, 0, 1)
+        piece = lax.dynamic_slice(halves, (k, 0, (q % 2) * quarter), (1, halves.shape[1], quarter))
+        pieces.append(piece[0])
+    rotated = jnp.concatenate(pieces, axis=1)
+    products = jnp.dot(normed, rotated, preferred_element_type=F32)
 
-    def block(q):
-        k = jnp.where(q // 2 == c, 0, 1)
-        wq = lax.dynamic_slice(halves, (k, 0, (q % 2) * quarter), (1, halves.shape[1], quarter))[0]
-        return jnp.dot(normed, wq, preferred_element_type=F32)
+    def block(o):
+        return products[:, o * quarter : (o + 1) * quarter]
 
     right = jnp.zeros((tok_count, quarter), F32)
     left = jnp.zeros((tok_count, quarter), F32)
     for s in range(1, n):
-        qr = jnp.clip(h + n - s, 0, n - 1)
-        ql = jnp.clip(h - n + s, 0, n - 1)
-        send_r = (block(qr) + right).astype(BF16)
-        send_l = (block(ql) + left).astype(BF16)
+        send_r = (block(n - s) + right).astype(BF16)
+        send_l = (block(s) + left).astype(BF16)
         send_r, send_l = lax.optimization_barrier((send_r, send_l))
         rpairs = [(j, j + 1) for j in range(s) if j + 1 < n]
         lpairs = [(j, j - 1) for j in range(n - s, n) if j - 1 >= 0]
         right = lax.ppermute(send_r, "head", rpairs).astype(F32)
         left = lax.ppermute(send_l, "head", lpairs).astype(F32)
-    mixed = (block(h) + right + left).astype(BF16)
+    mixed = (block(0) + right + left).astype(BF16)
     return mixed.reshape(1, tok_count, quarter)
 
 

time: 119 us -> 109 us (0.916)
  matrix products: 41.4 us -> 21.3 us
  waiting for transfers between devices: 19.3 us -> 27 us
  other arithmetic: 6.29 us -> 11.7 us
  starting transfers between devices: 44.2 us -> 41.3 us
    dot_general x7 -> x1, matrix products: 21.3 us -> 1.23 us  [shards(): products = jnp.dot(normed, rotated, preferred_element_type=F32)]
    ppermute x3, waiting for transfers between devices: 5.07 us -> 13.4 us  [shards(): right = lax.ppermute(send_r, 'head', rpairs).astype(F32)]
    squeeze x0 -> x1, other arithmetic: none -> 4.33 us  [shards(): pieces.append(piece[0])]
    ppermute x3, starting transfers between devices: 20.2 us -> 18.6 us  [shards(): right = lax.ppermute(send_r, 'head', rpairs).astype(F32)]
    ppermute x3, starting transfers between devices: 4.05 us -> 2.66 us  [shards(): left = lax.ppermute(send_l, 'head', lpairs).astype(F32)]
  transfers between devices with their start and end apart: 18 -> 18, of which waited for: 9 -> 9; matrix products, arithmetic and copies ran while one was open for 32% -> 28% of each run, Pallas kernels for 0% -> 0%
where the time goes in v5:
time: 109 us; the launch traced here: 108 us
  starting transfers between devices  41.3 us (38%)
  waiting for transfers between devices  27 us (25%)
  matrix products  21.3 us (20%)
  other arithmetic  11.7 us (11%)
  local copies, waits for them, and re-layouts  6.73 us (6%)
    ppermute x7, starting transfers between devices, shifted(): return lax.ppermute(x, axis, pairs)  18.9 us
    ppermute x3, starting transfers between devices, shards(): right = lax.ppermute(send_r, 'head', rpairs).astype(F32)  18.6 us
    ppermute x3, waiting for transfers between devices, shards(): right = lax.ppermute(send_r, 'head', rpairs).astype(F32)  13.4 us
    ppermute x7, waiting for transfers between devices, shifted(): return lax.ppermute(x, axis, pairs)  9.13 us
    dot_general x3, matrix products, shards(): lent = swap_cores(jnp.dot(got_cols, w, preferred_element_type=F32))  6.9 us
    dot_general x3, matrix products, shards(): own = jnp.dot(mine_cols, w, preferred_element_type=F32)  6.87 us
    ppermute x3, waiting for transfers between devices, shards(): left = lax.ppermute(send_l, 'head', lpairs).astype(F32)  4.42 us
    squeeze x1, other arithmetic, shards(): pieces.append(piece[0])  4.33 us
  transfers between devices with their start and end apart: 18, of which 9 were waited for; matrix products, arithmetic and copies ran while one was open for 28% of the time, Pallas kernels for 0%

profile of v5, /device:TPU:10, one launch (start us, length us, event | category | flops | bytes accessed | tf_op | source)
XLA Modules:
  0.0 108.2 jit_solution(10244692200857574250)
XLA Ops:
  0.0 2.1 %dynamic-slice_bitcast_fusion = bf16[128,2560]{1,0:T(8,128)(2,1)} fusion(bf16[1,128,5120]{2,1,0:T(8,128)(2,1)} %param.5, s32[]{:T(128)S(6)} %select_n.157), kind=kLoop, calls=%fused_computation.41 | loop fusion | bytes 1310724 | tf_op jit(solution)/shard_map/dynamic_slice | solution.py:59
  2.1 0.0 collective-permute-start
  2.1 0.5 collective-permute-start.11
  2.6 0.0 copy-done
  2.6 2.6 %fusion.24 = f32[128,640]{1,0:T(8,128)} fusion(bf16[2560,640]{1,0:T(8,128)(2,1)S(1)} %copy-done, bf16[1,128,5120]{2,1,0:T(8,128)(2,1)} %param.5, s32[]{:T(128)S(6)} %select_n.156), kind=kOutput, calls=%fused_computation.35 | convolution fusion | flops 419430400 | bytes 4259844 | tf_op jit(solution)/shard_map/dot_general | solution.py:64
  5.3 0.0 collective-permute-done
  5.3 2.6 %fusion.58 = f32[128,640]{1,0:T(8,128)} fusion(bf16[128,2560]{1,0:T(8,128)(2,1)} %collective-permute-done, bf16[2560,640]{1,0:T(8,128)(2,1)S(1)} %copy-done), kind=kOutput, calls=%fused_computation.93 | convolution fusion | flops 419430400 | bytes 4259840 | tf_op jit(solution)/shard_map/dot_general | solution.py:63
  7.9 0.0 collective-permute-start.1
  7.9 2.5 %fusion.60 = f32[128,640]{1,0:T(8,128)} fusion(bf16[128,2560]{1,0:T(8,128)(2,1)} %collective-permute-done, bf16[2560,640]{1,0:T(8,128)(2,1)S(1)} %copy-done.1), kind=kOutput, calls=%fused_computation.95 | convolution fusion | flops 419430400 | bytes 4259840 | tf_op jit(solution)/shard_map/dot_general | solution.py:63
  10.4 0.5 collective-permute-start.3
  10.9 1.4 %fusion.20 = f32[128,640]{1,0:T(8,128)} fusion(bf16[2560,640]{1,0:T(8,128)(2,1)S(1)} %copy-done.1, bf16[1,128,5120]{2,1,0:T(8,128)(2,1)S(1)} %copy-done.3, s32[]{:T(128)S(6)} %select_n.156), kind=kOutput, calls=%fused_computation.31 | convolution fusion | flops 419430400 | bytes 4259844 | tf_op jit(solution)/shard_map/dot_general | solution.py:64
  12.4 0.0 collective-permute-done.1
  12.4 1.8 %add_convert_fusion.4 = bf16[128,640]{1,0:T(8,128)(2,1)} fusion(f32[128,640]{1,0:T(8,128)} %fusion.24, f32[128,640]{1,0:T(8,128)} %collective-permute-done.1), kind=kLoop, calls=%fused_computation.73 | loop fusion | flops 163840 | bytes 819200 | tf_op jit(solution)/shard_map/convert_element_type | solution.py:70
  14.1 1.1 copy.11
  15.2 0.0 collective-permute-done.3
  15.2 1.8 %multiply_convert_fusion.1 = bf16[128,640]{1,0:T(8,128)(2,1)} fusion(f32[128,640]{1,0:T(8,128)} %fusion.20, f32[128,640]{1,0:T(8,128)} %collective-permute-done.3), kind=kLoop, calls=%fused_computation.71 | loop fusion | flops 491520 | bytes 819200 | tf_op jit(solution)/shard_map/convert_element_type | solution.py:69
  17.0 1.7 %copy.13 = bf16[128,640]{0,1:T(8,128)(2,1)} copy(bf16[128,640]{1,0:T(8,128)(2,1)} %multiply_convert_fusion.1) | data formatting | bytes 327680 | tf_op jit(solution)/shard_map/convert_element_type | solution.py:69
  18.8 1.3 %fusion.57 = (bf16[5,128,128]{2,1,0:T(8,128)(2,1)S(1)}, f32[5,128,128]{2,1,0:T(8,128)S(1)}) fusion(bf16[128,5,128]{0,2,1:T(8,128)(2,1)} %bitcast.46, bf16[128,5,128]{0,2,1:T(8,128)(2,1)S(1)} %bitcast.44), kind=kOutput, calls=%fused_computation.92 | convolution fusion | flops 21053440 | bytes 819200 | tf_op jit(solution)/shard_map/thd,the->hde/dot_general | solution.py:71
  20.1 1.5 %collective-permute-start.4 = (bf16[5,128,128]{2,1,0:T(8,128)(2,1)S(1)}, bf16[5,128,128]{2,1,0:T(8,128)(2,1)S(1)}, u32[]{:S(2)}, u32[]{:S(2)}) collective-permute-start(bf16[5,128,128]{2,1,0:T(8,128)(2,1)S(1)} %get-tuple-element.27), channel_id=1, source_target_pairs={{0,8},{8,16},{16,24},{24,0},{32,40},{40,48},{48,56},{56,32},{64,72... | collective-permute-start | bytes 491528 | tf_op jit(solution)/shard_map/ppermute | solution.py:16
  21.6 1.1 %collective-permute-start.5 = (bf16[5,128,128]{2,1,0:T(8,128)(2,1)S(1)}, bf16[5,128,128]{2,1,0:T(8,128)(2,1)S(1)}, u32[]{:S(2)}, u32[]{:S(2)}) collective-permute-start(bf16[5,128,128]{2,1,0:T(8,128)(2,1)S(1)} %get-tuple-element.27), channel_id=1, source_target_pairs={{0,16},{8,24},{16,0},{24,8},{32,48},{40,56},{48,32},{56,40},{64,80... | collective-permute-start | bytes 491528 | tf_op jit(solution)/shard_map/ppermute | solution.py:16
  22.7 2.2 %collective-permute-start.6 = (bf16[5,128,128]{2,1,0:T(8,128)(2,1)S(1)}, bf16[5,128,128]{2,1,0:T(8,128)(2,1)S(1)}, u32[]{:S(2)}, u32[]{:S(2)}) collective-permute-start(bf16[5,128,128]{2,1,0:T(8,128)(2,1)S(1)} %get-tuple-element.27), channel_id=1, source_target_pairs={{0,24},{8,0},{16,8},{24,16},{32,56},{40,32},{48,40},{56,48},{64,88... | collective-permute-start | bytes 491528 | tf_op jit(solution)/shard_map/ppermute | solution.py:16
  24.9 2.8 %fusion.22 = f32[128,640]{1,0:T(8,128)S(1)} fusion(bf16[2560,640]{1,0:T(8,128)(2,1)} %param.6, bf16[1,128,5120]{2,1,0:T(8,128)(2,1)} %param.5, s32[]{:T(128)S(6)} %select_n.156), kind=kOutput, calls=%fused_computation.33 | convolution fusion | flops 419430400 | bytes 4259844 | tf_op jit(solution)/shard_map/dot_general | solution.py:64
  27.7 0.0 collective-permute-done.4
  27.7 2.5 %collective-permute-done.5 = bf16[5,128,128]{2,1,0:T(8,128)(2,1)S(1)} collective-permute-done((bf16[5,128,128]{2,1,0:T(8,128)(2,1)S(1)}, bf16[5,128,128]{2,1,0:T(8,128)(2,1)S(1)}, u32[]{:S(2)}, u32[]{:S(2)}) %collective-permute-start.5) | collective-permute-done | bytes 163872 | tf_op jit(solution)/shard_map/ppermute | solution.py:16
  30.2 1.6 %collective-permute-done.6 = bf16[5,128,128]{2,1,0:T(8,128)(2,1)S(1)} collective-permute-done((bf16[5,128,128]{2,1,0:T(8,128)(2,1)S(1)}, bf16[5,128,128]{2,1,0:T(8,128)(2,1)S(1)}, u32[]{:S(2)}, u32[]{:S(2)}) %collective-permute-start.6) | collective-permute-done | bytes 163872 | tf_op jit(solution)/shard_map/ppermute | solution.py:16
  31.8 0.1 fusion.50
  31.9 1.7 %collective-permute-start.7 = (bf16[5,128,128]{2,1,0:T(8,128)(2,1)S(1)}, bf16[5,128,128]{2,1,0:T(8,128)(2,1)S(1)}, u32[]{:S(2)}, u32[]{:S(2)}) collective-permute-start(bf16[5,128,128]{2,1,0:T(8,128)(2,1)S(1)} %fusion.50), channel_id=1, source_target_pairs={{0,32},{8,40},{16,48},{24,56},{32,64},{40,72},{48,80},{56,88},{64,... | collective-permute-start | bytes 491528 | tf_op jit(solution)/shard_map/ppermute | solution.py:16
  33.6 1.6 %collective-permute-start.8 = (bf16[5,128,128]{2,1,0:T(8,128)(2,1)S(1)}, bf16[5,128,128]{2,1,0:T(8,128)(2,1)S(1)}, u32[]{:S(2)}, u32[]{:S(2)}) collective-permute-start(bf16[5,128,128]{2,1,0:T(8,128)(2,1)S(1)} %fusion.50), channel_id=1, source_target_pairs={{0,64},{8,72},{16,80},{24,88},{32,96},{40,104},{48,112},{56,120},{... | collective-permute-start | bytes 491528 | tf_op jit(solution)/shard_map/ppermute | solution.py:16
  35.1 1.8 %collective-permute-start.9 = (bf16[5,128,128]{2,1,0:T(8,128)(2,1)S(1)}, bf16[5,128,128]{2,1,0:T(8,128)(2,1)S(1)}, u32[]{:S(2)}, u32[]{:S(2)}) collective-permute-start(bf16[5,128,128]{2,1,0:T(8,128)(2,1)S(1)} %fusion.50), channel_id=1, source_target_pairs={{0,96},{8,104},{16,112},{24,120},{32,0},{40,8},{48,16},{56,24},{64... | collective-permute-start | bytes 491528 | tf_op jit(solution)/shard_map/ppermute | solution.py:16
  36.9 1.8 %fusion.59 = f32[128,640]{1,0:T(8,128)S(1)} fusion(bf16[128,2560]{1,0:T(8,128)(2,1)} %collective-permute-done, bf16[2560,640]{1,0:T(8,128)(2,1)S(1)} %copy-done.2), kind=kOutput, calls=%fused_computation.94 | convolution fusion | flops 419430400 | bytes 4259840 | tf_op jit(solution)/shard_map/dot_general | solution.py:63
  38.7 0.1 collective-permute-start.2
  38.8 0.0 collective-permute-done.7
  38.8 3.2 %collective-permute-done.8 = bf16[5,128,128]{2,1,0:T(8,128)(2,1)S(1)} collective-permute-done((bf16[5,128,128]{2,1,0:T(8,128)(2,1)S(1)}, bf16[5,128,128]{2,1,0:T(8,128)(2,1)S(1)}, u32[]{:S(2)}, u32[]{:S(2)}) %collective-permute-start.8) | collective-permute-done | bytes 163872 | tf_op jit(solution)/shard_map/ppermute | solution.py:16
  42.0 1.8 %collective-permute-done.9 = bf16[5,128,128]{2,1,0:T(8,128)(2,1)S(1)} collective-permute-done((bf16[5,128,128]{2,1,0:T(8,128)(2,1)S(1)}, bf16[5,128,128]{2,1,0:T(8,128)(2,1)S(1)}, u32[]{:S(2)}, u32[]{:S(2)}) %collective-permute-start.9) | collective-permute-done | bytes 163872 | tf_op jit(solution)/shard_map/ppermute | solution.py:16
  43.8 0.8 fusion.38
  44.6 0.0 copy-done.4
  44.6 0.0 copy-done.6
  44.6 9.0 %collective-permute-start.10 = (bf16[5,128,128]{2,1,0:T(8,128)(2,1)}, bf16[5,128,128]{2,1,0:T(8,128)(2,1)}, u32[]{:S(2)}, u32[]{:S(2)}) collective-permute-start(bf16[5,128,128]{2,1,0:T(8,128)(2,1)} %fusion.38), channel_id=1, source_target_pairs={{0,128},{8,136},{16,144},{24,152},{32,160},{40,168},{48,176},{56,1... | collective-permute-start | bytes 491528 | tf_op jit(solution)/shard_map/ppermute | solution.py:16
  53.6 0.0 collective-permute-done.2
  53.6 0.8 multiply_convert_fusion.2
  54.4 1.7 %copy.12 = bf16[128,640]{0,1:T(8,128)(2,1)} copy(bf16[128,640]{1,0:T(8,128)(2,1)} %multiply_convert_fusion.2) | data formatting | bytes 327680 | tf_op jit(solution)/shard_map/convert_element_type | solution.py:68
  56.1 0.1 collective-permute-done.10
  56.2 2.7 %fusion.33 = f32[5,128,128]{2,1,0:T(8,128)} fusion(bf16[128,5,128]{0,2,1:T(8,128)(2,1)} %bitcast.48, bf16[5,128,128]{2,1,0:T(8,128)(2,1)} %copy-done.4, bf16[5,128,128]{2,1,0:T(8,128)(2,1)} %copy-done.5, bf16[5,128,128]{2,1,0:T(8,128)(2,1)} %copy-done.6, bf16[5,128,128]{2,1,0:T(8,128)(2,1)} %copy-done.7, bf16[5,128,128]{2,1,0:T(8,128)(2,1)} %copy-done.8, ...), kind=kOutput, calls=%fused_computation.63 | convolution fusion | flops 127385600 | bytes 1638406 | tf_op jit(solution)/shard_map/thd,hde->the/dot_general | solution.py:79
  58.9 2.3 %multiply_reduce_fusion = (f32[128,5]{0,1:T(8,128)S(1)}, f32[128,5,128]{0,2,1:T(8,128)}) fusion(f32[5,128,128]{2,1,0:T(8,128)} %fusion.33, bf16[128,5,128]{0,2,1:T(8,128)(2,1)S(1)} %bitcast.45, bf16[128,5,128]{0,2,1:T(8,128)(2,1)} %bitcast.49, bf16[128,5,128]{0,2,1:T(8,128)(2,1)} %bitcast.47, f32[128,128]{1,0:T(8,128)S(1)} %fusion.49), kind=kOutput, calls=%fused_computation.69 | convolution fusion | flops 42352000 | bytes 1214976 | tf_op jit(solution)/shard_map/hts,shd->thd/dot_general | solution.py:78
  61.2 1.0 multiply_convert_fusion
  62.2 0.0 collective-permute-done.11
  62.2 4.3 %fusion.11 = (bf16[640,1280]{1,0:T(8,128)(2,1)S(1)}, bf16[640,1280]{1,0:T(8,128)(2,1)S(1)}, bf16[640,1280]{1,0:T(8,128)(2,1)S(1)}, bf16[640,1280]{1,0:T(8,128)(2,1)S(1)}) fusion(s32[]{:T(128)S(6)} %select_n.181, s32[]{:T(128)S(6)} %select_n.183, bf16[1,640,2560]{2,1,0:T(8,128)(2,1)} %bitcast.43, bf16[1,640,2560]{2,1,0:T(8,128)(2,1)} %bitcast.8, ...), kind=kLoop, calls=%fused_computation.19 | loop fusion | flops 13107200 | bytes 13107232 | tf_op jit(solution)/shard_map/squeeze | solution.py:97
  66.6 1.2 %fusion = f32[128,5120]{1,0:T(8,128)S(1)} fusion(bf16[128,640]{0,1:T(8,128)(2,1)S(1)} %bitcast.50, bf16[640,1280]{1,0:T(8,128)(2,1)S(1)} %get-tuple-element.20, bf16[640,1280]{1,0:T(8,128)(2,1)S(1)} %get-tuple-element.19, bf16[640,1280]{1,0:T(8,128)(2,1)S(1)} %get-tuple-element.18, bf16[640,1280]{1,0:T(8,128)(2,1)S(1)} %get-tuple-element.17), kind=kOutput, calls=%fused_computation.8 | convolution fusion | flops 865075200 | bytes 9338880 | tf_op jit(solution)/shard_map/dot_general | solution.py:99
  67.8 0.1 fusion.56
  67.9 6.5 %collective-permute-start.12 = (bf16[128,1280]{1,0:T(8,128)(2,1)S(1)}, bf16[128,1280]{1,0:T(8,128)(2,1)S(1)}, u32[]{:S(2)}, u32[]{:S(2)}) collective-permute-start(bf16[128,1280]{1,0:T(8,128)(2,1)S(1)} %get-tuple-element.11), channel_id=1, source_target_pairs={{0,1},{4,5},{8,9},{12,13},{16,17},{20,21},{24,25},{28,29},{32,33},... | collective-permute-start | bytes 983048 | tf_op jit(solution)/shard_map/ppermute | solution.py:112
  74.4 0.7 collective-permute-start.13
  75.1 5.5 %collective-permute-done.12 = bf16[128,1280]{1,0:T(8,128)(2,1)S(1)} collective-permute-done((bf16[128,1280]{1,0:T(8,128)(2,1)S(1)}, bf16[128,1280]{1,0:T(8,128)(2,1)S(1)}, u32[]{:S(2)}, u32[]{:S(2)}) %collective-permute-start.12) | collective-permute-done | bytes 327712 | tf_op jit(solution)/shard_map/ppermute | solution.py:112
  80.6 0.0 collective-permute-done.13
  80.6 0.1 add_convert_fusion.2
  80.7 4.4 %collective-permute-start.14 = (bf16[128,1280]{1,0:T(8,128)(2,1)S(1)}, bf16[128,1280]{1,0:T(8,128)(2,1)S(1)}, u32[]{:S(2)}, u32[]{:S(2)}) collective-permute-start(bf16[128,1280]{1,0:T(8,128)(2,1)S(1)} %get-tuple-element.13), channel_id=1, source_target_pairs={{0,1},{1,2},{4,5},{5,6},{8,9},{9,10},{12,13},{13,14},{16,17},{17,1... | collective-permute-start | bytes 983048 | tf_op jit(solution)/shard_map/ppermute | solution.py:112
  85.1 0.7 collective-permute-start.15
  85.8 4.6 %collective-permute-done.14 = bf16[128,1280]{1,0:T(8,128)(2,1)S(1)} collective-permute-done((bf16[128,1280]{1,0:T(8,128)(2,1)S(1)}, bf16[128,1280]{1,0:T(8,128)(2,1)S(1)}, u32[]{:S(2)}, u32[]{:S(2)}) %collective-permute-start.14) | collective-permute-done | bytes 327712 | tf_op jit(solution)/shard_map/ppermute | solution.py:112
  90.4 0.0 collective-permute-done.15
  90.5 0.2 add_convert_fusion
  90.6 7.8 %collective-permute-start.16 = (bf16[128,1280]{1,0:T(8,128)(2,1)S(1)}, bf16[128,1280]{1,0:T(8,128)(2,1)S(1)}, u32[]{:S(2)}, u32[]{:S(2)}) collective-permute-start(bf16[128,1280]{1,0:T(8,128)(2,1)S(1)} %get-tuple-element.15), channel_id=1, source_target_pairs={{0,1},{1,2},{2,3},{4,5},{5,6},{6,7},{8,9},{9,10},{10,11},{12,13},{... | collective-permute-start | bytes 983048 | tf_op jit(solution)/shard_map/ppermute | solution.py:112
  98.4 1.3 %collective-permute-start.17 = (bf16[128,1280]{1,0:T(8,128)(2,1)S(1)}, bf16[128,1280]{1,0:T(8,128)(2,1)S(1)}, u32[]{:S(2)}, u32[]{:S(2)}) collective-permute-start(bf16[128,1280]{1,0:T(8,128)(2,1)S(1)} %get-tuple-element.16), channel_id=1, source_target_pairs={{1,0},{2,1},{3,2},{5,4},{6,5},{7,6},{9,8},{10,9},{11,10},{13,12},{... | collective-permute-start | bytes 983048 | tf_op jit(solution)/shard_map/ppermute | solution.py:113
  99.7 3.3 %collective-permute-done.16 = bf16[128,1280]{1,0:T(8,128)(2,1)S(1)} collective-permute-done((bf16[128,1280]{1,0:T(8,128)(2,1)S(1)}, bf16[128,1280]{1,0:T(8,128)(2,1)S(1)}, u32[]{:S(2)}, u32[]{:S(2)}) %collective-permute-start.16) | collective-permute-done | bytes 327712 | tf_op jit(solution)/shard_map/ppermute | solution.py:112
  103.0 4.4 %collective-permute-done.17 = bf16[128,1280]{1,0:T(8,128)(2,1)S(1)} collective-permute-done((bf16[128,1280]{1,0:T(8,128)(2,1)S(1)}, bf16[128,1280]{1,0:T(8,128)(2,1)S(1)}, u32[]{:S(2)}, u32[]{:S(2)}) %collective-permute-start.17) | collective-permute-done | bytes 327712 | tf_op jit(solution)/shard_map/ppermute | solution.py:113
  107.4 0.8 fusion.39
  (19 shorter events, 0.0 us)
Async XLA Ops:
  0.0 2.6 %copy-start = (bf16[2560,640]{1,0:T(8,128)(2,1)S(1)}, bf16[2560,640]{1,0:T(8,128)(2,1)}, u32[]{:S(2)}) copy-start(bf16[2560,640]{1,0:T(8,128)(2,1)} %param.8) | copy-start | bytes 9830404
  2.1 3.2 %collective-permute-start = (bf16[128,2560]{1,0:T(8,128)(2,1)}, bf16[128,2560]{1,0:T(8,128)(2,1)}, u32[]{:S(2)}, u32[]{:S(2)}) collective-permute-start(bf16[128,2560]{1,0:T(8,128)(2,1)} %dynamic-slice_bitcast_fusion), channel_id=1, source_target_pairs={{0,4},{4,0},{1,5},{5,1},{2,6},{6,2},{3,7},{7,3},{8,12},{12,8},{9,1... | collective-permute-start | bytes 1966088 | tf_op jit(solution)/shard_map/ppermute | solution.py:12
  2.1 60.1 %collective-permute-start.11 = (bf16[640,2560]{1,0:T(8,128)(2,1)}, bf16[640,2560]{1,0:T(8,128)(2,1)}, u32[]{:S(2)}, u32[]{:S(2)}) collective-permute-start(bf16[640,2560]{1,0:T(8,128)(2,1)} %param.9), channel_id=1, source_target_pairs={{0,4},{4,0},{1,5},{5,1},{2,6},{6,2},{3,7},{7,3},{8,12},{12,8},{9,1... | collective-permute-start | bytes 9830408 | tf_op jit(solution)/shard_map/ppermute | solution.py:12
  2.6 5.3 %copy-start.1 = (bf16[2560,640]{1,0:T(8,128)(2,1)S(1)}, bf16[2560,640]{1,0:T(8,128)(2,1)}, u32[]{:S(2)}) copy-start(bf16[2560,640]{1,0:T(8,128)(2,1)} %param.7) | copy-start | bytes 9830404
  5.3 5.7 %copy-start.3 = (bf16[1,128,5120]{2,1,0:T(8,128)(2,1)S(1)}, bf16[1,128,5120]{2,1,0:T(8,128)(2,1)}, u32[]{:S(2)}) copy-start(bf16[1,128,5120]{2,1,0:T(8,128)(2,1)} %param.5) | copy-start | bytes 3932164
  7.9 4.5 %collective-permute-start.1 = (f32[128,640]{1,0:T(8,128)}, f32[128,640]{1,0:T(8,128)}, u32[]{:S(2)}, u32[]{:S(2)}) collective-permute-start(f32[128,640]{1,0:T(8,128)} %fusion.58), channel_id=1, source_target_pairs={{0,4},{4,0},{1,5},{5,1},{2,6},{6,2},{3,7},{7,3},{8,12},{12,8},{9,1... | collective-permute-start | bytes 983048 | tf_op jit(solution)/shard_map/ppermute | solution.py:12
  10.4 4.8 %collective-permute-start.3 = (f32[128,640]{1,0:T(8,128)}, f32[128,640]{1,0:T(8,128)}, u32[]{:S(2)}, u32[]{:S(2)}) collective-permute-start(f32[128,640]{1,0:T(8,128)} %fusion.60), channel_id=1, source_target_pairs={{0,4},{4,0},{1,5},{5,1},{2,6},{6,2},{3,7},{7,3},{8,12},{12,8},{9,1... | collective-permute-start | bytes 983048 | tf_op jit(solution)/shard_map/ppermute | solution.py:12
  18.7 18.2 %copy-start.2 = (bf16[2560,640]{1,0:T(8,128)(2,1)S(1)}, bf16[2560,640]{1,0:T(8,128)(2,1)}, u32[]{:S(2)}) copy-start(bf16[2560,640]{1,0:T(8,128)(2,1)} %param.6) | copy-start | bytes 9830404
  20.1 7.6 %collective-permute-start.4 = (bf16[5,128,128]{2,1,0:T(8,128)(2,1)S(1)}, bf16[5,128,128]{2,1,0:T(8,128)(2,1)S(1)}, u32[]{:S(2)}, u32[]{:S(2)}) collective-permute-start(bf16[5,128,128]{2,1,0:T(8,128)(2,1)S(1)} %get-tuple-element.27), channel_id=1, source_target_pairs={{0,8},{8,16},{16,24},{24,0},{32,40},{40,48},{48,56},{56,32},{64,72... | collective-permute-start | bytes 491528 | tf_op jit(solution)/shard_map/ppermute | solution.py:16
  21.6 8.6 %collective-permute-start.5 = (bf16[5,128,128]{2,1,0:T(8,128)(2,1)S(1)}, bf16[5,128,128]{2,1,0:T(8,128)(2,1)S(1)}, u32[]{:S(2)}, u32[]{:S(2)}) collective-permute-start(bf16[5,128,128]{2,1,0:T(8,128)(2,1)S(1)} %get-tuple-element.27), channel_id=1, source_target_pairs={{0,16},{8,24},{16,0},{24,8},{32,48},{40,56},{48,32},{56,40},{64,80... | collective-permute-start | bytes 491528 | tf_op jit(solution)/shard_map/ppermute | solution.py:16
  22.7 9.1 %collective-permute-start.6 = (bf16[5,128,128]{2,1,0:T(8,128)(2,1)S(1)}, bf16[5,128,128]{2,1,0:T(8,128)(2,1)S(1)}, u32[]{:S(2)}, u32[]{:S(2)}) collective-permute-start(bf16[5,128,128]{2,1,0:T(8,128)(2,1)S(1)} %get-tuple-element.27), channel_id=1, source_target_pairs={{0,24},{8,0},{16,8},{24,16},{32,56},{40,32},{48,40},{56,48},{64,88... | collective-permute-start | bytes 491528 | tf_op jit(solution)/shard_map/ppermute | solution.py:16
  27.7 16.9 %copy-start.4 = (bf16[5,128,128]{2,1,0:T(8,128)(2,1)}, bf16[5,128,128]{2,1,0:T(8,128)(2,1)S(1)}, u32[]{:S(2)}) copy-start(bf16[5,128,128]{2,1,0:T(8,128)(2,1)S(1)} %collective-permute-done.4) | copy-start | bytes 491524
  30.2 14.4 %copy-start.5 = (bf16[5,128,128]{2,1,0:T(8,128)(2,1)}, bf16[5,128,128]{2,1,0:T(8,128)(2,1)S(1)}, u32[]{:S(2)}) copy-start(bf16[5,128,128]{2,1,0:T(8,128)(2,1)S(1)} %collective-permute-done.5) | copy-start | bytes 491524
  31.8 12.8 %copy-start.6 = (bf16[5,128,128]{2,1,0:T(8,128)(2,1)}, bf16[5,128,128]{2,1,0:T(8,128)(2,1)S(1)}, u32[]{:S(2)}) copy-start(bf16[5,128,128]{2,1,0:T(8,128)(2,1)S(1)} %collective-permute-done.6) | copy-start | bytes 491524
  31.9 6.9 %collective-permute-start.7 = (bf16[5,128,128]{2,1,0:T(8,128)(2,1)S(1)}, bf16[5,128,128]{2,1,0:T(8,128)(2,1)S(1)}, u32[]{:S(2)}, u32[]{:S(2)}) collective-permute-start(bf16[5,128,128]{2,1,0:T(8,128)(2,1)S(1)} %fusion.50), channel_id=1, source_target_pairs={{0,32},{8,40},{16,48},{24,56},{32,64},{40,72},{48,80},{56,88},{64,... | collective-permute-start | bytes 491528 | tf_op jit(solution)/shard_map/ppermute | solution.py:16
  33.6 8.4 %collective-permute-start.8 = (bf16[5,128,128]{2,1,0:T(8,128)(2,1)S(1)}, bf16[5,128,128]{2,1,0:T(8,128)(2,1)S(1)}, u32[]{:S(2)}, u32[]{:S(2)}) collective-permute-start(bf16[5,128,128]{2,1,0:T(8,128)(2,1)S(1)} %fusion.50), channel_id=1, source_target_pairs={{0,64},{8,72},{16,80},{24,88},{32,96},{40,104},{48,112},{56,120},{... | collective-permute-start | bytes 491528 | tf_op jit(solution)/shard_map/ppermute | solution.py:16
  35.1 8.6 %collective-permute-start.9 = (bf16[5,128,128]{2,1,0:T(8,128)(2,1)S(1)}, bf16[5,128,128]{2,1,0:T(8,128)(2,1)S(1)}, u32[]{:S(2)}, u32[]{:S(2)}) collective-permute-start(bf16[5,128,128]{2,1,0:T(8,128)(2,1)S(1)} %fusion.50), channel_id=1, source_target_pairs={{0,96},{8,104},{16,112},{24,120},{32,0},{40,8},{48,16},{56,24},{64... | collective-permute-start | bytes 491528 | tf_op jit(solution)/shard_map/ppermute | solution.py:16
  38.7 14.9 %collective-permute-start.2 = (f32[128,640]{1,0:T(8,128)S(1)}, f32[128,640]{1,0:T(8,128)S(1)}, u32[]{:S(2)}, u32[]{:S(2)}) collective-permute-start(f32[128,640]{1,0:T(8,128)S(1)} %fusion.59), channel_id=1, source_target_pairs={{0,4},{4,0},{1,5},{5,1},{2,6},{6,2},{3,7},{7,3},{8,12},{12,8},{9,1... | collective-permute-start | bytes 983048 | tf_op jit(solution)/shard_map/ppermute | solution.py:12
  38.8 14.8 %copy-start.7 = (bf16[5,128,128]{2,1,0:T(8,128)(2,1)}, bf16[5,128,128]{2,1,0:T(8,128)(2,1)S(1)}, u32[]{:S(2)}) copy-start(bf16[5,128,128]{2,1,0:T(8,128)(2,1)S(1)} %collective-permute-done.7) | copy-start | bytes 491524
  42.0 11.6 %copy-start.8 = (bf16[5,128,128]{2,1,0:T(8,128)(2,1)}, bf16[5,128,128]{2,1,0:T(8,128)(2,1)S(1)}, u32[]{:S(2)}) copy-start(bf16[5,128,128]{2,1,0:T(8,128)(2,1)S(1)} %collective-permute-done.8) | copy-start | bytes 491524
  43.8 9.9 %copy-start.9 = (bf16[5,128,128]{2,1,0:T(8,128)(2,1)}, bf16[5,128,128]{2,1,0:T(8,128)(2,1)S(1)}, u32[]{:S(2)}) copy-start(bf16[5,128,128]{2,1,0:T(8,128)(2,1)S(1)} %collective-permute-done.9) | copy-start | bytes 491524
  44.6 11.6 %collective-permute-start.10 = (bf16[5,128,128]{2,1,0:T(8,128)(2,1)}, bf16[5,128,128]{2,1,0:T(8,128)(2,1)}, u32[]{:S(2)}, u32[]{:S(2)}) collective-permute-start(bf16[5,128,128]{2,1,0:T(8,128)(2,1)} %fusion.38), channel_id=1, source_target_pairs={{0,128},{8,136},{16,144},{24,152},{32,160},{40,168},{48,176},{56,1... | collective-permute-start | bytes 491528 | tf_op jit(solution)/shard_map/ppermute | solution.py:16
  67.9 12.7 %collective-permute-start.12 = (bf16[128,1280]{1,0:T(8,128)(2,1)S(1)}, bf16[128,1280]{1,0:T(8,128)(2,1)S(1)}, u32[]{:S(2)}, u32[]{:S(2)}) collective-permute-start(bf16[128,1280]{1,0:T(8,128)(2,1)S(1)} %get-tuple-element.11), channel_id=1, source_target_pairs={{0,1},{4,5},{8,9},{12,13},{16,17},{20,21},{24,25},{28,29},{32,33},... | collective-permute-start | bytes 983048 | tf_op jit(solution)/shard_map/ppermute | solution.py:112
  74.4 6.2 %collective-permute-start.13 = (bf16[128,1280]{1,0:T(8,128)(2,1)S(1)}, bf16[128,1280]{1,0:T(8,128)(2,1)S(1)}, u32[]{:S(2)}, u32[]{:S(2)}) collective-permute-start(bf16[128,1280]{1,0:T(8,128)(2,1)S(1)} %get-tuple-element.12), channel_id=1, source_target_pairs={{3,2},{7,6},{11,10},{15,14},{19,18},{23,22},{27,26},{31,30},{35,34... | collective-permute-start | bytes 983048 | tf_op jit(solution)/shard_map/ppermute | solution.py:113
  80.7 9.7 %collective-permute-start.14 = (bf16[128,1280]{1,0:T(8,128)(2,1)S(1)}, bf16[128,1280]{1,0:T(8,128)(2,1)S(1)}, u32[]{:S(2)}, u32[]{:S(2)}) collective-permute-start(bf16[128,1280]{1,0:T(8,128)(2,1)S(1)} %get-tuple-element.13), channel_id=1, source_target_pairs={{0,1},{1,2},{4,5},{5,6},{8,9},{9,10},{12,13},{13,14},{16,17},{17,1... | collective-permute-start | bytes 983048 | tf_op jit(solution)/shard_map/ppermute | solution.py:112
  85.1 5.3 %collective-permute-start.15 = (bf16[128,1280]{1,0:T(8,128)(2,1)S(1)}, bf16[128,1280]{1,0:T(8,128)(2,1)S(1)}, u32[]{:S(2)}, u32[]{:S(2)}) collective-permute-start(bf16[128,1280]{1,0:T(8,128)(2,1)S(1)} %get-tuple-element.14), channel_id=1, source_target_pairs={{2,1},{3,2},{6,5},{7,6},{10,9},{11,10},{14,13},{15,14},{18,17},{19... | collective-permute-start | bytes 983048 | tf_op jit(solution)/shard_map/ppermute | solution.py:113
  90.6 12.3 %collective-permute-start.16 = (bf16[128,1280]{1,0:T(8,128)(2,1)S(1)}, bf16[128,1280]{1,0:T(8,128)(2,1)S(1)}, u32[]{:S(2)}, u32[]{:S(2)}) collective-permute-start(bf16[128,1280]{1,0:T(8,128)(2,1)S(1)} %get-tuple-element.15), channel_id=1, source_target_pairs={{0,1},{1,2},{2,3},{4,5},{5,6},{6,7},{8,9},{9,10},{10,11},{12,13},{... | collective-permute-start | bytes 983048 | tf_op jit(solution)/shard_map/ppermute | solution.py:112
  98.4 9.0 %collective-permute-start.17 = (bf16[128,1280]{1,0:T(8,128)(2,1)S(1)}, bf16[128,1280]{1,0:T(8,128)(2,1)S(1)}, u32[]{:S(2)}, u32[]{:S(2)}) collective-permute-start(bf16[128,1280]{1,0:T(8,128)(2,1)S(1)} %get-tuple-element.16), channel_id=1, source_target_pairs={{1,0},{2,1},{3,2},{5,4},{6,5},{7,6},{9,8},{10,9},{11,10},{13,12},{... | collective-permute-start | bytes 983048 | tf_op jit(solution)/shard_map/ppermute | solution.py:113

commit v6 on v5

--- a/solution.py
+++ b/solution.py
@@ -56,8 +56,7 @@
     c = lax.axis_index("wt")
 
     mine_cols = lax.dynamic_slice_in_dim(rows_in, c * half, half, axis=1)
-    their_cols = lax.dynamic_slice_in_dim(rows_in, (1 - c) * half, half, axis=1)
-    got_cols = swap_cores(their_cols)
+    got_cols = lax.dynamic_slice_in_dim(swap_cores(rows_in), c * half, half, axis=1)
     sums = []
     for w in (w_query, w_key, w_value):
         lent = swap_cores(jnp.dot(got_cols, w, preferred_element_type=F32))
@@ -95,11 +94,8 @@
         k = jnp.where(q // 2 == c, 0, 1)
         piece = lax.dynamic_slice(halves, (k, 0, (q % 2) * quarter), (1, halves.shape[1], quarter))
         pieces.append(piece[0])
-    rotated = jnp.concatenate(pieces, axis=1)
-    products = jnp.dot(normed, rotated, preferred_element_type=F32)
-
     def block(o):
-        return products[:, o * quarter : (o + 1) * quarter]
+        return jnp.dot(normed, pieces[o], preferred_element_type=F32)
 
     right = jnp.zeros((tok_count, quarter), F32)
     left = jnp.zeros((tok_count, quarter), F32)

time: 109 us -> 123 us (1.13)
  the two profiles are of different devices: /device:TPU:10 before, /device:TPU:128 now
where the time goes in v6:
time: 123 us
  waiting for transfers between devices  42.9 us (35%)
  starting transfers between devices  33.5 us (27%)
  matrix products  32.2 us (26%)
  other arithmetic  7.92 us (6%)
  local copies, waits for them, and re-layouts  5.97 us (5%)
    ppermute x7, waiting for transfers between devices, shifted(): return lax.ppermute(x, axis, pairs)  22.1 us
    ppermute x3, starting transfers between devices, shards(): right = lax.ppermute(send_r, 'head', rpairs).astype(F32)  18.3 us
    ppermute x3, waiting for transfers between devices, shards(): right = lax.ppermute(send_r, 'head', rpairs).astype(F32)  16 us
    dot_general x4, matrix products, block(): return jnp.dot(normed, pieces[o], preferred_element_type=F32)  12.2 us
    ppermute x7, starting transfers between devices, shifted(): return lax.ppermute(x, axis, pairs)  10.7 us
    dot_general x3, matrix products, shards(): lent = swap_cores(jnp.dot(got_cols, w, preferred_element_type=F32))  6.88 us
    dot_general x3, matrix products, shards(): own = jnp.dot(mine_cols, w, preferred_element_type=F32)  6.87 us
    ppermute x3, waiting for transfers between devices, shards(): left = lax.ppermute(send_l, 'head', lpairs).astype(F32)  4.82 us
  transfers between devices with their start and end apart: 18, of which 11 were waited for; matrix products, arithmetic and copies ran while one was open for 26% of the time, Pallas kernels for 0%

profile of v6, /device:TPU:128, one launch (start us, length us, event | category | flops | bytes accessed | tf_op | source)
XLA Modules:
  0.0 122.7 jit_solution(6705731080665249923)
XLA Ops:
  0.0 0.0 collective-permute-start
  0.0 0.5 collective-permute-start.11
  0.5 1.4 %copy-done = bf16[2560,640]{1,0:T(8,128)(2,1)S(1)} copy-done((bf16[2560,640]{1,0:T(8,128)(2,1)S(1)}, bf16[2560,640]{1,0:T(8,128)(2,1)}, u32[]{:S(2)}) %copy-start) | copy-done | bytes 3276824
  1.9 2.6 %fusion.30 = f32[128,640]{1,0:T(8,128)} fusion(bf16[2560,640]{1,0:T(8,128)(2,1)S(1)} %copy-done, bf16[1,128,5120]{2,1,0:T(8,128)(2,1)} %param.5, s32[]{:T(128)S(6)} %select_n.154), kind=kOutput, calls=%fused_computation.28 | convolution fusion | flops 419430400 | bytes 4259844 | tf_op jit(solution)/shard_map/dot_general | solution.py:63
  4.6 0.0 collective-permute-done
  4.6 2.6 %fusion.40 = f32[128,640]{1,0:T(8,128)} fusion(bf16[2560,640]{1,0:T(8,128)(2,1)S(1)} %copy-done.2, bf16[128,5120]{1,0:T(8,128)(2,1)} %collective-permute-done, s32[]{:T(128)S(6)} %select_n.154), kind=kOutput, calls=%fused_computation.42 | convolution fusion | flops 419430400 | bytes 4259844 | tf_op jit(solution)/shard_map/dot_general | solution.py:62
  7.2 0.0 collective-permute-start.1
  7.2 2.5 %fusion.36 = f32[128,640]{1,0:T(8,128)} fusion(bf16[2560,640]{1,0:T(8,128)(2,1)S(1)} %copy-done, bf16[128,5120]{1,0:T(8,128)(2,1)} %collective-permute-done, s32[]{:T(128)S(6)} %select_n.154), kind=kOutput, calls=%fused_computation.38 | convolution fusion | flops 419430400 | bytes 4259844 | tf_op jit(solution)/shard_map/dot_general | solution.py:62
  9.7 0.5 collective-permute-start.3
  10.2 1.4 %fusion.34 = f32[128,640]{1,0:T(8,128)} fusion(bf16[2560,640]{1,0:T(8,128)(2,1)S(1)} %copy-done.2, bf16[1,128,5120]{2,1,0:T(8,128)(2,1)S(1)} %copy-done.4, s32[]{:T(128)S(6)} %select_n.154), kind=kOutput, calls=%fused_computation.32 | convolution fusion | flops 419430400 | bytes 4259844 | tf_op jit(solution)/shard_map/dot_general | solution.py:63
  11.6 0.0 collective-permute-done.1
  11.6 1.8 %add_convert_fusion.4 = bf16[128,640]{1,0:T(8,128)(2,1)} fusion(f32[128,640]{1,0:T(8,128)} %fusion.34, f32[128,640]{1,0:T(8,128)} %collective-permute-done.1), kind=kLoop, calls=%fused_computation.72 | loop fusion | flops 163840 | bytes 819200 | tf_op jit(solution)/shard_map/convert_element_type | solution.py:69
  13.4 1.1 copy.11
  14.5 0.0 collective-permute-done.3
  14.5 1.9 %multiply_convert_fusion.1 = bf16[128,640]{1,0:T(8,128)(2,1)} fusion(f32[128,640]{1,0:T(8,128)} %fusion.30, f32[128,640]{1,0:T(8,128)} %collective-permute-done.3), kind=kLoop, calls=%fused_computation.70 | loop fusion | flops 491520 | bytes 819200 | tf_op jit(solution)/shard_map/convert_element_type | solution.py:68
  16.3 1.7 %copy.13 = bf16[128,640]{0,1:T(8,128)(2,1)} copy(bf16[128,640]{1,0:T(8,128)(2,1)} %multiply_convert_fusion.1) | data formatting | bytes 327680 | tf_op jit(solution)/shard_map/convert_element_type | solution.py:68
  18.1 1.3 %fusion.81 = (bf16[5,128,128]{2,1,0:T(8,128)(2,1)S(1)}, f32[5,128,128]{2,1,0:T(8,128)S(1)}) fusion(bf16[128,5,128]{0,2,1:T(8,128)(2,1)} %bitcast.71, bf16[128,5,128]{0,2,1:T(8,128)(2,1)S(1)} %bitcast.69), kind=kOutput, calls=%fused_computation.100 | convolution fusion | flops 21053440 | bytes 819200 | tf_op jit(solution)/shard_map/thd,the->hde/dot_general | solution.py:70
  19.4 2.8 %collective-permute-start.6 = (bf16[5,128,128]{2,1,0:T(8,128)(2,1)S(1)}, bf16[5,128,128]{2,1,0:T(8,128)(2,1)S(1)}, u32[]{:S(2)}, u32[]{:S(2)}) collective-permute-start(bf16[5,128,128]{2,1,0:T(8,128)(2,1)S(1)} %get-tuple-element.19), channel_id=1, source_target_pairs={{0,24},{8,0},{16,8},{24,16},{32,56},{40,32},{48,40},{56,48},{64,88... | collective-permute-start | bytes 491528 | tf_op jit(solution)/shard_map/ppermute | solution.py:16
  22.2 0.8 collective-permute-start.5
  23.0 0.9 collective-permute-start.4
  23.9 2.8 %fusion.32 = f32[128,640]{1,0:T(8,128)S(1)} fusion(bf16[2560,640]{1,0:T(8,128)(2,1)} %param.6, bf16[1,128,5120]{2,1,0:T(8,128)(2,1)} %param.5, s32[]{:T(128)S(6)} %select_n.154), kind=kOutput, calls=%fused_computation.30 | convolution fusion | flops 419430400 | bytes 4259844 | tf_op jit(solution)/shard_map/dot_general | solution.py:63
  26.7 2.7 %collective-permute-done.6 = bf16[5,128,128]{2,1,0:T(8,128)(2,1)S(1)} collective-permute-done((bf16[5,128,128]{2,1,0:T(8,128)(2,1)S(1)}, bf16[5,128,128]{2,1,0:T(8,128)(2,1)S(1)}, u32[]{:S(2)}, u32[]{:S(2)}) %collective-permute-start.6) | collective-permute-done | bytes 163872 | tf_op jit(solution)/shard_map/ppermute | solution.py:16
  29.4 1.4 %collective-permute-done.5 = bf16[5,128,128]{2,1,0:T(8,128)(2,1)S(1)} collective-permute-done((bf16[5,128,128]{2,1,0:T(8,128)(2,1)S(1)}, bf16[5,128,128]{2,1,0:T(8,128)(2,1)S(1)}, u32[]{:S(2)}, u32[]{:S(2)}) %collective-permute-start.5) | collective-permute-done | bytes 163872 | tf_op jit(solution)/shard_map/ppermute | solution.py:16
  30.8 2.2 %collective-permute-done.4 = bf16[5,128,128]{2,1,0:T(8,128)(2,1)S(1)} collective-permute-done((bf16[5,128,128]{2,1,0:T(8,128)(2,1)S(1)}, bf16[5,128,128]{2,1,0:T(8,128)(2,1)S(1)}, u32[]{:S(2)}, u32[]{:S(2)}) %collective-permute-start.4) | collective-permute-done | bytes 163872 | tf_op jit(solution)/shard_map/ppermute | solution.py:16
  33.1 0.1 fusion.65
  33.2 3.1 %collective-permute-start.9 = (bf16[5,128,128]{2,1,0:T(8,128)(2,1)S(1)}, bf16[5,128,128]{2,1,0:T(8,128)(2,1)S(1)}, u32[]{:S(2)}, u32[]{:S(2)}) collective-permute-start(bf16[5,128,128]{2,1,0:T(8,128)(2,1)S(1)} %fusion.65), channel_id=1, source_target_pairs={{0,96},{8,104},{16,112},{24,120},{32,0},{40,8},{48,16},{56,24},{64... | collective-permute-start | bytes 491528 | tf_op jit(solution)/shard_map/ppermute | solution.py:16
  36.3 0.6 collective-permute-start.8
  36.9 1.0 collective-permute-start.7
  37.9 0.0 copy-done.3
  37.9 1.8 %fusion.38 = f32[128,640]{1,0:T(8,128)S(1)} fusion(bf16[2560,640]{1,0:T(8,128)(2,1)S(1)} %copy-done.3, bf16[128,5120]{1,0:T(8,128)(2,1)} %collective-permute-done, s32[]{:T(128)S(6)} %select_n.154), kind=kOutput, calls=%fused_computation.40 | convolution fusion | flops 419430400 | bytes 4259844 | tf_op jit(solution)/shard_map/dot_general | solution.py:62
  39.6 0.1 collective-permute-start.2
  39.7 3.7 %collective-permute-done.9 = bf16[5,128,128]{2,1,0:T(8,128)(2,1)S(1)} collective-permute-done((bf16[5,128,128]{2,1,0:T(8,128)(2,1)S(1)}, bf16[5,128,128]{2,1,0:T(8,128)(2,1)S(1)}, u32[]{:S(2)}, u32[]{:S(2)}) %collective-permute-start.9) | collective-permute-done | bytes 163872 | tf_op jit(solution)/shard_map/ppermute | solution.py:16
  43.4 1.5 %collective-permute-done.8 = bf16[5,128,128]{2,1,0:T(8,128)(2,1)S(1)} collective-permute-done((bf16[5,128,128]{2,1,0:T(8,128)(2,1)S(1)}, bf16[5,128,128]{2,1,0:T(8,128)(2,1)S(1)}, u32[]{:S(2)}, u32[]{:S(2)}) %collective-permute-start.8) | collective-permute-done | bytes 163872 | tf_op jit(solution)/shard_map/ppermute | solution.py:16
  44.9 2.2 %collective-permute-done.7 = bf16[5,128,128]{2,1,0:T(8,128)(2,1)S(1)} collective-permute-done((bf16[5,128,128]{2,1,0:T(8,128)(2,1)S(1)}, bf16[5,128,128]{2,1,0:T(8,128)(2,1)S(1)}, u32[]{:S(2)}, u32[]{:S(2)}) %collective-permute-start.7) | collective-permute-done | bytes 163872 | tf_op jit(solution)/shard_map/ppermute | solution.py:16
  47.1 0.8 fusion.54
  47.9 0.0 copy-done.7
  47.9 1.5 %collective-permute-start.10 = (bf16[5,128,128]{2,1,0:T(8,128)(2,1)}, bf16[5,128,128]{2,1,0:T(8,128)(2,1)}, u32[]{:S(2)}, u32[]{:S(2)}) collective-permute-start(bf16[5,128,128]{2,1,0:T(8,128)(2,1)} %fusion.54), channel_id=1, source_target_pairs={{0,128},{8,136},{16,144},{24,152},{32,160},{40,168},{48,176},{56,1... | collective-permute-start | bytes 491528 | tf_op jit(solution)/shard_map/ppermute | solution.py:16
  49.4 0.0 collective-permute-done.2
  49.5 0.8 multiply_convert_fusion.2
  50.2 1.7 %copy.12 = bf16[128,640]{0,1:T(8,128)(2,1)} copy(bf16[128,640]{1,0:T(8,128)(2,1)} %multiply_convert_fusion.2) | data formatting | bytes 327680 | tf_op jit(solution)/shard_map/convert_element_type | solution.py:67
  51.9 8.3 %collective-permute-done.10 = bf16[5,128,128]{2,1,0:T(8,128)(2,1)} collective-permute-done((bf16[5,128,128]{2,1,0:T(8,128)(2,1)}, bf16[5,128,128]{2,1,0:T(8,128)(2,1)}, u32[]{:S(2)}, u32[]{:S(2)}) %collective-permute-start.10) | collective-permute-done | bytes 163872 | tf_op jit(solution)/shard_map/ppermute | solution.py:16
  60.3 2.7 %fusion.49 = f32[5,128,128]{2,1,0:T(8,128)} fusion(bf16[128,5,128]{0,2,1:T(8,128)(2,1)} %bitcast.73, bf16[5,128,128]{2,1,0:T(8,128)(2,1)} %copy-done.9, bf16[5,128,128]{2,1,0:T(8,128)(2,1)} %copy-done.8, bf16[5,128,128]{2,1,0:T(8,128)(2,1)} %copy-done.7, bf16[5,128,128]{2,1,0:T(8,128)(2,1)} %copy-done.12, bf16[5,128,128]{2,1,0:T(8,128)(2,1)} %copy-done.11, ...), kind=kOutput, calls=%fused_computation.63 | convolution fusion | flops 127385600 | bytes 1638406 | tf_op jit(solution)/shard_map/thd,hde->the/dot_general | solution.py:78
  63.0 2.3 %multiply_reduce_fusion = (f32[128,5]{0,1:T(8,128)S(1)}, f32[128,5,128]{0,2,1:T(8,128)}) fusion(f32[5,128,128]{2,1,0:T(8,128)} %fusion.49, bf16[128,5,128]{0,2,1:T(8,128)(2,1)S(1)} %bitcast.70, bf16[128,5,128]{0,2,1:T(8,128)(2,1)} %bitcast.74, bf16[128,5,128]{0,2,1:T(8,128)(2,1)} %bitcast.72, f32[128,128]{1,0:T(8,128)S(1)} %fusion.64), kind=kOutput, calls=%fused_computation.68 | convolution fusion | flops 42352000 | bytes 1214976 | tf_op jit(solution)/shard_map/hts,shd->thd/dot_general | solution.py:77
  65.3 1.0 multiply_convert_fusion
  66.3 0.0 collective-permute-done.11
  66.3 0.0 copy-start.1
  66.3 3.4 %fusion.83 = (bf16[128,1280]{1,0:T(8,128)(2,1)}, f32[128,1280]{1,0:T(8,128)}) fusion(bf16[128,640]{0,1:T(8,128)(2,1)S(1)} %bitcast.64, s32[]{:T(128)S(6)} %select_n.183, s32[]{:T(128)S(6)} %select_n.185, bf16[1,640,2560]{2,1,0:T(8,128)(2,1)} %bitcast.60, bf16[1,640,2560]{2,1,0:T(8,128)(2,1)} %bitcast.8), kind=kOutput, calls=%fused_computation.102 | convolution fusion | flops 213155840 | bytes 7700488 | tf_op jit(solution)/shard_map/dot_general | solution.py:98
  69.7 3.2 %fusion.82 = (bf16[128,1280]{1,0:T(8,128)(2,1)}, f32[128,1280]{1,0:T(8,128)}) fusion(bf16[128,640]{0,1:T(8,128)(2,1)S(1)} %bitcast.65, s32[]{:T(128)S(6)} %select_n.193, s32[]{:T(128)S(6)} %select_n.195, bf16[1,640,2560]{2,1,0:T(8,128)(2,1)S(1)} %bitcast.63, bf16[1,640,2560]{2,1,0:T(8,128)(2,1)} %bitcast.8), kind=kOutput, calls=%fused_computation.101 | convolution fusion | flops 213155840 | bytes 7700488 | tf_op jit(solution)/shard_map/dot_general | solution.py:98
  72.9 5.6 %collective-permute-start.12 = (bf16[128,1280]{1,0:T(8,128)(2,1)}, bf16[128,1280]{1,0:T(8,128)(2,1)}, u32[]{:S(2)}, u32[]{:S(2)}) collective-permute-start(bf16[128,1280]{1,0:T(8,128)(2,1)} %get-tuple-element.11), channel_id=1, source_target_pairs={{0,1},{4,5},{8,9},{12,13},{16,17},{20,21},{24,25},{28,29},{32,33},... | collective-permute-start | bytes 983048 | tf_op jit(solution)/shard_map/ppermute | solution.py:108
  78.5 1.4 %collective-permute-start.13 = (bf16[128,1280]{1,0:T(8,128)(2,1)}, bf16[128,1280]{1,0:T(8,128)(2,1)}, u32[]{:S(2)}, u32[]{:S(2)}) collective-permute-start(bf16[128,1280]{1,0:T(8,128)(2,1)} %get-tuple-element.12), channel_id=1, source_target_pairs={{3,2},{7,6},{11,10},{15,14},{19,18},{23,22},{27,26},{31,30},{35,34... | collective-permute-start | bytes 983048 | tf_op jit(solution)/shard_map/ppermute | solution.py:109
  79.9 5.9 %collective-permute-done.12 = bf16[128,1280]{1,0:T(8,128)(2,1)} collective-permute-done((bf16[128,1280]{1,0:T(8,128)(2,1)}, bf16[128,1280]{1,0:T(8,128)(2,1)}, u32[]{:S(2)}, u32[]{:S(2)}) %collective-permute-start.12) | collective-permute-done | bytes 327712 | tf_op jit(solution)/shard_map/ppermute | solution.py:108
  85.8 0.0 collective-permute-done.13
  85.8 2.4 %add_convert_fusion.2 = (bf16[128,1280]{1,0:T(8,128)(2,1)S(1)}, bf16[128,1280]{1,0:T(8,128)(2,1)S(1)}) fusion(bf16[128,1280]{1,0:T(8,128)(2,1)} %collective-permute-done.13, bf16[128,1280]{1,0:T(8,128)(2,1)} %collective-permute-done.12, bf16[128,640]{0,1:T(8,128)(2,1)S(1)} %bitcast.66, s32[]{:T(128)S(6)} %select_n.188, s32[]{:T(128)S(6)} %select_n.190, ...), kind=kOutput, calls=%fused_computation.36 | convolution fusion | flops 213975040 | bytes 8028168 | tf_op jit(solution)/shard_map/dot_general | solution.py:98
  88.2 4.4 %collective-permute-start.14 = (bf16[128,1280]{1,0:T(8,128)(2,1)S(1)}, bf16[128,1280]{1,0:T(8,128)(2,1)S(1)}, u32[]{:S(2)}, u32[]{:S(2)}) collective-permute-start(bf16[128,1280]{1,0:T(8,128)(2,1)S(1)} %get-tuple-element.13), channel_id=1, source_target_pairs={{0,1},{1,2},{4,5},{5,6},{8,9},{9,10},{12,13},{13,14},{16,17},{17,1... | collective-permute-start | bytes 983048 | tf_op jit(solution)/shard_map/ppermute | solution.py:108
  92.7 0.7 collective-permute-start.15
  93.3 6.2 %collective-permute-done.14 = bf16[128,1280]{1,0:T(8,128)(2,1)S(1)} collective-permute-done((bf16[128,1280]{1,0:T(8,128)(2,1)S(1)}, bf16[128,1280]{1,0:T(8,128)(2,1)S(1)}, u32[]{:S(2)}, u32[]{:S(2)}) %collective-permute-start.14) | collective-permute-done | bytes 327712 | tf_op jit(solution)/shard_map/ppermute | solution.py:108
  99.5 0.8 add_convert_fusion.1
  100.3 0.0 collective-permute-done.15
  100.3 0.8 add_convert_fusion
  101.1 8.3 %collective-permute-start.16 = (bf16[128,1280]{1,0:T(8,128)(2,1)}, bf16[128,1280]{1,0:T(8,128)(2,1)}, u32[]{:S(2)}, u32[]{:S(2)}) collective-permute-start(bf16[128,1280]{1,0:T(8,128)(2,1)} %add_convert_fusion.1), channel_id=1, source_target_pairs={{0,1},{1,2},{2,3},{4,5},{5,6},{6,7},{8,9},{9,10},{10,11},{12,13},{... | collective-permute-start | bytes 983048 | tf_op jit(solution)/shard_map/ppermute | solution.py:108
  109.4 1.3 %collective-permute-start.17 = (bf16[128,1280]{1,0:T(8,128)(2,1)}, bf16[128,1280]{1,0:T(8,128)(2,1)}, u32[]{:S(2)}, u32[]{:S(2)}) collective-permute-start(bf16[128,1280]{1,0:T(8,128)(2,1)} %add_convert_fusion), channel_id=1, source_target_pairs={{1,0},{2,1},{3,2},{5,4},{6,5},{7,6},{9,8},{10,9},{11,10},{13,12},{... | collective-permute-start | bytes 983048 | tf_op jit(solution)/shard_map/ppermute | solution.py:109
  110.8 4.0 %collective-permute-done.16 = bf16[128,1280]{1,0:T(8,128)(2,1)} collective-permute-done((bf16[128,1280]{1,0:T(8,128)(2,1)}, bf16[128,1280]{1,0:T(8,128)(2,1)}, u32[]{:S(2)}, u32[]{:S(2)}) %collective-permute-start.16) | collective-permute-done | bytes 327712 | tf_op jit(solution)/shard_map/ppermute | solution.py:108
  114.7 4.8 %collective-permute-done.17 = bf16[128,1280]{1,0:T(8,128)(2,1)} collective-permute-done((bf16[128,1280]{1,0:T(8,128)(2,1)}, bf16[128,1280]{1,0:T(8,128)(2,1)}, u32[]{:S(2)}, u32[]{:S(2)}) %collective-permute-start.17) | collective-permute-done | bytes 327712 | tf_op jit(solution)/shard_map/ppermute | solution.py:109
  119.6 3.1 %fusion.23 = bf16[1,128,1280]{2,1,0:T(8,128)(2,1)} fusion(bf16[128,640]{0,1:T(8,128)(2,1)S(1)} %bitcast.67, s32[]{:T(128)S(6)} %select_n.178, s32[]{:T(128)S(6)} %select_n.180, bf16[1,640,2560]{2,1,0:T(8,128)(2,1)} %bitcast.62, bf16[1,640,2560]{2,1,0:T(8,128)(2,1)} %bitcast.8, bf16[128,1280]{1,0:T(8,128)(2,1)} %collective-permute-done.17, ...), kind=kOutput, calls=%fused_computation.22 | convolution fusion | flops 213811200 | bytes 7700488 | tf_op jit(solution)/shard_map/dot_general | solution.py:98
  (24 shorter events, 0.1 us)
Async XLA Ops:
  0.0 1.9 %copy-start = (bf16[2560,640]{1,0:T(8,128)(2,1)S(1)}, bf16[2560,640]{1,0:T(8,128)(2,1)}, u32[]{:S(2)}) copy-start(bf16[2560,640]{1,0:T(8,128)(2,1)} %param.7) | copy-start | bytes 9830404
  0.0 4.6 %collective-permute-start = (bf16[128,5120]{1,0:T(8,128)(2,1)}, bf16[128,5120]{1,0:T(8,128)(2,1)}, u32[]{:S(2)}, u32[]{:S(2)}) collective-permute-start(bf16[128,5120]{1,0:T(8,128)(2,1)} %bitcast.68), channel_id=1, source_target_pairs={{0,4},{4,0},{1,5},{5,1},{2,6},{6,2},{3,7},{7,3},{8,12},{12,8},{9,1... | collective-permute-start | bytes 3932168 | tf_op jit(solution)/shard_map/ppermute | solution.py:12
  0.0 66.3 %collective-permute-start.11 = (bf16[640,2560]{1,0:T(8,128)(2,1)}, bf16[640,2560]{1,0:T(8,128)(2,1)}, u32[]{:S(2)}, u32[]{:S(2)}) collective-permute-start(bf16[640,2560]{1,0:T(8,128)(2,1)} %param.9), channel_id=1, source_target_pairs={{0,4},{4,0},{1,5},{5,1},{2,6},{6,2},{3,7},{7,3},{8,12},{12,8},{9,1... | collective-permute-start | bytes 9830408 | tf_op jit(solution)/shard_map/ppermute | solution.py:12
  1.9 2.7 %copy-start.2 = (bf16[2560,640]{1,0:T(8,128)(2,1)S(1)}, bf16[2560,640]{1,0:T(8,128)(2,1)}, u32[]{:S(2)}) copy-start(bf16[2560,640]{1,0:T(8,128)(2,1)} %param.8) | copy-start | bytes 9830404
  4.6 5.6 %copy-start.4 = (bf16[1,128,5120]{2,1,0:T(8,128)(2,1)S(1)}, bf16[1,128,5120]{2,1,0:T(8,128)(2,1)}, u32[]{:S(2)}) copy-start(bf16[1,128,5120]{2,1,0:T(8,128)(2,1)} %param.5) | copy-start | bytes 3932164
  7.2 4.4 %collective-permute-start.1 = (f32[128,640]{1,0:T(8,128)}, f32[128,640]{1,0:T(8,128)}, u32[]{:S(2)}, u32[]{:S(2)}) collective-permute-start(f32[128,640]{1,0:T(8,128)} %fusion.40), channel_id=1, source_target_pairs={{0,4},{4,0},{1,5},{5,1},{2,6},{6,2},{3,7},{7,3},{8,12},{12,8},{9,1... | collective-permute-start | bytes 983048 | tf_op jit(solution)/shard_map/ppermute | solution.py:12
  9.7 4.8 %collective-permute-start.3 = (f32[128,640]{1,0:T(8,128)}, f32[128,640]{1,0:T(8,128)}, u32[]{:S(2)}, u32[]{:S(2)}) collective-permute-start(f32[128,640]{1,0:T(8,128)} %fusion.36), channel_id=1, source_target_pairs={{0,4},{4,0},{1,5},{5,1},{2,6},{6,2},{3,7},{7,3},{8,12},{12,8},{9,1... | collective-permute-start | bytes 983048 | tf_op jit(solution)/shard_map/ppermute | solution.py:12
  18.1 19.8 %copy-start.3 = (bf16[2560,640]{1,0:T(8,128)(2,1)S(1)}, bf16[2560,640]{1,0:T(8,128)(2,1)}, u32[]{:S(2)}) copy-start(bf16[2560,640]{1,0:T(8,128)(2,1)} %param.6) | copy-start | bytes 9830404
  19.4 10.0 %collective-permute-start.6 = (bf16[5,128,128]{2,1,0:T(8,128)(2,1)S(1)}, bf16[5,128,128]{2,1,0:T(8,128)(2,1)S(1)}, u32[]{:S(2)}, u32[]{:S(2)}) collective-permute-start(bf16[5,128,128]{2,1,0:T(8,128)(2,1)S(1)} %get-tuple-element.19), channel_id=1, source_target_pairs={{0,24},{8,0},{16,8},{24,16},{32,56},{40,32},{48,40},{56,48},{64,88... | collective-permute-start | bytes 491528 | tf_op jit(solution)/shard_map/ppermute | solution.py:16
  22.2 8.6 %collective-permute-start.5 = (bf16[5,128,128]{2,1,0:T(8,128)(2,1)S(1)}, bf16[5,128,128]{2,1,0:T(8,128)(2,1)S(1)}, u32[]{:S(2)}, u32[]{:S(2)}) collective-permute-start(bf16[5,128,128]{2,1,0:T(8,128)(2,1)S(1)} %get-tuple-element.19), channel_id=1, source_target_pairs={{0,16},{8,24},{16,0},{24,8},{32,48},{40,56},{48,32},{56,40},{64,80... | collective-permute-start | bytes 491528 | tf_op jit(solution)/shard_map/ppermute | solution.py:16
  23.0 10.1 %collective-permute-start.4 = (bf16[5,128,128]{2,1,0:T(8,128)(2,1)S(1)}, bf16[5,128,128]{2,1,0:T(8,128)(2,1)S(1)}, u32[]{:S(2)}, u32[]{:S(2)}) collective-permute-start(bf16[5,128,128]{2,1,0:T(8,128)(2,1)S(1)} %get-tuple-element.19), channel_id=1, source_target_pairs={{0,8},{8,16},{16,24},{24,0},{32,40},{40,48},{48,56},{56,32},{64,72... | collective-permute-start | bytes 491528 | tf_op jit(solution)/shard_map/ppermute | solution.py:16
  29.4 18.5 %copy-start.7 = (bf16[5,128,128]{2,1,0:T(8,128)(2,1)}, bf16[5,128,128]{2,1,0:T(8,128)(2,1)S(1)}, u32[]{:S(2)}) copy-start(bf16[5,128,128]{2,1,0:T(8,128)(2,1)S(1)} %collective-permute-done.6) | copy-start | bytes 491524
  30.8 17.1 %copy-start.8 = (bf16[5,128,128]{2,1,0:T(8,128)(2,1)}, bf16[5,128,128]{2,1,0:T(8,128)(2,1)S(1)}, u32[]{:S(2)}) copy-start(bf16[5,128,128]{2,1,0:T(8,128)(2,1)S(1)} %collective-permute-done.5) | copy-start | bytes 491524
  33.1 14.9 %copy-start.9 = (bf16[5,128,128]{2,1,0:T(8,128)(2,1)}, bf16[5,128,128]{2,1,0:T(8,128)(2,1)S(1)}, u32[]{:S(2)}) copy-start(bf16[5,128,128]{2,1,0:T(8,128)(2,1)S(1)} %collective-permute-done.4) | copy-start | bytes 491524
  33.2 10.2 %collective-permute-start.9 = (bf16[5,128,128]{2,1,0:T(8,128)(2,1)S(1)}, bf16[5,128,128]{2,1,0:T(8,128)(2,1)S(1)}, u32[]{:S(2)}, u32[]{:S(2)}) collective-permute-start(bf16[5,128,128]{2,1,0:T(8,128)(2,1)S(1)} %fusion.65), channel_id=1, source_target_pairs={{0,96},{8,104},{16,112},{24,120},{32,0},{40,8},{48,16},{56,24},{64... | collective-permute-start | bytes 491528 | tf_op jit(solution)/shard_map/ppermute | solution.py:16
  36.3 8.6 %collective-permute-start.8 = (bf16[5,128,128]{2,1,0:T(8,128)(2,1)S(1)}, bf16[5,128,128]{2,1,0:T(8,128)(2,1)S(1)}, u32[]{:S(2)}, u32[]{:S(2)}) collective-permute-start(bf16[5,128,128]{2,1,0:T(8,128)(2,1)S(1)} %fusion.65), channel_id=1, source_target_pairs={{0,64},{8,72},{16,80},{24,88},{32,96},{40,104},{48,112},{56,120},{... | collective-permute-start | bytes 491528 | tf_op jit(solution)/shard_map/ppermute | solution.py:16
  36.9 10.2 %collective-permute-start.7 = (bf16[5,128,128]{2,1,0:T(8,128)(2,1)S(1)}, bf16[5,128,128]{2,1,0:T(8,128)(2,1)S(1)}, u32[]{:S(2)}, u32[]{:S(2)}) collective-permute-start(bf16[5,128,128]{2,1,0:T(8,128)(2,1)S(1)} %fusion.65), channel_id=1, source_target_pairs={{0,32},{8,40},{16,48},{24,56},{32,64},{40,72},{48,80},{56,88},{64,... | collective-permute-start | bytes 491528 | tf_op jit(solution)/shard_map/ppermute | solution.py:16
  39.6 9.8 %collective-permute-start.2 = (f32[128,640]{1,0:T(8,128)S(1)}, f32[128,640]{1,0:T(8,128)S(1)}, u32[]{:S(2)}, u32[]{:S(2)}) collective-permute-start(f32[128,640]{1,0:T(8,128)S(1)} %fusion.38), channel_id=1, source_target_pairs={{0,4},{4,0},{1,5},{5,1},{2,6},{6,2},{3,7},{7,3},{8,12},{12,8},{9,1... | collective-permute-start | bytes 983048 | tf_op jit(solution)/shard_map/ppermute | solution.py:12
  43.4 6.0 %copy-start.10 = (bf16[5,128,128]{2,1,0:T(8,128)(2,1)}, bf16[5,128,128]{2,1,0:T(8,128)(2,1)S(1)}, u32[]{:S(2)}) copy-start(bf16[5,128,128]{2,1,0:T(8,128)(2,1)S(1)} %collective-permute-done.9) | copy-start | bytes 491524
  44.9 4.6 %copy-start.11 = (bf16[5,128,128]{2,1,0:T(8,128)(2,1)}, bf16[5,128,128]{2,1,0:T(8,128)(2,1)S(1)}, u32[]{:S(2)}) copy-start(bf16[5,128,128]{2,1,0:T(8,128)(2,1)S(1)} %collective-permute-done.8) | copy-start | bytes 491524
  47.1 2.3 %copy-start.12 = (bf16[5,128,128]{2,1,0:T(8,128)(2,1)}, bf16[5,128,128]{2,1,0:T(8,128)(2,1)S(1)}, u32[]{:S(2)}) copy-start(bf16[5,128,128]{2,1,0:T(8,128)(2,1)S(1)} %collective-permute-done.7) | copy-start | bytes 491524
  47.9 12.3 %collective-permute-start.10 = (bf16[5,128,128]{2,1,0:T(8,128)(2,1)}, bf16[5,128,128]{2,1,0:T(8,128)(2,1)}, u32[]{:S(2)}, u32[]{:S(2)}) collective-permute-start(bf16[5,128,128]{2,1,0:T(8,128)(2,1)} %fusion.54), channel_id=1, source_target_pairs={{0,128},{8,136},{16,144},{24,152},{32,160},{40,168},{48,176},{56,1... | collective-permute-start | bytes 491528 | tf_op jit(solution)/shard_map/ppermute | solution.py:16
  66.3 3.4 %copy-start.1 = (bf16[640,2560]{1,0:T(8,128)(2,1)S(1)}, bf16[640,2560]{1,0:T(8,128)(2,1)}, u32[]{:S(2)}) copy-start(bf16[640,2560]{1,0:T(8,128)(2,1)} %param.9) | copy-start | bytes 9830404
  72.9 12.9 %collective-permute-start.12 = (bf16[128,1280]{1,0:T(8,128)(2,1)}, bf16[128,1280]{1,0:T(8,128)(2,1)}, u32[]{:S(2)}, u32[]{:S(2)}) collective-permute-start(bf16[128,1280]{1,0:T(8,128)(2,1)} %get-tuple-element.11), channel_id=1, source_target_pairs={{0,1},{4,5},{8,9},{12,13},{16,17},{20,21},{24,25},{28,29},{32,33},... | collective-permute-start | bytes 983048 | tf_op jit(solution)/shard_map/ppermute | solution.py:108
  78.5 7.3 %collective-permute-start.13 = (bf16[128,1280]{1,0:T(8,128)(2,1)}, bf16[128,1280]{1,0:T(8,128)(2,1)}, u32[]{:S(2)}, u32[]{:S(2)}) collective-permute-start(bf16[128,1280]{1,0:T(8,128)(2,1)} %get-tuple-element.12), channel_id=1, source_target_pairs={{3,2},{7,6},{11,10},{15,14},{19,18},{23,22},{27,26},{31,30},{35,34... | collective-permute-start | bytes 983048 | tf_op jit(solution)/shard_map/ppermute | solution.py:109
  79.9 19.6 %copy-start.6 = (f32[128,1280]{1,0:T(8,128)S(1)}, f32[128,1280]{1,0:T(8,128)}, u32[]{:S(2)}) copy-start(f32[128,1280]{1,0:T(8,128)} %get-tuple-element.26) | copy-start | bytes 1966084
  79.9 20.4 %copy-start.5 = (f32[128,1280]{1,0:T(8,128)S(1)}, f32[128,1280]{1,0:T(8,128)}, u32[]{:S(2)}) copy-start(f32[128,1280]{1,0:T(8,128)} %get-tuple-element.24) | copy-start | bytes 1966084
  88.2 11.3 %collective-permute-start.14 = (bf16[128,1280]{1,0:T(8,128)(2,1)S(1)}, bf16[128,1280]{1,0:T(8,128)(2,1)S(1)}, u32[]{:S(2)}, u32[]{:S(2)}) collective-permute-start(bf16[128,1280]{1,0:T(8,128)(2,1)S(1)} %get-tuple-element.13), channel_id=1, source_target_pairs={{0,1},{1,2},{4,5},{5,6},{8,9},{9,10},{12,13},{13,14},{16,17},{17,1... | collective-permute-start | bytes 983048 | tf_op jit(solution)/shard_map/ppermute | solution.py:108
  92.7 7.7 %collective-permute-start.15 = (bf16[128,1280]{1,0:T(8,128)(2,1)S(1)}, bf16[128,1280]{1,0:T(8,128)(2,1)S(1)}, u32[]{:S(2)}, u32[]{:S(2)}) collective-permute-start(bf16[128,1280]{1,0:T(8,128)(2,1)S(1)} %get-tuple-element.14), channel_id=1, source_target_pairs={{2,1},{3,2},{6,5},{7,6},{10,9},{11,10},{14,13},{15,14},{18,17},{19... | collective-permute-start | bytes 983048 | tf_op jit(solution)/shard_map/ppermute | solution.py:109
  101.1 13.6 %collective-permute-start.16 = (bf16[128,1280]{1,0:T(8,128)(2,1)}, bf16[128,1280]{1,0:T(8,128)(2,1)}, u32[]{:S(2)}, u32[]{:S(2)}) collective-permute-start(bf16[128,1280]{1,0:T(8,128)(2,1)} %add_convert_fusion.1), channel_id=1, source_target_pairs={{0,1},{1,2},{2,3},{4,5},{5,6},{6,7},{8,9},{9,10},{10,11},{12,13},{... | collective-permute-start | bytes 983048 | tf_op jit(solution)/shard_map/ppermute | solution.py:108
  109.4 10.1 %collective-permute-start.17 = (bf16[128,1280]{1,0:T(8,128)(2,1)}, bf16[128,1280]{1,0:T(8,128)(2,1)}, u32[]{:S(2)}, u32[]{:S(2)}) collective-permute-start(bf16[128,1280]{1,0:T(8,128)(2,1)} %add_convert_fusion), channel_id=1, source_target_pairs={{1,0},{2,1},{3,2},{5,4},{6,5},{7,6},{9,8},{10,9},{11,10},{13,12},{... | collective-permute-start | bytes 983048 | tf_op jit(solution)/shard_map/ppermute | solution.py:109

commit v7 on v5

--- a/solution.py
+++ b/solution.py
@@ -77,7 +77,7 @@
     scores = (scores * causal[None, :, :]).astype(BF16)
     local_part = jnp.einsum("hts,shd->thd", scores, values, preferred_element_type=F32)
     carried = jnp.einsum(
-        "thd,hde->the", queries.astype(F32), prefix_state, precision=lax.Precision.HIGHEST
+        "thd,hde->the", queries.astype(F32), prefix_state.astype(BF16).astype(F32), preferred_element_type=F32
     )
     attended = local_part + carried
     scale = lax.rsqrt(jnp.mean(attended * attended, axis=2, keepdims=True) + 1e-06)

time: 109 us -> 109 us (level)
  no operation moved by 1% of the time
where the time goes in v7:
time: 109 us; the launch traced here: 108 us
  starting transfers between devices  41.3 us (38%)
  waiting for transfers between devices  27 us (25%)
  matrix products  21.1 us (19%)
  other arithmetic  11.7 us (11%)
  local copies, waits for them, and re-layouts  6.73 us (6%)
    ppermute x7, starting transfers between devices, shifted(): return lax.ppermute(x, axis, pairs)  18.9 us
    ppermute x3, starting transfers between devices, shards(): right = lax.ppermute(send_r, 'head', rpairs).astype(F32)  18.7 us
    ppermute x3, waiting for transfers between devices, shards(): right = lax.ppermute(send_r, 'head', rpairs).astype(F32)  13.4 us
    ppermute x7, waiting for transfers between devices, shifted(): return lax.ppermute(x, axis, pairs)  9.13 us
    dot_general x3, matrix products, shards(): lent = swap_cores(jnp.dot(got_cols, w, preferred_element_type=F32))  6.9 us
    dot_general x3, matrix products, shards(): own = jnp.dot(mine_cols, w, preferred_element_type=F32)  6.87 us
    ppermute x3, waiting for transfers between devices, shards(): left = lax.ppermute(send_l, 'head', lpairs).astype(F32)  4.42 us
    squeeze x1, other arithmetic, shards(): pieces.append(piece[0])  4.33 us
  transfers between devices with their start and end apart: 18, of which 9 were waited for; matrix products, arithmetic and copies ran while one was open for 28% of the time, Pallas kernels for 0%

profile of v7, /device:TPU:10, one launch (start us, length us, event | category | flops | bytes accessed | tf_op | source)
XLA Modules:
  0.0 108.1 jit_solution(6139010565173251020)
XLA Ops:
  0.0 0.0 copy-start
  0.0 2.1 %dynamic-slice_bitcast_fusion = bf16[128,2560]{1,0:T(8,128)(2,1)} fusion(bf16[1,128,5120]{2,1,0:T(8,128)(2,1)} %param.5, s32[]{:T(128)S(6)} %select_n.157), kind=kLoop, calls=%fused_computation.41 | loop fusion | bytes 1310724 | tf_op jit(solution)/shard_map/dynamic_slice | solution.py:59
  2.1 0.0 collective-permute-start
  2.1 0.5 collective-permute-start.11
  2.6 2.6 %fusion.24 = f32[128,640]{1,0:T(8,128)} fusion(bf16[2560,640]{1,0:T(8,128)(2,1)S(1)} %copy-done, bf16[1,128,5120]{2,1,0:T(8,128)(2,1)} %param.5, s32[]{:T(128)S(6)} %select_n.156), kind=kOutput, calls=%fused_computation.35 | convolution fusion | flops 419430400 | bytes 4259844 | tf_op jit(solution)/shard_map/dot_general | solution.py:64
  5.3 0.0 collective-permute-done
  5.3 2.6 %fusion.56 = f32[128,640]{1,0:T(8,128)} fusion(bf16[128,2560]{1,0:T(8,128)(2,1)} %collective-permute-done, bf16[2560,640]{1,0:T(8,128)(2,1)S(1)} %copy-done), kind=kOutput, calls=%fused_computation.92 | convolution fusion | flops 419430400 | bytes 4259840 | tf_op jit(solution)/shard_map/dot_general | solution.py:63
  7.9 0.0 collective-permute-start.1
  7.9 2.5 %fusion.58 = f32[128,640]{1,0:T(8,128)} fusion(bf16[128,2560]{1,0:T(8,128)(2,1)} %collective-permute-done, bf16[2560,640]{1,0:T(8,128)(2,1)S(1)} %copy-done.1), kind=kOutput, calls=%fused_computation.94 | convolution fusion | flops 419430400 | bytes 4259840 | tf_op jit(solution)/shard_map/dot_general | solution.py:63
  10.4 0.5 collective-permute-start.3
  10.9 1.4 %fusion.20 = f32[128,640]{1,0:T(8,128)} fusion(bf16[2560,640]{1,0:T(8,128)(2,1)S(1)} %copy-done.1, bf16[1,128,5120]{2,1,0:T(8,128)(2,1)S(1)} %copy-done.3, s32[]{:T(128)S(6)} %select_n.156), kind=kOutput, calls=%fused_computation.31 | convolution fusion | flops 419430400 | bytes 4259844 | tf_op jit(solution)/shard_map/dot_general | solution.py:64
  12.4 0.0 collective-permute-done.1
  12.4 1.8 %add_convert_fusion.4 = bf16[128,640]{1,0:T(8,128)(2,1)} fusion(f32[128,640]{1,0:T(8,128)} %fusion.24, f32[128,640]{1,0:T(8,128)} %collective-permute-done.1), kind=kLoop, calls=%fused_computation.72 | loop fusion | flops 163840 | bytes 819200 | tf_op jit(solution)/shard_map/convert_element_type | solution.py:70
  14.1 1.1 copy.11
  15.2 0.0 collective-permute-done.3
  15.2 1.8 %multiply_convert_fusion.1 = bf16[128,640]{1,0:T(8,128)(2,1)} fusion(f32[128,640]{1,0:T(8,128)} %fusion.20, f32[128,640]{1,0:T(8,128)} %collective-permute-done.3), kind=kLoop, calls=%fused_computation.70 | loop fusion | flops 491520 | bytes 819200 | tf_op jit(solution)/shard_map/convert_element_type | solution.py:69
  17.0 1.7 %copy.13 = bf16[128,640]{0,1:T(8,128)(2,1)} copy(bf16[128,640]{1,0:T(8,128)(2,1)} %multiply_convert_fusion.1) | data formatting | bytes 327680 | tf_op jit(solution)/shard_map/convert_element_type | solution.py:69
  18.8 1.3 %fusion.55 = (bf16[5,128,128]{2,1,0:T(8,128)(2,1)S(1)}, f32[5,128,128]{2,1,0:T(8,128)S(1)}) fusion(bf16[128,5,128]{0,2,1:T(8,128)(2,1)} %bitcast.46, bf16[128,5,128]{0,2,1:T(8,128)(2,1)S(1)} %bitcast.44), kind=kOutput, calls=%fused_computation.91 | convolution fusion | flops 21053440 | bytes 819200 | tf_op jit(solution)/shard_map/thd,the->hde/dot_general | solution.py:71
  20.1 1.5 %collective-permute-start.4 = (bf16[5,128,128]{2,1,0:T(8,128)(2,1)S(1)}, bf16[5,128,128]{2,1,0:T(8,128)(2,1)S(1)}, u32[]{:S(2)}, u32[]{:S(2)}) collective-permute-start(bf16[5,128,128]{2,1,0:T(8,128)(2,1)S(1)} %get-tuple-element.27), channel_id=1, source_target_pairs={{0,8},{8,16},{16,24},{24,0},{32,40},{40,48},{48,56},{56,32},{64,72... | collective-permute-start | bytes 491528 | tf_op jit(solution)/shard_map/ppermute | solution.py:16
  21.6 1.1 %collective-permute-start.5 = (bf16[5,128,128]{2,1,0:T(8,128)(2,1)S(1)}, bf16[5,128,128]{2,1,0:T(8,128)(2,1)S(1)}, u32[]{:S(2)}, u32[]{:S(2)}) collective-permute-start(bf16[5,128,128]{2,1,0:T(8,128)(2,1)S(1)} %get-tuple-element.27), channel_id=1, source_target_pairs={{0,16},{8,24},{16,0},{24,8},{32,48},{40,56},{48,32},{56,40},{64,80... | collective-permute-start | bytes 491528 | tf_op jit(solution)/shard_map/ppermute | solution.py:16
  22.7 2.2 %collective-permute-start.6 = (bf16[5,128,128]{2,1,0:T(8,128)(2,1)S(1)}, bf16[5,128,128]{2,1,0:T(8,128)(2,1)S(1)}, u32[]{:S(2)}, u32[]{:S(2)}) collective-permute-start(bf16[5,128,128]{2,1,0:T(8,128)(2,1)S(1)} %get-tuple-element.27), channel_id=1, source_target_pairs={{0,24},{8,0},{16,8},{24,16},{32,56},{40,32},{48,40},{56,48},{64,88... | collective-permute-start | bytes 491528 | tf_op jit(solution)/shard_map/ppermute | solution.py:16
  24.9 2.8 %fusion.22 = f32[128,640]{1,0:T(8,128)S(1)} fusion(bf16[2560,640]{1,0:T(8,128)(2,1)} %param.6, bf16[1,128,5120]{2,1,0:T(8,128)(2,1)} %param.5, s32[]{:T(128)S(6)} %select_n.156), kind=kOutput, calls=%fused_computation.33 | convolution fusion | flops 419430400 | bytes 4259844 | tf_op jit(solution)/shard_map/dot_general | solution.py:64
  27.7 0.0 collective-permute-done.4
  27.7 2.5 %collective-permute-done.5 = bf16[5,128,128]{2,1,0:T(8,128)(2,1)S(1)} collective-permute-done((bf16[5,128,128]{2,1,0:T(8,128)(2,1)S(1)}, bf16[5,128,128]{2,1,0:T(8,128)(2,1)S(1)}, u32[]{:S(2)}, u32[]{:S(2)}) %collective-permute-start.5) | collective-permute-done | bytes 163872 | tf_op jit(solution)/shard_map/ppermute | solution.py:16
  30.2 1.6 %collective-permute-done.6 = bf16[5,128,128]{2,1,0:T(8,128)(2,1)S(1)} collective-permute-done((bf16[5,128,128]{2,1,0:T(8,128)(2,1)S(1)}, bf16[5,128,128]{2,1,0:T(8,128)(2,1)S(1)}, u32[]{:S(2)}, u32[]{:S(2)}) %collective-permute-start.6) | collective-permute-done | bytes 163872 | tf_op jit(solution)/shard_map/ppermute | solution.py:16
  31.8 0.1 fusion.48
  31.9 1.7 %collective-permute-start.7 = (bf16[5,128,128]{2,1,0:T(8,128)(2,1)S(1)}, bf16[5,128,128]{2,1,0:T(8,128)(2,1)S(1)}, u32[]{:S(2)}, u32[]{:S(2)}) collective-permute-start(bf16[5,128,128]{2,1,0:T(8,128)(2,1)S(1)} %fusion.48), channel_id=1, source_target_pairs={{0,32},{8,40},{16,48},{24,56},{32,64},{40,72},{48,80},{56,88},{64,... | collective-permute-start | bytes 491528 | tf_op jit(solution)/shard_map/ppermute | solution.py:16
  33.6 1.6 %collective-permute-start.8 = (bf16[5,128,128]{2,1,0:T(8,128)(2,1)S(1)}, bf16[5,128,128]{2,1,0:T(8,128)(2,1)S(1)}, u32[]{:S(2)}, u32[]{:S(2)}) collective-permute-start(bf16[5,128,128]{2,1,0:T(8,128)(2,1)S(1)} %fusion.48), channel_id=1, source_target_pairs={{0,64},{8,72},{16,80},{24,88},{32,96},{40,104},{48,112},{56,120},{... | collective-permute-start | bytes 491528 | tf_op jit(solution)/shard_map/ppermute | solution.py:16
  35.1 1.8 %collective-permute-start.9 = (bf16[5,128,128]{2,1,0:T(8,128)(2,1)S(1)}, bf16[5,128,128]{2,1,0:T(8,128)(2,1)S(1)}, u32[]{:S(2)}, u32[]{:S(2)}) collective-permute-start(bf16[5,128,128]{2,1,0:T(8,128)(2,1)S(1)} %fusion.48), channel_id=1, source_target_pairs={{0,96},{8,104},{16,112},{24,120},{32,0},{40,8},{48,16},{56,24},{64... | collective-permute-start | bytes 491528 | tf_op jit(solution)/shard_map/ppermute | solution.py:16
  36.9 1.8 %fusion.57 = f32[128,640]{1,0:T(8,128)S(1)} fusion(bf16[128,2560]{1,0:T(8,128)(2,1)} %collective-permute-done, bf16[2560,640]{1,0:T(8,128)(2,1)S(1)} %copy-done.2), kind=kOutput, calls=%fused_computation.93 | convolution fusion | flops 419430400 | bytes 4259840 | tf_op jit(solution)/shard_map/dot_general | solution.py:63
  38.7 0.1 collective-permute-start.2
  38.8 0.0 collective-permute-done.7
  38.8 0.0 copy-start.7
  38.8 3.2 %collective-permute-done.8 = bf16[5,128,128]{2,1,0:T(8,128)(2,1)S(1)} collective-permute-done((bf16[5,128,128]{2,1,0:T(8,128)(2,1)S(1)}, bf16[5,128,128]{2,1,0:T(8,128)(2,1)S(1)}, u32[]{:S(2)}, u32[]{:S(2)}) %collective-permute-start.8) | collective-permute-done | bytes 163872 | tf_op jit(solution)/shard_map/ppermute | solution.py:16
  42.0 1.8 %collective-permute-done.9 = bf16[5,128,128]{2,1,0:T(8,128)(2,1)S(1)} collective-permute-done((bf16[5,128,128]{2,1,0:T(8,128)(2,1)S(1)}, bf16[5,128,128]{2,1,0:T(8,128)(2,1)S(1)}, u32[]{:S(2)}, u32[]{:S(2)}) %collective-permute-start.9) | collective-permute-done | bytes 163872 | tf_op jit(solution)/shard_map/ppermute | solution.py:16
  43.8 0.8 fusion.36
  44.6 0.0 copy-done.6
  44.6 9.0 %collective-permute-start.10 = (bf16[5,128,128]{2,1,0:T(8,128)(2,1)}, bf16[5,128,128]{2,1,0:T(8,128)(2,1)}, u32[]{:S(2)}, u32[]{:S(2)}) collective-permute-start(bf16[5,128,128]{2,1,0:T(8,128)(2,1)} %fusion.36), channel_id=1, source_target_pairs={{0,128},{8,136},{16,144},{24,152},{32,160},{40,168},{48,176},{56,1... | collective-permute-start | bytes 491528 | tf_op jit(solution)/shard_map/ppermute | solution.py:16
  53.6 0.0 collective-permute-done.2
  53.6 0.8 multiply_convert_fusion.2
  54.4 1.7 %copy.12 = bf16[128,640]{0,1:T(8,128)(2,1)} copy(bf16[128,640]{1,0:T(8,128)(2,1)} %multiply_convert_fusion.2) | data formatting | bytes 327680 | tf_op jit(solution)/shard_map/convert_element_type | solution.py:68
  56.1 0.1 collective-permute-done.10
  56.2 2.5 %fusion.39 = f32[5,128,128]{2,1,0:T(8,128)} fusion(bf16[128,5,128]{0,2,1:T(8,128)(2,1)} %bitcast.48, bf16[5,128,128]{2,1,0:T(8,128)(2,1)} %copy-done.4, bf16[5,128,128]{2,1,0:T(8,128)(2,1)} %copy-done.5, bf16[5,128,128]{2,1,0:T(8,128)(2,1)} %copy-done.6, bf16[5,128,128]{2,1,0:T(8,128)(2,1)} %copy-done.7, bf16[5,128,128]{2,1,0:T(8,128)(2,1)} %copy-done.8, ...), kind=kOutput, calls=%fused_computation.74 | convolution fusion | flops 22609920 | bytes 1638406 | tf_op jit(solution)/shard_map/thd,hde->the/dot_general | solution.py:79
  58.7 2.3 %multiply_reduce_fusion = (f32[128,5]{0,1:T(8,128)S(1)}, f32[128,5,128]{0,2,1:T(8,128)}) fusion(f32[5,128,128]{2,1,0:T(8,128)} %fusion.39, bf16[128,5,128]{0,2,1:T(8,128)(2,1)S(1)} %bitcast.45, bf16[128,5,128]{0,2,1:T(8,128)(2,1)} %bitcast.49, bf16[128,5,128]{0,2,1:T(8,128)(2,1)} %bitcast.47, f32[128,128]{1,0:T(8,128)S(1)} %fusion.47), kind=kOutput, calls=%fused_computation.69 | convolution fusion | flops 42352000 | bytes 1214976 | tf_op jit(solution)/shard_map/hts,shd->thd/dot_general | solution.py:78
  61.0 1.0 multiply_convert_fusion
  62.0 0.0 collective-permute-done.11
  62.0 4.3 %fusion.11 = (bf16[640,1280]{1,0:T(8,128)(2,1)S(1)}, bf16[640,1280]{1,0:T(8,128)(2,1)S(1)}, bf16[640,1280]{1,0:T(8,128)(2,1)S(1)}, bf16[640,1280]{1,0:T(8,128)(2,1)S(1)}) fusion(s32[]{:T(128)S(6)} %select_n.181, s32[]{:T(128)S(6)} %select_n.183, bf16[1,640,2560]{2,1,0:T(8,128)(2,1)} %bitcast.43, bf16[1,640,2560]{2,1,0:T(8,128)(2,1)} %bitcast.8, ...), kind=kLoop, calls=%fused_computation.19 | loop fusion | flops 13107200 | bytes 13107232 | tf_op jit(solution)/shard_map/squeeze | solution.py:97
  66.4 1.2 %fusion = f32[128,5120]{1,0:T(8,128)S(1)} fusion(bf16[128,640]{0,1:T(8,128)(2,1)S(1)} %bitcast.50, bf16[640,1280]{1,0:T(8,128)(2,1)S(1)} %get-tuple-element.20, bf16[640,1280]{1,0:T(8,128)(2,1)S(1)} %get-tuple-element.19, bf16[640,1280]{1,0:T(8,128)(2,1)S(1)} %get-tuple-element.18, bf16[640,1280]{1,0:T(8,128)(2,1)S(1)} %get-tuple-element.17), kind=kOutput, calls=%fused_computation.8 | convolution fusion | flops 865075200 | bytes 9338880 | tf_op jit(solution)/shard_map/dot_general | solution.py:99
  67.6 0.1 fusion.54
  67.7 6.5 %collective-permute-start.12 = (bf16[128,1280]{1,0:T(8,128)(2,1)S(1)}, bf16[128,1280]{1,0:T(8,128)(2,1)S(1)}, u32[]{:S(2)}, u32[]{:S(2)}) collective-permute-start(bf16[128,1280]{1,0:T(8,128)(2,1)S(1)} %get-tuple-element.11), channel_id=1, source_target_pairs={{0,1},{4,5},{8,9},{12,13},{16,17},{20,21},{24,25},{28,29},{32,33},... | collective-permute-start | bytes 983048 | tf_op jit(solution)/shard_map/ppermute | solution.py:112
  74.2 0.7 collective-permute-start.13
  74.9 5.5 %collective-permute-done.12 = bf16[128,1280]{1,0:T(8,128)(2,1)S(1)} collective-permute-done((bf16[128,1280]{1,0:T(8,128)(2,1)S(1)}, bf16[128,1280]{1,0:T(8,128)(2,1)S(1)}, u32[]{:S(2)}, u32[]{:S(2)}) %collective-permute-start.12) | collective-permute-done | bytes 327712 | tf_op jit(solution)/shard_map/ppermute | solution.py:112
  80.4 0.0 collective-permute-done.13
  80.4 0.1 add_convert_fusion.2
  80.5 4.4 %collective-permute-start.14 = (bf16[128,1280]{1,0:T(8,128)(2,1)S(1)}, bf16[128,1280]{1,0:T(8,128)(2,1)S(1)}, u32[]{:S(2)}, u32[]{:S(2)}) collective-permute-start(bf16[128,1280]{1,0:T(8,128)(2,1)S(1)} %get-tuple-element.13), channel_id=1, source_target_pairs={{0,1},{1,2},{4,5},{5,6},{8,9},{9,10},{12,13},{13,14},{16,17},{17,1... | collective-permute-start | bytes 983048 | tf_op jit(solution)/shard_map/ppermute | solution.py:112
  84.9 0.7 collective-permute-start.15
  85.6 4.7 %collective-permute-done.14 = bf16[128,1280]{1,0:T(8,128)(2,1)S(1)} collective-permute-done((bf16[128,1280]{1,0:T(8,128)(2,1)S(1)}, bf16[128,1280]{1,0:T(8,128)(2,1)S(1)}, u32[]{:S(2)}, u32[]{:S(2)}) %collective-permute-start.14) | collective-permute-done | bytes 327712 | tf_op jit(solution)/shard_map/ppermute | solution.py:112
  90.3 0.0 collective-permute-done.15
  90.3 0.2 add_convert_fusion
  90.5 7.8 %collective-permute-start.16 = (bf16[128,1280]{1,0:T(8,128)(2,1)S(1)}, bf16[128,1280]{1,0:T(8,128)(2,1)S(1)}, u32[]{:S(2)}, u32[]{:S(2)}) collective-permute-start(bf16[128,1280]{1,0:T(8,128)(2,1)S(1)} %get-tuple-element.15), channel_id=1, source_target_pairs={{0,1},{1,2},{2,3},{4,5},{5,6},{6,7},{8,9},{9,10},{10,11},{12,13},{... | collective-permute-start | bytes 983048 | tf_op jit(solution)/shard_map/ppermute | solution.py:112
  98.2 1.3 %collective-permute-start.17 = (bf16[128,1280]{1,0:T(8,128)(2,1)S(1)}, bf16[128,1280]{1,0:T(8,128)(2,1)S(1)}, u32[]{:S(2)}, u32[]{:S(2)}) collective-permute-start(bf16[128,1280]{1,0:T(8,128)(2,1)S(1)} %get-tuple-element.16), channel_id=1, source_target_pairs={{1,0},{2,1},{3,2},{5,4},{6,5},{7,6},{9,8},{10,9},{11,10},{13,12},{... | collective-permute-start | bytes 983048 | tf_op jit(solution)/shard_map/ppermute | solution.py:113
  99.5 3.3 %collective-permute-done.16 = bf16[128,1280]{1,0:T(8,128)(2,1)S(1)} collective-permute-done((bf16[128,1280]{1,0:T(8,128)(2,1)S(1)}, bf16[128,1280]{1,0:T(8,128)(2,1)S(1)}, u32[]{:S(2)}, u32[]{:S(2)}) %collective-permute-start.16) | collective-permute-done | bytes 327712 | tf_op jit(solution)/shard_map/ppermute | solution.py:112
  102.8 4.4 %collective-permute-done.17 = bf16[128,1280]{1,0:T(8,128)(2,1)S(1)} collective-permute-done((bf16[128,1280]{1,0:T(8,128)(2,1)S(1)}, bf16[128,1280]{1,0:T(8,128)(2,1)S(1)}, u32[]{:S(2)}, u32[]{:S(2)}) %collective-permute-start.17) | collective-permute-done | bytes 327712 | tf_op jit(solution)/shard_map/ppermute | solution.py:113
  107.2 0.8 fusion.37
  (19 shorter events, 0.0 us)
Async XLA Ops:
  0.0 2.6 %copy-start = (bf16[2560,640]{1,0:T(8,128)(2,1)S(1)}, bf16[2560,640]{1,0:T(8,128)(2,1)}, u32[]{:S(2)}) copy-start(bf16[2560,640]{1,0:T(8,128)(2,1)} %param.8) | copy-start | bytes 9830404
  2.1 3.2 %collective-permute-start = (bf16[128,2560]{1,0:T(8,128)(2,1)}, bf16[128,2560]{1,0:T(8,128)(2,1)}, u32[]{:S(2)}, u32[]{:S(2)}) collective-permute-start(bf16[128,2560]{1,0:T(8,128)(2,1)} %dynamic-slice_bitcast_fusion), channel_id=1, source_target_pairs={{0,4},{4,0},{1,5},{5,1},{2,6},{6,2},{3,7},{7,3},{8,12},{12,8},{9,1... | collective-permute-start | bytes 1966088 | tf_op jit(solution)/shard_map/ppermute | solution.py:12
  2.1 59.9 %collective-permute-start.11 = (bf16[640,2560]{1,0:T(8,128)(2,1)}, bf16[640,2560]{1,0:T(8,128)(2,1)}, u32[]{:S(2)}, u32[]{:S(2)}) collective-permute-start(bf16[640,2560]{1,0:T(8,128)(2,1)} %param.9), channel_id=1, source_target_pairs={{0,4},{4,0},{1,5},{5,1},{2,6},{6,2},{3,7},{7,3},{8,12},{12,8},{9,1... | collective-permute-start | bytes 9830408 | tf_op jit(solution)/shard_map/ppermute | solution.py:12
  2.6 5.3 %copy-start.1 = (bf16[2560,640]{1,0:T(8,128)(2,1)S(1)}, bf16[2560,640]{1,0:T(8,128)(2,1)}, u32[]{:S(2)}) copy-start(bf16[2560,640]{1,0:T(8,128)(2,1)} %param.7) | copy-start | bytes 9830404
  5.3 5.7 %copy-start.3 = (bf16[1,128,5120]{2,1,0:T(8,128)(2,1)S(1)}, bf16[1,128,5120]{2,1,0:T(8,128)(2,1)}, u32[]{:S(2)}) copy-start(bf16[1,128,5120]{2,1,0:T(8,128)(2,1)} %param.5) | copy-start | bytes 3932164
  7.9 4.5 %collective-permute-start.1 = (f32[128,640]{1,0:T(8,128)}, f32[128,640]{1,0:T(8,128)}, u32[]{:S(2)}, u32[]{:S(2)}) collective-permute-start(f32[128,640]{1,0:T(8,128)} %fusion.56), channel_id=1, source_target_pairs={{0,4},{4,0},{1,5},{5,1},{2,6},{6,2},{3,7},{7,3},{8,12},{12,8},{9,1... | collective-permute-start | bytes 983048 | tf_op jit(solution)/shard_map/ppermute | solution.py:12
  10.4 4.8 %collective-permute-start.3 = (f32[128,640]{1,0:T(8,128)}, f32[128,640]{1,0:T(8,128)}, u32[]{:S(2)}, u32[]{:S(2)}) collective-permute-start(f32[128,640]{1,0:T(8,128)} %fusion.58), channel_id=1, source_target_pairs={{0,4},{4,0},{1,5},{5,1},{2,6},{6,2},{3,7},{7,3},{8,12},{12,8},{9,1... | collective-permute-start | bytes 983048 | tf_op jit(solution)/shard_map/ppermute | solution.py:12
  18.7 18.2 %copy-start.2 = (bf16[2560,640]{1,0:T(8,128)(2,1)S(1)}, bf16[2560,640]{1,0:T(8,128)(2,1)}, u32[]{:S(2)}) copy-start(bf16[2560,640]{1,0:T(8,128)(2,1)} %param.6) | copy-start | bytes 9830404
  20.1 7.6 %collective-permute-start.4 = (bf16[5,128,128]{2,1,0:T(8,128)(2,1)S(1)}, bf16[5,128,128]{2,1,0:T(8,128)(2,1)S(1)}, u32[]{:S(2)}, u32[]{:S(2)}) collective-permute-start(bf16[5,128,128]{2,1,0:T(8,128)(2,1)S(1)} %get-tuple-element.27), channel_id=1, source_target_pairs={{0,8},{8,16},{16,24},{24,0},{32,40},{40,48},{48,56},{56,32},{64,72... | collective-permute-start | bytes 491528 | tf_op jit(solution)/shard_map/ppermute | solution.py:16
  21.6 8.6 %collective-permute-start.5 = (bf16[5,128,128]{2,1,0:T(8,128)(2,1)S(1)}, bf16[5,128,128]{2,1,0:T(8,128)(2,1)S(1)}, u32[]{:S(2)}, u32[]{:S(2)}) collective-permute-start(bf16[5,128,128]{2,1,0:T(8,128)(2,1)S(1)} %get-tuple-element.27), channel_id=1, source_target_pairs={{0,16},{8,24},{16,0},{24,8},{32,48},{40,56},{48,32},{56,40},{64,80... | collective-permute-start | bytes 491528 | tf_op jit(solution)/shard_map/ppermute | solution.py:16
  22.7 9.1 %collective-permute-start.6 = (bf16[5,128,128]{2,1,0:T(8,128)(2,1)S(1)}, bf16[5,128,128]{2,1,0:T(8,128)(2,1)S(1)}, u32[]{:S(2)}, u32[]{:S(2)}) collective-permute-start(bf16[5,128,128]{2,1,0:T(8,128)(2,1)S(1)} %get-tuple-element.27), channel_id=1, source_target_pairs={{0,24},{8,0},{16,8},{24,16},{32,56},{40,32},{48,40},{56,48},{64,88... | collective-permute-start | bytes 491528 | tf_op jit(solution)/shard_map/ppermute | solution.py:16
  27.7 16.9 %copy-start.4 = (bf16[5,128,128]{2,1,0:T(8,128)(2,1)}, bf16[5,128,128]{2,1,0:T(8,128)(2,1)S(1)}, u32[]{:S(2)}) copy-start(bf16[5,128,128]{2,1,0:T(8,128)(2,1)S(1)} %collective-permute-done.4) | copy-start | bytes 491524
  30.2 14.4 %copy-start.5 = (bf16[5,128,128]{2,1,0:T(8,128)(2,1)}, bf16[5,128,128]{2,1,0:T(8,128)(2,1)S(1)}, u32[]{:S(2)}) copy-start(bf16[5,128,128]{2,1,0:T(8,128)(2,1)S(1)} %collective-permute-done.5) | copy-start | bytes 491524
  31.8 12.8 %copy-start.6 = (bf16[5,128,128]{2,1,0:T(8,128)(2,1)}, bf16[5,128,128]{2,1,0:T(8,128)(2,1)S(1)}, u32[]{:S(2)}) copy-start(bf16[5,128,128]{2,1,0:T(8,128)(2,1)S(1)} %collective-permute-done.6) | copy-start | bytes 491524
  31.9 6.9 %collective-permute-start.7 = (bf16[5,128,128]{2,1,0:T(8,128)(2,1)S(1)}, bf16[5,128,128]{2,1,0:T(8,128)(2,1)S(1)}, u32[]{:S(2)}, u32[]{:S(2)}) collective-permute-start(bf16[5,128,128]{2,1,0:T(8,128)(2,1)S(1)} %fusion.48), channel_id=1, source_target_pairs={{0,32},{8,40},{16,48},{24,56},{32,64},{40,72},{48,80},{56,88},{64,... | collective-permute-start | bytes 491528 | tf_op jit(solution)/shard_map/ppermute | solution.py:16
  33.6 8.4 %collective-permute-start.8 = (bf16[5,128,128]{2,1,0:T(8,128)(2,1)S(1)}, bf16[5,128,128]{2,1,0:T(8,128)(2,1)S(1)}, u32[]{:S(2)}, u32[]{:S(2)}) collective-permute-start(bf16[5,128,128]{2,1,0:T(8,128)(2,1)S(1)} %fusion.48), channel_id=1, source_target_pairs={{0,64},{8,72},{16,80},{24,88},{32,96},{40,104},{48,112},{56,120},{... | collective-permute-start | bytes 491528 | tf_op jit(solution)/shard_map/ppermute | solution.py:16
  35.1 8.6 %collective-permute-start.9 = (bf16[5,128,128]{2,1,0:T(8,128)(2,1)S(1)}, bf16[5,128,128]{2,1,0:T(8,128)(2,1)S(1)}, u32[]{:S(2)}, u32[]{:S(2)}) collective-permute-start(bf16[5,128,128]{2,1,0:T(8,128)(2,1)S(1)} %fusion.48), channel_id=1, source_target_pairs={{0,96},{8,104},{16,112},{24,120},{32,0},{40,8},{48,16},{56,24},{64... | collective-permute-start | bytes 491528 | tf_op jit(solution)/shard_map/ppermute | solution.py:16
  38.7 14.9 %collective-permute-start.2 = (f32[128,640]{1,0:T(8,128)S(1)}, f32[128,640]{1,0:T(8,128)S(1)}, u32[]{:S(2)}, u32[]{:S(2)}) collective-permute-start(f32[128,640]{1,0:T(8,128)S(1)} %fusion.57), channel_id=1, source_target_pairs={{0,4},{4,0},{1,5},{5,1},{2,6},{6,2},{3,7},{7,3},{8,12},{12,8},{9,1... | collective-permute-start | bytes 983048 | tf_op jit(solution)/shard_map/ppermute | solution.py:12
  38.8 14.8 %copy-start.7 = (bf16[5,128,128]{2,1,0:T(8,128)(2,1)}, bf16[5,128,128]{2,1,0:T(8,128)(2,1)S(1)}, u32[]{:S(2)}) copy-start(bf16[5,128,128]{2,1,0:T(8,128)(2,1)S(1)} %collective-permute-done.7) | copy-start | bytes 491524
  42.0 11.6 %copy-start.8 = (bf16[5,128,128]{2,1,0:T(8,128)(2,1)}, bf16[5,128,128]{2,1,0:T(8,128)(2,1)S(1)}, u32[]{:S(2)}) copy-start(bf16[5,128,128]{2,1,0:T(8,128)(2,1)S(1)} %collective-permute-done.8) | copy-start | bytes 491524
  43.8 9.9 %copy-start.9 = (bf16[5,128,128]{2,1,0:T(8,128)(2,1)}, bf16[5,128,128]{2,1,0:T(8,128)(2,1)S(1)}, u32[]{:S(2)}) copy-start(bf16[5,128,128]{2,1,0:T(8,128)(2,1)S(1)} %collective-permute-done.9) | copy-start | bytes 491524
  44.6 11.6 %collective-permute-start.10 = (bf16[5,128,128]{2,1,0:T(8,128)(2,1)}, bf16[5,128,128]{2,1,0:T(8,128)(2,1)}, u32[]{:S(2)}, u32[]{:S(2)}) collective-permute-start(bf16[5,128,128]{2,1,0:T(8,128)(2,1)} %fusion.36), channel_id=1, source_target_pairs={{0,128},{8,136},{16,144},{24,152},{32,160},{40,168},{48,176},{56,1... | collective-permute-start | bytes 491528 | tf_op jit(solution)/shard_map/ppermute | solution.py:16
  67.7 12.7 %collective-permute-start.12 = (bf16[128,1280]{1,0:T(8,128)(2,1)S(1)}, bf16[128,1280]{1,0:T(8,128)(2,1)S(1)}, u32[]{:S(2)}, u32[]{:S(2)}) collective-permute-start(bf16[128,1280]{1,0:T(8,128)(2,1)S(1)} %get-tuple-element.11), channel_id=1, source_target_pairs={{0,1},{4,5},{8,9},{12,13},{16,17},{20,21},{24,25},{28,29},{32,33},... | collective-permute-start | bytes 983048 | tf_op jit(solution)/shard_map/ppermute | solution.py:112
  74.2 6.2 %collective-permute-start.13 = (bf16[128,1280]{1,0:T(8,128)(2,1)S(1)}, bf16[128,1280]{1,0:T(8,128)(2,1)S(1)}, u32[]{:S(2)}, u32[]{:S(2)}) collective-permute-start(bf16[128,1280]{1,0:T(8,128)(2,1)S(1)} %get-tuple-element.12), channel_id=1, source_target_pairs={{3,2},{7,6},{11,10},{15,14},{19,18},{23,22},{27,26},{31,30},{35,34... | collective-permute-start | bytes 983048 | tf_op jit(solution)/shard_map/ppermute | solution.py:113
  80.5 9.8 %collective-permute-start.14 = (bf16[128,1280]{1,0:T(8,128)(2,1)S(1)}, bf16[128,1280]{1,0:T(8,128)(2,1)S(1)}, u32[]{:S(2)}, u32[]{:S(2)}) collective-permute-start(bf16[128,1280]{1,0:T(8,128)(2,1)S(1)} %get-tuple-element.13), channel_id=1, source_target_pairs={{0,1},{1,2},{4,5},{5,6},{8,9},{9,10},{12,13},{13,14},{16,17},{17,1... | collective-permute-start | bytes 983048 | tf_op jit(solution)/shard_map/ppermute | solution.py:112
  84.9 5.3 %collective-permute-start.15 = (bf16[128,1280]{1,0:T(8,128)(2,1)S(1)}, bf16[128,1280]{1,0:T(8,128)(2,1)S(1)}, u32[]{:S(2)}, u32[]{:S(2)}) collective-permute-start(bf16[128,1280]{1,0:T(8,128)(2,1)S(1)} %get-tuple-element.14), channel_id=1, source_target_pairs={{2,1},{3,2},{6,5},{7,6},{10,9},{11,10},{14,13},{15,14},{18,17},{19... | collective-permute-start | bytes 983048 | tf_op jit(solution)/shard_map/ppermute | solution.py:113
  90.5 12.3 %collective-permute-start.16 = (bf16[128,1280]{1,0:T(8,128)(2,1)S(1)}, bf16[128,1280]{1,0:T(8,128)(2,1)S(1)}, u32[]{:S(2)}, u32[]{:S(2)}) collective-permute-start(bf16[128,1280]{1,0:T(8,128)(2,1)S(1)} %get-tuple-element.15), channel_id=1, source_target_pairs={{0,1},{1,2},{2,3},{4,5},{5,6},{6,7},{8,9},{9,10},{10,11},{12,13},{... | collective-permute-start | bytes 983048 | tf_op jit(solution)/shard_map/ppermute | solution.py:112
  98.2 9.0 %collective-permute-start.17 = (bf16[128,1280]{1,0:T(8,128)(2,1)S(1)}, bf16[128,1280]{1,0:T(8,128)(2,1)S(1)}, u32[]{:S(2)}, u32[]{:S(2)}) collective-permute-start(bf16[128,1280]{1,0:T(8,128)(2,1)S(1)} %get-tuple-element.16), channel_id=1, source_target_pairs={{1,0},{2,1},{3,2},{5,4},{6,5},{7,6},{9,8},{10,9},{11,10},{13,12},{... | collective-permute-start | bytes 983048 | tf_op jit(solution)/shard_map/ppermute | solution.py:113

commit v8 on v7

--- a/solution.py
+++ b/solution.py
@@ -56,8 +56,7 @@
     c = lax.axis_index("wt")
 
     mine_cols = lax.dynamic_slice_in_dim(rows_in, c * half, half, axis=1)
-    their_cols = lax.dynamic_slice_in_dim(rows_in, (1 - c) * half, half, axis=1)
-    got_cols = swap_cores(their_cols)
+    got_cols = lax.dynamic_slice_in_dim(swap_cores(rows_in), c * half, half, axis=1)
     sums = []
     for w in (w_query, w_key, w_value):
         lent = swap_cores(jnp.dot(got_cols, w, preferred_element_type=F32))

time: 109 us -> 108 us (level)
    dynamic_slice x1 -> x0, local copies, waits for them, and re-layouts: 2.13 us -> none  [shards(): their_cols = lax.dynamic_slice_in_dim(rows_in, (1 - c) * half, half, axis=1)]
    unnamed x20, local copies, waits for them, and re-layouts: 0.04 us -> 1.45 us
  transfers between devices with their start and end apart: 18 -> 18, of which waited for: 9 -> 9; matrix products, arithmetic and copies ran while one was open for 28% -> 29% of each run, Pallas kernels for 0% -> 0%
where the time goes in v8:
time: 108 us; the launch traced here: 107 us
  starting transfers between devices  41.3 us (38%)
  waiting for transfers between devices  26.9 us (25%)
  matrix products  21.1 us (20%)
  other arithmetic  11.8 us (11%)
  local copies, waits for them, and re-layouts  6 us (6%)
    ppermute x7, starting transfers between devices, shifted(): return lax.ppermute(x, axis, pairs)  18.9 us
    ppermute x3, starting transfers between devices, shards(): right = lax.ppermute(send_r, 'head', rpairs).astype(F32)  18.7 us
    ppermute x3, waiting for transfers between devices, shards(): right = lax.ppermute(send_r, 'head', rpairs).astype(F32)  13.4 us
    ppermute x7, waiting for transfers between devices, shifted(): return lax.ppermute(x, axis, pairs)  9.08 us
    dot_general x3, matrix products, shards(): own = jnp.dot(mine_cols, w, preferred_element_type=F32)  6.88 us
    dot_general x3, matrix products, shards(): lent = swap_cores(jnp.dot(got_cols, w, preferred_element_type=F32))  6.86 us
    ppermute x3, waiting for transfers between devices, shards(): left = lax.ppermute(send_l, 'head', lpairs).astype(F32)  4.42 us
    squeeze x1, other arithmetic, shards(): pieces.append(piece[0])  4.33 us
  transfers between devices with their start and end apart: 18, of which 9 were waited for; matrix products, arithmetic and copies ran while one was open for 29% of the time, Pallas kernels for 0%

profile of v8, /device:TPU:10, one launch (start us, length us, event | category | flops | bytes accessed | tf_op | source)
XLA Modules:
  0.0 107.3 jit_solution(12628222347587571185)
XLA Ops:
  0.0 0.0 copy-start
  0.0 0.0 collective-permute-start
  0.0 0.5 collective-permute-start.11
  0.5 1.4 %copy-done = bf16[2560,640]{1,0:T(8,128)(2,1)S(1)} copy-done((bf16[2560,640]{1,0:T(8,128)(2,1)S(1)}, bf16[2560,640]{1,0:T(8,128)(2,1)}, u32[]{:S(2)}) %copy-start) | copy-done | bytes 3276824
  1.9 2.7 %fusion.24 = f32[128,640]{1,0:T(8,128)} fusion(bf16[2560,640]{1,0:T(8,128)(2,1)S(1)} %copy-done, bf16[1,128,5120]{2,1,0:T(8,128)(2,1)} %param.5, s32[]{:T(128)S(6)} %select_n.154), kind=kOutput, calls=%fused_computation.35 | convolution fusion | flops 419430400 | bytes 4259844 | tf_op jit(solution)/shard_map/dot_general | solution.py:63
  4.6 0.0 collective-permute-done
  4.6 2.6 %fusion.30 = f32[128,640]{1,0:T(8,128)} fusion(bf16[2560,640]{1,0:T(8,128)(2,1)S(1)} %copy-done, bf16[128,5120]{1,0:T(8,128)(2,1)} %collective-permute-done, s32[]{:T(128)S(6)} %select_n.154), kind=kOutput, calls=%fused_computation.47 | convolution fusion | flops 419430400 | bytes 4259844 | tf_op jit(solution)/shard_map/dot_general | solution.py:62
  7.2 0.0 collective-permute-start.1
  7.2 0.0 copy-done.1
  7.2 2.5 %fusion.26 = f32[128,640]{1,0:T(8,128)} fusion(bf16[2560,640]{1,0:T(8,128)(2,1)S(1)} %copy-done.1, bf16[128,5120]{1,0:T(8,128)(2,1)} %collective-permute-done, s32[]{:T(128)S(6)} %select_n.154), kind=kOutput, calls=%fused_computation.43 | convolution fusion | flops 419430400 | bytes 4259844 | tf_op jit(solution)/shard_map/dot_general | solution.py:62
  9.7 0.5 collective-permute-start.3
  10.2 1.4 %fusion.20 = f32[128,640]{1,0:T(8,128)} fusion(bf16[2560,640]{1,0:T(8,128)(2,1)S(1)} %copy-done.1, bf16[1,128,5120]{2,1,0:T(8,128)(2,1)S(1)} %copy-done.3, s32[]{:T(128)S(6)} %select_n.154), kind=kOutput, calls=%fused_computation.31 | convolution fusion | flops 419430400 | bytes 4259844 | tf_op jit(solution)/shard_map/dot_general | solution.py:63
  11.6 0.0 collective-permute-done.1
  11.6 1.8 %add_convert_fusion.4 = bf16[128,640]{1,0:T(8,128)(2,1)} fusion(f32[128,640]{1,0:T(8,128)} %fusion.24, f32[128,640]{1,0:T(8,128)} %collective-permute-done.1), kind=kLoop, calls=%fused_computation.77 | loop fusion | flops 163840 | bytes 819200 | tf_op jit(solution)/shard_map/convert_element_type | solution.py:69
  13.4 1.1 copy.11
  14.5 0.0 collective-permute-done.3
  14.5 1.8 %multiply_convert_fusion.1 = bf16[128,640]{1,0:T(8,128)(2,1)} fusion(f32[128,640]{1,0:T(8,128)} %fusion.20, f32[128,640]{1,0:T(8,128)} %collective-permute-done.3), kind=kLoop, calls=%fused_computation.75 | loop fusion | flops 491520 | bytes 819200 | tf_op jit(solution)/shard_map/convert_element_type | solution.py:68
  16.3 1.7 %copy.13 = bf16[128,640]{0,1:T(8,128)(2,1)} copy(bf16[128,640]{1,0:T(8,128)(2,1)} %multiply_convert_fusion.1) | data formatting | bytes 327680 | tf_op jit(solution)/shard_map/convert_element_type | solution.py:68
  18.0 1.3 %fusion.64 = (bf16[5,128,128]{2,1,0:T(8,128)(2,1)S(1)}, f32[5,128,128]{2,1,0:T(8,128)S(1)}) fusion(bf16[128,5,128]{0,2,1:T(8,128)(2,1)} %bitcast.43, bf16[128,5,128]{0,2,1:T(8,128)(2,1)S(1)} %bitcast.41), kind=kOutput, calls=%fused_computation.99 | convolution fusion | flops 21053440 | bytes 819200 | tf_op jit(solution)/shard_map/thd,the->hde/dot_general | solution.py:70
  19.3 1.6 %collective-permute-start.4 = (bf16[5,128,128]{2,1,0:T(8,128)(2,1)S(1)}, bf16[5,128,128]{2,1,0:T(8,128)(2,1)S(1)}, u32[]{:S(2)}, u32[]{:S(2)}) collective-permute-start(bf16[5,128,128]{2,1,0:T(8,128)(2,1)S(1)} %get-tuple-element.27), channel_id=1, source_target_pairs={{0,8},{8,16},{16,24},{24,0},{32,40},{40,48},{48,56},{56,32},{64,72... | collective-permute-start | bytes 491528 | tf_op jit(solution)/shard_map/ppermute | solution.py:16
  20.9 1.1 %collective-permute-start.5 = (bf16[5,128,128]{2,1,0:T(8,128)(2,1)S(1)}, bf16[5,128,128]{2,1,0:T(8,128)(2,1)S(1)}, u32[]{:S(2)}, u32[]{:S(2)}) collective-permute-start(bf16[5,128,128]{2,1,0:T(8,128)(2,1)S(1)} %get-tuple-element.27), channel_id=1, source_target_pairs={{0,16},{8,24},{16,0},{24,8},{32,48},{40,56},{48,32},{56,40},{64,80... | collective-permute-start | bytes 491528 | tf_op jit(solution)/shard_map/ppermute | solution.py:16
  22.0 2.2 %collective-permute-start.6 = (bf16[5,128,128]{2,1,0:T(8,128)(2,1)S(1)}, bf16[5,128,128]{2,1,0:T(8,128)(2,1)S(1)}, u32[]{:S(2)}, u32[]{:S(2)}) collective-permute-start(bf16[5,128,128]{2,1,0:T(8,128)(2,1)S(1)} %get-tuple-element.27), channel_id=1, source_target_pairs={{0,24},{8,0},{16,8},{24,16},{32,56},{40,32},{48,40},{56,48},{64,88... | collective-permute-start | bytes 491528 | tf_op jit(solution)/shard_map/ppermute | solution.py:16
  24.2 2.8 %fusion.22 = f32[128,640]{1,0:T(8,128)S(1)} fusion(bf16[2560,640]{1,0:T(8,128)(2,1)} %param.6, bf16[1,128,5120]{2,1,0:T(8,128)(2,1)} %param.5, s32[]{:T(128)S(6)} %select_n.154), kind=kOutput, calls=%fused_computation.33 | convolution fusion | flops 419430400 | bytes 4259844 | tf_op jit(solution)/shard_map/dot_general | solution.py:63
  27.0 0.0 collective-permute-done.4
  27.0 2.5 %collective-permute-done.5 = bf16[5,128,128]{2,1,0:T(8,128)(2,1)S(1)} collective-permute-done((bf16[5,128,128]{2,1,0:T(8,128)(2,1)S(1)}, bf16[5,128,128]{2,1,0:T(8,128)(2,1)S(1)}, u32[]{:S(2)}, u32[]{:S(2)}) %collective-permute-start.5) | collective-permute-done | bytes 163872 | tf_op jit(solution)/shard_map/ppermute | solution.py:16
  29.5 1.6 %collective-permute-done.6 = bf16[5,128,128]{2,1,0:T(8,128)(2,1)S(1)} collective-permute-done((bf16[5,128,128]{2,1,0:T(8,128)(2,1)S(1)}, bf16[5,128,128]{2,1,0:T(8,128)(2,1)S(1)}, u32[]{:S(2)}, u32[]{:S(2)}) %collective-permute-start.6) | collective-permute-done | bytes 163872 | tf_op jit(solution)/shard_map/ppermute | solution.py:16
  31.1 0.1 fusion.54
  31.2 1.7 %collective-permute-start.7 = (bf16[5,128,128]{2,1,0:T(8,128)(2,1)S(1)}, bf16[5,128,128]{2,1,0:T(8,128)(2,1)S(1)}, u32[]{:S(2)}, u32[]{:S(2)}) collective-permute-start(bf16[5,128,128]{2,1,0:T(8,128)(2,1)S(1)} %fusion.54), channel_id=1, source_target_pairs={{0,32},{8,40},{16,48},{24,56},{32,64},{40,72},{48,80},{56,88},{64,... | collective-permute-start | bytes 491528 | tf_op jit(solution)/shard_map/ppermute | solution.py:16
  32.8 1.6 %collective-permute-start.8 = (bf16[5,128,128]{2,1,0:T(8,128)(2,1)S(1)}, bf16[5,128,128]{2,1,0:T(8,128)(2,1)S(1)}, u32[]{:S(2)}, u32[]{:S(2)}) collective-permute-start(bf16[5,128,128]{2,1,0:T(8,128)(2,1)S(1)} %fusion.54), channel_id=1, source_target_pairs={{0,64},{8,72},{16,80},{24,88},{32,96},{40,104},{48,112},{56,120},{... | collective-permute-start | bytes 491528 | tf_op jit(solution)/shard_map/ppermute | solution.py:16
  34.4 1.7 %collective-permute-start.9 = (bf16[5,128,128]{2,1,0:T(8,128)(2,1)S(1)}, bf16[5,128,128]{2,1,0:T(8,128)(2,1)S(1)}, u32[]{:S(2)}, u32[]{:S(2)}) collective-permute-start(bf16[5,128,128]{2,1,0:T(8,128)(2,1)S(1)} %fusion.54), channel_id=1, source_target_pairs={{0,96},{8,104},{16,112},{24,120},{32,0},{40,8},{48,16},{56,24},{64... | collective-permute-start | bytes 491528 | tf_op jit(solution)/shard_map/ppermute | solution.py:16
  36.2 1.8 %fusion.28 = f32[128,640]{1,0:T(8,128)S(1)} fusion(bf16[2560,640]{1,0:T(8,128)(2,1)S(1)} %copy-done.2, bf16[128,5120]{1,0:T(8,128)(2,1)} %collective-permute-done, s32[]{:T(128)S(6)} %select_n.154), kind=kOutput, calls=%fused_computation.45 | convolution fusion | flops 419430400 | bytes 4259844 | tf_op jit(solution)/shard_map/dot_general | solution.py:62
  38.0 0.1 collective-permute-start.2
  38.1 0.0 collective-permute-done.7
  38.1 3.2 %collective-permute-done.8 = bf16[5,128,128]{2,1,0:T(8,128)(2,1)S(1)} collective-permute-done((bf16[5,128,128]{2,1,0:T(8,128)(2,1)S(1)}, bf16[5,128,128]{2,1,0:T(8,128)(2,1)S(1)}, u32[]{:S(2)}, u32[]{:S(2)}) %collective-permute-start.8) | collective-permute-done | bytes 163872 | tf_op jit(solution)/shard_map/ppermute | solution.py:16
  41.2 1.8 %collective-permute-done.9 = bf16[5,128,128]{2,1,0:T(8,128)(2,1)S(1)} collective-permute-done((bf16[5,128,128]{2,1,0:T(8,128)(2,1)S(1)}, bf16[5,128,128]{2,1,0:T(8,128)(2,1)S(1)}, u32[]{:S(2)}, u32[]{:S(2)}) %collective-permute-start.9) | collective-permute-done | bytes 163872 | tf_op jit(solution)/shard_map/ppermute | solution.py:16
  43.0 0.8 fusion.42
  43.8 9.1 %collective-permute-start.10 = (bf16[5,128,128]{2,1,0:T(8,128)(2,1)}, bf16[5,128,128]{2,1,0:T(8,128)(2,1)}, u32[]{:S(2)}, u32[]{:S(2)}) collective-permute-start(bf16[5,128,128]{2,1,0:T(8,128)(2,1)} %fusion.42), channel_id=1, source_target_pairs={{0,128},{8,136},{16,144},{24,152},{32,160},{40,168},{48,176},{56,1... | collective-permute-start | bytes 491528 | tf_op jit(solution)/shard_map/ppermute | solution.py:16
  52.9 0.0 collective-permute-done.2
  52.9 0.0 copy-done.7
  52.9 0.8 multiply_convert_fusion.2
  53.7 1.7 %copy.12 = bf16[128,640]{0,1:T(8,128)(2,1)} copy(bf16[128,640]{1,0:T(8,128)(2,1)} %multiply_convert_fusion.2) | data formatting | bytes 327680 | tf_op jit(solution)/shard_map/convert_element_type | solution.py:67
  55.4 0.1 collective-permute-done.10
  55.5 2.5 %fusion.45 = f32[5,128,128]{2,1,0:T(8,128)} fusion(bf16[128,5,128]{0,2,1:T(8,128)(2,1)} %bitcast.45, bf16[5,128,128]{2,1,0:T(8,128)(2,1)} %copy-done.4, bf16[5,128,128]{2,1,0:T(8,128)(2,1)} %copy-done.5, bf16[5,128,128]{2,1,0:T(8,128)(2,1)} %copy-done.6, bf16[5,128,128]{2,1,0:T(8,128)(2,1)} %copy-done.7, bf16[5,128,128]{2,1,0:T(8,128)(2,1)} %copy-done.8, ...), kind=kOutput, calls=%fused_computation.79 | convolution fusion | flops 22609920 | bytes 1638406 | tf_op jit(solution)/shard_map/thd,hde->the/dot_general | solution.py:78
  58.0 2.3 %multiply_reduce_fusion = (f32[128,5]{0,1:T(8,128)S(1)}, f32[128,5,128]{0,2,1:T(8,128)}) fusion(f32[5,128,128]{2,1,0:T(8,128)} %fusion.45, bf16[128,5,128]{0,2,1:T(8,128)(2,1)S(1)} %bitcast.42, bf16[128,5,128]{0,2,1:T(8,128)(2,1)} %bitcast.46, bf16[128,5,128]{0,2,1:T(8,128)(2,1)} %bitcast.44, f32[128,128]{1,0:T(8,128)S(1)} %fusion.53), kind=kOutput, calls=%fused_computation.74 | convolution fusion | flops 42352000 | bytes 1214976 | tf_op jit(solution)/shard_map/hts,shd->thd/dot_general | solution.py:77
  60.3 1.0 multiply_convert_fusion
  61.3 0.0 collective-permute-done.11
  61.3 4.3 %fusion.11 = (bf16[640,1280]{1,0:T(8,128)(2,1)S(1)}, bf16[640,1280]{1,0:T(8,128)(2,1)S(1)}, bf16[640,1280]{1,0:T(8,128)(2,1)S(1)}, bf16[640,1280]{1,0:T(8,128)(2,1)S(1)}) fusion(s32[]{:T(128)S(6)} %select_n.178, s32[]{:T(128)S(6)} %select_n.180, bf16[1,640,2560]{2,1,0:T(8,128)(2,1)} %bitcast.39, bf16[1,640,2560]{2,1,0:T(8,128)(2,1)} %bitcast.8, ...), kind=kLoop, calls=%fused_computation.19 | loop fusion | flops 13107200 | bytes 13107232 | tf_op jit(solution)/shard_map/squeeze | solution.py:96
  65.7 1.2 %fusion = f32[128,5120]{1,0:T(8,128)S(1)} fusion(bf16[128,640]{0,1:T(8,128)(2,1)S(1)} %bitcast.47, bf16[640,1280]{1,0:T(8,128)(2,1)S(1)} %get-tuple-element.20, bf16[640,1280]{1,0:T(8,128)(2,1)S(1)} %get-tuple-element.19, bf16[640,1280]{1,0:T(8,128)(2,1)S(1)} %get-tuple-element.18, bf16[640,1280]{1,0:T(8,128)(2,1)S(1)} %get-tuple-element.17), kind=kOutput, calls=%fused_computation.8 | convolution fusion | flops 865075200 | bytes 9338880 | tf_op jit(solution)/shard_map/dot_general | solution.py:98
  66.9 0.1 fusion.63
  67.0 6.5 %collective-permute-start.12 = (bf16[128,1280]{1,0:T(8,128)(2,1)S(1)}, bf16[128,1280]{1,0:T(8,128)(2,1)S(1)}, u32[]{:S(2)}, u32[]{:S(2)}) collective-permute-start(bf16[128,1280]{1,0:T(8,128)(2,1)S(1)} %get-tuple-element.11), channel_id=1, source_target_pairs={{0,1},{4,5},{8,9},{12,13},{16,17},{20,21},{24,25},{28,29},{32,33},... | collective-permute-start | bytes 983048 | tf_op jit(solution)/shard_map/ppermute | solution.py:111
  73.4 0.7 collective-permute-start.13
  74.1 5.5 %collective-permute-done.12 = bf16[128,1280]{1,0:T(8,128)(2,1)S(1)} collective-permute-done((bf16[128,1280]{1,0:T(8,128)(2,1)S(1)}, bf16[128,1280]{1,0:T(8,128)(2,1)S(1)}, u32[]{:S(2)}, u32[]{:S(2)}) %collective-permute-start.12) | collective-permute-done | bytes 327712 | tf_op jit(solution)/shard_map/ppermute | solution.py:111
  79.7 0.0 collective-permute-done.13
  79.7 0.1 add_convert_fusion.2
  79.8 4.4 %collective-permute-start.14 = (bf16[128,1280]{1,0:T(8,128)(2,1)S(1)}, bf16[128,1280]{1,0:T(8,128)(2,1)S(1)}, u32[]{:S(2)}, u32[]{:S(2)}) collective-permute-start(bf16[128,1280]{1,0:T(8,128)(2,1)S(1)} %get-tuple-element.13), channel_id=1, source_target_pairs={{0,1},{1,2},{4,5},{5,6},{8,9},{9,10},{12,13},{13,14},{16,17},{17,1... | collective-permute-start | bytes 983048 | tf_op jit(solution)/shard_map/ppermute | solution.py:111
  84.2 0.7 collective-permute-start.15
  84.9 4.7 %collective-permute-done.14 = bf16[128,1280]{1,0:T(8,128)(2,1)S(1)} collective-permute-done((bf16[128,1280]{1,0:T(8,128)(2,1)S(1)}, bf16[128,1280]{1,0:T(8,128)(2,1)S(1)}, u32[]{:S(2)}, u32[]{:S(2)}) %collective-permute-start.14) | collective-permute-done | bytes 327712 | tf_op jit(solution)/shard_map/ppermute | solution.py:111
  89.6 0.0 collective-permute-done.15
  89.6 0.2 add_convert_fusion
  89.7 7.8 %collective-permute-start.16 = (bf16[128,1280]{1,0:T(8,128)(2,1)S(1)}, bf16[128,1280]{1,0:T(8,128)(2,1)S(1)}, u32[]{:S(2)}, u32[]{:S(2)}) collective-permute-start(bf16[128,1280]{1,0:T(8,128)(2,1)S(1)} %get-tuple-element.15), channel_id=1, source_target_pairs={{0,1},{1,2},{2,3},{4,5},{5,6},{6,7},{8,9},{9,10},{10,11},{12,13},{... | collective-permute-start | bytes 983048 | tf_op jit(solution)/shard_map/ppermute | solution.py:111
  97.5 1.3 %collective-permute-start.17 = (bf16[128,1280]{1,0:T(8,128)(2,1)S(1)}, bf16[128,1280]{1,0:T(8,128)(2,1)S(1)}, u32[]{:S(2)}, u32[]{:S(2)}) collective-permute-start(bf16[128,1280]{1,0:T(8,128)(2,1)S(1)} %get-tuple-element.16), channel_id=1, source_target_pairs={{1,0},{2,1},{3,2},{5,4},{6,5},{7,6},{9,8},{10,9},{11,10},{13,12},{... | collective-permute-start | bytes 983048 | tf_op jit(solution)/shard_map/ppermute | solution.py:112
  98.8 3.3 %collective-permute-done.16 = bf16[128,1280]{1,0:T(8,128)(2,1)S(1)} collective-permute-done((bf16[128,1280]{1,0:T(8,128)(2,1)S(1)}, bf16[128,1280]{1,0:T(8,128)(2,1)S(1)}, u32[]{:S(2)}, u32[]{:S(2)}) %collective-permute-start.16) | collective-permute-done | bytes 327712 | tf_op jit(solution)/shard_map/ppermute | solution.py:111
  102.1 4.4 %collective-permute-done.17 = bf16[128,1280]{1,0:T(8,128)(2,1)S(1)} collective-permute-done((bf16[128,1280]{1,0:T(8,128)(2,1)S(1)}, bf16[128,1280]{1,0:T(8,128)(2,1)S(1)}, u32[]{:S(2)}, u32[]{:S(2)}) %collective-permute-start.17) | collective-permute-done | bytes 327712 | tf_op jit(solution)/shard_map/ppermute | solution.py:112
  106.5 0.8 fusion.43
  (18 shorter events, 0.0 us)
Async XLA Ops:
  0.0 1.9 %copy-start = (bf16[2560,640]{1,0:T(8,128)(2,1)S(1)}, bf16[2560,640]{1,0:T(8,128)(2,1)}, u32[]{:S(2)}) copy-start(bf16[2560,640]{1,0:T(8,128)(2,1)} %param.8) | copy-start | bytes 9830404
  0.0 4.6 %collective-permute-start = (bf16[128,5120]{1,0:T(8,128)(2,1)}, bf16[128,5120]{1,0:T(8,128)(2,1)}, u32[]{:S(2)}, u32[]{:S(2)}) collective-permute-start(bf16[128,5120]{1,0:T(8,128)(2,1)} %bitcast.40), channel_id=1, source_target_pairs={{0,4},{4,0},{1,5},{5,1},{2,6},{6,2},{3,7},{7,3},{8,12},{12,8},{9,1... | collective-permute-start | bytes 3932168 | tf_op jit(solution)/shard_map/ppermute | solution.py:12
  0.0 61.3 %collective-permute-start.11 = (bf16[640,2560]{1,0:T(8,128)(2,1)}, bf16[640,2560]{1,0:T(8,128)(2,1)}, u32[]{:S(2)}, u32[]{:S(2)}) collective-permute-start(bf16[640,2560]{1,0:T(8,128)(2,1)} %param.9), channel_id=1, source_target_pairs={{0,4},{4,0},{1,5},{5,1},{2,6},{6,2},{3,7},{7,3},{8,12},{12,8},{9,1... | collective-permute-start | bytes 9830408 | tf_op jit(solution)/shard_map/ppermute | solution.py:12
  1.9 5.3 %copy-start.1 = (bf16[2560,640]{1,0:T(8,128)(2,1)S(1)}, bf16[2560,640]{1,0:T(8,128)(2,1)}, u32[]{:S(2)}) copy-start(bf16[2560,640]{1,0:T(8,128)(2,1)} %param.7) | copy-start | bytes 9830404
  4.6 5.6 %copy-start.3 = (bf16[1,128,5120]{2,1,0:T(8,128)(2,1)S(1)}, bf16[1,128,5120]{2,1,0:T(8,128)(2,1)}, u32[]{:S(2)}) copy-start(bf16[1,128,5120]{2,1,0:T(8,128)(2,1)} %param.5) | copy-start | bytes 3932164
  7.2 4.4 %collective-permute-start.1 = (f32[128,640]{1,0:T(8,128)}, f32[128,640]{1,0:T(8,128)}, u32[]{:S(2)}, u32[]{:S(2)}) collective-permute-start(f32[128,640]{1,0:T(8,128)} %fusion.30), channel_id=1, source_target_pairs={{0,4},{4,0},{1,5},{5,1},{2,6},{6,2},{3,7},{7,3},{8,12},{12,8},{9,1... | collective-permute-start | bytes 983048 | tf_op jit(solution)/shard_map/ppermute | solution.py:12
  9.7 4.8 %collective-permute-start.3 = (f32[128,640]{1,0:T(8,128)}, f32[128,640]{1,0:T(8,128)}, u32[]{:S(2)}, u32[]{:S(2)}) collective-permute-start(f32[128,640]{1,0:T(8,128)} %fusion.26), channel_id=1, source_target_pairs={{0,4},{4,0},{1,5},{5,1},{2,6},{6,2},{3,7},{7,3},{8,12},{12,8},{9,1... | collective-permute-start | bytes 983048 | tf_op jit(solution)/shard_map/ppermute | solution.py:12
  18.0 18.2 %copy-start.2 = (bf16[2560,640]{1,0:T(8,128)(2,1)S(1)}, bf16[2560,640]{1,0:T(8,128)(2,1)}, u32[]{:S(2)}) copy-start(bf16[2560,640]{1,0:T(8,128)(2,1)} %param.6) | copy-start | bytes 9830404
  19.3 7.7 %collective-permute-start.4 = (bf16[5,128,128]{2,1,0:T(8,128)(2,1)S(1)}, bf16[5,128,128]{2,1,0:T(8,128)(2,1)S(1)}, u32[]{:S(2)}, u32[]{:S(2)}) collective-permute-start(bf16[5,128,128]{2,1,0:T(8,128)(2,1)S(1)} %get-tuple-element.27), channel_id=1, source_target_pairs={{0,8},{8,16},{16,24},{24,0},{32,40},{40,48},{48,56},{56,32},{64,72... | collective-permute-start | bytes 491528 | tf_op jit(solution)/shard_map/ppermute | solution.py:16
  20.9 8.6 %collective-permute-start.5 = (bf16[5,128,128]{2,1,0:T(8,128)(2,1)S(1)}, bf16[5,128,128]{2,1,0:T(8,128)(2,1)S(1)}, u32[]{:S(2)}, u32[]{:S(2)}) collective-permute-start(bf16[5,128,128]{2,1,0:T(8,128)(2,1)S(1)} %get-tuple-element.27), channel_id=1, source_target_pairs={{0,16},{8,24},{16,0},{24,8},{32,48},{40,56},{48,32},{56,40},{64,80... | collective-permute-start | bytes 491528 | tf_op jit(solution)/shard_map/ppermute | solution.py:16
  22.0 9.1 %collective-permute-start.6 = (bf16[5,128,128]{2,1,0:T(8,128)(2,1)S(1)}, bf16[5,128,128]{2,1,0:T(8,128)(2,1)S(1)}, u32[]{:S(2)}, u32[]{:S(2)}) collective-permute-start(bf16[5,128,128]{2,1,0:T(8,128)(2,1)S(1)} %get-tuple-element.27), channel_id=1, source_target_pairs={{0,24},{8,0},{16,8},{24,16},{32,56},{40,32},{48,40},{56,48},{64,88... | collective-permute-start | bytes 491528 | tf_op jit(solution)/shard_map/ppermute | solution.py:16
  27.0 16.8 %copy-start.4 = (bf16[5,128,128]{2,1,0:T(8,128)(2,1)}, bf16[5,128,128]{2,1,0:T(8,128)(2,1)S(1)}, u32[]{:S(2)}) copy-start(bf16[5,128,128]{2,1,0:T(8,128)(2,1)S(1)} %collective-permute-done.4) | copy-start | bytes 491524
  29.5 14.4 %copy-start.5 = (bf16[5,128,128]{2,1,0:T(8,128)(2,1)}, bf16[5,128,128]{2,1,0:T(8,128)(2,1)S(1)}, u32[]{:S(2)}) copy-start(bf16[5,128,128]{2,1,0:T(8,128)(2,1)S(1)} %collective-permute-done.5) | copy-start | bytes 491524
  31.1 12.8 %copy-start.6 = (bf16[5,128,128]{2,1,0:T(8,128)(2,1)}, bf16[5,128,128]{2,1,0:T(8,128)(2,1)S(1)}, u32[]{:S(2)}) copy-start(bf16[5,128,128]{2,1,0:T(8,128)(2,1)S(1)} %collective-permute-done.6) | copy-start | bytes 491524
  31.2 6.9 %collective-permute-start.7 = (bf16[5,128,128]{2,1,0:T(8,128)(2,1)S(1)}, bf16[5,128,128]{2,1,0:T(8,128)(2,1)S(1)}, u32[]{:S(2)}, u32[]{:S(2)}) collective-permute-start(bf16[5,128,128]{2,1,0:T(8,128)(2,1)S(1)} %fusion.54), channel_id=1, source_target_pairs={{0,32},{8,40},{16,48},{24,56},{32,64},{40,72},{48,80},{56,88},{64,... | collective-permute-start | bytes 491528 | tf_op jit(solution)/shard_map/ppermute | solution.py:16
  32.8 8.4 %collective-permute-start.8 = (bf16[5,128,128]{2,1,0:T(8,128)(2,1)S(1)}, bf16[5,128,128]{2,1,0:T(8,128)(2,1)S(1)}, u32[]{:S(2)}, u32[]{:S(2)}) collective-permute-start(bf16[5,128,128]{2,1,0:T(8,128)(2,1)S(1)} %fusion.54), channel_id=1, source_target_pairs={{0,64},{8,72},{16,80},{24,88},{32,96},{40,104},{48,112},{56,120},{... | collective-permute-start | bytes 491528 | tf_op jit(solution)/shard_map/ppermute | solution.py:16
  34.4 8.6 %collective-permute-start.9 = (bf16[5,128,128]{2,1,0:T(8,128)(2,1)S(1)}, bf16[5,128,128]{2,1,0:T(8,128)(2,1)S(1)}, u32[]{:S(2)}, u32[]{:S(2)}) collective-permute-start(bf16[5,128,128]{2,1,0:T(8,128)(2,1)S(1)} %fusion.54), channel_id=1, source_target_pairs={{0,96},{8,104},{16,112},{24,120},{32,0},{40,8},{48,16},{56,24},{64... | collective-permute-start | bytes 491528 | tf_op jit(solution)/shard_map/ppermute | solution.py:16
  38.0 15.0 %collective-permute-start.2 = (f32[128,640]{1,0:T(8,128)S(1)}, f32[128,640]{1,0:T(8,128)S(1)}, u32[]{:S(2)}, u32[]{:S(2)}) collective-permute-start(f32[128,640]{1,0:T(8,128)S(1)} %fusion.28), channel_id=1, source_target_pairs={{0,4},{4,0},{1,5},{5,1},{2,6},{6,2},{3,7},{7,3},{8,12},{12,8},{9,1... | collective-permute-start | bytes 983048 | tf_op jit(solution)/shard_map/ppermute | solution.py:12
  38.1 14.8 %copy-start.7 = (bf16[5,128,128]{2,1,0:T(8,128)(2,1)}, bf16[5,128,128]{2,1,0:T(8,128)(2,1)S(1)}, u32[]{:S(2)}) copy-start(bf16[5,128,128]{2,1,0:T(8,128)(2,1)S(1)} %collective-permute-done.7) | copy-start | bytes 491524
  41.2 11.7 %copy-start.8 = (bf16[5,128,128]{2,1,0:T(8,128)(2,1)}, bf16[5,128,128]{2,1,0:T(8,128)(2,1)S(1)}, u32[]{:S(2)}) copy-start(bf16[5,128,128]{2,1,0:T(8,128)(2,1)S(1)} %collective-permute-done.8) | copy-start | bytes 491524
  43.0 9.9 %copy-start.9 = (bf16[5,128,128]{2,1,0:T(8,128)(2,1)}, bf16[5,128,128]{2,1,0:T(8,128)(2,1)S(1)}, u32[]{:S(2)}) copy-start(bf16[5,128,128]{2,1,0:T(8,128)(2,1)S(1)} %collective-permute-done.9) | copy-start | bytes 491524
  43.8 11.7 %collective-permute-start.10 = (bf16[5,128,128]{2,1,0:T(8,128)(2,1)}, bf16[5,128,128]{2,1,0:T(8,128)(2,1)}, u32[]{:S(2)}, u32[]{:S(2)}) collective-permute-start(bf16[5,128,128]{2,1,0:T(8,128)(2,1)} %fusion.42), channel_id=1, source_target_pairs={{0,128},{8,136},{16,144},{24,152},{32,160},{40,168},{48,176},{56,1... | collective-permute-start | bytes 491528 | tf_op jit(solution)/shard_map/ppermute | solution.py:16
  67.0 12.7 %collective-permute-start.12 = (bf16[128,1280]{1,0:T(8,128)(2,1)S(1)}, bf16[128,1280]{1,0:T(8,128)(2,1)S(1)}, u32[]{:S(2)}, u32[]{:S(2)}) collective-permute-start(bf16[128,1280]{1,0:T(8,128)(2,1)S(1)} %get-tuple-element.11), channel_id=1, source_target_pairs={{0,1},{4,5},{8,9},{12,13},{16,17},{20,21},{24,25},{28,29},{32,33},... | collective-permute-start | bytes 983048 | tf_op jit(solution)/shard_map/ppermute | solution.py:111
  73.4 6.2 %collective-permute-start.13 = (bf16[128,1280]{1,0:T(8,128)(2,1)S(1)}, bf16[128,1280]{1,0:T(8,128)(2,1)S(1)}, u32[]{:S(2)}, u32[]{:S(2)}) collective-permute-start(bf16[128,1280]{1,0:T(8,128)(2,1)S(1)} %get-tuple-element.12), channel_id=1, source_target_pairs={{3,2},{7,6},{11,10},{15,14},{19,18},{23,22},{27,26},{31,30},{35,34... | collective-permute-start | bytes 983048 | tf_op jit(solution)/shard_map/ppermute | solution.py:112
  79.8 9.8 %collective-permute-start.14 = (bf16[128,1280]{1,0:T(8,128)(2,1)S(1)}, bf16[128,1280]{1,0:T(8,128)(2,1)S(1)}, u32[]{:S(2)}, u32[]{:S(2)}) collective-permute-start(bf16[128,1280]{1,0:T(8,128)(2,1)S(1)} %get-tuple-element.13), channel_id=1, source_target_pairs={{0,1},{1,2},{4,5},{5,6},{8,9},{9,10},{12,13},{13,14},{16,17},{17,1... | collective-permute-start | bytes 983048 | tf_op jit(solution)/shard_map/ppermute | solution.py:111
  84.2 5.3 %collective-permute-start.15 = (bf16[128,1280]{1,0:T(8,128)(2,1)S(1)}, bf16[128,1280]{1,0:T(8,128)(2,1)S(1)}, u32[]{:S(2)}, u32[]{:S(2)}) collective-permute-start(bf16[128,1280]{1,0:T(8,128)(2,1)S(1)} %get-tuple-element.14), channel_id=1, source_target_pairs={{2,1},{3,2},{6,5},{7,6},{10,9},{11,10},{14,13},{15,14},{18,17},{19... | collective-permute-start | bytes 983048 | tf_op jit(solution)/shard_map/ppermute | solution.py:112
  89.7 12.4 %collective-permute-start.16 = (bf16[128,1280]{1,0:T(8,128)(2,1)S(1)}, bf16[128,1280]{1,0:T(8,128)(2,1)S(1)}, u32[]{:S(2)}, u32[]{:S(2)}) collective-permute-start(bf16[128,1280]{1,0:T(8,128)(2,1)S(1)} %get-tuple-element.15), channel_id=1, source_target_pairs={{0,1},{1,2},{2,3},{4,5},{5,6},{6,7},{8,9},{9,10},{10,11},{12,13},{... | collective-permute-start | bytes 983048 | tf_op jit(solution)/shard_map/ppermute | solution.py:111
  97.5 9.0 %collective-permute-start.17 = (bf16[128,1280]{1,0:T(8,128)(2,1)S(1)}, bf16[128,1280]{1,0:T(8,128)(2,1)S(1)}, u32[]{:S(2)}, u32[]{:S(2)}) collective-permute-start(bf16[128,1280]{1,0:T(8,128)(2,1)S(1)} %get-tuple-element.16), channel_id=1, source_target_pairs={{1,0},{2,1},{3,2},{5,4},{6,5},{7,6},{9,8},{10,9},{11,10},{13,12},{... | collective-permute-start | bytes 983048 | tf_op jit(solution)/shard_map/ppermute | solution.py:112

commit v9 on v8

--- a/solution.py
+++ b/solution.py
@@ -55,14 +55,13 @@
     head_count = width_local // HD
     c = lax.axis_index("wt")
 
-    mine_cols = lax.dynamic_slice_in_dim(rows_in, c * half, half, axis=1)
-    got_cols = lax.dynamic_slice_in_dim(swap_cores(rows_in), c * half, half, axis=1)
+    both_rows = jnp.concatenate([rows_in, swap_cores(rows_in)], axis=0)
+    both_cols = lax.dynamic_slice_in_dim(both_rows, c * half, half, axis=1)
     sums = []
-    for w in (w_query, w_key, w_value):
-        lent = swap_cores(jnp.dot(got_cols, w, preferred_element_type=F32))
-        own = jnp.dot(mine_cols, w, preferred_element_type=F32)
-        sums.append(own + lent)
-    query_sum, key_sum, value_sum = sums
+    for w in (w_key, w_value, w_query):
+        part = jnp.dot(both_cols, w, preferred_element_type=F32)
+        sums.append(part[:tok_count] + swap_cores(part[tok_count:]))
+    key_sum, value_sum, query_sum = sums
 
     queries = jax.nn.silu(query_sum).astype(BF16).reshape(tok_count, head_count, HD)
     keys_all = jax.nn.silu(key_sum).astype(BF16).reshape(tok_count, head_count, HD)

time: 108 us -> 108 us (level)
  matrix products: 21.1 us -> 13.9 us
  waiting for transfers between devices: 26.9 us -> 31.5 us
  other arithmetic: 11.8 us -> 14.4 us
    dot_general x6 -> x3, matrix products: 13.7 us -> 5.9 us  [shards(): part = jnp.dot(both_cols, w, preferred_element_type=F32)]
    ppermute x5, waiting for transfers between devices: 0.01 us -> 2.88 us  [swap_cores(): return lax.ppermute(x, 'wt', [(0, 1), (1, 0)])]
    ppermute x7, waiting for transfers between devices: 9.08 us -> 10.8 us  [shifted(): return lax.ppermute(x, axis, pairs)]
    concatenate x0 -> x1, other arithmetic: none -> 1.37 us  [shards(): both_rows = jnp.concatenate([rows_in, swap_cores(rows_in)], axis=0)]
    convert_element_type x1, other arithmetic: 0.08 us -> 1.26 us  [along(): sent = value.astype(BF16)]
    convert_element_type x1, other arithmetic: 0.82 us -> 1.95 us  [prefix_over_seq(): ez = shifted(plane_total.astype(BF16), 'seq', zpairs).astype(F32)]
  transfers between devices with their start and end apart: 18 -> 18, of which waited for: 9 -> 11; matrix products, arithmetic and copies ran while one was open for 29% -> 25% of each run, Pallas kernels for 0% -> 0%
where the time goes in v9:
time: 108 us
  starting transfers between devices  41.1 us (38%)
  waiting for transfers between devices  31.5 us (29%)
  other arithmetic  14.4 us (13%)
  matrix products  13.9 us (13%)
  local copies, waits for them, and re-layouts  6.43 us (6%)
    ppermute x7, starting transfers between devices, shifted(): return lax.ppermute(x, axis, pairs)  18.8 us
    ppermute x3, starting transfers between devices, shards(): right = lax.ppermute(send_r, 'head', rpairs).astype(F32)  18.6 us
    ppermute x3, waiting for transfers between devices, shards(): right = lax.ppermute(send_r, 'head', rpairs).astype(F32)  13.4 us
    ppermute x7, waiting for transfers between devices, shifted(): return lax.ppermute(x, axis, pairs)  10.8 us
    dot_general x3, matrix products, shards(): part = jnp.dot(both_cols, w, preferred_element_type=F32)  5.9 us
    ppermute x3, waiting for transfers between devices, shards(): left = lax.ppermute(send_l, 'head', lpairs).astype(F32)  4.42 us
    squeeze x1, other arithmetic, shards(): pieces.append(piece[0])  4.33 us
    ppermute x5, waiting for transfers between devices, swap_cores(): return lax.ppermute(x, 'wt', [(0, 1), (1, 0)])  2.88 us
  transfers between devices with their start and end apart: 18, of which 11 were waited for; matrix products, arithmetic and copies ran while one was open for 25% of the time, Pallas kernels for 0%

profile of v9, /device:TPU:10, one launch (start us, length us, event | category | flops | bytes accessed | tf_op | source)
XLA Modules:
  0.0 107.5 jit_solution(6068809377749174722)
XLA Ops:
  0.0 0.0 collective-permute-start
  0.0 0.5 collective-permute-start.11
  0.5 2.9 %collective-permute-done = bf16[128,5120]{1,0:T(8,128)(2,1)} collective-permute-done((bf16[128,5120]{1,0:T(8,128)(2,1)}, bf16[128,5120]{1,0:T(8,128)(2,1)}, u32[]{:S(2)}, u32[]{:S(2)}) %collective-permute-start) | collective-permute-done | bytes 1310752 | tf_op jit(solution)/shard_map/ppermute | solution.py:12
  3.4 1.4 %fusion.16 = bf16[256,2560]{1,0:T(8,128)(2,1)S(1)} fusion(s32[]{:T(128)S(6)} %select_n.153, bf16[128,5120]{1,0:T(8,128)(2,1)} %bitcast.38, bf16[128,5120]{1,0:T(8,128)(2,1)} %collective-permute-done), kind=kLoop, calls=%fused_computation.26 | loop fusion | flops 2621440 | bytes 3932164 | tf_op jit(solution)/shard_map/concatenate | solution.py:58
  4.8 0.0 copy-start.7
  4.8 1.2 %fusion.46 = f32[256,640]{1,0:T(8,128)S(1)} fusion(bf16[256,2560]{1,0:T(8,128)(2,1)S(1)} %fusion.16, bf16[2560,640]{1,0:T(8,128)(2,1)S(1)} %copy-done), kind=kOutput, calls=%fused_computation.85 | convolution fusion | flops 838860800 | bytes 5242880 | tf_op jit(solution)/shard_map/dot_general | solution.py:62
  6.0 0.2 collective-permute-start.1
  6.3 0.0 copy-done.2
  6.3 0.9 copy-done.7
  7.2 1.2 %fusion.48 = f32[256,640]{1,0:T(8,128)S(1)} fusion(bf16[256,2560]{1,0:T(8,128)(2,1)S(1)} %fusion.16, bf16[2560,640]{1,0:T(8,128)(2,1)S(1)} %copy-done.7), kind=kOutput, calls=%fused_computation.87 | convolution fusion | flops 838860800 | bytes 5242880 | tf_op jit(solution)/shard_map/dot_general | solution.py:62
  8.4 0.8 slice.48
  9.2 0.1 collective-permute-start.3
  9.3 0.0 collective-permute-done.1
  9.3 0.0 copy-done.3
  9.4 0.7 fusion.30
  10.1 1.1 copy.11
  11.2 0.0 collective-permute-done.3
  11.2 1.8 %multiply_convert_fusion.1 = bf16[128,640]{1,0:T(8,128)(2,1)} fusion(f32[128,640]{1,0:T(8,128)} %collective-permute-done.3, f32[256,640]{1,0:T(8,128)} %copy-done.3), kind=kLoop, calls=%fused_computation.67 | loop fusion | flops 491520 | bytes 819200 | tf_op jit(solution)/shard_map/convert_element_type | solution.py:67
  13.0 1.7 %copy.13 = bf16[128,640]{0,1:T(8,128)(2,1)} copy(bf16[128,640]{1,0:T(8,128)(2,1)} %multiply_convert_fusion.1) | data formatting | bytes 327680 | tf_op jit(solution)/shard_map/convert_element_type | solution.py:67
  14.7 1.9 %fusion.45 = (bf16[5,128,128]{2,1,0:T(8,128)(2,1)}, f32[5,128,128]{2,1,0:T(8,128)}) fusion(bf16[128,5,128]{0,2,1:T(8,128)(2,1)} %bitcast.35, bf16[128,5,128]{0,2,1:T(8,128)(2,1)S(1)} %bitcast.33), kind=kOutput, calls=%fused_computation.84 | convolution fusion | flops 21053440 | bytes 819200 | tf_op jit(solution)/shard_map/thd,the->hde/dot_general | solution.py:69
  16.7 1.5 %collective-permute-start.4 = (bf16[5,128,128]{2,1,0:T(8,128)(2,1)}, bf16[5,128,128]{2,1,0:T(8,128)(2,1)}, u32[]{:S(2)}, u32[]{:S(2)}) collective-permute-start(bf16[5,128,128]{2,1,0:T(8,128)(2,1)} %get-tuple-element.27), channel_id=1, source_target_pairs={{0,8},{8,16},{16,24},{24,0},{32,40},{40,48},{48,56},{56,32},{64,72... | collective-permute-start | bytes 491528 | tf_op jit(solution)/shard_map/ppermute | solution.py:16
  18.1 1.1 %collective-permute-start.5 = (bf16[5,128,128]{2,1,0:T(8,128)(2,1)}, bf16[5,128,128]{2,1,0:T(8,128)(2,1)}, u32[]{:S(2)}, u32[]{:S(2)}) collective-permute-start(bf16[5,128,128]{2,1,0:T(8,128)(2,1)} %get-tuple-element.27), channel_id=1, source_target_pairs={{0,16},{8,24},{16,0},{24,8},{32,48},{40,56},{48,32},{56,40},{64,80... | collective-permute-start | bytes 491528 | tf_op jit(solution)/shard_map/ppermute | solution.py:16
  19.3 2.2 %collective-permute-start.6 = (bf16[5,128,128]{2,1,0:T(8,128)(2,1)}, bf16[5,128,128]{2,1,0:T(8,128)(2,1)}, u32[]{:S(2)}, u32[]{:S(2)}) collective-permute-start(bf16[5,128,128]{2,1,0:T(8,128)(2,1)} %get-tuple-element.27), channel_id=1, source_target_pairs={{0,24},{8,0},{16,8},{24,16},{32,56},{40,32},{48,40},{56,48},{64,88... | collective-permute-start | bytes 491528 | tf_op jit(solution)/shard_map/ppermute | solution.py:16
  21.4 2.6 %collective-permute-done.4 = bf16[5,128,128]{2,1,0:T(8,128)(2,1)} collective-permute-done((bf16[5,128,128]{2,1,0:T(8,128)(2,1)}, bf16[5,128,128]{2,1,0:T(8,128)(2,1)}, u32[]{:S(2)}, u32[]{:S(2)}) %collective-permute-start.4) | collective-permute-done | bytes 163872 | tf_op jit(solution)/shard_map/ppermute | solution.py:16
  24.0 3.0 %collective-permute-done.5 = bf16[5,128,128]{2,1,0:T(8,128)(2,1)} collective-permute-done((bf16[5,128,128]{2,1,0:T(8,128)(2,1)}, bf16[5,128,128]{2,1,0:T(8,128)(2,1)}, u32[]{:S(2)}, u32[]{:S(2)}) %collective-permute-start.5) | collective-permute-done | bytes 163872 | tf_op jit(solution)/shard_map/ppermute | solution.py:16
  27.1 1.9 %collective-permute-done.6 = bf16[5,128,128]{2,1,0:T(8,128)(2,1)} collective-permute-done((bf16[5,128,128]{2,1,0:T(8,128)(2,1)}, bf16[5,128,128]{2,1,0:T(8,128)(2,1)}, u32[]{:S(2)}, u32[]{:S(2)}) %collective-permute-start.6) | collective-permute-done | bytes 163872 | tf_op jit(solution)/shard_map/ppermute | solution.py:16
  29.0 1.3 %fusion.41 = bf16[5,128,128]{2,1,0:T(8,128)(2,1)S(1)} fusion(bf16[5,128,128]{2,1,0:T(8,128)(2,1)} %collective-permute-done.6, bf16[5,128,128]{2,1,0:T(8,128)(2,1)} %collective-permute-done.5, f32[5,128,128]{2,1,0:T(8,128)} %get-tuple-element.28, bf16[5,128,128]{2,1,0:T(8,128)(2,1)} %collective-permute-done.4), kind=kLoop, calls=%fused_computation.79 | loop fusion | flops 573440 | bytes 983040 | tf_op jit(solution)/shard_map/convert_element_type | solution.py:27
  30.2 0.0 copy-start.1
  30.2 1.7 %collective-permute-start.7 = (bf16[5,128,128]{2,1,0:T(8,128)(2,1)S(1)}, bf16[5,128,128]{2,1,0:T(8,128)(2,1)S(1)}, u32[]{:S(2)}, u32[]{:S(2)}) collective-permute-start(bf16[5,128,128]{2,1,0:T(8,128)(2,1)S(1)} %fusion.41), channel_id=1, source_target_pairs={{0,32},{8,40},{16,48},{24,56},{32,64},{40,72},{48,80},{56,88},{64,... | collective-permute-start | bytes 491528 | tf_op jit(solution)/shard_map/ppermute | solution.py:16
  31.9 1.6 %collective-permute-start.8 = (bf16[5,128,128]{2,1,0:T(8,128)(2,1)S(1)}, bf16[5,128,128]{2,1,0:T(8,128)(2,1)S(1)}, u32[]{:S(2)}, u32[]{:S(2)}) collective-permute-start(bf16[5,128,128]{2,1,0:T(8,128)(2,1)S(1)} %fusion.41), channel_id=1, source_target_pairs={{0,64},{8,72},{16,80},{24,88},{32,96},{40,104},{48,112},{56,120},{... | collective-permute-start | bytes 491528 | tf_op jit(solution)/shard_map/ppermute | solution.py:16
  33.5 1.7 %collective-permute-start.9 = (bf16[5,128,128]{2,1,0:T(8,128)(2,1)S(1)}, bf16[5,128,128]{2,1,0:T(8,128)(2,1)S(1)}, u32[]{:S(2)}, u32[]{:S(2)}) collective-permute-start(bf16[5,128,128]{2,1,0:T(8,128)(2,1)S(1)} %fusion.41), channel_id=1, source_target_pairs={{0,96},{8,104},{16,112},{24,120},{32,0},{40,8},{48,16},{56,24},{64... | collective-permute-start | bytes 491528 | tf_op jit(solution)/shard_map/ppermute | solution.py:16
  35.3 3.5 %fusion.47 = f32[256,640]{1,0:T(8,128)S(1)} fusion(bf16[256,2560]{1,0:T(8,128)(2,1)} %copy-done.2, bf16[2560,640]{1,0:T(8,128)(2,1)} %param.6), kind=kOutput, calls=%fused_computation.86 | convolution fusion | flops 838860800 | bytes 5242880 | tf_op jit(solution)/shard_map/dot_general | solution.py:62
  38.8 0.1 collective-permute-start.2
  38.9 0.0 collective-permute-done.7
  38.9 1.4 %collective-permute-done.8 = bf16[5,128,128]{2,1,0:T(8,128)(2,1)S(1)} collective-permute-done((bf16[5,128,128]{2,1,0:T(8,128)(2,1)S(1)}, bf16[5,128,128]{2,1,0:T(8,128)(2,1)S(1)}, u32[]{:S(2)}, u32[]{:S(2)}) %collective-permute-start.8) | collective-permute-done | bytes 163872 | tf_op jit(solution)/shard_map/ppermute | solution.py:16
  40.3 1.8 %collective-permute-done.9 = bf16[5,128,128]{2,1,0:T(8,128)(2,1)S(1)} collective-permute-done((bf16[5,128,128]{2,1,0:T(8,128)(2,1)S(1)}, bf16[5,128,128]{2,1,0:T(8,128)(2,1)S(1)}, u32[]{:S(2)}, u32[]{:S(2)}) %collective-permute-start.9) | collective-permute-done | bytes 163872 | tf_op jit(solution)/shard_map/ppermute | solution.py:16
  42.1 2.0 %fusion.28 = bf16[5,128,128]{2,1,0:T(8,128)(2,1)} fusion(bf16[5,128,128]{2,1,0:T(8,128)(2,1)S(1)} %collective-permute-done.9, bf16[5,128,128]{2,1,0:T(8,128)(2,1)S(1)} %collective-permute-done.8, bf16[5,128,128]{2,1,0:T(8,128)(2,1)S(1)} %collective-permute-done.7, bf16[5,128,128]{2,1,0:T(8,128)(2,1)} %collective-permute-done.6, ...), kind=kLoop, calls=%fused_computation.59 | loop fusion | flops 1064960 | bytes 1474560 | tf_op jit(solution)/shard_map/convert_element_type | solution.py:46
  44.0 9.1 %collective-permute-start.10 = (bf16[5,128,128]{2,1,0:T(8,128)(2,1)}, bf16[5,128,128]{2,1,0:T(8,128)(2,1)}, u32[]{:S(2)}, u32[]{:S(2)}) collective-permute-start(bf16[5,128,128]{2,1,0:T(8,128)(2,1)} %fusion.28), channel_id=1, source_target_pairs={{0,128},{8,136},{16,144},{24,152},{32,160},{40,168},{48,176},{56,1... | collective-permute-start | bytes 491528 | tf_op jit(solution)/shard_map/ppermute | solution.py:16
  53.1 0.0 collective-permute-done.2
  53.1 0.8 multiply_convert_fusion.2
  53.9 1.7 %copy.12 = bf16[128,640]{0,1:T(8,128)(2,1)} copy(bf16[128,640]{1,0:T(8,128)(2,1)} %multiply_convert_fusion.2) | data formatting | bytes 327680 | tf_op jit(solution)/shard_map/convert_element_type | solution.py:66
  55.6 0.1 collective-permute-done.10
  55.7 2.5 %fusion.32 = f32[5,128,128]{2,1,0:T(8,128)} fusion(bf16[128,5,128]{0,2,1:T(8,128)(2,1)} %bitcast.39, bf16[5,128,128]{2,1,0:T(8,128)(2,1)} %collective-permute-done.4, bf16[5,128,128]{2,1,0:T(8,128)(2,1)} %collective-permute-done.5, bf16[5,128,128]{2,1,0:T(8,128)(2,1)} %collective-permute-done.6, bf16[5,128,128]{2,1,0:T(8,128)(2,1)} %copy-done.4, ...), kind=kOutput, calls=%fused_computation.70 | convolution fusion | flops 22609920 | bytes 1638406 | tf_op jit(solution)/shard_map/thd,hde->the/dot_general | solution.py:77
  58.2 2.3 %multiply_reduce_fusion = (f32[128,5]{0,1:T(8,128)S(1)}, f32[128,5,128]{0,2,1:T(8,128)}) fusion(f32[5,128,128]{2,1,0:T(8,128)} %fusion.32, bf16[128,5,128]{0,2,1:T(8,128)(2,1)S(1)} %bitcast.34, bf16[128,5,128]{0,2,1:T(8,128)(2,1)} %bitcast.40, bf16[128,5,128]{0,2,1:T(8,128)(2,1)} %bitcast.36, f32[128,128]{1,0:T(8,128)S(1)} %fusion.40), kind=kOutput, calls=%fused_computation.66 | convolution fusion | flops 42352000 | bytes 1214976 | tf_op jit(solution)/shard_map/hts,shd->thd/dot_general | solution.py:76
  60.5 1.0 multiply_convert_fusion
  61.5 0.0 collective-permute-done.11
  61.5 4.3 %fusion.11 = (bf16[640,1280]{1,0:T(8,128)(2,1)S(1)}, bf16[640,1280]{1,0:T(8,128)(2,1)S(1)}, bf16[640,1280]{1,0:T(8,128)(2,1)S(1)}, bf16[640,1280]{1,0:T(8,128)(2,1)S(1)}) fusion(s32[]{:T(128)S(6)} %select_n.177, s32[]{:T(128)S(6)} %select_n.179, bf16[1,640,2560]{2,1,0:T(8,128)(2,1)} %bitcast.32, bf16[1,640,2560]{2,1,0:T(8,128)(2,1)} %bitcast.7, ...), kind=kLoop, calls=%fused_computation.21 | loop fusion | flops 13107200 | bytes 13107232 | tf_op jit(solution)/shard_map/squeeze | solution.py:95
  65.9 1.2 %fusion = f32[128,5120]{1,0:T(8,128)S(1)} fusion(bf16[128,640]{0,1:T(8,128)(2,1)S(1)} %bitcast.41, bf16[640,1280]{1,0:T(8,128)(2,1)S(1)} %get-tuple-element.20, bf16[640,1280]{1,0:T(8,128)(2,1)S(1)} %get-tuple-element.19, bf16[640,1280]{1,0:T(8,128)(2,1)S(1)} %get-tuple-element.18, bf16[640,1280]{1,0:T(8,128)(2,1)S(1)} %get-tuple-element.17), kind=kOutput, calls=%fused_computation.8 | convolution fusion | flops 865075200 | bytes 9338880 | tf_op jit(solution)/shard_map/dot_general | solution.py:97
  67.1 0.1 fusion.44
  67.2 6.5 %collective-permute-start.12 = (bf16[128,1280]{1,0:T(8,128)(2,1)S(1)}, bf16[128,1280]{1,0:T(8,128)(2,1)S(1)}, u32[]{:S(2)}, u32[]{:S(2)}) collective-permute-start(bf16[128,1280]{1,0:T(8,128)(2,1)S(1)} %get-tuple-element.11), channel_id=1, source_target_pairs={{0,1},{4,5},{8,9},{12,13},{16,17},{20,21},{24,25},{28,29},{32,33},... | collective-permute-start | bytes 983048 | tf_op jit(solution)/shard_map/ppermute | solution.py:110
  73.7 0.7 collective-permute-start.13
  74.3 5.5 %collective-permute-done.12 = bf16[128,1280]{1,0:T(8,128)(2,1)S(1)} collective-permute-done((bf16[128,1280]{1,0:T(8,128)(2,1)S(1)}, bf16[128,1280]{1,0:T(8,128)(2,1)S(1)}, u32[]{:S(2)}, u32[]{:S(2)}) %collective-permute-start.12) | collective-permute-done | bytes 327712 | tf_op jit(solution)/shard_map/ppermute | solution.py:110
  79.9 0.0 collective-permute-done.13
  79.9 0.1 add_convert_fusion.2
  80.0 4.4 %collective-permute-start.14 = (bf16[128,1280]{1,0:T(8,128)(2,1)S(1)}, bf16[128,1280]{1,0:T(8,128)(2,1)S(1)}, u32[]{:S(2)}, u32[]{:S(2)}) collective-permute-start(bf16[128,1280]{1,0:T(8,128)(2,1)S(1)} %get-tuple-element.13), channel_id=1, source_target_pairs={{0,1},{1,2},{4,5},{5,6},{8,9},{9,10},{12,13},{13,14},{16,17},{17,1... | collective-permute-start | bytes 983048 | tf_op jit(solution)/shard_map/ppermute | solution.py:110
  84.4 0.7 collective-permute-start.15
  85.1 4.7 %collective-permute-done.14 = bf16[128,1280]{1,0:T(8,128)(2,1)S(1)} collective-permute-done((bf16[128,1280]{1,0:T(8,128)(2,1)S(1)}, bf16[128,1280]{1,0:T(8,128)(2,1)S(1)}, u32[]{:S(2)}, u32[]{:S(2)}) %collective-permute-start.14) | collective-permute-done | bytes 327712 | tf_op jit(solution)/shard_map/ppermute | solution.py:110
  89.8 0.0 collective-permute-done.15
  89.8 0.2 add_convert_fusion
  89.9 7.8 %collective-permute-start.16 = (bf16[128,1280]{1,0:T(8,128)(2,1)S(1)}, bf16[128,1280]{1,0:T(8,128)(2,1)S(1)}, u32[]{:S(2)}, u32[]{:S(2)}) collective-permute-start(bf16[128,1280]{1,0:T(8,128)(2,1)S(1)} %get-tuple-element.15), channel_id=1, source_target_pairs={{0,1},{1,2},{2,3},{4,5},{5,6},{6,7},{8,9},{9,10},{10,11},{12,13},{... | collective-permute-start | bytes 983048 | tf_op jit(solution)/shard_map/ppermute | solution.py:110
  97.7 1.3 %collective-permute-start.17 = (bf16[128,1280]{1,0:T(8,128)(2,1)S(1)}, bf16[128,1280]{1,0:T(8,128)(2,1)S(1)}, u32[]{:S(2)}, u32[]{:S(2)}) collective-permute-start(bf16[128,1280]{1,0:T(8,128)(2,1)S(1)} %get-tuple-element.16), channel_id=1, source_target_pairs={{1,0},{2,1},{3,2},{5,4},{6,5},{7,6},{9,8},{10,9},{11,10},{13,12},{... | collective-permute-start | bytes 983048 | tf_op jit(solution)/shard_map/ppermute | solution.py:111
  99.0 3.3 %collective-permute-done.16 = bf16[128,1280]{1,0:T(8,128)(2,1)S(1)} collective-permute-done((bf16[128,1280]{1,0:T(8,128)(2,1)S(1)}, bf16[128,1280]{1,0:T(8,128)(2,1)S(1)}, u32[]{:S(2)}, u32[]{:S(2)}) %collective-permute-start.16) | collective-permute-done | bytes 327712 | tf_op jit(solution)/shard_map/ppermute | solution.py:110
  102.3 4.4 %collective-permute-done.17 = bf16[128,1280]{1,0:T(8,128)(2,1)S(1)} collective-permute-done((bf16[128,1280]{1,0:T(8,128)(2,1)S(1)}, bf16[128,1280]{1,0:T(8,128)(2,1)S(1)}, u32[]{:S(2)}, u32[]{:S(2)}) %collective-permute-start.17) | collective-permute-done | bytes 327712 | tf_op jit(solution)/shard_map/ppermute | solution.py:111
  106.7 0.8 fusion.29
  (15 shorter events, 0.1 us)
Async XLA Ops:
  0.0 4.8 %copy-start = (bf16[2560,640]{1,0:T(8,128)(2,1)S(1)}, bf16[2560,640]{1,0:T(8,128)(2,1)}, u32[]{:S(2)}) copy-start(bf16[2560,640]{1,0:T(8,128)(2,1)} %param.8) | copy-start | bytes 9830404
  0.0 3.4 %collective-permute-start = (bf16[128,5120]{1,0:T(8,128)(2,1)}, bf16[128,5120]{1,0:T(8,128)(2,1)}, u32[]{:S(2)}, u32[]{:S(2)}) collective-permute-start(bf16[128,5120]{1,0:T(8,128)(2,1)} %bitcast.37), channel_id=1, source_target_pairs={{0,4},{4,0},{1,5},{5,1},{2,6},{6,2},{3,7},{7,3},{8,12},{12,8},{9,1... | collective-permute-start | bytes 3932168 | tf_op jit(solution)/shard_map/ppermute | solution.py:12
  0.0 61.5 %collective-permute-start.11 = (bf16[640,2560]{1,0:T(8,128)(2,1)}, bf16[640,2560]{1,0:T(8,128)(2,1)}, u32[]{:S(2)}, u32[]{:S(2)}) collective-permute-start(bf16[640,2560]{1,0:T(8,128)(2,1)} %param.9), channel_id=1, source_target_pairs={{0,4},{4,0},{1,5},{5,1},{2,6},{6,2},{3,7},{7,3},{8,12},{12,8},{9,1... | collective-permute-start | bytes 9830408 | tf_op jit(solution)/shard_map/ppermute | solution.py:12
  4.8 1.5 %copy-start.2 = (bf16[256,2560]{1,0:T(8,128)(2,1)}, bf16[256,2560]{1,0:T(8,128)(2,1)S(1)}, u32[]{:S(2)}) copy-start(bf16[256,2560]{1,0:T(8,128)(2,1)S(1)} %fusion.16) | copy-start | bytes 3932164
  4.8 2.4 %copy-start.7 = (bf16[2560,640]{1,0:T(8,128)(2,1)S(1)}, bf16[2560,640]{1,0:T(8,128)(2,1)}, u32[]{:S(2)}) copy-start(bf16[2560,640]{1,0:T(8,128)(2,1)} %param.7) | copy-start | bytes 9830404
  6.0 3.3 %collective-permute-start.1 = (f32[128,640]{1,0:T(8,128)S(1)}, f32[128,640]{1,0:T(8,128)S(1)}, u32[]{:S(2)}, u32[]{:S(2)}) collective-permute-start(f32[128,640]{1,0:T(8,128)S(1)} %slice.44), channel_id=1, source_target_pairs={{0,4},{4,0},{1,5},{5,1},{2,6},{6,2},{3,7},{7,3},{8,12},{12,8},{9,1... | collective-permute-start | bytes 983048 | tf_op jit(solution)/shard_map/ppermute | solution.py:12
  8.4 1.0 copy-start.3
  9.2 2.0 %collective-permute-start.3 = (f32[128,640]{1,0:T(8,128)}, f32[128,640]{1,0:T(8,128)}, u32[]{:S(2)}, u32[]{:S(2)}) collective-permute-start(f32[128,640]{1,0:T(8,128)} %slice.48), channel_id=1, source_target_pairs={{0,4},{4,0},{1,5},{5,1},{2,6},{6,2},{3,7},{7,3},{8,12},{12,8},{9,1... | collective-permute-start | bytes 983048 | tf_op jit(solution)/shard_map/ppermute | solution.py:12
  16.7 7.4 %collective-permute-start.4 = (bf16[5,128,128]{2,1,0:T(8,128)(2,1)}, bf16[5,128,128]{2,1,0:T(8,128)(2,1)}, u32[]{:S(2)}, u32[]{:S(2)}) collective-permute-start(bf16[5,128,128]{2,1,0:T(8,128)(2,1)} %get-tuple-element.27), channel_id=1, source_target_pairs={{0,8},{8,16},{16,24},{24,0},{32,40},{40,48},{48,56},{56,32},{64,72... | collective-permute-start | bytes 491528 | tf_op jit(solution)/shard_map/ppermute | solution.py:16
  18.1 8.9 %collective-permute-start.5 = (bf16[5,128,128]{2,1,0:T(8,128)(2,1)}, bf16[5,128,128]{2,1,0:T(8,128)(2,1)}, u32[]{:S(2)}, u32[]{:S(2)}) collective-permute-start(bf16[5,128,128]{2,1,0:T(8,128)(2,1)} %get-tuple-element.27), channel_id=1, source_target_pairs={{0,16},{8,24},{16,0},{24,8},{32,48},{40,56},{48,32},{56,40},{64,80... | collective-permute-start | bytes 491528 | tf_op jit(solution)/shard_map/ppermute | solution.py:16
  19.3 9.7 %collective-permute-start.6 = (bf16[5,128,128]{2,1,0:T(8,128)(2,1)}, bf16[5,128,128]{2,1,0:T(8,128)(2,1)}, u32[]{:S(2)}, u32[]{:S(2)}) collective-permute-start(bf16[5,128,128]{2,1,0:T(8,128)(2,1)} %get-tuple-element.27), channel_id=1, source_target_pairs={{0,24},{8,0},{16,8},{24,16},{32,56},{40,32},{48,40},{56,48},{64,88... | collective-permute-start | bytes 491528 | tf_op jit(solution)/shard_map/ppermute | solution.py:16
  30.2 11.8 %copy-start.1 = (f32[5,128,128]{2,1,0:T(8,128)S(1)}, f32[5,128,128]{2,1,0:T(8,128)}, u32[]{:S(2)}) copy-start(f32[5,128,128]{2,1,0:T(8,128)} %get-tuple-element.28) | copy-start | bytes 983044
  30.2 8.7 %collective-permute-start.7 = (bf16[5,128,128]{2,1,0:T(8,128)(2,1)S(1)}, bf16[5,128,128]{2,1,0:T(8,128)(2,1)S(1)}, u32[]{:S(2)}, u32[]{:S(2)}) collective-permute-start(bf16[5,128,128]{2,1,0:T(8,128)(2,1)S(1)} %fusion.41), channel_id=1, source_target_pairs={{0,32},{8,40},{16,48},{24,56},{32,64},{40,72},{48,80},{56,88},{64,... | collective-permute-start | bytes 491528 | tf_op jit(solution)/shard_map/ppermute | solution.py:16
  31.9 8.4 %collective-permute-start.8 = (bf16[5,128,128]{2,1,0:T(8,128)(2,1)S(1)}, bf16[5,128,128]{2,1,0:T(8,128)(2,1)S(1)}, u32[]{:S(2)}, u32[]{:S(2)}) collective-permute-start(bf16[5,128,128]{2,1,0:T(8,128)(2,1)S(1)} %fusion.41), channel_id=1, source_target_pairs={{0,64},{8,72},{16,80},{24,88},{32,96},{40,104},{48,112},{56,120},{... | collective-permute-start | bytes 491528 | tf_op jit(solution)/shard_map/ppermute | solution.py:16
  33.5 8.6 %collective-permute-start.9 = (bf16[5,128,128]{2,1,0:T(8,128)(2,1)S(1)}, bf16[5,128,128]{2,1,0:T(8,128)(2,1)S(1)}, u32[]{:S(2)}, u32[]{:S(2)}) collective-permute-start(bf16[5,128,128]{2,1,0:T(8,128)(2,1)S(1)} %fusion.41), channel_id=1, source_target_pairs={{0,96},{8,104},{16,112},{24,120},{32,0},{40,8},{48,16},{56,24},{64... | collective-permute-start | bytes 491528 | tf_op jit(solution)/shard_map/ppermute | solution.py:16
  38.8 14.3 %collective-permute-start.2 = (f32[128,640]{1,0:T(8,128)S(1)}, f32[128,640]{1,0:T(8,128)S(1)}, u32[]{:S(2)}, u32[]{:S(2)}) collective-permute-start(f32[128,640]{1,0:T(8,128)S(1)} %slice.46), channel_id=1, source_target_pairs={{0,4},{4,0},{1,5},{5,1},{2,6},{6,2},{3,7},{7,3},{8,12},{12,8},{9,1... | collective-permute-start | bytes 983048 | tf_op jit(solution)/shard_map/ppermute | solution.py:12
  38.9 14.2 %copy-start.4 = (bf16[5,128,128]{2,1,0:T(8,128)(2,1)}, bf16[5,128,128]{2,1,0:T(8,128)(2,1)S(1)}, u32[]{:S(2)}) copy-start(bf16[5,128,128]{2,1,0:T(8,128)(2,1)S(1)} %collective-permute-done.7) | copy-start | bytes 491524
  40.3 12.8 %copy-start.5 = (bf16[5,128,128]{2,1,0:T(8,128)(2,1)}, bf16[5,128,128]{2,1,0:T(8,128)(2,1)S(1)}, u32[]{:S(2)}) copy-start(bf16[5,128,128]{2,1,0:T(8,128)(2,1)S(1)} %collective-permute-done.8) | copy-start | bytes 491524
  42.1 11.0 %copy-start.6 = (bf16[5,128,128]{2,1,0:T(8,128)(2,1)}, bf16[5,128,128]{2,1,0:T(8,128)(2,1)S(1)}, u32[]{:S(2)}) copy-start(bf16[5,128,128]{2,1,0:T(8,128)(2,1)S(1)} %collective-permute-done.9) | copy-start | bytes 491524
  44.0 11.7 %collective-permute-start.10 = (bf16[5,128,128]{2,1,0:T(8,128)(2,1)}, bf16[5,128,128]{2,1,0:T(8,128)(2,1)}, u32[]{:S(2)}, u32[]{:S(2)}) collective-permute-start(bf16[5,128,128]{2,1,0:T(8,128)(2,1)} %fusion.28), channel_id=1, source_target_pairs={{0,128},{8,136},{16,144},{24,152},{32,160},{40,168},{48,176},{56,1... | collective-permute-start | bytes 491528 | tf_op jit(solution)/shard_map/ppermute | solution.py:16
  67.2 12.7 %collective-permute-start.12 = (bf16[128,1280]{1,0:T(8,128)(2,1)S(1)}, bf16[128,1280]{1,0:T(8,128)(2,1)S(1)}, u32[]{:S(2)}, u32[]{:S(2)}) collective-permute-start(bf16[128,1280]{1,0:T(8,128)(2,1)S(1)} %get-tuple-element.11), channel_id=1, source_target_pairs={{0,1},{4,5},{8,9},{12,13},{16,17},{20,21},{24,25},{28,29},{32,33},... | collective-permute-start | bytes 983048 | tf_op jit(solution)/shard_map/ppermute | solution.py:110
  73.7 6.2 %collective-permute-start.13 = (bf16[128,1280]{1,0:T(8,128)(2,1)S(1)}, bf16[128,1280]{1,0:T(8,128)(2,1)S(1)}, u32[]{:S(2)}, u32[]{:S(2)}) collective-permute-start(bf16[128,1280]{1,0:T(8,128)(2,1)S(1)} %get-tuple-element.12), channel_id=1, source_target_pairs={{3,2},{7,6},{11,10},{15,14},{19,18},{23,22},{27,26},{31,30},{35,34... | collective-permute-start | bytes 983048 | tf_op jit(solution)/shard_map/ppermute | solution.py:111
  80.0 9.8 %collective-permute-start.14 = (bf16[128,1280]{1,0:T(8,128)(2,1)S(1)}, bf16[128,1280]{1,0:T(8,128)(2,1)S(1)}, u32[]{:S(2)}, u32[]{:S(2)}) collective-permute-start(bf16[128,1280]{1,0:T(8,128)(2,1)S(1)} %get-tuple-element.13), channel_id=1, source_target_pairs={{0,1},{1,2},{4,5},{5,6},{8,9},{9,10},{12,13},{13,14},{16,17},{17,1... | collective-permute-start | bytes 983048 | tf_op jit(solution)/shard_map/ppermute | solution.py:110
  84.4 5.3 %collective-permute-start.15 = (bf16[128,1280]{1,0:T(8,128)(2,1)S(1)}, bf16[128,1280]{1,0:T(8,128)(2,1)S(1)}, u32[]{:S(2)}, u32[]{:S(2)}) collective-permute-start(bf16[128,1280]{1,0:T(8,128)(2,1)S(1)} %get-tuple-element.14), channel_id=1, source_target_pairs={{2,1},{3,2},{6,5},{7,6},{10,9},{11,10},{14,13},{15,14},{18,17},{19... | collective-permute-start | bytes 983048 | tf_op jit(solution)/shard_map/ppermute | solution.py:111
  89.9 12.3 %collective-permute-start.16 = (bf16[128,1280]{1,0:T(8,128)(2,1)S(1)}, bf16[128,1280]{1,0:T(8,128)(2,1)S(1)}, u32[]{:S(2)}, u32[]{:S(2)}) collective-permute-start(bf16[128,1280]{1,0:T(8,128)(2,1)S(1)} %get-tuple-element.15), channel_id=1, source_target_pairs={{0,1},{1,2},{2,3},{4,5},{5,6},{6,7},{8,9},{9,10},{10,11},{12,13},{... | collective-permute-start | bytes 983048 | tf_op jit(solution)/shard_map/ppermute | solution.py:110
  97.7 9.0 %collective-permute-start.17 = (bf16[128,1280]{1,0:T(8,128)(2,1)S(1)}, bf16[128,1280]{1,0:T(8,128)(2,1)S(1)}, u32[]{:S(2)}, u32[]{:S(2)}) collective-permute-start(bf16[128,1280]{1,0:T(8,128)(2,1)S(1)} %get-tuple-element.16), channel_id=1, source_target_pairs={{1,0},{2,1},{3,2},{5,4},{6,5},{7,6},{9,8},{10,9},{11,10},{13,12},{... | collective-permute-start | bytes 983048 | tf_op jit(solution)/shard_map/ppermute | solution.py:111

commit v10 on v8

--- a/solution.py
+++ b/solution.py
@@ -100,17 +100,26 @@
     def block(o):
         return products[:, o * quarter : (o + 1) * quarter]
 
-    right = jnp.zeros((tok_count, quarter), F32)
-    left = jnp.zeros((tok_count, quarter), F32)
+    part = quarter // 2
+    outs = []
+    rights = [jnp.zeros((tok_count, part), F32) for _ in range(2)]
+    lefts = [jnp.zeros((tok_count, part), F32) for _ in range(2)]
+
+    def piece(o, g):
+        return products[:, o * quarter + g * part : o * quarter + (g + 1) * part]
+
     for s in range(1, n):
-        send_r = (block(n - s) + right).astype(BF16)
-        send_l = (block(s) + left).astype(BF16)
-        send_r, send_l = lax.optimization_barrier((send_r, send_l))
         rpairs = [(j, j + 1) for j in range(s) if j + 1 < n]
         lpairs = [(j, j - 1) for j in range(n - s, n) if j - 1 >= 0]
-        right = lax.ppermute(send_r, "head", rpairs).astype(F32)
-        left = lax.ppermute(send_l, "head", lpairs).astype(F32)
-    mixed = (block(0) + right + left).astype(BF16)
+        for g in range(2):
+            send_r = (piece(n - s, g) + rights[g]).astype(BF16)
+            send_l = (piece(s, g) + lefts[g]).astype(BF16)
+            send_r, send_l = lax.optimization_barrier((send_r, send_l))
+            rights[g] = lax.ppermute(send_r, "head", rpairs).astype(F32)
+            lefts[g] = lax.ppermute(send_l, "head", lpairs).astype(F32)
+    for g in range(2):
+        outs.append(piece(0, g) + rights[g] + lefts[g])
+    mixed = jnp.concatenate(outs, axis=1).astype(BF16)
     return mixed.reshape(1, tok_count, quarter)
 
 

time: 108 us -> 117 us (1.083)
  starting transfers between devices: 41.3 us -> 51.9 us
  waiting for transfers between devices: 26.9 us -> 25.4 us
    ppermute x6 -> x12, starting transfers between devices: 21.3 us -> 31.9 us  [the longest x6 26.6 us: shards(): rights[g] = lax.ppermute(send_r, 'head', rpairs).astype(F32)]
    ppermute x6 -> x12, waiting for transfers between devices: 17.8 us -> 16.3 us  [the longest x6 9.44 us: shards(): lefts[g] = lax.ppermute(send_l, 'head', lpairs).astype(F32)]
  transfers between devices with their start and end apart: 18 -> 24, of which waited for: 9 -> 11; matrix products, arithmetic and copies ran while one was open for 29% -> 26% of each run, Pallas kernels for 0% -> 0%
where the time goes in v10:
time: 117 us
  starting transfers between devices  51.9 us (44%)
  waiting for transfers between devices  25.4 us (22%)
  matrix products  21.1 us (18%)
  other arithmetic  11.8 us (10%)
  local copies, waits for them, and re-layouts  6.03 us (5%)
    ppermute x6, starting transfers between devices, shards(): rights[g] = lax.ppermute(send_r, 'head', rpairs).astype(F32)  26.6 us
    ppermute x7, starting transfers between devices, shifted(): return lax.ppermute(x, axis, pairs)  18.9 us
    ppermute x6, waiting for transfers between devices, shards(): lefts[g] = lax.ppermute(send_l, 'head', lpairs).astype(F32)  9.44 us
    ppermute x7, waiting for transfers between devices, shifted(): return lax.ppermute(x, axis, pairs)  9.09 us
    dot_general x3, matrix products, shards(): own = jnp.dot(mine_cols, w, preferred_element_type=F32)  6.88 us
    dot_general x3, matrix products, shards(): lent = swap_cores(jnp.dot(got_cols, w, preferred_element_type=F32))  6.88 us
    ppermute x6, waiting for transfers between devices, shards(): rights[g] = lax.ppermute(send_r, 'head', rpairs).astype(F32)  6.88 us
    ppermute x6, starting transfers between devices, shards(): lefts[g] = lax.ppermute(send_l, 'head', lpairs).astype(F32)  5.27 us
  transfers between devices with their start and end apart: 24, of which 11 were waited for; matrix products, arithmetic and copies ran while one was open for 26% of the time, Pallas kernels for 0%

profile of v10, /device:TPU:10, one launch (start us, length us, event | category | flops | bytes accessed | tf_op | source)
XLA Modules:
  0.0 116.5 jit_solution(3627888117131526238)
XLA Ops:
  0.0 0.0 collective-permute-start
  0.0 0.5 collective-permute-start.11
  0.5 1.4 %copy-done = bf16[2560,640]{1,0:T(8,128)(2,1)S(1)} copy-done((bf16[2560,640]{1,0:T(8,128)(2,1)S(1)}, bf16[2560,640]{1,0:T(8,128)(2,1)}, u32[]{:S(2)}) %copy-start) | copy-done | bytes 3276824
  1.9 2.7 %fusion.22 = f32[128,640]{1,0:T(8,128)} fusion(bf16[2560,640]{1,0:T(8,128)(2,1)S(1)} %copy-done, bf16[1,128,5120]{2,1,0:T(8,128)(2,1)} %param.5, s32[]{:T(128)S(6)} %select_n.154), kind=kOutput, calls=%fused_computation.32 | convolution fusion | flops 419430400 | bytes 4259844 | tf_op jit(solution)/shard_map/dot_general | solution.py:63
  4.6 2.6 %fusion.28 = f32[128,640]{1,0:T(8,128)} fusion(bf16[2560,640]{1,0:T(8,128)(2,1)S(1)} %copy-done, bf16[128,5120]{1,0:T(8,128)(2,1)} %collective-permute-done, s32[]{:T(128)S(6)} %select_n.154), kind=kOutput, calls=%fused_computation.38 | convolution fusion | flops 419430400 | bytes 4259844 | tf_op jit(solution)/shard_map/dot_general | solution.py:62
  7.2 2.5 %fusion.24 = f32[128,640]{1,0:T(8,128)} fusion(bf16[2560,640]{1,0:T(8,128)(2,1)S(1)} %copy-done.1, bf16[128,5120]{1,0:T(8,128)(2,1)} %collective-permute-done, s32[]{:T(128)S(6)} %select_n.154), kind=kOutput, calls=%fused_computation.34 | convolution fusion | flops 419430400 | bytes 4259844 | tf_op jit(solution)/shard_map/dot_general | solution.py:62
  9.7 0.5 collective-permute-start.3
  10.2 1.4 %fusion.18 = f32[128,640]{1,0:T(8,128)} fusion(bf16[2560,640]{1,0:T(8,128)(2,1)S(1)} %copy-done.1, bf16[1,128,5120]{2,1,0:T(8,128)(2,1)S(1)} %copy-done.3, s32[]{:T(128)S(6)} %select_n.154), kind=kOutput, calls=%fused_computation.28 | convolution fusion | flops 419430400 | bytes 4259844 | tf_op jit(solution)/shard_map/dot_general | solution.py:63
  11.6 1.8 %add_convert_fusion.8 = bf16[128,640]{1,0:T(8,128)(2,1)} fusion(f32[128,640]{1,0:T(8,128)} %fusion.22, f32[128,640]{1,0:T(8,128)} %collective-permute-done.1), kind=kLoop, calls=%fused_computation.82 | loop fusion | flops 163840 | bytes 819200 | tf_op jit(solution)/shard_map/convert_element_type | solution.py:69
  13.4 1.1 copy.11
  14.5 1.9 %multiply_convert_fusion.1 = bf16[128,640]{1,0:T(8,128)(2,1)} fusion(f32[128,640]{1,0:T(8,128)} %fusion.18, f32[128,640]{1,0:T(8,128)} %collective-permute-done.3), kind=kLoop, calls=%fused_computation.80 | loop fusion | flops 491520 | bytes 819200 | tf_op jit(solution)/shard_map/convert_element_type | solution.py:68
  16.3 1.7 %copy.13 = bf16[128,640]{0,1:T(8,128)(2,1)} copy(bf16[128,640]{1,0:T(8,128)(2,1)} %multiply_convert_fusion.1) | data formatting | bytes 327680 | tf_op jit(solution)/shard_map/convert_element_type | solution.py:68
  18.1 1.3 %fusion.67 = (bf16[5,128,128]{2,1,0:T(8,128)(2,1)S(1)}, f32[5,128,128]{2,1,0:T(8,128)S(1)}) fusion(bf16[128,5,128]{0,2,1:T(8,128)(2,1)} %bitcast.45, bf16[128,5,128]{0,2,1:T(8,128)(2,1)S(1)} %bitcast.43), kind=kOutput, calls=%fused_computation.110 | convolution fusion | flops 21053440 | bytes 819200 | tf_op jit(solution)/shard_map/thd,the->hde/dot_general | solution.py:70
  19.4 1.6 %collective-permute-start.4 = (bf16[5,128,128]{2,1,0:T(8,128)(2,1)S(1)}, bf16[5,128,128]{2,1,0:T(8,128)(2,1)S(1)}, u32[]{:S(2)}, u32[]{:S(2)}) collective-permute-start(bf16[5,128,128]{2,1,0:T(8,128)(2,1)S(1)} %get-tuple-element.46), channel_id=1, source_target_pairs={{0,8},{8,16},{16,24},{24,0},{32,40},{40,48},{48,56},{56,32},{64,72... | collective-permute-start | bytes 491528 | tf_op jit(solution)/shard_map/ppermute | solution.py:16
  20.9 1.1 collective-permute-start.5
  22.0 2.2 %collective-permute-start.6 = (bf16[5,128,128]{2,1,0:T(8,128)(2,1)S(1)}, bf16[5,128,128]{2,1,0:T(8,128)(2,1)S(1)}, u32[]{:S(2)}, u32[]{:S(2)}) collective-permute-start(bf16[5,128,128]{2,1,0:T(8,128)(2,1)S(1)} %get-tuple-element.46), channel_id=1, source_target_pairs={{0,24},{8,0},{16,8},{24,16},{32,56},{40,32},{48,40},{56,48},{64,88... | collective-permute-start | bytes 491528 | tf_op jit(solution)/shard_map/ppermute | solution.py:16
  24.2 2.8 %fusion.20 = f32[128,640]{1,0:T(8,128)S(1)} fusion(bf16[2560,640]{1,0:T(8,128)(2,1)} %param.6, bf16[1,128,5120]{2,1,0:T(8,128)(2,1)} %param.5, s32[]{:T(128)S(6)} %select_n.154), kind=kOutput, calls=%fused_computation.30 | convolution fusion | flops 419430400 | bytes 4259844 | tf_op jit(solution)/shard_map/dot_general | solution.py:63
  27.0 0.0 collective-permute-done.4
  27.1 2.5 %collective-permute-done.5 = bf16[5,128,128]{2,1,0:T(8,128)(2,1)S(1)} collective-permute-done((bf16[5,128,128]{2,1,0:T(8,128)(2,1)S(1)}, bf16[5,128,128]{2,1,0:T(8,128)(2,1)S(1)}, u32[]{:S(2)}, u32[]{:S(2)}) %collective-permute-start.5) | collective-permute-done | bytes 163872 | tf_op jit(solution)/shard_map/ppermute | solution.py:16
  29.5 1.6 %collective-permute-done.6 = bf16[5,128,128]{2,1,0:T(8,128)(2,1)S(1)} collective-permute-done((bf16[5,128,128]{2,1,0:T(8,128)(2,1)S(1)}, bf16[5,128,128]{2,1,0:T(8,128)(2,1)S(1)}, u32[]{:S(2)}, u32[]{:S(2)}) %collective-permute-start.6) | collective-permute-done | bytes 163872 | tf_op jit(solution)/shard_map/ppermute | solution.py:16
  31.1 0.1 fusion.57
  31.2 1.7 %collective-permute-start.7 = (bf16[5,128,128]{2,1,0:T(8,128)(2,1)S(1)}, bf16[5,128,128]{2,1,0:T(8,128)(2,1)S(1)}, u32[]{:S(2)}, u32[]{:S(2)}) collective-permute-start(bf16[5,128,128]{2,1,0:T(8,128)(2,1)S(1)} %fusion.57), channel_id=1, source_target_pairs={{0,32},{8,40},{16,48},{24,56},{32,64},{40,72},{48,80},{56,88},{64,... | collective-permute-start | bytes 491528 | tf_op jit(solution)/shard_map/ppermute | solution.py:16
  32.9 1.6 %collective-permute-start.8 = (bf16[5,128,128]{2,1,0:T(8,128)(2,1)S(1)}, bf16[5,128,128]{2,1,0:T(8,128)(2,1)S(1)}, u32[]{:S(2)}, u32[]{:S(2)}) collective-permute-start(bf16[5,128,128]{2,1,0:T(8,128)(2,1)S(1)} %fusion.57), channel_id=1, source_target_pairs={{0,64},{8,72},{16,80},{24,88},{32,96},{40,104},{48,112},{56,120},{... | collective-permute-start | bytes 491528 | tf_op jit(solution)/shard_map/ppermute | solution.py:16
  34.5 1.8 %collective-permute-start.9 = (bf16[5,128,128]{2,1,0:T(8,128)(2,1)S(1)}, bf16[5,128,128]{2,1,0:T(8,128)(2,1)S(1)}, u32[]{:S(2)}, u32[]{:S(2)}) collective-permute-start(bf16[5,128,128]{2,1,0:T(8,128)(2,1)S(1)} %fusion.57), channel_id=1, source_target_pairs={{0,96},{8,104},{16,112},{24,120},{32,0},{40,8},{48,16},{56,24},{64... | collective-permute-start | bytes 491528 | tf_op jit(solution)/shard_map/ppermute | solution.py:16
  36.2 1.8 %fusion.26 = f32[128,640]{1,0:T(8,128)S(1)} fusion(bf16[2560,640]{1,0:T(8,128)(2,1)S(1)} %copy-done.2, bf16[128,5120]{1,0:T(8,128)(2,1)} %collective-permute-done, s32[]{:T(128)S(6)} %select_n.154), kind=kOutput, calls=%fused_computation.36 | convolution fusion | flops 419430400 | bytes 4259844 | tf_op jit(solution)/shard_map/dot_general | solution.py:62
  38.0 0.1 collective-permute-start.2
  38.1 0.0 collective-permute-done.7
  38.2 3.2 %collective-permute-done.8 = bf16[5,128,128]{2,1,0:T(8,128)(2,1)S(1)} collective-permute-done((bf16[5,128,128]{2,1,0:T(8,128)(2,1)S(1)}, bf16[5,128,128]{2,1,0:T(8,128)(2,1)S(1)}, u32[]{:S(2)}, u32[]{:S(2)}) %collective-permute-start.8) | collective-permute-done | bytes 163872 | tf_op jit(solution)/shard_map/ppermute | solution.py:16
  41.3 1.8 %collective-permute-done.9 = bf16[5,128,128]{2,1,0:T(8,128)(2,1)S(1)} collective-permute-done((bf16[5,128,128]{2,1,0:T(8,128)(2,1)S(1)}, bf16[5,128,128]{2,1,0:T(8,128)(2,1)S(1)}, u32[]{:S(2)}, u32[]{:S(2)}) %collective-permute-start.9) | collective-permute-done | bytes 163872 | tf_op jit(solution)/shard_map/ppermute | solution.py:16
  43.1 0.8 fusion.40
  43.9 9.0 %collective-permute-start.10 = (bf16[5,128,128]{2,1,0:T(8,128)(2,1)}, bf16[5,128,128]{2,1,0:T(8,128)(2,1)}, u32[]{:S(2)}, u32[]{:S(2)}) collective-permute-start(bf16[5,128,128]{2,1,0:T(8,128)(2,1)} %fusion.40), channel_id=1, source_target_pairs={{0,128},{8,136},{16,144},{24,152},{32,160},{40,168},{48,176},{56,1... | collective-permute-start | bytes 491528 | tf_op jit(solution)/shard_map/ppermute | solution.py:16
  52.9 0.0 collective-permute-done.2
  53.0 0.8 multiply_convert_fusion.2
  53.7 1.7 %copy.12 = bf16[128,640]{0,1:T(8,128)(2,1)} copy(bf16[128,640]{1,0:T(8,128)(2,1)} %multiply_convert_fusion.2) | data formatting | bytes 327680 | tf_op jit(solution)/shard_map/convert_element_type | solution.py:67
  55.4 0.1 collective-permute-done.10
  55.5 2.5 %fusion.48 = f32[5,128,128]{2,1,0:T(8,128)} fusion(bf16[128,5,128]{0,2,1:T(8,128)(2,1)} %bitcast.47, bf16[5,128,128]{2,1,0:T(8,128)(2,1)} %copy-done.4, bf16[5,128,128]{2,1,0:T(8,128)(2,1)} %copy-done.5, bf16[5,128,128]{2,1,0:T(8,128)(2,1)} %copy-done.6, bf16[5,128,128]{2,1,0:T(8,128)(2,1)} %copy-done.7, bf16[5,128,128]{2,1,0:T(8,128)(2,1)} %copy-done.8, ...), kind=kOutput, calls=%fused_computation.90 | convolution fusion | flops 22609920 | bytes 1638406 | tf_op jit(solution)/shard_map/thd,hde->the/dot_general | solution.py:78
  58.0 2.3 %multiply_reduce_fusion = (f32[128,5]{0,1:T(8,128)S(1)}, f32[128,5,128]{0,2,1:T(8,128)}) fusion(f32[5,128,128]{2,1,0:T(8,128)} %fusion.48, bf16[128,5,128]{0,2,1:T(8,128)(2,1)S(1)} %bitcast.44, bf16[128,5,128]{0,2,1:T(8,128)(2,1)} %bitcast.48, bf16[128,5,128]{0,2,1:T(8,128)(2,1)} %bitcast.46, f32[128,128]{1,0:T(8,128)S(1)} %fusion.56), kind=kOutput, calls=%fused_computation.79 | convolution fusion | flops 42352000 | bytes 1214976 | tf_op jit(solution)/shard_map/hts,shd->thd/dot_general | solution.py:77
  60.3 1.0 multiply_convert_fusion
  61.4 4.3 %fusion.11 = (bf16[640,1280]{1,0:T(8,128)(2,1)S(1)}, bf16[640,1280]{1,0:T(8,128)(2,1)S(1)}, bf16[640,1280]{1,0:T(8,128)(2,1)S(1)}, bf16[640,1280]{1,0:T(8,128)(2,1)S(1)}) fusion(s32[]{:T(128)S(6)} %select_n.178, s32[]{:T(128)S(6)} %select_n.180, bf16[1,640,2560]{2,1,0:T(8,128)(2,1)} %bitcast.41, bf16[1,640,2560]{2,1,0:T(8,128)(2,1)} %bitcast.8, ...), kind=kLoop, calls=%fused_computation.19 | loop fusion | flops 13107200 | bytes 13107232 | tf_op jit(solution)/shard_map/squeeze | solution.py:96
  65.7 1.2 %fusion = f32[128,5120]{1,0:T(8,128)S(1)} fusion(bf16[128,640]{0,1:T(8,128)(2,1)S(1)} %bitcast.49, bf16[640,1280]{1,0:T(8,128)(2,1)S(1)} %get-tuple-element.32, bf16[640,1280]{1,0:T(8,128)(2,1)S(1)} %get-tuple-element.31, bf16[640,1280]{1,0:T(8,128)(2,1)S(1)} %get-tuple-element.30, bf16[640,1280]{1,0:T(8,128)(2,1)S(1)} %get-tuple-element.29), kind=kOutput, calls=%fused_computation.8 | convolution fusion | flops 865075200 | bytes 9338880 | tf_op jit(solution)/shard_map/dot_general | solution.py:98
  66.9 0.1 fusion.66
  67.0 6.5 %collective-permute-start.12 = (bf16[128,640]{1,0:T(8,128)(2,1)S(1)}, bf16[128,640]{1,0:T(8,128)(2,1)S(1)}, u32[]{:S(2)}, u32[]{:S(2)}) collective-permute-start(bf16[128,640]{1,0:T(8,128)(2,1)S(1)} %get-tuple-element.17), channel_id=1, source_target_pairs={{0,1},{4,5},{8,9},{12,13},{16,17},{20,21},{24,25},{28,29},{32,33},... | collective-permute-start | bytes 491528 | tf_op jit(solution)/shard_map/ppermute | solution.py:118
  73.5 0.7 collective-permute-start.13
  74.2 1.3 %collective-permute-start.18 = (bf16[128,640]{1,0:T(8,128)(2,1)S(1)}, bf16[128,640]{1,0:T(8,128)(2,1)S(1)}, u32[]{:S(2)}, u32[]{:S(2)}) collective-permute-start(bf16[128,640]{1,0:T(8,128)(2,1)S(1)} %get-tuple-element.23), channel_id=1, source_target_pairs={{0,1},{4,5},{8,9},{12,13},{16,17},{20,21},{24,25},{28,29},{32,33},... | collective-permute-start | bytes 491528 | tf_op jit(solution)/shard_map/ppermute | solution.py:118
  75.5 0.7 collective-permute-start.19
  76.2 1.8 %collective-permute-done.12 = bf16[128,640]{1,0:T(8,128)(2,1)S(1)} collective-permute-done((bf16[128,640]{1,0:T(8,128)(2,1)S(1)}, bf16[128,640]{1,0:T(8,128)(2,1)S(1)}, u32[]{:S(2)}, u32[]{:S(2)}) %collective-permute-start.12) | collective-permute-done | bytes 163872 | tf_op jit(solution)/shard_map/ppermute | solution.py:118
  77.9 0.1 add_convert_fusion.6
  78.0 4.4 %collective-permute-start.14 = (bf16[128,640]{1,0:T(8,128)(2,1)S(1)}, bf16[128,640]{1,0:T(8,128)(2,1)S(1)}, u32[]{:S(2)}, u32[]{:S(2)}) collective-permute-start(bf16[128,640]{1,0:T(8,128)(2,1)S(1)} %get-tuple-element.19), channel_id=1, source_target_pairs={{0,1},{1,2},{4,5},{5,6},{8,9},{9,10},{12,13},{13,14},{16,17},{17,1... | collective-permute-start | bytes 491528 | tf_op jit(solution)/shard_map/ppermute | solution.py:118
  82.4 0.7 collective-permute-start.15
  83.1 2.1 %collective-permute-done.14 = bf16[128,640]{1,0:T(8,128)(2,1)S(1)} collective-permute-done((bf16[128,640]{1,0:T(8,128)(2,1)S(1)}, bf16[128,640]{1,0:T(8,128)(2,1)S(1)}, u32[]{:S(2)}, u32[]{:S(2)}) %collective-permute-start.14) | collective-permute-done | bytes 163872 | tf_op jit(solution)/shard_map/ppermute | solution.py:118
  85.2 0.1 add_convert_fusion.4
  85.4 8.0 %collective-permute-start.20 = (bf16[128,640]{1,0:T(8,128)(2,1)S(1)}, bf16[128,640]{1,0:T(8,128)(2,1)S(1)}, u32[]{:S(2)}, u32[]{:S(2)}) collective-permute-start(bf16[128,640]{1,0:T(8,128)(2,1)S(1)} %get-tuple-element.25), channel_id=1, source_target_pairs={{0,1},{1,2},{4,5},{5,6},{8,9},{9,10},{12,13},{13,14},{16,17},{17,1... | collective-permute-start | bytes 491528 | tf_op jit(solution)/shard_map/ppermute | solution.py:118
  93.4 0.7 collective-permute-start.21
  94.0 2.5 %collective-permute-start.16 = (bf16[128,640]{1,0:T(8,128)(2,1)S(1)}, bf16[128,640]{1,0:T(8,128)(2,1)S(1)}, u32[]{:S(2)}, u32[]{:S(2)}) collective-permute-start(bf16[128,640]{1,0:T(8,128)(2,1)S(1)} %get-tuple-element.21), channel_id=1, source_target_pairs={{0,1},{1,2},{2,3},{4,5},{5,6},{6,7},{8,9},{9,10},{10,11},{12,13},{... | collective-permute-start | bytes 491528 | tf_op jit(solution)/shard_map/ppermute | solution.py:118
  96.6 1.3 %collective-permute-start.17 = (bf16[128,640]{1,0:T(8,128)(2,1)S(1)}, bf16[128,640]{1,0:T(8,128)(2,1)S(1)}, u32[]{:S(2)}, u32[]{:S(2)}) collective-permute-start(bf16[128,640]{1,0:T(8,128)(2,1)S(1)} %get-tuple-element.22), channel_id=1, source_target_pairs={{1,0},{2,1},{3,2},{5,4},{6,5},{7,6},{9,8},{10,9},{11,10},{13,12},{... | collective-permute-start | bytes 491528 | tf_op jit(solution)/shard_map/ppermute | solution.py:119
  97.9 1.5 %collective-permute-done.16 = bf16[128,640]{1,0:T(8,128)(2,1)S(1)} collective-permute-done((bf16[128,640]{1,0:T(8,128)(2,1)S(1)}, bf16[128,640]{1,0:T(8,128)(2,1)S(1)}, u32[]{:S(2)}, u32[]{:S(2)}) %collective-permute-start.16) | collective-permute-done | bytes 163872 | tf_op jit(solution)/shard_map/ppermute | solution.py:118
  99.4 5.0 %collective-permute-done.17 = bf16[128,640]{1,0:T(8,128)(2,1)S(1)} collective-permute-done((bf16[128,640]{1,0:T(8,128)(2,1)S(1)}, bf16[128,640]{1,0:T(8,128)(2,1)S(1)}, u32[]{:S(2)}, u32[]{:S(2)}) %collective-permute-start.17) | collective-permute-done | bytes 163872 | tf_op jit(solution)/shard_map/ppermute | solution.py:119
  104.4 0.1 fusion.45
  104.6 3.9 %collective-permute-start.22 = (bf16[128,640]{1,0:T(8,128)(2,1)S(1)}, bf16[128,640]{1,0:T(8,128)(2,1)S(1)}, u32[]{:S(2)}, u32[]{:S(2)}) collective-permute-start(bf16[128,640]{1,0:T(8,128)(2,1)S(1)} %get-tuple-element.27), channel_id=1, source_target_pairs={{0,1},{1,2},{2,3},{4,5},{5,6},{6,7},{8,9},{9,10},{10,11},{12,13},{... | collective-permute-start | bytes 491528 | tf_op jit(solution)/shard_map/ppermute | solution.py:118
  108.5 1.3 %collective-permute-start.23 = (bf16[128,640]{1,0:T(8,128)(2,1)S(1)}, bf16[128,640]{1,0:T(8,128)(2,1)S(1)}, u32[]{:S(2)}, u32[]{:S(2)}) collective-permute-start(bf16[128,640]{1,0:T(8,128)(2,1)S(1)} %get-tuple-element.28), channel_id=1, source_target_pairs={{1,0},{2,1},{3,2},{5,4},{6,5},{7,6},{9,8},{10,9},{11,10},{13,12},{... | collective-permute-start | bytes 491528 | tf_op jit(solution)/shard_map/ppermute | solution.py:119
  109.8 1.5 %collective-permute-done.22 = bf16[128,640]{1,0:T(8,128)(2,1)S(1)} collective-permute-done((bf16[128,640]{1,0:T(8,128)(2,1)S(1)}, bf16[128,640]{1,0:T(8,128)(2,1)S(1)}, u32[]{:S(2)}, u32[]{:S(2)}) %collective-permute-start.22) | collective-permute-done | bytes 163872 | tf_op jit(solution)/shard_map/ppermute | solution.py:118
  111.3 4.4 %collective-permute-done.23 = bf16[128,640]{1,0:T(8,128)(2,1)S(1)} collective-permute-done((bf16[128,640]{1,0:T(8,128)(2,1)S(1)}, bf16[128,640]{1,0:T(8,128)(2,1)S(1)}, u32[]{:S(2)}, u32[]{:S(2)}) %collective-permute-start.23) | collective-permute-done | bytes 163872 | tf_op jit(solution)/shard_map/ppermute | solution.py:119
  115.7 0.1 fusion.46
  115.8 0.8 pad_maximum_fusion
  (32 shorter events, 0.1 us)
Async XLA Ops:
  0.0 1.9 %copy-start = (bf16[2560,640]{1,0:T(8,128)(2,1)S(1)}, bf16[2560,640]{1,0:T(8,128)(2,1)}, u32[]{:S(2)}) copy-start(bf16[2560,640]{1,0:T(8,128)(2,1)} %param.8) | copy-start | bytes 9830404
  0.0 4.6 %collective-permute-start = (bf16[128,5120]{1,0:T(8,128)(2,1)}, bf16[128,5120]{1,0:T(8,128)(2,1)}, u32[]{:S(2)}, u32[]{:S(2)}) collective-permute-start(bf16[128,5120]{1,0:T(8,128)(2,1)} %bitcast.42), channel_id=1, source_target_pairs={{0,4},{4,0},{1,5},{5,1},{2,6},{6,2},{3,7},{7,3},{8,12},{12,8},{9,1... | collective-permute-start | bytes 3932168 | tf_op jit(solution)/shard_map/ppermute | solution.py:12
  0.0 61.3 %collective-permute-start.11 = (bf16[640,2560]{1,0:T(8,128)(2,1)}, bf16[640,2560]{1,0:T(8,128)(2,1)}, u32[]{:S(2)}, u32[]{:S(2)}) collective-permute-start(bf16[640,2560]{1,0:T(8,128)(2,1)} %param.9), channel_id=1, source_target_pairs={{0,4},{4,0},{1,5},{5,1},{2,6},{6,2},{3,7},{7,3},{8,12},{12,8},{9,1... | collective-permute-start | bytes 9830408 | tf_op jit(solution)/shard_map/ppermute | solution.py:12
  1.9 5.3 %copy-start.1 = (bf16[2560,640]{1,0:T(8,128)(2,1)S(1)}, bf16[2560,640]{1,0:T(8,128)(2,1)}, u32[]{:S(2)}) copy-start(bf16[2560,640]{1,0:T(8,128)(2,1)} %param.7) | copy-start | bytes 9830404
  4.6 5.6 %copy-start.3 = (bf16[1,128,5120]{2,1,0:T(8,128)(2,1)S(1)}, bf16[1,128,5120]{2,1,0:T(8,128)(2,1)}, u32[]{:S(2)}) copy-start(bf16[1,128,5120]{2,1,0:T(8,128)(2,1)} %param.5) | copy-start | bytes 3932164
  7.2 4.4 %collective-permute-start.1 = (f32[128,640]{1,0:T(8,128)}, f32[128,640]{1,0:T(8,128)}, u32[]{:S(2)}, u32[]{:S(2)}) collective-permute-start(f32[128,640]{1,0:T(8,128)} %fusion.28), channel_id=1, source_target_pairs={{0,4},{4,0},{1,5},{5,1},{2,6},{6,2},{3,7},{7,3},{8,12},{12,8},{9,1... | collective-permute-start | bytes 983048 | tf_op jit(solution)/shard_map/ppermute | solution.py:12
  9.7 4.8 %collective-permute-start.3 = (f32[128,640]{1,0:T(8,128)}, f32[128,640]{1,0:T(8,128)}, u32[]{:S(2)}, u32[]{:S(2)}) collective-permute-start(f32[128,640]{1,0:T(8,128)} %fusion.24), channel_id=1, source_target_pairs={{0,4},{4,0},{1,5},{5,1},{2,6},{6,2},{3,7},{7,3},{8,12},{12,8},{9,1... | collective-permute-start | bytes 983048 | tf_op jit(solution)/shard_map/ppermute | solution.py:12
  18.1 18.2 %copy-start.2 = (bf16[2560,640]{1,0:T(8,128)(2,1)S(1)}, bf16[2560,640]{1,0:T(8,128)(2,1)}, u32[]{:S(2)}) copy-start(bf16[2560,640]{1,0:T(8,128)(2,1)} %param.6) | copy-start | bytes 9830404
  19.4 7.7 %collective-permute-start.4 = (bf16[5,128,128]{2,1,0:T(8,128)(2,1)S(1)}, bf16[5,128,128]{2,1,0:T(8,128)(2,1)S(1)}, u32[]{:S(2)}, u32[]{:S(2)}) collective-permute-start(bf16[5,128,128]{2,1,0:T(8,128)(2,1)S(1)} %get-tuple-element.46), channel_id=1, source_target_pairs={{0,8},{8,16},{16,24},{24,0},{32,40},{40,48},{48,56},{56,32},{64,72... | collective-permute-start | bytes 491528 | tf_op jit(solution)/shard_map/ppermute | solution.py:16
  20.9 8.6 %collective-permute-start.5 = (bf16[5,128,128]{2,1,0:T(8,128)(2,1)S(1)}, bf16[5,128,128]{2,1,0:T(8,128)(2,1)S(1)}, u32[]{:S(2)}, u32[]{:S(2)}) collective-permute-start(bf16[5,128,128]{2,1,0:T(8,128)(2,1)S(1)} %get-tuple-element.46), channel_id=1, source_target_pairs={{0,16},{8,24},{16,0},{24,8},{32,48},{40,56},{48,32},{56,40},{64,80... | collective-permute-start | bytes 491528 | tf_op jit(solution)/shard_map/ppermute | solution.py:16
  22.0 9.1 %collective-permute-start.6 = (bf16[5,128,128]{2,1,0:T(8,128)(2,1)S(1)}, bf16[5,128,128]{2,1,0:T(8,128)(2,1)S(1)}, u32[]{:S(2)}, u32[]{:S(2)}) collective-permute-start(bf16[5,128,128]{2,1,0:T(8,128)(2,1)S(1)} %get-tuple-element.46), channel_id=1, source_target_pairs={{0,24},{8,0},{16,8},{24,16},{32,56},{40,32},{48,40},{56,48},{64,88... | collective-permute-start | bytes 491528 | tf_op jit(solution)/shard_map/ppermute | solution.py:16
  27.0 16.9 %copy-start.4 = (bf16[5,128,128]{2,1,0:T(8,128)(2,1)}, bf16[5,128,128]{2,1,0:T(8,128)(2,1)S(1)}, u32[]{:S(2)}) copy-start(bf16[5,128,128]{2,1,0:T(8,128)(2,1)S(1)} %collective-permute-done.4) | copy-start | bytes 491524
  29.5 14.4 %copy-start.5 = (bf16[5,128,128]{2,1,0:T(8,128)(2,1)}, bf16[5,128,128]{2,1,0:T(8,128)(2,1)S(1)}, u32[]{:S(2)}) copy-start(bf16[5,128,128]{2,1,0:T(8,128)(2,1)S(1)} %collective-permute-done.5) | copy-start | bytes 491524
  31.1 12.8 %copy-start.6 = (bf16[5,128,128]{2,1,0:T(8,128)(2,1)}, bf16[5,128,128]{2,1,0:T(8,128)(2,1)S(1)}, u32[]{:S(2)}) copy-start(bf16[5,128,128]{2,1,0:T(8,128)(2,1)S(1)} %collective-permute-done.6) | copy-start | bytes 491524
  31.2 6.9 %collective-permute-start.7 = (bf16[5,128,128]{2,1,0:T(8,128)(2,1)S(1)}, bf16[5,128,128]{2,1,0:T(8,128)(2,1)S(1)}, u32[]{:S(2)}, u32[]{:S(2)}) collective-permute-start(bf16[5,128,128]{2,1,0:T(8,128)(2,1)S(1)} %fusion.57), channel_id=1, source_target_pairs={{0,32},{8,40},{16,48},{24,56},{32,64},{40,72},{48,80},{56,88},{64,... | collective-permute-start | bytes 491528 | tf_op jit(solution)/shard_map/ppermute | solution.py:16
  32.9 8.4 %collective-permute-start.8 = (bf16[5,128,128]{2,1,0:T(8,128)(2,1)S(1)}, bf16[5,128,128]{2,1,0:T(8,128)(2,1)S(1)}, u32[]{:S(2)}, u32[]{:S(2)}) collective-permute-start(bf16[5,128,128]{2,1,0:T(8,128)(2,1)S(1)} %fusion.57), channel_id=1, source_target_pairs={{0,64},{8,72},{16,80},{24,88},{32,96},{40,104},{48,112},{56,120},{... | collective-permute-start | bytes 491528 | tf_op jit(solution)/shard_map/ppermute | solution.py:16
  34.5 8.6 %collective-permute-start.9 = (bf16[5,128,128]{2,1,0:T(8,128)(2,1)S(1)}, bf16[5,128,128]{2,1,0:T(8,128)(2,1)S(1)}, u32[]{:S(2)}, u32[]{:S(2)}) collective-permute-start(bf16[5,128,128]{2,1,0:T(8,128)(2,1)S(1)} %fusion.57), channel_id=1, source_target_pairs={{0,96},{8,104},{16,112},{24,120},{32,0},{40,8},{48,16},{56,24},{64... | collective-permute-start | bytes 491528 | tf_op jit(solution)/shard_map/ppermute | solution.py:16
  38.0 14.9 %collective-permute-start.2 = (f32[128,640]{1,0:T(8,128)S(1)}, f32[128,640]{1,0:T(8,128)S(1)}, u32[]{:S(2)}, u32[]{:S(2)}) collective-permute-start(f32[128,640]{1,0:T(8,128)S(1)} %fusion.26), channel_id=1, source_target_pairs={{0,4},{4,0},{1,5},{5,1},{2,6},{6,2},{3,7},{7,3},{8,12},{12,8},{9,1... | collective-permute-start | bytes 983048 | tf_op jit(solution)/shard_map/ppermute | solution.py:12
  38.1 14.8 %copy-start.7 = (bf16[5,128,128]{2,1,0:T(8,128)(2,1)}, bf16[5,128,128]{2,1,0:T(8,128)(2,1)S(1)}, u32[]{:S(2)}) copy-start(bf16[5,128,128]{2,1,0:T(8,128)(2,1)S(1)} %collective-permute-done.7) | copy-start | bytes 491524
  41.3 11.6 %copy-start.8 = (bf16[5,128,128]{2,1,0:T(8,128)(2,1)}, bf16[5,128,128]{2,1,0:T(8,128)(2,1)S(1)}, u32[]{:S(2)}) copy-start(bf16[5,128,128]{2,1,0:T(8,128)(2,1)S(1)} %collective-permute-done.8) | copy-start | bytes 491524
  43.1 9.9 %copy-start.9 = (bf16[5,128,128]{2,1,0:T(8,128)(2,1)}, bf16[5,128,128]{2,1,0:T(8,128)(2,1)S(1)}, u32[]{:S(2)}) copy-start(bf16[5,128,128]{2,1,0:T(8,128)(2,1)S(1)} %collective-permute-done.9) | copy-start | bytes 491524
  43.9 11.6 %collective-permute-start.10 = (bf16[5,128,128]{2,1,0:T(8,128)(2,1)}, bf16[5,128,128]{2,1,0:T(8,128)(2,1)}, u32[]{:S(2)}, u32[]{:S(2)}) collective-permute-start(bf16[5,128,128]{2,1,0:T(8,128)(2,1)} %fusion.40), channel_id=1, source_target_pairs={{0,128},{8,136},{16,144},{24,152},{32,160},{40,168},{48,176},{56,1... | collective-permute-start | bytes 491528 | tf_op jit(solution)/shard_map/ppermute | solution.py:16
  67.0 10.9 %collective-permute-start.12 = (bf16[128,640]{1,0:T(8,128)(2,1)S(1)}, bf16[128,640]{1,0:T(8,128)(2,1)S(1)}, u32[]{:S(2)}, u32[]{:S(2)}) collective-permute-start(bf16[128,640]{1,0:T(8,128)(2,1)S(1)} %get-tuple-element.17), channel_id=1, source_target_pairs={{0,1},{4,5},{8,9},{12,13},{16,17},{20,21},{24,25},{28,29},{32,33},... | collective-permute-start | bytes 491528 | tf_op jit(solution)/shard_map/ppermute | solution.py:118
  73.5 4.4 %collective-permute-start.13 = (bf16[128,640]{1,0:T(8,128)(2,1)S(1)}, bf16[128,640]{1,0:T(8,128)(2,1)S(1)}, u32[]{:S(2)}, u32[]{:S(2)}) collective-permute-start(bf16[128,640]{1,0:T(8,128)(2,1)S(1)} %get-tuple-element.18), channel_id=1, source_target_pairs={{3,2},{7,6},{11,10},{15,14},{19,18},{23,22},{27,26},{31,30},{35,34... | collective-permute-start | bytes 491528 | tf_op jit(solution)/shard_map/ppermute | solution.py:119
  74.2 8.9 %collective-permute-start.18 = (bf16[128,640]{1,0:T(8,128)(2,1)S(1)}, bf16[128,640]{1,0:T(8,128)(2,1)S(1)}, u32[]{:S(2)}, u32[]{:S(2)}) collective-permute-start(bf16[128,640]{1,0:T(8,128)(2,1)S(1)} %get-tuple-element.23), channel_id=1, source_target_pairs={{0,1},{4,5},{8,9},{12,13},{16,17},{20,21},{24,25},{28,29},{32,33},... | collective-permute-start | bytes 491528 | tf_op jit(solution)/shard_map/ppermute | solution.py:118
  75.5 7.6 %collective-permute-start.19 = (bf16[128,640]{1,0:T(8,128)(2,1)S(1)}, bf16[128,640]{1,0:T(8,128)(2,1)S(1)}, u32[]{:S(2)}, u32[]{:S(2)}) collective-permute-start(bf16[128,640]{1,0:T(8,128)(2,1)S(1)} %get-tuple-element.24), channel_id=1, source_target_pairs={{3,2},{7,6},{11,10},{15,14},{19,18},{23,22},{27,26},{31,30},{35,34... | collective-permute-start | bytes 491528 | tf_op jit(solution)/shard_map/ppermute | solution.py:119
  78.0 7.2 %collective-permute-start.14 = (bf16[128,640]{1,0:T(8,128)(2,1)S(1)}, bf16[128,640]{1,0:T(8,128)(2,1)S(1)}, u32[]{:S(2)}, u32[]{:S(2)}) collective-permute-start(bf16[128,640]{1,0:T(8,128)(2,1)S(1)} %get-tuple-element.19), channel_id=1, source_target_pairs={{0,1},{1,2},{4,5},{5,6},{8,9},{9,10},{12,13},{13,14},{16,17},{17,1... | collective-permute-start | bytes 491528 | tf_op jit(solution)/shard_map/ppermute | solution.py:118
  82.4 2.8 %collective-permute-start.15 = (bf16[128,640]{1,0:T(8,128)(2,1)S(1)}, bf16[128,640]{1,0:T(8,128)(2,1)S(1)}, u32[]{:S(2)}, u32[]{:S(2)}) collective-permute-start(bf16[128,640]{1,0:T(8,128)(2,1)S(1)} %get-tuple-element.20), channel_id=1, source_target_pairs={{2,1},{3,2},{6,5},{7,6},{10,9},{11,10},{14,13},{15,14},{18,17},{19... | collective-permute-start | bytes 491528 | tf_op jit(solution)/shard_map/ppermute | solution.py:119
  85.4 12.5 %collective-permute-start.20 = (bf16[128,640]{1,0:T(8,128)(2,1)S(1)}, bf16[128,640]{1,0:T(8,128)(2,1)S(1)}, u32[]{:S(2)}, u32[]{:S(2)}) collective-permute-start(bf16[128,640]{1,0:T(8,128)(2,1)S(1)} %get-tuple-element.25), channel_id=1, source_target_pairs={{0,1},{1,2},{4,5},{5,6},{8,9},{9,10},{12,13},{13,14},{16,17},{17,1... | collective-permute-start | bytes 491528 | tf_op jit(solution)/shard_map/ppermute | solution.py:118
  93.4 4.5 %collective-permute-start.21 = (bf16[128,640]{1,0:T(8,128)(2,1)S(1)}, bf16[128,640]{1,0:T(8,128)(2,1)S(1)}, u32[]{:S(2)}, u32[]{:S(2)}) collective-permute-start(bf16[128,640]{1,0:T(8,128)(2,1)S(1)} %get-tuple-element.26), channel_id=1, source_target_pairs={{2,1},{3,2},{6,5},{7,6},{10,9},{11,10},{14,13},{15,14},{18,17},{19... | collective-permute-start | bytes 491528 | tf_op jit(solution)/shard_map/ppermute | solution.py:119
  94.0 5.4 %collective-permute-start.16 = (bf16[128,640]{1,0:T(8,128)(2,1)S(1)}, bf16[128,640]{1,0:T(8,128)(2,1)S(1)}, u32[]{:S(2)}, u32[]{:S(2)}) collective-permute-start(bf16[128,640]{1,0:T(8,128)(2,1)S(1)} %get-tuple-element.21), channel_id=1, source_target_pairs={{0,1},{1,2},{2,3},{4,5},{5,6},{6,7},{8,9},{9,10},{10,11},{12,13},{... | collective-permute-start | bytes 491528 | tf_op jit(solution)/shard_map/ppermute | solution.py:118
  96.6 7.8 %collective-permute-start.17 = (bf16[128,640]{1,0:T(8,128)(2,1)S(1)}, bf16[128,640]{1,0:T(8,128)(2,1)S(1)}, u32[]{:S(2)}, u32[]{:S(2)}) collective-permute-start(bf16[128,640]{1,0:T(8,128)(2,1)S(1)} %get-tuple-element.22), channel_id=1, source_target_pairs={{1,0},{2,1},{3,2},{5,4},{6,5},{7,6},{9,8},{10,9},{11,10},{13,12},{... | collective-permute-start | bytes 491528 | tf_op jit(solution)/shard_map/ppermute | solution.py:119
  104.6 6.7 %collective-permute-start.22 = (bf16[128,640]{1,0:T(8,128)(2,1)S(1)}, bf16[128,640]{1,0:T(8,128)(2,1)S(1)}, u32[]{:S(2)}, u32[]{:S(2)}) collective-permute-start(bf16[128,640]{1,0:T(8,128)(2,1)S(1)} %get-tuple-element.27), channel_id=1, source_target_pairs={{0,1},{1,2},{2,3},{4,5},{5,6},{6,7},{8,9},{9,10},{10,11},{12,13},{... | collective-permute-start | bytes 491528 | tf_op jit(solution)/shard_map/ppermute | solution.py:118
  108.5 7.2 %collective-permute-start.23 = (bf16[128,640]{1,0:T(8,128)(2,1)S(1)}, bf16[128,640]{1,0:T(8,128)(2,1)S(1)}, u32[]{:S(2)}, u32[]{:S(2)}) collective-permute-start(bf16[128,640]{1,0:T(8,128)(2,1)S(1)} %get-tuple-element.28), channel_id=1, source_target_pairs={{1,0},{2,1},{3,2},{5,4},{6,5},{7,6},{9,8},{10,9},{11,10},{13,12},{... | collective-permute-start | bytes 491528 | tf_op jit(solution)/shard_map/ppermute | solution.py:119

commit v11 on v8

--- a/solution.py
+++ b/solution.py
@@ -16,38 +16,25 @@
     return lax.ppermute(x, axis, pairs)
 
 
-def prefix_over_seq(state, seq_size):
-    nx, ny = 4, 4
-    nz = seq_size // (nx * ny)
-    i = lax.axis_index("seq")
-    x = i % nx
-    y = (i // nx) % ny
-
-    def along(value, stride, size, pos):
-        sent = value.astype(BF16)
-        before = jnp.zeros_like(value)
-        total = value
-        for d in range(1, size):
-            pairs = []
-            for j in range(seq_size):
-                jp = (j // stride) % size
-                pairs.append((j, j + (((jp + d) % size) - jp) * stride))
-            got = shifted(sent, "seq", pairs).astype(F32)
-            before = before + jnp.where((pos - d) % size < pos, got, 0.0)
-            total = total + got
+def prefix_over_seq(state):
+    def along(value, axis):
+        size = lax.psum(1, axis)
+        pos = lax.axis_index(axis)
+        sent = jnp.broadcast_to(value.astype(BF16)[None], (size,) + value.shape)
+        got = lax.all_to_all(sent, axis, 0, 0).astype(F32)
+        order = lax.broadcasted_iota(jnp.int32, (size,) + (1,) * value.ndim, 0)
+        before = jnp.sum(jnp.where(order < pos, got, 0.0), axis=0)
+        total = jnp.sum(got, axis=0)
         return before, total
 
-    ex, row_total = along(state, 1, nx, x)
-    ey, plane_total = along(row_total, nx, ny, y)
-    ez = jnp.zeros_like(state)
-    if nz > 1:
-        plane = nx * ny
-        zpairs = [(j, j + plane) for j in range(seq_size - plane)]
-        ez = shifted(plane_total.astype(BF16), "seq", zpairs).astype(F32)
+    ex, row_total = along(state, "x")
+    ey, plane_total = along(row_total, "y")
+    nz = lax.psum(1, "zh")
+    ez = lax.ppermute(plane_total.astype(BF16), "zh", [(j, j + 1) for j in range(nz - 1)]).astype(F32)
     return ex + ey + ez
 
 
-def shards(seq_size, tokens, w_query, w_key, w_value, w_output):
+def shards(tokens, w_query, w_key, w_value, w_output):
     rows_in = tokens.reshape(tokens.shape[1], tokens.shape[2])
     tok_count = rows_in.shape[0]
     half = w_query.shape[0]
@@ -68,7 +55,7 @@
     keys_all = jax.nn.silu(key_sum).astype(BF16).reshape(tok_count, head_count, HD)
     values = value_sum.astype(BF16).reshape(tok_count, head_count, HD)
     local_state = jnp.einsum("thd,the->hde", keys_all, values, preferred_element_type=F32)
-    prefix_state = prefix_over_seq(local_state, seq_size)
+    prefix_state = prefix_over_seq(local_state)
 
     scores = jnp.einsum("thd,shd->hts", queries, keys_all, preferred_element_type=F32)
     positions = jnp.arange(tok_count)
@@ -115,19 +102,26 @@
 
 
 def solution(mesh):
-    import functools
+    from jax.sharding import Mesh
 
+    seq_size = mesh.shape["seq"]
+    nz = seq_size // 16
+    split = Mesh(
+        mesh.devices.reshape(nz, 4, 4, mesh.shape["wt"], mesh.shape["head"]),
+        ("zh", "y", "x", "wt", "head"),
+    )
+    seq = ("zh", "y", "x")
     placed = (
-        P("wt", "seq", None),
+        P("wt", seq, None),
         P("wt", "head"),
         P("wt", "head"),
         P("wt", "head"),
         P("head", "wt"),
     )
     return jax.shard_map(
-        functools.partial(shards, mesh.shape["seq"]),
-        mesh=mesh,
+        shards,
+        mesh=split,
         in_specs=placed,
-        out_specs=P("wt", "seq", "head"),
+        out_specs=P("wt", seq, "head"),
         check_vma=False,
     )

time: 108 us -> 111 us (1.028); the launches traced: 107 us -> 109 us
  other arithmetic: 11.8 us -> 16.6 us
  starting transfers between devices: 41.3 us -> 39.5 us
  waiting for transfers between devices: 26.9 us -> 25.6 us
    ppermute x7 -> x1, starting transfers between devices: 18.9 us -> 7.31 us  [prefix_over_seq(): lax.ppermute(plane_total.astype(BF16), 'zh', [(j, j + 1) for j in range(n...]
    all_to_all x0 -> x2, starting transfers between devices: none -> 11.1 us  [along(): got = lax.all_to_all(sent, axis, 0, 0).astype(F32)]
    all_to_all x0 -> x2, waiting for transfers between devices: none -> 9.71 us  [along(): got = lax.all_to_all(sent, axis, 0, 0).astype(F32)]
    ppermute x7 -> x1, waiting for transfers between devices: 9.08 us -> 0.49 us  [prefix_over_seq(): lax.ppermute(plane_total.astype(BF16), 'zh', [(j, j + 1) for j in range(n...]
    reduce_sum x0 -> x4, other arithmetic: none -> 5.73 us  [the longest x2 3.1 us: along(): total = jnp.sum(got, axis=0)]
    ppermute x3, waiting for transfers between devices: 13.4 us -> 11 us  [shards(): right = lax.ppermute(send_r, 'head', rpairs).astype(F32)]
    broadcast_in_dim x0 -> x2, local copies, waits for them, and re-layouts: none -> 1.97 us  [along(): sent = jnp.broadcast_to(value.astype(BF16)[None], (size,) + value.shape)]
    dot_general x1, matrix products: 2.51 us -> 0.99 us  [shards(): jnp.einsum('thd,hde->the', queries.astype(F32), prefix_state.astype(BF16)...]
  transfers between devices with their start and end apart: 18 -> 14, of which waited for: 9 -> 7; matrix products, arithmetic and copies ran while one was open for 29% -> 34% of each run, Pallas kernels for 0% -> 0%
where the time goes in v11:
time: 111 us; the launch traced here: 109 us
  starting transfers between devices  39.5 us (36%)
  waiting for transfers between devices  25.6 us (23%)
  matrix products  21 us (19%)
  other arithmetic  16.6 us (15%)
  local copies, waits for them, and re-layouts  5.93 us (5%)
    ppermute x3, starting transfers between devices, shards(): right = lax.ppermute(send_r, 'head', rpairs).astype(F32)  17.4 us
    all_to_all x2, starting transfers between devices, along(): got = lax.all_to_all(sent, axis, 0, 0).astype(F32)  11.1 us
    ppermute x3, waiting for transfers between devices, shards(): right = lax.ppermute(send_r, 'head', rpairs).astype(F32)  11 us
    all_to_all x2, waiting for transfers between devices, along(): got = lax.all_to_all(sent, axis, 0, 0).astype(F32)  9.71 us
    dot_general x3, matrix products, shards(): lent = swap_cores(jnp.dot(got_cols, w, preferred_element_type=F32))  8.08 us
    ppermute x1, starting transfers between devices, prefix_over_seq(): lax.ppermute(plane_total.astype(BF16), 'zh', [(j, j + 1) for j in range(n...  7.31 us
    dot_general x3, matrix products, shards(): own = jnp.dot(mine_cols, w, preferred_element_type=F32)  7.28 us
    ppermute x3, waiting for transfers between devices, shards(): left = lax.ppermute(send_l, 'head', lpairs).astype(F32)  4.42 us
  transfers between devices with their start and end apart: 14, of which 7 were waited for; matrix products, arithmetic and copies ran while one was open for 34% of the time, Pallas kernels for 0%

profile of v11, /device:TPU:10, one launch (start us, length us, event | category | flops | bytes accessed | tf_op | source)
XLA Modules:
  0.0 109.1 jit_solution(4832502294556011329)
XLA Ops:
  0.0 0.0 copy-start
  0.0 0.0 collective-permute-start
  0.0 0.5 collective-permute-start.5
  0.5 0.0 copy-start.2
  0.5 3.8 %fusion.20 = f32[128,640]{1,0:T(8,128)} fusion(bf16[2560,640]{1,0:T(8,128)(2,1)} %param.7, bf16[1,128,5120]{2,1,0:T(8,128)(2,1)} %param.5, s32[]{:T(128)S(6)} %select_n.88), kind=kOutput, calls=%fused_computation.34 | convolution fusion | flops 419430400 | bytes 4259844 | tf_op jit(solution)/shard_map/dot_general | solution.py:50
  4.3 0.0 copy-done
  4.3 0.0 copy-done.2
  4.3 0.0 copy-start.1
  4.3 0.7 fusion.24
  5.0 0.0 collective-permute-done
  5.0 2.0 %fusion.30 = f32[128,640]{1,0:T(8,128)S(1)} fusion(bf16[2560,640]{1,0:T(8,128)(2,1)S(1)} %copy-done, bf16[128,5120]{1,0:T(8,128)(2,1)} %collective-permute-done, s32[]{:T(128)S(6)} %select_n.88), kind=kOutput, calls=%fused_computation.50 | convolution fusion | flops 419430400 | bytes 4259844 | tf_op jit(solution)/shard_map/dot_general | solution.py:49
  7.1 0.1 collective-permute-start.1
  7.2 0.0 copy-done.1
  7.2 2.5 %fusion.26 = f32[128,640]{1,0:T(8,128)} fusion(bf16[2560,640]{1,0:T(8,128)(2,1)S(1)} %copy-done.1, bf16[128,5120]{1,0:T(8,128)(2,1)} %collective-permute-done, s32[]{:T(128)S(6)} %select_n.88), kind=kOutput, calls=%fused_computation.46 | convolution fusion | flops 419430400 | bytes 4259844 | tf_op jit(solution)/shard_map/dot_general | solution.py:49
  9.7 0.4 collective-permute-start.3
  10.2 0.0 collective-permute-done.1
  10.2 0.7 add_convert_fusion.5
  10.9 1.1 copy.15
  12.0 0.0 copy-start.3
  12.0 0.0 collective-permute-done.3
  12.0 1.9 %multiply_convert_fusion.1 = bf16[128,640]{1,0:T(8,128)(2,1)} fusion(f32[128,640]{1,0:T(8,128)} %fusion.20, f32[128,640]{1,0:T(8,128)} %collective-permute-done.3), kind=kLoop, calls=%fused_computation.59 | loop fusion | flops 491520 | bytes 819200 | tf_op jit(solution)/shard_map/convert_element_type | solution.py:55
  13.9 1.7 %copy.17 = bf16[128,640]{0,1:T(8,128)(2,1)} copy(bf16[128,640]{1,0:T(8,128)(2,1)} %multiply_convert_fusion.1) | data formatting | bytes 327680 | tf_op jit(solution)/shard_map/convert_element_type | solution.py:55
  15.6 1.1 %convolution_convert_fusion = bf16[5,128,128]{2,1,0:T(8,128)(2,1)S(1)} fusion(bf16[128,5,128]{0,2,1:T(8,128)(2,1)} %bitcast.45, bf16[128,5,128]{0,2,1:T(8,128)(2,1)S(1)} %bitcast.43), kind=kOutput, calls=%fused_computation.30 | convolution fusion | flops 21053440 | bytes 491520 | tf_op jit(solution)/shard_map/thd,the->hde/dot_general | solution.py:57
  16.8 1.0 broadcast_in_dim.35
  17.8 4.8 %all-to-all-start = ((bf16[4,5,128,128]{3,2,1,0:T(8,128)(2,1)}), bf16[4,5,128,128]{3,2,1,0:T(8,128)(2,1)}, u32[]{:S(2)}, u32[]{:S(2)}) async-start(bf16[4,5,128,128]{3,2,1,0:T(8,128)(2,1)} %broadcast_in_dim.35), calls=%async_computation | async-start | bytes 1310720 | tf_op jit(solution)/shard_map/all_to_all | solution.py:24
  22.6 3.5 %fusion.28 = f32[128,640]{1,0:T(8,128)} fusion(bf16[2560,640]{1,0:T(8,128)(2,1)} %param.6, bf16[128,5120]{1,0:T(8,128)(2,1)} %collective-permute-done, s32[]{:T(128)S(6)} %select_n.88), kind=kOutput, calls=%fused_computation.48 | convolution fusion | flops 419430400 | bytes 4259844 | tf_op jit(solution)/shard_map/dot_general | solution.py:49
  26.1 0.0 copy-done.3
  26.1 0.0 collective-permute-start.2
  26.3 6.2 %all-to-all-done = bf16[4,5,128,128]{3,2,1,0:T(8,128)(2,1)} async-done(((bf16[4,5,128,128]{3,2,1,0:T(8,128)(2,1)}), bf16[4,5,128,128]{3,2,1,0:T(8,128)(2,1)}, u32[]{:S(2)}, u32[]{:S(2)}) %all-to-all-start) | async-done | bytes 655392 | tf_op jit(solution)/shard_map/all_to_all | solution.py:24
  32.5 1.2 %reduce_sum.52 = bf16[5,128,128]{2,1,0:T(8,128)(2,1)S(1)} reduce(bf16[4,5,128,128]{3,2,1,0:T(8,128)(2,1)} %all-to-all-done, bf16[]{:T(256)} %constant.114.clone.1), dimensions={0}, to_apply=%region_1.2 | reduce | flops 245760 | bytes 819202 | tf_op jit(solution)/shard_map/reduce_sum | solution.py:27
  33.7 1.0 broadcast_in_dim.38
  34.7 6.3 %all-to-all-start.1 = ((bf16[4,5,128,128]{3,2,1,0:T(8,128)(2,1)}), bf16[4,5,128,128]{3,2,1,0:T(8,128)(2,1)}, u32[]{:S(2)}, u32[]{:S(2)}) async-start(bf16[4,5,128,128]{3,2,1,0:T(8,128)(2,1)} %broadcast_in_dim.38), calls=%async_computation.1 | async-start | bytes 1310720 | tf_op jit(solution)/shard_map/all_to_all | solution.py:24
  40.9 2.8 %fusion.22 = f32[128,640]{1,0:T(8,128)S(1)} fusion(bf16[2560,640]{1,0:T(8,128)(2,1)} %param.6, bf16[1,128,5120]{2,1,0:T(8,128)(2,1)} %param.5, s32[]{:T(128)S(6)} %select_n.88), kind=kOutput, calls=%fused_computation.36 | convolution fusion | flops 419430400 | bytes 4259844 | tf_op jit(solution)/shard_map/dot_general | solution.py:50
  43.8 0.0 collective-permute-done.2
  43.8 1.7 %multiply_convert_fusion.2 = bf16[128,640]{1,0:T(8,128)(2,1)} fusion(f32[128,640]{1,0:T(8,128)S(1)} %fusion.22, f32[128,640]{1,0:T(8,128)} %collective-permute-done.2), kind=kLoop, calls=%fused_computation.60 | loop fusion | flops 491520 | bytes 819200 | tf_op jit(solution)/shard_map/convert_element_type | solution.py:54
  45.5 1.1 copy.16
  46.6 3.6 %all-to-all-done.1 = bf16[4,5,128,128]{3,2,1,0:T(8,128)(2,1)} async-done(((bf16[4,5,128,128]{3,2,1,0:T(8,128)(2,1)}), bf16[4,5,128,128]{3,2,1,0:T(8,128)(2,1)}, u32[]{:S(2)}, u32[]{:S(2)}) %all-to-all-start.1) | async-done | bytes 655392 | tf_op jit(solution)/shard_map/all_to_all | solution.py:24
  50.1 1.9 %reduce_sum.54 = bf16[5,128,128]{2,1,0:T(8,128)(2,1)} reduce(bf16[4,5,128,128]{3,2,1,0:T(8,128)(2,1)} %all-to-all-done.1, bf16[]{:T(256)} %constant.114.clone.1), dimensions={0}, to_apply=%region_3.4 | reduce | flops 245760 | bytes 819202 | tf_op jit(solution)/shard_map/reduce_sum | solution.py:27
  52.0 7.3 %collective-permute-start.4 = (bf16[5,128,128]{2,1,0:T(8,128)(2,1)}, bf16[5,128,128]{2,1,0:T(8,128)(2,1)S(1)}, u32[]{:S(2)}, u32[]{:S(2)}) collective-permute-start(bf16[5,128,128]{2,1,0:T(8,128)(2,1)} %reduce_sum.54), channel_id=1, source_target_pairs={{0,128},{1,129},{2,130},{3,131},{4,132},{5,133},{6,134},{7,135},{8... | collective-permute-start | bytes 491528 | tf_op jit(solution)/shard_map/ppermute | solution.py:33
  59.4 1.3 %select_reduce_fusion.1 = f32[5,128,128]{2,1,0:T(8,128)S(1)} fusion(bf16[4,5,128,128]{3,2,1,0:T(8,128)(2,1)} %all-to-all-done, pred[4]{0:T(512)(128)(4,1)S(1)} %iota_compare_fusion.2), kind=kLoop, calls=%fused_computation.25 | loop fusion | flops 901120 | bytes 983044 | tf_op jit(solution)/shard_map/reduce_sum | solution.py:26
  60.7 1.3 %select_reduce_fusion = f32[5,128,128]{2,1,0:T(8,128)S(1)} fusion(bf16[4,5,128,128]{3,2,1,0:T(8,128)(2,1)} %all-to-all-done.1, pred[4]{0:T(512)(128)(4,1)S(1)} %iota_compare_fusion.1), kind=kLoop, calls=%fused_computation.24 | loop fusion | flops 901120 | bytes 983044 | tf_op jit(solution)/shard_map/reduce_sum | solution.py:26
  62.0 0.5 collective-permute-done.4
  62.5 1.0 fusion.36
  63.5 2.3 %multiply_reduce_fusion = (f32[128,5]{0,1:T(8,128)S(1)}, f32[128,5,128]{0,2,1:T(8,128)}) fusion(f32[5,128,128]{2,1,0:T(8,128)} %fusion.36, bf16[128,5,128]{0,2,1:T(8,128)(2,1)} %bitcast.44, bf16[128,5,128]{0,2,1:T(8,128)(2,1)S(1)} %bitcast.42, bf16[128,5,128]{0,2,1:T(8,128)(2,1)} %bitcast.46, f32[128,128]{1,0:T(8,128)S(1)} %fusion.38), kind=kOutput, calls=%fused_computation.57 | convolution fusion | flops 42352000 | bytes 1214976 | tf_op jit(solution)/shard_map/hts,shd->thd/dot_general | solution.py:64
  65.8 1.0 multiply_convert_fusion
  66.8 0.0 collective-permute-done.5
  66.8 4.3 %fusion.11 = (bf16[640,1280]{1,0:T(8,128)(2,1)S(1)}, bf16[640,1280]{1,0:T(8,128)(2,1)S(1)}, bf16[640,1280]{1,0:T(8,128)(2,1)S(1)}, bf16[640,1280]{1,0:T(8,128)(2,1)S(1)}) fusion(s32[]{:T(128)S(6)} %select_n.93, s32[]{:T(128)S(6)} %select_n.95, bf16[1,640,2560]{2,1,0:T(8,128)(2,1)} %bitcast.39, bf16[1,640,2560]{2,1,0:T(8,128)(2,1)} %bitcast.8, ...), kind=kLoop, calls=%fused_computation.19 | loop fusion | flops 13107200 | bytes 13107232 | tf_op jit(solution)/shard_map/squeeze | solution.py:83
  71.1 1.2 %fusion = f32[128,5120]{1,0:T(8,128)S(1)} fusion(bf16[128,640]{0,1:T(8,128)(2,1)S(1)} %bitcast.47, bf16[640,1280]{1,0:T(8,128)(2,1)S(1)} %get-tuple-element.20, bf16[640,1280]{1,0:T(8,128)(2,1)S(1)} %get-tuple-element.19, bf16[640,1280]{1,0:T(8,128)(2,1)S(1)} %get-tuple-element.18, bf16[640,1280]{1,0:T(8,128)(2,1)S(1)} %get-tuple-element.17), kind=kOutput, calls=%fused_computation.8 | convolution fusion | flops 865075200 | bytes 9338880 | tf_op jit(solution)/shard_map/dot_general | solution.py:85
  72.4 0.1 fusion.46
  72.4 4.9 %collective-permute-start.6 = (bf16[128,1280]{1,0:T(8,128)(2,1)S(1)}, bf16[128,1280]{1,0:T(8,128)(2,1)S(1)}, u32[]{:S(2)}, u32[]{:S(2)}) collective-permute-start(bf16[128,1280]{1,0:T(8,128)(2,1)S(1)} %get-tuple-element.11), channel_id=1, source_target_pairs={{0,1},{4,5},{8,9},{12,13},{16,17},{20,21},{24,25},{28,29},{32,33},... | collective-permute-start | bytes 983048 | tf_op jit(solution)/shard_map/ppermute | solution.py:98
  77.4 0.7 collective-permute-start.7
  78.1 3.9 %collective-permute-done.6 = bf16[128,1280]{1,0:T(8,128)(2,1)S(1)} collective-permute-done((bf16[128,1280]{1,0:T(8,128)(2,1)S(1)}, bf16[128,1280]{1,0:T(8,128)(2,1)S(1)}, u32[]{:S(2)}, u32[]{:S(2)}) %collective-permute-start.6) | collective-permute-done | bytes 327712 | tf_op jit(solution)/shard_map/ppermute | solution.py:98
  81.9 0.0 collective-permute-done.7
  81.9 0.1 add_convert_fusion.2
  82.1 4.4 %collective-permute-start.8 = (bf16[128,1280]{1,0:T(8,128)(2,1)S(1)}, bf16[128,1280]{1,0:T(8,128)(2,1)S(1)}, u32[]{:S(2)}, u32[]{:S(2)}) collective-permute-start(bf16[128,1280]{1,0:T(8,128)(2,1)S(1)} %get-tuple-element.13), channel_id=1, source_target_pairs={{0,1},{1,2},{4,5},{5,6},{8,9},{9,10},{12,13},{13,14},{16,17},{17,1... | collective-permute-start | bytes 983048 | tf_op jit(solution)/shard_map/ppermute | solution.py:98
  86.5 0.7 collective-permute-start.9
  87.2 3.9 %collective-permute-done.8 = bf16[128,1280]{1,0:T(8,128)(2,1)S(1)} collective-permute-done((bf16[128,1280]{1,0:T(8,128)(2,1)S(1)}, bf16[128,1280]{1,0:T(8,128)(2,1)S(1)}, u32[]{:S(2)}, u32[]{:S(2)}) %collective-permute-start.8) | collective-permute-done | bytes 327712 | tf_op jit(solution)/shard_map/ppermute | solution.py:98
  91.0 0.0 collective-permute-done.9
  91.0 0.2 add_convert_fusion
  91.2 8.0 %collective-permute-start.10 = (bf16[128,1280]{1,0:T(8,128)(2,1)S(1)}, bf16[128,1280]{1,0:T(8,128)(2,1)S(1)}, u32[]{:S(2)}, u32[]{:S(2)}) collective-permute-start(bf16[128,1280]{1,0:T(8,128)(2,1)S(1)} %get-tuple-element.15), channel_id=1, source_target_pairs={{0,1},{1,2},{2,3},{4,5},{5,6},{6,7},{8,9},{9,10},{10,11},{12,13},{... | collective-permute-start | bytes 983048 | tf_op jit(solution)/shard_map/ppermute | solution.py:98
  99.3 1.3 %collective-permute-start.11 = (bf16[128,1280]{1,0:T(8,128)(2,1)S(1)}, bf16[128,1280]{1,0:T(8,128)(2,1)S(1)}, u32[]{:S(2)}, u32[]{:S(2)}) collective-permute-start(bf16[128,1280]{1,0:T(8,128)(2,1)S(1)} %get-tuple-element.16), channel_id=1, source_target_pairs={{1,0},{2,1},{3,2},{5,4},{6,5},{7,6},{9,8},{10,9},{11,10},{13,12},{... | collective-permute-start | bytes 983048 | tf_op jit(solution)/shard_map/ppermute | solution.py:99
  100.6 3.3 %collective-permute-done.10 = bf16[128,1280]{1,0:T(8,128)(2,1)S(1)} collective-permute-done((bf16[128,1280]{1,0:T(8,128)(2,1)S(1)}, bf16[128,1280]{1,0:T(8,128)(2,1)S(1)}, u32[]{:S(2)}, u32[]{:S(2)}) %collective-permute-start.10) | collective-permute-done | bytes 327712 | tf_op jit(solution)/shard_map/ppermute | solution.py:98
  103.8 4.4 %collective-permute-done.11 = bf16[128,1280]{1,0:T(8,128)(2,1)S(1)} collective-permute-done((bf16[128,1280]{1,0:T(8,128)(2,1)S(1)}, bf16[128,1280]{1,0:T(8,128)(2,1)S(1)}, u32[]{:S(2)}, u32[]{:S(2)}) %collective-permute-start.11) | collective-permute-done | bytes 327712 | tf_op jit(solution)/shard_map/ppermute | solution.py:99
  108.2 0.8 fusion.35
  (4 shorter events, 0.0 us)
Async XLA Ops:
  0.0 4.3 %copy-start = (bf16[2560,640]{1,0:T(8,128)(2,1)S(1)}, bf16[2560,640]{1,0:T(8,128)(2,1)}, u32[]{:S(2)}) copy-start(bf16[2560,640]{1,0:T(8,128)(2,1)} %param.8) | copy-start | bytes 9830404
  0.0 5.0 %collective-permute-start = (bf16[128,5120]{1,0:T(8,128)(2,1)}, bf16[128,5120]{1,0:T(8,128)(2,1)}, u32[]{:S(2)}, u32[]{:S(2)}) collective-permute-start(bf16[128,5120]{1,0:T(8,128)(2,1)} %bitcast.40), channel_id=1, source_target_pairs={{0,4},{4,0},{1,5},{5,1},{2,6},{6,2},{3,7},{7,3},{8,12},{12,8},{9,1... | collective-permute-start | bytes 3932168 | tf_op jit(solution)/shard_map/ppermute | solution.py:12
  0.0 66.8 %collective-permute-start.5 = (bf16[640,2560]{1,0:T(8,128)(2,1)}, bf16[640,2560]{1,0:T(8,128)(2,1)}, u32[]{:S(2)}, u32[]{:S(2)}) collective-permute-start(bf16[640,2560]{1,0:T(8,128)(2,1)} %param.9), channel_id=1, source_target_pairs={{0,4},{4,0},{1,5},{5,1},{2,6},{6,2},{3,7},{7,3},{8,12},{12,8},{9,1... | collective-permute-start | bytes 9830408 | tf_op jit(solution)/shard_map/ppermute | solution.py:12
  0.5 3.8 %copy-start.2 = (bf16[1,128,5120]{2,1,0:T(8,128)(2,1)S(1)}, bf16[1,128,5120]{2,1,0:T(8,128)(2,1)}, u32[]{:S(2)}) copy-start(bf16[1,128,5120]{2,1,0:T(8,128)(2,1)} %param.5) | copy-start | bytes 3932164
  4.3 2.9 %copy-start.1 = (bf16[2560,640]{1,0:T(8,128)(2,1)S(1)}, bf16[2560,640]{1,0:T(8,128)(2,1)}, u32[]{:S(2)}) copy-start(bf16[2560,640]{1,0:T(8,128)(2,1)} %param.7) | copy-start | bytes 9830404
  7.1 3.1 %collective-permute-start.1 = (f32[128,640]{1,0:T(8,128)S(1)}, f32[128,640]{1,0:T(8,128)S(1)}, u32[]{:S(2)}, u32[]{:S(2)}) collective-permute-start(f32[128,640]{1,0:T(8,128)S(1)} %fusion.30), channel_id=1, source_target_pairs={{0,4},{4,0},{1,5},{5,1},{2,6},{6,2},{3,7},{7,3},{8,12},{12,8},{9,1... | collective-permute-start | bytes 983048 | tf_op jit(solution)/shard_map/ppermute | solution.py:12
  9.7 2.3 %collective-permute-start.3 = (f32[128,640]{1,0:T(8,128)}, f32[128,640]{1,0:T(8,128)}, u32[]{:S(2)}, u32[]{:S(2)}) collective-permute-start(f32[128,640]{1,0:T(8,128)} %fusion.26), channel_id=1, source_target_pairs={{0,4},{4,0},{1,5},{5,1},{2,6},{6,2},{3,7},{7,3},{8,12},{12,8},{9,1... | collective-permute-start | bytes 983048 | tf_op jit(solution)/shard_map/ppermute | solution.py:12
  12.0 14.2 %copy-start.3 = (bf16[128,640]{0,1:T(8,128)(2,1)}, bf16[128,640]{0,1:T(8,128)(2,1)S(1)}, u32[]{:S(2)}) copy-start(bf16[128,640]{0,1:T(8,128)(2,1)S(1)} %copy.15) | copy-start | bytes 491524
  17.8 14.7 %all-to-all-start = ((bf16[4,5,128,128]{3,2,1,0:T(8,128)(2,1)}), bf16[4,5,128,128]{3,2,1,0:T(8,128)(2,1)}, u32[]{:S(2)}, u32[]{:S(2)}) async-start(bf16[4,5,128,128]{3,2,1,0:T(8,128)(2,1)} %broadcast_in_dim.35), calls=%async_computation | async-start | bytes 1310720 | tf_op jit(solution)/shard_map/all_to_all | solution.py:24
  26.1 17.6 %collective-permute-start.2 = (f32[128,640]{1,0:T(8,128)}, f32[128,640]{1,0:T(8,128)}, u32[]{:S(2)}, u32[]{:S(2)}) collective-permute-start(f32[128,640]{1,0:T(8,128)} %fusion.28), channel_id=1, source_target_pairs={{0,4},{4,0},{1,5},{5,1},{2,6},{6,2},{3,7},{7,3},{8,12},{12,8},{9,1... | collective-permute-start | bytes 983048 | tf_op jit(solution)/shard_map/ppermute | solution.py:12
  34.7 15.5 %all-to-all-start.1 = ((bf16[4,5,128,128]{3,2,1,0:T(8,128)(2,1)}), bf16[4,5,128,128]{3,2,1,0:T(8,128)(2,1)}, u32[]{:S(2)}, u32[]{:S(2)}) async-start(bf16[4,5,128,128]{3,2,1,0:T(8,128)(2,1)} %broadcast_in_dim.38), calls=%async_computation.1 | async-start | bytes 1310720 | tf_op jit(solution)/shard_map/all_to_all | solution.py:24
  52.0 10.4 %collective-permute-start.4 = (bf16[5,128,128]{2,1,0:T(8,128)(2,1)}, bf16[5,128,128]{2,1,0:T(8,128)(2,1)S(1)}, u32[]{:S(2)}, u32[]{:S(2)}) collective-permute-start(bf16[5,128,128]{2,1,0:T(8,128)(2,1)} %reduce_sum.54), channel_id=1, source_target_pairs={{0,128},{1,129},{2,130},{3,131},{4,132},{5,133},{6,134},{7,135},{8... | collective-permute-start | bytes 491528 | tf_op jit(solution)/shard_map/ppermute | solution.py:33
  72.4 9.5 %collective-permute-start.6 = (bf16[128,1280]{1,0:T(8,128)(2,1)S(1)}, bf16[128,1280]{1,0:T(8,128)(2,1)S(1)}, u32[]{:S(2)}, u32[]{:S(2)}) collective-permute-start(bf16[128,1280]{1,0:T(8,128)(2,1)S(1)} %get-tuple-element.11), channel_id=1, source_target_pairs={{0,1},{4,5},{8,9},{12,13},{16,17},{20,21},{24,25},{28,29},{32,33},... | collective-permute-start | bytes 983048 | tf_op jit(solution)/shard_map/ppermute | solution.py:98
  77.4 4.6 %collective-permute-start.7 = (bf16[128,1280]{1,0:T(8,128)(2,1)S(1)}, bf16[128,1280]{1,0:T(8,128)(2,1)S(1)}, u32[]{:S(2)}, u32[]{:S(2)}) collective-permute-start(bf16[128,1280]{1,0:T(8,128)(2,1)S(1)} %get-tuple-element.12), channel_id=1, source_target_pairs={{3,2},{7,6},{11,10},{15,14},{19,18},{23,22},{27,26},{31,30},{35,34... | collective-permute-start | bytes 983048 | tf_op jit(solution)/shard_map/ppermute | solution.py:99
  82.1 9.0 %collective-permute-start.8 = (bf16[128,1280]{1,0:T(8,128)(2,1)S(1)}, bf16[128,1280]{1,0:T(8,128)(2,1)S(1)}, u32[]{:S(2)}, u32[]{:S(2)}) collective-permute-start(bf16[128,1280]{1,0:T(8,128)(2,1)S(1)} %get-tuple-element.13), channel_id=1, source_target_pairs={{0,1},{1,2},{4,5},{5,6},{8,9},{9,10},{12,13},{13,14},{16,17},{17,1... | collective-permute-start | bytes 983048 | tf_op jit(solution)/shard_map/ppermute | solution.py:98
  86.5 4.6 %collective-permute-start.9 = (bf16[128,1280]{1,0:T(8,128)(2,1)S(1)}, bf16[128,1280]{1,0:T(8,128)(2,1)S(1)}, u32[]{:S(2)}, u32[]{:S(2)}) collective-permute-start(bf16[128,1280]{1,0:T(8,128)(2,1)S(1)} %get-tuple-element.14), channel_id=1, source_target_pairs={{2,1},{3,2},{6,5},{7,6},{10,9},{11,10},{14,13},{15,14},{18,17},{19... | collective-permute-start | bytes 983048 | tf_op jit(solution)/shard_map/ppermute | solution.py:99
  91.2 12.6 %collective-permute-start.10 = (bf16[128,1280]{1,0:T(8,128)(2,1)S(1)}, bf16[128,1280]{1,0:T(8,128)(2,1)S(1)}, u32[]{:S(2)}, u32[]{:S(2)}) collective-permute-start(bf16[128,1280]{1,0:T(8,128)(2,1)S(1)} %get-tuple-element.15), channel_id=1, source_target_pairs={{0,1},{1,2},{2,3},{4,5},{5,6},{6,7},{8,9},{9,10},{10,11},{12,13},{... | collective-permute-start | bytes 983048 | tf_op jit(solution)/shard_map/ppermute | solution.py:98
  99.3 9.0 %collective-permute-start.11 = (bf16[128,1280]{1,0:T(8,128)(2,1)S(1)}, bf16[128,1280]{1,0:T(8,128)(2,1)S(1)}, u32[]{:S(2)}, u32[]{:S(2)}) collective-permute-start(bf16[128,1280]{1,0:T(8,128)(2,1)S(1)} %get-tuple-element.16), channel_id=1, source_target_pairs={{1,0},{2,1},{3,2},{5,4},{6,5},{7,6},{9,8},{10,9},{11,10},{13,12},{... | collective-permute-start | bytes 983048 | tf_op jit(solution)/shard_map/ppermute | solution.py:99

commit v12 on v8

--- a/solution.py
+++ b/solution.py
@@ -94,11 +94,13 @@
         k = jnp.where(q // 2 == c, 0, 1)
         piece = lax.dynamic_slice(halves, (k, 0, (q % 2) * quarter), (1, halves.shape[1], quarter))
         pieces.append(piece[0])
-    rotated = jnp.concatenate(pieces, axis=1)
-    products = jnp.dot(normed, rotated, preferred_element_type=F32)
+    early = jnp.dot(normed, jnp.concatenate([pieces[3], pieces[1]], axis=1), preferred_element_type=F32)
+    late = jnp.dot(normed, jnp.concatenate([pieces[2], pieces[0]], axis=1), preferred_element_type=F32)
+    where_is = {3: (early, 0), 1: (early, 1), 2: (late, 0), 0: (late, 1)}
 
     def block(o):
-        return products[:, o * quarter : (o + 1) * quarter]
+        held, k = where_is[o]
+        return held[:, k * quarter : (k + 1) * quarter]
 
     right = jnp.zeros((tok_count, quarter), F32)
     left = jnp.zeros((tok_count, quarter), F32)

time: 108 us -> 107 us (level)
  no operation moved by 1% of the time
where the time goes in v12:
time: 107 us
  starting transfers between devices  41.4 us (39%)
  waiting for transfers between devices  26.2 us (24%)
  matrix products  21.3 us (20%)
  other arithmetic  11.7 us (11%)
  local copies, waits for them, and re-layouts  6 us (6%)
    ppermute x7, starting transfers between devices, shifted(): return lax.ppermute(x, axis, pairs)  18.9 us
    ppermute x3, starting transfers between devices, shards(): right = lax.ppermute(send_r, 'head', rpairs).astype(F32)  18.7 us
    ppermute x3, waiting for transfers between devices, shards(): right = lax.ppermute(send_r, 'head', rpairs).astype(F32)  12.7 us
    ppermute x7, waiting for transfers between devices, shifted(): return lax.ppermute(x, axis, pairs)  9.08 us
    dot_general x3, matrix products, shards(): own = jnp.dot(mine_cols, w, preferred_element_type=F32)  6.88 us
    dot_general x3, matrix products, shards(): lent = swap_cores(jnp.dot(got_cols, w, preferred_element_type=F32))  6.86 us
    ppermute x3, waiting for transfers between devices, shards(): left = lax.ppermute(send_l, 'head', lpairs).astype(F32)  4.42 us
    squeeze x1, other arithmetic, shards(): pieces.append(piece[0])  4.34 us
  transfers between devices with their start and end apart: 18, of which 9 were waited for; matrix products, arithmetic and copies ran while one was open for 29% of the time, Pallas kernels for 0%

profile of v12, /device:TPU:10, one launch (start us, length us, event | category | flops | bytes accessed | tf_op | source)
XLA Modules:
  0.0 106.8 jit_solution(4646863478817392957)
XLA Ops:
  0.0 0.0 collective-permute-start
  0.0 0.5 collective-permute-start.11
  0.5 1.4 %copy-done = bf16[2560,640]{1,0:T(8,128)(2,1)S(1)} copy-done((bf16[2560,640]{1,0:T(8,128)(2,1)S(1)}, bf16[2560,640]{1,0:T(8,128)(2,1)}, u32[]{:S(2)}) %copy-start) | copy-done | bytes 3276824
  1.9 2.7 %fusion.24 = f32[128,640]{1,0:T(8,128)} fusion(bf16[2560,640]{1,0:T(8,128)(2,1)S(1)} %copy-done, bf16[1,128,5120]{2,1,0:T(8,128)(2,1)} %param.5, s32[]{:T(128)S(6)} %select_n.154), kind=kOutput, calls=%fused_computation.35 | convolution fusion | flops 419430400 | bytes 4259844 | tf_op jit(solution)/shard_map/dot_general | solution.py:63
  4.6 0.0 collective-permute-done
  4.6 2.6 %fusion.30 = f32[128,640]{1,0:T(8,128)} fusion(bf16[2560,640]{1,0:T(8,128)(2,1)S(1)} %copy-done, bf16[128,5120]{1,0:T(8,128)(2,1)} %collective-permute-done, s32[]{:T(128)S(6)} %select_n.154), kind=kOutput, calls=%fused_computation.47 | convolution fusion | flops 419430400 | bytes 4259844 | tf_op jit(solution)/shard_map/dot_general | solution.py:62
  7.2 0.0 collective-permute-start.1
  7.2 0.0 copy-done.1
  7.2 2.5 %fusion.26 = f32[128,640]{1,0:T(8,128)} fusion(bf16[2560,640]{1,0:T(8,128)(2,1)S(1)} %copy-done.1, bf16[128,5120]{1,0:T(8,128)(2,1)} %collective-permute-done, s32[]{:T(128)S(6)} %select_n.154), kind=kOutput, calls=%fused_computation.43 | convolution fusion | flops 419430400 | bytes 4259844 | tf_op jit(solution)/shard_map/dot_general | solution.py:62
  9.7 0.5 collective-permute-start.3
  10.2 1.4 %fusion.20 = f32[128,640]{1,0:T(8,128)} fusion(bf16[2560,640]{1,0:T(8,128)(2,1)S(1)} %copy-done.1, bf16[1,128,5120]{2,1,0:T(8,128)(2,1)S(1)} %copy-done.3, s32[]{:T(128)S(6)} %select_n.154), kind=kOutput, calls=%fused_computation.31 | convolution fusion | flops 419430400 | bytes 4259844 | tf_op jit(solution)/shard_map/dot_general | solution.py:63
  11.6 0.0 collective-permute-done.1
  11.6 1.8 %add_convert_fusion.4 = bf16[128,640]{1,0:T(8,128)(2,1)} fusion(f32[128,640]{1,0:T(8,128)} %fusion.24, f32[128,640]{1,0:T(8,128)} %collective-permute-done.1), kind=kLoop, calls=%fused_computation.77 | loop fusion | flops 163840 | bytes 819200 | tf_op jit(solution)/shard_map/convert_element_type | solution.py:69
  13.4 1.1 %copy.11 = bf16[128,640]{0,1:T(8,128)(2,1)S(1)} copy(bf16[128,640]{1,0:T(8,128)(2,1)} %add_convert_fusion.4) | data formatting | bytes 327680 | tf_op jit(solution)/shard_map/convert_element_type | solution.py:69
  14.5 0.0 collective-permute-done.3
  14.5 1.8 %multiply_convert_fusion.1 = bf16[128,640]{1,0:T(8,128)(2,1)} fusion(f32[128,640]{1,0:T(8,128)} %fusion.20, f32[128,640]{1,0:T(8,128)} %collective-permute-done.3), kind=kLoop, calls=%fused_computation.75 | loop fusion | flops 491520 | bytes 819200 | tf_op jit(solution)/shard_map/convert_element_type | solution.py:68
  16.3 1.7 %copy.13 = bf16[128,640]{0,1:T(8,128)(2,1)} copy(bf16[128,640]{1,0:T(8,128)(2,1)} %multiply_convert_fusion.1) | data formatting | bytes 327680 | tf_op jit(solution)/shard_map/convert_element_type | solution.py:68
  18.0 1.3 %fusion.65 = (bf16[5,128,128]{2,1,0:T(8,128)(2,1)S(1)}, f32[5,128,128]{2,1,0:T(8,128)S(1)}) fusion(bf16[128,5,128]{0,2,1:T(8,128)(2,1)} %bitcast.44, bf16[128,5,128]{0,2,1:T(8,128)(2,1)S(1)} %bitcast.42), kind=kOutput, calls=%fused_computation.100 | convolution fusion | flops 21053440 | bytes 819200 | tf_op jit(solution)/shard_map/thd,the->hde/dot_general | solution.py:70
  19.3 1.6 %collective-permute-start.4 = (bf16[5,128,128]{2,1,0:T(8,128)(2,1)S(1)}, bf16[5,128,128]{2,1,0:T(8,128)(2,1)S(1)}, u32[]{:S(2)}, u32[]{:S(2)}) collective-permute-start(bf16[5,128,128]{2,1,0:T(8,128)(2,1)S(1)} %get-tuple-element.27), channel_id=1, source_target_pairs={{0,8},{8,16},{16,24},{24,0},{32,40},{40,48},{48,56},{56,32},{64,72... | collective-permute-start | bytes 491528 | tf_op jit(solution)/shard_map/ppermute | solution.py:16
  20.9 1.1 %collective-permute-start.5 = (bf16[5,128,128]{2,1,0:T(8,128)(2,1)S(1)}, bf16[5,128,128]{2,1,0:T(8,128)(2,1)S(1)}, u32[]{:S(2)}, u32[]{:S(2)}) collective-permute-start(bf16[5,128,128]{2,1,0:T(8,128)(2,1)S(1)} %get-tuple-element.27), channel_id=1, source_target_pairs={{0,16},{8,24},{16,0},{24,8},{32,48},{40,56},{48,32},{56,40},{64,80... | collective-permute-start | bytes 491528 | tf_op jit(solution)/shard_map/ppermute | solution.py:16
  22.0 2.2 %collective-permute-start.6 = (bf16[5,128,128]{2,1,0:T(8,128)(2,1)S(1)}, bf16[5,128,128]{2,1,0:T(8,128)(2,1)S(1)}, u32[]{:S(2)}, u32[]{:S(2)}) collective-permute-start(bf16[5,128,128]{2,1,0:T(8,128)(2,1)S(1)} %get-tuple-element.27), channel_id=1, source_target_pairs={{0,24},{8,0},{16,8},{24,16},{32,56},{40,32},{48,40},{56,48},{64,88... | collective-permute-start | bytes 491528 | tf_op jit(solution)/shard_map/ppermute | solution.py:16
  24.2 2.8 %fusion.22 = f32[128,640]{1,0:T(8,128)S(1)} fusion(bf16[2560,640]{1,0:T(8,128)(2,1)} %param.6, bf16[1,128,5120]{2,1,0:T(8,128)(2,1)} %param.5, s32[]{:T(128)S(6)} %select_n.154), kind=kOutput, calls=%fused_computation.33 | convolution fusion | flops 419430400 | bytes 4259844 | tf_op jit(solution)/shard_map/dot_general | solution.py:63
  27.0 0.0 collective-permute-done.4
  27.0 2.5 %collective-permute-done.5 = bf16[5,128,128]{2,1,0:T(8,128)(2,1)S(1)} collective-permute-done((bf16[5,128,128]{2,1,0:T(8,128)(2,1)S(1)}, bf16[5,128,128]{2,1,0:T(8,128)(2,1)S(1)}, u32[]{:S(2)}, u32[]{:S(2)}) %collective-permute-start.5) | collective-permute-done | bytes 163872 | tf_op jit(solution)/shard_map/ppermute | solution.py:16
  29.5 1.6 %collective-permute-done.6 = bf16[5,128,128]{2,1,0:T(8,128)(2,1)S(1)} collective-permute-done((bf16[5,128,128]{2,1,0:T(8,128)(2,1)S(1)}, bf16[5,128,128]{2,1,0:T(8,128)(2,1)S(1)}, u32[]{:S(2)}, u32[]{:S(2)}) %collective-permute-start.6) | collective-permute-done | bytes 163872 | tf_op jit(solution)/shard_map/ppermute | solution.py:16
  31.1 0.1 fusion.54
  31.2 1.7 %collective-permute-start.7 = (bf16[5,128,128]{2,1,0:T(8,128)(2,1)S(1)}, bf16[5,128,128]{2,1,0:T(8,128)(2,1)S(1)}, u32[]{:S(2)}, u32[]{:S(2)}) collective-permute-start(bf16[5,128,128]{2,1,0:T(8,128)(2,1)S(1)} %fusion.54), channel_id=1, source_target_pairs={{0,32},{8,40},{16,48},{24,56},{32,64},{40,72},{48,80},{56,88},{64,... | collective-permute-start | bytes 491528 | tf_op jit(solution)/shard_map/ppermute | solution.py:16
  32.8 1.6 %collective-permute-start.8 = (bf16[5,128,128]{2,1,0:T(8,128)(2,1)S(1)}, bf16[5,128,128]{2,1,0:T(8,128)(2,1)S(1)}, u32[]{:S(2)}, u32[]{:S(2)}) collective-permute-start(bf16[5,128,128]{2,1,0:T(8,128)(2,1)S(1)} %fusion.54), channel_id=1, source_target_pairs={{0,64},{8,72},{16,80},{24,88},{32,96},{40,104},{48,112},{56,120},{... | collective-permute-start | bytes 491528 | tf_op jit(solution)/shard_map/ppermute | solution.py:16
  34.4 1.7 %collective-permute-start.9 = (bf16[5,128,128]{2,1,0:T(8,128)(2,1)S(1)}, bf16[5,128,128]{2,1,0:T(8,128)(2,1)S(1)}, u32[]{:S(2)}, u32[]{:S(2)}) collective-permute-start(bf16[5,128,128]{2,1,0:T(8,128)(2,1)S(1)} %fusion.54), channel_id=1, source_target_pairs={{0,96},{8,104},{16,112},{24,120},{32,0},{40,8},{48,16},{56,24},{64... | collective-permute-start | bytes 491528 | tf_op jit(solution)/shard_map/ppermute | solution.py:16
  36.2 1.8 %fusion.28 = f32[128,640]{1,0:T(8,128)S(1)} fusion(bf16[2560,640]{1,0:T(8,128)(2,1)S(1)} %copy-done.2, bf16[128,5120]{1,0:T(8,128)(2,1)} %collective-permute-done, s32[]{:T(128)S(6)} %select_n.154), kind=kOutput, calls=%fused_computation.45 | convolution fusion | flops 419430400 | bytes 4259844 | tf_op jit(solution)/shard_map/dot_general | solution.py:62
  38.0 0.1 collective-permute-start.2
  38.1 0.0 collective-permute-done.7
  38.1 3.2 %collective-permute-done.8 = bf16[5,128,128]{2,1,0:T(8,128)(2,1)S(1)} collective-permute-done((bf16[5,128,128]{2,1,0:T(8,128)(2,1)S(1)}, bf16[5,128,128]{2,1,0:T(8,128)(2,1)S(1)}, u32[]{:S(2)}, u32[]{:S(2)}) %collective-permute-start.8) | collective-permute-done | bytes 163872 | tf_op jit(solution)/shard_map/ppermute | solution.py:16
  41.2 1.8 %collective-permute-done.9 = bf16[5,128,128]{2,1,0:T(8,128)(2,1)S(1)} collective-permute-done((bf16[5,128,128]{2,1,0:T(8,128)(2,1)S(1)}, bf16[5,128,128]{2,1,0:T(8,128)(2,1)S(1)}, u32[]{:S(2)}, u32[]{:S(2)}) %collective-permute-start.9) | collective-permute-done | bytes 163872 | tf_op jit(solution)/shard_map/ppermute | solution.py:16
  43.0 0.8 fusion.42
  43.8 9.1 %collective-permute-start.10 = (bf16[5,128,128]{2,1,0:T(8,128)(2,1)}, bf16[5,128,128]{2,1,0:T(8,128)(2,1)}, u32[]{:S(2)}, u32[]{:S(2)}) collective-permute-start(bf16[5,128,128]{2,1,0:T(8,128)(2,1)} %fusion.42), channel_id=1, source_target_pairs={{0,128},{8,136},{16,144},{24,152},{32,160},{40,168},{48,176},{56,1... | collective-permute-start | bytes 491528 | tf_op jit(solution)/shard_map/ppermute | solution.py:16
  52.9 0.0 collective-permute-done.2
  52.9 0.0 copy-done.7
  52.9 0.8 multiply_convert_fusion.2
  53.7 1.7 %copy.12 = bf16[128,640]{0,1:T(8,128)(2,1)} copy(bf16[128,640]{1,0:T(8,128)(2,1)} %multiply_convert_fusion.2) | data formatting | bytes 327680 | tf_op jit(solution)/shard_map/convert_element_type | solution.py:67
  55.4 0.1 collective-permute-done.10
  55.5 2.5 %fusion.45 = f32[5,128,128]{2,1,0:T(8,128)} fusion(bf16[128,5,128]{0,2,1:T(8,128)(2,1)} %bitcast.46, bf16[5,128,128]{2,1,0:T(8,128)(2,1)} %copy-done.4, bf16[5,128,128]{2,1,0:T(8,128)(2,1)} %copy-done.5, bf16[5,128,128]{2,1,0:T(8,128)(2,1)} %copy-done.6, bf16[5,128,128]{2,1,0:T(8,128)(2,1)} %copy-done.7, bf16[5,128,128]{2,1,0:T(8,128)(2,1)} %copy-done.8, ...), kind=kOutput, calls=%fused_computation.79 | convolution fusion | flops 22609920 | bytes 1638406 | tf_op jit(solution)/shard_map/thd,hde->the/dot_general | solution.py:78
  58.0 2.3 %multiply_reduce_fusion = (f32[128,5]{0,1:T(8,128)S(1)}, f32[128,5,128]{0,2,1:T(8,128)}) fusion(f32[5,128,128]{2,1,0:T(8,128)} %fusion.45, bf16[128,5,128]{0,2,1:T(8,128)(2,1)S(1)} %bitcast.43, bf16[128,5,128]{0,2,1:T(8,128)(2,1)} %bitcast.47, bf16[128,5,128]{0,2,1:T(8,128)(2,1)} %bitcast.45, f32[128,128]{1,0:T(8,128)S(1)} %fusion.53), kind=kOutput, calls=%fused_computation.74 | convolution fusion | flops 42352000 | bytes 1214976 | tf_op jit(solution)/shard_map/hts,shd->thd/dot_general | solution.py:77
  60.3 1.0 multiply_convert_fusion
  61.3 0.0 collective-permute-done.11
  61.3 4.3 %fusion.11 = (bf16[640,1280]{1,0:T(8,128)(2,1)S(1)}, bf16[640,1280]{1,0:T(8,128)(2,1)S(1)}, bf16[640,1280]{1,0:T(8,128)(2,1)S(1)}, bf16[640,1280]{1,0:T(8,128)(2,1)S(1)}) fusion(s32[]{:T(128)S(6)} %select_n.178, s32[]{:T(128)S(6)} %select_n.180, bf16[1,640,2560]{2,1,0:T(8,128)(2,1)} %bitcast.40, bf16[1,640,2560]{2,1,0:T(8,128)(2,1)} %bitcast.8, ...), kind=kLoop, calls=%fused_computation.19 | loop fusion | flops 13107200 | bytes 13107232 | tf_op jit(solution)/shard_map/squeeze | solution.py:96
  65.7 0.7 fusion.4
  66.4 0.1 fusion.64
  66.5 6.5 %collective-permute-start.12 = (bf16[128,1280]{1,0:T(8,128)(2,1)S(1)}, bf16[128,1280]{1,0:T(8,128)(2,1)S(1)}, u32[]{:S(2)}, u32[]{:S(2)}) collective-permute-start(bf16[128,1280]{1,0:T(8,128)(2,1)S(1)} %get-tuple-element.11), channel_id=1, source_target_pairs={{0,1},{4,5},{8,9},{12,13},{16,17},{20,21},{24,25},{28,29},{32,33},... | collective-permute-start | bytes 983048 | tf_op jit(solution)/shard_map/ppermute | solution.py:113
  72.9 0.7 collective-permute-start.13
  73.6 0.7 fusion
  74.3 4.8 %collective-permute-done.12 = bf16[128,1280]{1,0:T(8,128)(2,1)S(1)} collective-permute-done((bf16[128,1280]{1,0:T(8,128)(2,1)S(1)}, bf16[128,1280]{1,0:T(8,128)(2,1)S(1)}, u32[]{:S(2)}, u32[]{:S(2)}) %collective-permute-start.12) | collective-permute-done | bytes 327712 | tf_op jit(solution)/shard_map/ppermute | solution.py:113
  79.1 0.0 collective-permute-done.13
  79.1 0.1 add_convert_fusion.2
  79.2 4.4 %collective-permute-start.14 = (bf16[128,1280]{1,0:T(8,128)(2,1)S(1)}, bf16[128,1280]{1,0:T(8,128)(2,1)S(1)}, u32[]{:S(2)}, u32[]{:S(2)}) collective-permute-start(bf16[128,1280]{1,0:T(8,128)(2,1)S(1)} %get-tuple-element.13), channel_id=1, source_target_pairs={{0,1},{1,2},{4,5},{5,6},{8,9},{9,10},{12,13},{13,14},{16,17},{17,1... | collective-permute-start | bytes 983048 | tf_op jit(solution)/shard_map/ppermute | solution.py:113
  83.7 0.7 collective-permute-start.15
  84.3 4.6 %collective-permute-done.14 = bf16[128,1280]{1,0:T(8,128)(2,1)S(1)} collective-permute-done((bf16[128,1280]{1,0:T(8,128)(2,1)S(1)}, bf16[128,1280]{1,0:T(8,128)(2,1)S(1)}, u32[]{:S(2)}, u32[]{:S(2)}) %collective-permute-start.14) | collective-permute-done | bytes 327712 | tf_op jit(solution)/shard_map/ppermute | solution.py:113
  89.0 0.0 collective-permute-done.15
  89.0 0.1 add_convert_fusion
  89.1 7.8 %collective-permute-start.16 = (bf16[128,1280]{1,0:T(8,128)(2,1)S(1)}, bf16[128,1280]{1,0:T(8,128)(2,1)S(1)}, u32[]{:S(2)}, u32[]{:S(2)}) collective-permute-start(bf16[128,1280]{1,0:T(8,128)(2,1)S(1)} %get-tuple-element.15), channel_id=1, source_target_pairs={{0,1},{1,2},{2,3},{4,5},{5,6},{6,7},{8,9},{9,10},{10,11},{12,13},{... | collective-permute-start | bytes 983048 | tf_op jit(solution)/shard_map/ppermute | solution.py:113
  97.0 1.3 %collective-permute-start.17 = (bf16[128,1280]{1,0:T(8,128)(2,1)S(1)}, bf16[128,1280]{1,0:T(8,128)(2,1)S(1)}, u32[]{:S(2)}, u32[]{:S(2)}) collective-permute-start(bf16[128,1280]{1,0:T(8,128)(2,1)S(1)} %get-tuple-element.16), channel_id=1, source_target_pairs={{1,0},{2,1},{3,2},{5,4},{6,5},{7,6},{9,8},{10,9},{11,10},{13,12},{... | collective-permute-start | bytes 983048 | tf_op jit(solution)/shard_map/ppermute | solution.py:114
  98.3 3.3 %collective-permute-done.16 = bf16[128,1280]{1,0:T(8,128)(2,1)S(1)} collective-permute-done((bf16[128,1280]{1,0:T(8,128)(2,1)S(1)}, bf16[128,1280]{1,0:T(8,128)(2,1)S(1)}, u32[]{:S(2)}, u32[]{:S(2)}) %collective-permute-start.16) | collective-permute-done | bytes 327712 | tf_op jit(solution)/shard_map/ppermute | solution.py:113
  101.5 4.4 %collective-permute-done.17 = bf16[128,1280]{1,0:T(8,128)(2,1)S(1)} collective-permute-done((bf16[128,1280]{1,0:T(8,128)(2,1)S(1)}, bf16[128,1280]{1,0:T(8,128)(2,1)S(1)}, u32[]{:S(2)}, u32[]{:S(2)}) %collective-permute-start.17) | collective-permute-done | bytes 327712 | tf_op jit(solution)/shard_map/ppermute | solution.py:114
  105.9 0.8 fusion.43
  (19 shorter events, 0.0 us)
Async XLA Ops:
  0.0 1.9 %copy-start = (bf16[2560,640]{1,0:T(8,128)(2,1)S(1)}, bf16[2560,640]{1,0:T(8,128)(2,1)}, u32[]{:S(2)}) copy-start(bf16[2560,640]{1,0:T(8,128)(2,1)} %param.8) | copy-start | bytes 9830404
  0.0 4.6 %collective-permute-start = (bf16[128,5120]{1,0:T(8,128)(2,1)}, bf16[128,5120]{1,0:T(8,128)(2,1)}, u32[]{:S(2)}, u32[]{:S(2)}) collective-permute-start(bf16[128,5120]{1,0:T(8,128)(2,1)} %bitcast.41), channel_id=1, source_target_pairs={{0,4},{4,0},{1,5},{5,1},{2,6},{6,2},{3,7},{7,3},{8,12},{12,8},{9,1... | collective-permute-start | bytes 3932168 | tf_op jit(solution)/shard_map/ppermute | solution.py:12
  0.0 61.3 %collective-permute-start.11 = (bf16[640,2560]{1,0:T(8,128)(2,1)}, bf16[640,2560]{1,0:T(8,128)(2,1)}, u32[]{:S(2)}, u32[]{:S(2)}) collective-permute-start(bf16[640,2560]{1,0:T(8,128)(2,1)} %param.9), channel_id=1, source_target_pairs={{0,4},{4,0},{1,5},{5,1},{2,6},{6,2},{3,7},{7,3},{8,12},{12,8},{9,1... | collective-permute-start | bytes 9830408 | tf_op jit(solution)/shard_map/ppermute | solution.py:12
  1.9 5.3 %copy-start.1 = (bf16[2560,640]{1,0:T(8,128)(2,1)S(1)}, bf16[2560,640]{1,0:T(8,128)(2,1)}, u32[]{:S(2)}) copy-start(bf16[2560,640]{1,0:T(8,128)(2,1)} %param.7) | copy-start | bytes 9830404
  4.6 5.6 %copy-start.3 = (bf16[1,128,5120]{2,1,0:T(8,128)(2,1)S(1)}, bf16[1,128,5120]{2,1,0:T(8,128)(2,1)}, u32[]{:S(2)}) copy-start(bf16[1,128,5120]{2,1,0:T(8,128)(2,1)} %param.5) | copy-start | bytes 3932164
  7.2 4.4 %collective-permute-start.1 = (f32[128,640]{1,0:T(8,128)}, f32[128,640]{1,0:T(8,128)}, u32[]{:S(2)}, u32[]{:S(2)}) collective-permute-start(f32[128,640]{1,0:T(8,128)} %fusion.30), channel_id=1, source_target_pairs={{0,4},{4,0},{1,5},{5,1},{2,6},{6,2},{3,7},{7,3},{8,12},{12,8},{9,1... | collective-permute-start | bytes 983048 | tf_op jit(solution)/shard_map/ppermute | solution.py:12
  9.7 4.8 %collective-permute-start.3 = (f32[128,640]{1,0:T(8,128)}, f32[128,640]{1,0:T(8,128)}, u32[]{:S(2)}, u32[]{:S(2)}) collective-permute-start(f32[128,640]{1,0:T(8,128)} %fusion.26), channel_id=1, source_target_pairs={{0,4},{4,0},{1,5},{5,1},{2,6},{6,2},{3,7},{7,3},{8,12},{12,8},{9,1... | collective-permute-start | bytes 983048 | tf_op jit(solution)/shard_map/ppermute | solution.py:12
  18.0 18.2 %copy-start.2 = (bf16[2560,640]{1,0:T(8,128)(2,1)S(1)}, bf16[2560,640]{1,0:T(8,128)(2,1)}, u32[]{:S(2)}) copy-start(bf16[2560,640]{1,0:T(8,128)(2,1)} %param.6) | copy-start | bytes 9830404
  19.3 7.7 %collective-permute-start.4 = (bf16[5,128,128]{2,1,0:T(8,128)(2,1)S(1)}, bf16[5,128,128]{2,1,0:T(8,128)(2,1)S(1)}, u32[]{:S(2)}, u32[]{:S(2)}) collective-permute-start(bf16[5,128,128]{2,1,0:T(8,128)(2,1)S(1)} %get-tuple-element.27), channel_id=1, source_target_pairs={{0,8},{8,16},{16,24},{24,0},{32,40},{40,48},{48,56},{56,32},{64,72... | collective-permute-start | bytes 491528 | tf_op jit(solution)/shard_map/ppermute | solution.py:16
  20.9 8.6 %collective-permute-start.5 = (bf16[5,128,128]{2,1,0:T(8,128)(2,1)S(1)}, bf16[5,128,128]{2,1,0:T(8,128)(2,1)S(1)}, u32[]{:S(2)}, u32[]{:S(2)}) collective-permute-start(bf16[5,128,128]{2,1,0:T(8,128)(2,1)S(1)} %get-tuple-element.27), channel_id=1, source_target_pairs={{0,16},{8,24},{16,0},{24,8},{32,48},{40,56},{48,32},{56,40},{64,80... | collective-permute-start | bytes 491528 | tf_op jit(solution)/shard_map/ppermute | solution.py:16
  22.0 9.1 %collective-permute-start.6 = (bf16[5,128,128]{2,1,0:T(8,128)(2,1)S(1)}, bf16[5,128,128]{2,1,0:T(8,128)(2,1)S(1)}, u32[]{:S(2)}, u32[]{:S(2)}) collective-permute-start(bf16[5,128,128]{2,1,0:T(8,128)(2,1)S(1)} %get-tuple-element.27), channel_id=1, source_target_pairs={{0,24},{8,0},{16,8},{24,16},{32,56},{40,32},{48,40},{56,48},{64,88... | collective-permute-start | bytes 491528 | tf_op jit(solution)/shard_map/ppermute | solution.py:16
  27.0 16.8 %copy-start.4 = (bf16[5,128,128]{2,1,0:T(8,128)(2,1)}, bf16[5,128,128]{2,1,0:T(8,128)(2,1)S(1)}, u32[]{:S(2)}) copy-start(bf16[5,128,128]{2,1,0:T(8,128)(2,1)S(1)} %collective-permute-done.4) | copy-start | bytes 491524
  29.5 14.4 %copy-start.5 = (bf16[5,128,128]{2,1,0:T(8,128)(2,1)}, bf16[5,128,128]{2,1,0:T(8,128)(2,1)S(1)}, u32[]{:S(2)}) copy-start(bf16[5,128,128]{2,1,0:T(8,128)(2,1)S(1)} %collective-permute-done.5) | copy-start | bytes 491524
  31.1 12.8 %copy-start.6 = (bf16[5,128,128]{2,1,0:T(8,128)(2,1)}, bf16[5,128,128]{2,1,0:T(8,128)(2,1)S(1)}, u32[]{:S(2)}) copy-start(bf16[5,128,128]{2,1,0:T(8,128)(2,1)S(1)} %collective-permute-done.6) | copy-start | bytes 491524
  31.2 6.9 %collective-permute-start.7 = (bf16[5,128,128]{2,1,0:T(8,128)(2,1)S(1)}, bf16[5,128,128]{2,1,0:T(8,128)(2,1)S(1)}, u32[]{:S(2)}, u32[]{:S(2)}) collective-permute-start(bf16[5,128,128]{2,1,0:T(8,128)(2,1)S(1)} %fusion.54), channel_id=1, source_target_pairs={{0,32},{8,40},{16,48},{24,56},{32,64},{40,72},{48,80},{56,88},{64,... | collective-permute-start | bytes 491528 | tf_op jit(solution)/shard_map/ppermute | solution.py:16
  32.8 8.4 %collective-permute-start.8 = (bf16[5,128,128]{2,1,0:T(8,128)(2,1)S(1)}, bf16[5,128,128]{2,1,0:T(8,128)(2,1)S(1)}, u32[]{:S(2)}, u32[]{:S(2)}) collective-permute-start(bf16[5,128,128]{2,1,0:T(8,128)(2,1)S(1)} %fusion.54), channel_id=1, source_target_pairs={{0,64},{8,72},{16,80},{24,88},{32,96},{40,104},{48,112},{56,120},{... | collective-permute-start | bytes 491528 | tf_op jit(solution)/shard_map/ppermute | solution.py:16
  34.4 8.6 %collective-permute-start.9 = (bf16[5,128,128]{2,1,0:T(8,128)(2,1)S(1)}, bf16[5,128,128]{2,1,0:T(8,128)(2,1)S(1)}, u32[]{:S(2)}, u32[]{:S(2)}) collective-permute-start(bf16[5,128,128]{2,1,0:T(8,128)(2,1)S(1)} %fusion.54), channel_id=1, source_target_pairs={{0,96},{8,104},{16,112},{24,120},{32,0},{40,8},{48,16},{56,24},{64... | collective-permute-start | bytes 491528 | tf_op jit(solution)/shard_map/ppermute | solution.py:16
  38.0 15.0 %collective-permute-start.2 = (f32[128,640]{1,0:T(8,128)S(1)}, f32[128,640]{1,0:T(8,128)S(1)}, u32[]{:S(2)}, u32[]{:S(2)}) collective-permute-start(f32[128,640]{1,0:T(8,128)S(1)} %fusion.28), channel_id=1, source_target_pairs={{0,4},{4,0},{1,5},{5,1},{2,6},{6,2},{3,7},{7,3},{8,12},{12,8},{9,1... | collective-permute-start | bytes 983048 | tf_op jit(solution)/shard_map/ppermute | solution.py:12
  38.1 14.8 %copy-start.7 = (bf16[5,128,128]{2,1,0:T(8,128)(2,1)}, bf16[5,128,128]{2,1,0:T(8,128)(2,1)S(1)}, u32[]{:S(2)}) copy-start(bf16[5,128,128]{2,1,0:T(8,128)(2,1)S(1)} %collective-permute-done.7) | copy-start | bytes 491524
  41.2 11.7 %copy-start.8 = (bf16[5,128,128]{2,1,0:T(8,128)(2,1)}, bf16[5,128,128]{2,1,0:T(8,128)(2,1)S(1)}, u32[]{:S(2)}) copy-start(bf16[5,128,128]{2,1,0:T(8,128)(2,1)S(1)} %collective-permute-done.8) | copy-start | bytes 491524
  43.0 9.9 %copy-start.9 = (bf16[5,128,128]{2,1,0:T(8,128)(2,1)}, bf16[5,128,128]{2,1,0:T(8,128)(2,1)S(1)}, u32[]{:S(2)}) copy-start(bf16[5,128,128]{2,1,0:T(8,128)(2,1)S(1)} %collective-permute-done.9) | copy-start | bytes 491524
  43.8 11.7 %collective-permute-start.10 = (bf16[5,128,128]{2,1,0:T(8,128)(2,1)}, bf16[5,128,128]{2,1,0:T(8,128)(2,1)}, u32[]{:S(2)}, u32[]{:S(2)}) collective-permute-start(bf16[5,128,128]{2,1,0:T(8,128)(2,1)} %fusion.42), channel_id=1, source_target_pairs={{0,128},{8,136},{16,144},{24,152},{32,160},{40,168},{48,176},{56,1... | collective-permute-start | bytes 491528 | tf_op jit(solution)/shard_map/ppermute | solution.py:16
  66.5 12.7 %collective-permute-start.12 = (bf16[128,1280]{1,0:T(8,128)(2,1)S(1)}, bf16[128,1280]{1,0:T(8,128)(2,1)S(1)}, u32[]{:S(2)}, u32[]{:S(2)}) collective-permute-start(bf16[128,1280]{1,0:T(8,128)(2,1)S(1)} %get-tuple-element.11), channel_id=1, source_target_pairs={{0,1},{4,5},{8,9},{12,13},{16,17},{20,21},{24,25},{28,29},{32,33},... | collective-permute-start | bytes 983048 | tf_op jit(solution)/shard_map/ppermute | solution.py:113
  72.9 6.2 %collective-permute-start.13 = (bf16[128,1280]{1,0:T(8,128)(2,1)S(1)}, bf16[128,1280]{1,0:T(8,128)(2,1)S(1)}, u32[]{:S(2)}, u32[]{:S(2)}) collective-permute-start(bf16[128,1280]{1,0:T(8,128)(2,1)S(1)} %get-tuple-element.12), channel_id=1, source_target_pairs={{3,2},{7,6},{11,10},{15,14},{19,18},{23,22},{27,26},{31,30},{35,34... | collective-permute-start | bytes 983048 | tf_op jit(solution)/shard_map/ppermute | solution.py:114
  79.2 9.7 %collective-permute-start.14 = (bf16[128,1280]{1,0:T(8,128)(2,1)S(1)}, bf16[128,1280]{1,0:T(8,128)(2,1)S(1)}, u32[]{:S(2)}, u32[]{:S(2)}) collective-permute-start(bf16[128,1280]{1,0:T(8,128)(2,1)S(1)} %get-tuple-element.13), channel_id=1, source_target_pairs={{0,1},{1,2},{4,5},{5,6},{8,9},{9,10},{12,13},{13,14},{16,17},{17,1... | collective-permute-start | bytes 983048 | tf_op jit(solution)/shard_map/ppermute | solution.py:113
  83.7 5.3 %collective-permute-start.15 = (bf16[128,1280]{1,0:T(8,128)(2,1)S(1)}, bf16[128,1280]{1,0:T(8,128)(2,1)S(1)}, u32[]{:S(2)}, u32[]{:S(2)}) collective-permute-start(bf16[128,1280]{1,0:T(8,128)(2,1)S(1)} %get-tuple-element.14), channel_id=1, source_target_pairs={{2,1},{3,2},{6,5},{7,6},{10,9},{11,10},{14,13},{15,14},{18,17},{19... | collective-permute-start | bytes 983048 | tf_op jit(solution)/shard_map/ppermute | solution.py:114
  89.1 12.4 %collective-permute-start.16 = (bf16[128,1280]{1,0:T(8,128)(2,1)S(1)}, bf16[128,1280]{1,0:T(8,128)(2,1)S(1)}, u32[]{:S(2)}, u32[]{:S(2)}) collective-permute-start(bf16[128,1280]{1,0:T(8,128)(2,1)S(1)} %get-tuple-element.15), channel_id=1, source_target_pairs={{0,1},{1,2},{2,3},{4,5},{5,6},{6,7},{8,9},{9,10},{10,11},{12,13},{... | collective-permute-start | bytes 983048 | tf_op jit(solution)/shard_map/ppermute | solution.py:113
  97.0 9.0 %collective-permute-start.17 = (bf16[128,1280]{1,0:T(8,128)(2,1)S(1)}, bf16[128,1280]{1,0:T(8,128)(2,1)S(1)}, u32[]{:S(2)}, u32[]{:S(2)}) collective-permute-start(bf16[128,1280]{1,0:T(8,128)(2,1)S(1)} %get-tuple-element.16), channel_id=1, source_target_pairs={{1,0},{2,1},{3,2},{5,4},{6,5},{7,6},{9,8},{10,9},{11,10},{13,12},{... | collective-permute-start | bytes 983048 | tf_op jit(solution)/shard_map/ppermute | solution.py:114

commit v13 on v12

--- a/solution.py
+++ b/solution.py
@@ -57,12 +57,14 @@
 
     mine_cols = lax.dynamic_slice_in_dim(rows_in, c * half, half, axis=1)
     got_cols = lax.dynamic_slice_in_dim(swap_cores(rows_in), c * half, half, axis=1)
-    sums = []
-    for w in (w_query, w_key, w_value):
-        lent = swap_cores(jnp.dot(got_cols, w, preferred_element_type=F32))
-        own = jnp.dot(mine_cols, w, preferred_element_type=F32)
-        sums.append(own + lent)
-    query_sum, key_sum, value_sum = sums
+    kv_lent = swap_cores(
+        jnp.concatenate([jnp.dot(got_cols, w, preferred_element_type=F32) for w in (w_key, w_value)], axis=1)
+    )
+    key_sum = jnp.dot(mine_cols, w_key, preferred_element_type=F32) + kv_lent[:, :width_local]
+    value_sum = jnp.dot(mine_cols, w_value, preferred_element_type=F32) + kv_lent[:, width_local:]
+    query_sum = jnp.dot(mine_cols, w_query, preferred_element_type=F32) + swap_cores(
+        jnp.dot(got_cols, w_query, preferred_element_type=F32)
+    )
 
     queries = jax.nn.silu(query_sum).astype(BF16).reshape(tok_count, head_count, HD)
     keys_all = jax.nn.silu(key_sum).astype(BF16).reshape(tok_count, head_count, HD)
@@ -110,6 +112,11 @@
         send_r, send_l = lax.optimization_barrier((send_r, send_l))
         rpairs = [(j, j + 1) for j in range(s) if j + 1 < n]
         lpairs = [(j, j - 1) for j in range(n - s, n) if j - 1 >= 0]
+        if s == 1:
+            got = lax.ppermute(jnp.where(h == 0, send_r, send_l), "head", rpairs + lpairs).astype(F32)
+            right = jnp.where(h == 1, got, 0.0)
+            left = jnp.where(h == n - 2, got, 0.0)
+            continue
         right = lax.ppermute(send_r, "head", rpairs).astype(F32)
         left = lax.ppermute(send_l, "head", lpairs).astype(F32)
     mixed = (block(0) + right + left).astype(BF16)

time: 107 us -> 112 us (1.047)
  matrix products: 21.3 us -> 24.6 us
  waiting for transfers between devices: 26.2 us -> 28 us
  starting transfers between devices: 41.4 us -> 39.9 us
  other arithmetic: 11.7 us -> 12.9 us
    ppermute x3 -> x2, starting transfers between devices: 18.7 us -> 11.4 us  [shards(): right = lax.ppermute(send_r, 'head', rpairs).astype(F32)]
    ppermute x0 -> x1, starting transfers between devices: none -> 7.14 us  [shards(): lax.ppermute(jnp.where(h == 0, send_r, send_l), 'head', rpairs + lpairs)]
    ppermute x3 -> x2, waiting for transfers between devices: 12.7 us -> 7.93 us  [shards(): right = lax.ppermute(send_r, 'head', rpairs).astype(F32)]
    convert_element_type x2 -> x0, other arithmetic: 3.62 us -> none  [the longest x1 1.84 us: shards(): jax.nn.silu(key_sum).astype(BF16).reshape(tok_count, head_count, HD)]
    ppermute x5 -> x4, waiting for transfers between devices: 0.01 us -> 3.36 us  [swap_cores(): return lax.ppermute(x, 'wt', [(0, 1), (1, 0)])]
    ppermute x0 -> x1, waiting for transfers between devices: none -> 3.11 us  [shards(): lax.ppermute(jnp.where(h == 0, send_r, send_l), 'head', rpairs + lpairs)]
    dot_general x6, matrix products: 13.7 us -> 15.9 us  [the longest x1 3.64 us: shards(): jnp.dot(mine_cols, w_query, preferred_element_type=F32)]
    dot_general x1, matrix products: 0.71 us -> 2.72 us  [shards(): jnp.dot(normed, jnp.concatenate([pieces[2], pieces[0]], axis=1), preferre...]
  transfers between devices with their start and end apart: 18 -> 16, of which waited for: 9 -> 10; matrix products, arithmetic and copies ran while one was open for 29% -> 26% of each run, Pallas kernels for 0% -> 0%
where the time goes in v13:
time: 112 us; the launch traced here: 111 us
  starting transfers between devices  39.9 us (36%)
  waiting for transfers between devices  28 us (25%)
  matrix products  24.6 us (22%)
  other arithmetic  12.9 us (12%)
  local copies, waits for them, and re-layouts  5.66 us (5%)
    ppermute x7, starting transfers between devices, shifted(): return lax.ppermute(x, axis, pairs)  18.8 us
    ppermute x2, starting transfers between devices, shards(): right = lax.ppermute(send_r, 'head', rpairs).astype(F32)  11.4 us
    ppermute x7, waiting for transfers between devices, shifted(): return lax.ppermute(x, axis, pairs)  9.18 us
    ppermute x2, waiting for transfers between devices, shards(): right = lax.ppermute(send_r, 'head', rpairs).astype(F32)  7.93 us
    ppermute x1, starting transfers between devices, shards(): lax.ppermute(jnp.where(h == 0, send_r, send_l), 'head', rpairs + lpairs)  7.14 us
    squeeze x1, other arithmetic, shards(): pieces.append(piece[0])  5.48 us
    ppermute x2, waiting for transfers between devices, shards(): left = lax.ppermute(send_l, 'head', lpairs).astype(F32)  4.42 us
    dot_general x1, matrix products, shards(): jnp.dot(mine_cols, w_query, preferred_element_type=F32)  3.64 us
  transfers between devices with their start and end apart: 16, of which 10 were waited for; matrix products, arithmetic and copies ran while one was open for 26% of the time, Pallas kernels for 0%

profile of v13, /device:TPU:10, one launch (start us, length us, event | category | flops | bytes accessed | tf_op | source)
XLA Modules:
  0.0 111.3 jit_solution(10753458048515498981)
XLA Ops:
  0.0 0.0 copy-start
  0.0 0.0 collective-permute-start
  0.0 0.0 copy-start.1
  0.0 3.4 %collective-permute-done = bf16[128,5120]{1,0:T(8,128)(2,1)} collective-permute-done((bf16[128,5120]{1,0:T(8,128)(2,1)}, bf16[128,5120]{1,0:T(8,128)(2,1)}, u32[]{:S(2)}, u32[]{:S(2)}) %collective-permute-start) | collective-permute-done | bytes 1310752 | tf_op jit(solution)/shard_map/ppermute | solution.py:12
  3.4 0.0 copy-done
  3.4 1.8 %fusion.35 = f32[128,640]{1,0:T(8,128)S(1)} fusion(bf16[2560,640]{1,0:T(8,128)(2,1)S(1)} %copy-done, bf16[128,5120]{1,0:T(8,128)(2,1)} %collective-permute-done, s32[]{:T(128)S(6)} %select_n.176), kind=kOutput, calls=%fused_computation.53 | convolution fusion | flops 419430400 | bytes 4259844 | tf_op jit(solution)/shard_map/dot_general | solution.py:61
  5.2 0.0 copy-done.1
  5.2 1.8 %fusion.33 = f32[128,640]{1,0:T(8,128)S(1)} fusion(bf16[2560,640]{1,0:T(8,128)(2,1)S(1)} %copy-done.1, bf16[128,5120]{1,0:T(8,128)(2,1)} %collective-permute-done, s32[]{:T(128)S(6)} %select_n.176), kind=kOutput, calls=%fused_computation.51 | convolution fusion | flops 419430400 | bytes 4259844 | tf_op jit(solution)/shard_map/dot_general | solution.py:61
  6.9 0.9 pad_maximum_fusion
  7.8 0.1 collective-permute-start.1
  8.0 0.4 collective-permute-start.10
  8.3 3.6 %fusion.27 = f32[128,640]{1,0:T(8,128)} fusion(bf16[2560,640]{1,0:T(8,128)(2,1)} %param.6, bf16[1,128,5120]{2,1,0:T(8,128)(2,1)} %param.5, s32[]{:T(128)S(6)} %select_n.176), kind=kOutput, calls=%fused_computation.41 | convolution fusion | flops 419430400 | bytes 4259844 | tf_op jit(solution)/shard_map/dot_general | solution.py:65
  12.0 0.0 collective-permute-done.1
  12.0 2.4 %multiply_convert_fusion.1 = bf16[128,640]{1,0:T(8,128)(2,1)} fusion(f32[128,1280]{1,0:T(8,128)} %collective-permute-done.1, bf16[2560,640]{1,0:T(8,128)(2,1)S(1)} %copy-done, bf16[1,128,5120]{2,1,0:T(8,128)(2,1)S(1)} %copy-done.6, s32[]{:T(128)S(6)} %select_n.176), kind=kOutput, calls=%fused_computation.84 | convolution fusion | flops 419921920 | bytes 4423684 | tf_op jit(solution)/shard_map/dot_general | solution.py:63
  14.3 1.1 copy.13
  15.4 3.5 %fusion.49 = bf16[128,640]{1,0:T(8,128)(2,1)} fusion(f32[128,1280]{1,0:T(8,128)} %collective-permute-done.1, bf16[2560,640]{1,0:T(8,128)(2,1)} %param.8, bf16[1,128,5120]{2,1,0:T(8,128)(2,1)} %param.5, s32[]{:T(128)S(6)} %select_n.176), kind=kOutput, calls=%fused_computation.81 | convolution fusion | flops 419594240 | bytes 4423684 | tf_op jit(solution)/shard_map/dot_general | solution.py:64
  18.9 1.7 %copy.11 = bf16[128,640]{0,1:T(8,128)(2,1)} copy(bf16[128,640]{1,0:T(8,128)(2,1)} %fusion.49) | data formatting | bytes 327680 | tf_op jit(solution)/shard_map/convert_element_type | solution.py:71
  20.6 1.2 %fusion.75 = (bf16[5,128,128]{2,1,0:T(8,128)(2,1)S(1)}, f32[5,128,128]{2,1,0:T(8,128)S(1)}) fusion(bf16[128,5,128]{0,2,1:T(8,128)(2,1)S(1)} %bitcast.44, bf16[128,5,128]{0,2,1:T(8,128)(2,1)} %bitcast.46), kind=kOutput, calls=%fused_computation.109 | convolution fusion | flops 21053440 | bytes 819200 | tf_op jit(solution)/shard_map/thd,the->hde/dot_general | solution.py:72
  21.9 1.6 %collective-permute-start.3 = (bf16[5,128,128]{2,1,0:T(8,128)(2,1)S(1)}, bf16[5,128,128]{2,1,0:T(8,128)(2,1)S(1)}, u32[]{:S(2)}, u32[]{:S(2)}) collective-permute-start(bf16[5,128,128]{2,1,0:T(8,128)(2,1)S(1)} %get-tuple-element.27), channel_id=1, source_target_pairs={{0,8},{8,16},{16,24},{24,0},{32,40},{40,48},{48,56},{56,32},{64,72... | collective-permute-start | bytes 491528 | tf_op jit(solution)/shard_map/ppermute | solution.py:16
  23.4 1.1 collective-permute-start.4
  24.5 2.2 %collective-permute-start.5 = (bf16[5,128,128]{2,1,0:T(8,128)(2,1)S(1)}, bf16[5,128,128]{2,1,0:T(8,128)(2,1)S(1)}, u32[]{:S(2)}, u32[]{:S(2)}) collective-permute-start(bf16[5,128,128]{2,1,0:T(8,128)(2,1)S(1)} %get-tuple-element.27), channel_id=1, source_target_pairs={{0,24},{8,0},{16,8},{24,16},{32,56},{40,32},{48,40},{56,48},{64,88... | collective-permute-start | bytes 491528 | tf_op jit(solution)/shard_map/ppermute | solution.py:16
  26.7 2.8 %fusion.31 = f32[128,640]{1,0:T(8,128)S(1)} fusion(bf16[2560,640]{1,0:T(8,128)(2,1)} %param.6, bf16[128,5120]{1,0:T(8,128)(2,1)} %collective-permute-done, s32[]{:T(128)S(6)} %select_n.176), kind=kOutput, calls=%fused_computation.49 | convolution fusion | flops 419430400 | bytes 4259844 | tf_op jit(solution)/shard_map/dot_general | solution.py:66
  29.5 0.1 collective-permute-start.2
  29.6 0.0 collective-permute-done.3
  29.7 2.4 %collective-permute-done.4 = bf16[5,128,128]{2,1,0:T(8,128)(2,1)S(1)} collective-permute-done((bf16[5,128,128]{2,1,0:T(8,128)(2,1)S(1)}, bf16[5,128,128]{2,1,0:T(8,128)(2,1)S(1)}, u32[]{:S(2)}, u32[]{:S(2)}) %collective-permute-start.4) | collective-permute-done | bytes 163872 | tf_op jit(solution)/shard_map/ppermute | solution.py:16
  32.0 1.7 %collective-permute-done.5 = bf16[5,128,128]{2,1,0:T(8,128)(2,1)S(1)} collective-permute-done((bf16[5,128,128]{2,1,0:T(8,128)(2,1)S(1)}, bf16[5,128,128]{2,1,0:T(8,128)(2,1)S(1)}, u32[]{:S(2)}, u32[]{:S(2)}) %collective-permute-start.5) | collective-permute-done | bytes 163872 | tf_op jit(solution)/shard_map/ppermute | solution.py:16
  33.8 0.8 fusion.60
  34.5 0.0 copy-done.7
  34.5 1.6 %collective-permute-start.6 = (bf16[5,128,128]{2,1,0:T(8,128)(2,1)}, bf16[5,128,128]{2,1,0:T(8,128)(2,1)}, u32[]{:S(2)}, u32[]{:S(2)}) collective-permute-start(bf16[5,128,128]{2,1,0:T(8,128)(2,1)} %fusion.60), channel_id=1, source_target_pairs={{0,32},{8,40},{16,48},{24,56},{32,64},{40,72},{48,80},{56,88},{64,... | collective-permute-start | bytes 491528 | tf_op jit(solution)/shard_map/ppermute | solution.py:16
  36.1 1.6 %collective-permute-start.7 = (bf16[5,128,128]{2,1,0:T(8,128)(2,1)}, bf16[5,128,128]{2,1,0:T(8,128)(2,1)}, u32[]{:S(2)}, u32[]{:S(2)}) collective-permute-start(bf16[5,128,128]{2,1,0:T(8,128)(2,1)} %fusion.60), channel_id=1, source_target_pairs={{0,64},{8,72},{16,80},{24,88},{32,96},{40,104},{48,112},{56,120},{... | collective-permute-start | bytes 491528 | tf_op jit(solution)/shard_map/ppermute | solution.py:16
  37.7 1.7 %collective-permute-start.8 = (bf16[5,128,128]{2,1,0:T(8,128)(2,1)}, bf16[5,128,128]{2,1,0:T(8,128)(2,1)}, u32[]{:S(2)}, u32[]{:S(2)}) collective-permute-start(bf16[5,128,128]{2,1,0:T(8,128)(2,1)} %fusion.60), channel_id=1, source_target_pairs={{0,96},{8,104},{16,112},{24,120},{32,0},{40,8},{48,16},{56,24},{64... | collective-permute-start | bytes 491528 | tf_op jit(solution)/shard_map/ppermute | solution.py:16
  39.4 0.0 collective-permute-done.2
  39.4 0.0 copy-done.5
  39.4 0.8 multiply_convert_fusion.2
  40.2 1.7 %copy.12 = bf16[128,640]{0,1:T(8,128)(2,1)} copy(bf16[128,640]{1,0:T(8,128)(2,1)} %multiply_convert_fusion.2) | data formatting | bytes 327680 | tf_op jit(solution)/shard_map/convert_element_type | solution.py:69
  41.9 0.0 collective-permute-done.6
  41.9 2.9 %collective-permute-done.7 = bf16[5,128,128]{2,1,0:T(8,128)(2,1)} collective-permute-done((bf16[5,128,128]{2,1,0:T(8,128)(2,1)}, bf16[5,128,128]{2,1,0:T(8,128)(2,1)}, u32[]{:S(2)}, u32[]{:S(2)}) %collective-permute-start.7) | collective-permute-done | bytes 163872 | tf_op jit(solution)/shard_map/ppermute | solution.py:16
  44.8 1.8 %collective-permute-done.8 = bf16[5,128,128]{2,1,0:T(8,128)(2,1)} collective-permute-done((bf16[5,128,128]{2,1,0:T(8,128)(2,1)}, bf16[5,128,128]{2,1,0:T(8,128)(2,1)}, u32[]{:S(2)}, u32[]{:S(2)}) %collective-permute-start.8) | collective-permute-done | bytes 163872 | tf_op jit(solution)/shard_map/ppermute | solution.py:16
  46.6 2.1 %fusion.47 = bf16[5,128,128]{2,1,0:T(8,128)(2,1)} fusion(bf16[5,128,128]{2,1,0:T(8,128)(2,1)} %collective-permute-done.8, bf16[5,128,128]{2,1,0:T(8,128)(2,1)} %collective-permute-done.7, bf16[5,128,128]{2,1,0:T(8,128)(2,1)} %collective-permute-done.6, bf16[5,128,128]{2,1,0:T(8,128)(2,1)} %copy-done.9, bf16[5,128,128]{2,1,0:T(8,128)(2,1)} %copy-done.8, ...), kind=kLoop, calls=%fused_computation.77 | loop fusion | flops 1064960 | bytes 1474560 | tf_op jit(solution)/shard_map/convert_element_type | solution.py:46
  48.7 9.1 %collective-permute-start.9 = (bf16[5,128,128]{2,1,0:T(8,128)(2,1)}, bf16[5,128,128]{2,1,0:T(8,128)(2,1)}, u32[]{:S(2)}, u32[]{:S(2)}) collective-permute-start(bf16[5,128,128]{2,1,0:T(8,128)(2,1)} %fusion.47), channel_id=1, source_target_pairs={{0,128},{8,136},{16,144},{24,152},{32,160},{40,168},{48,176},{56,1... | collective-permute-start | bytes 491528 | tf_op jit(solution)/shard_map/ppermute | solution.py:16
  57.8 2.2 %fusion.18 = f32[5,128,128]{2,1,0:T(8,128)} fusion(bf16[128,5,128]{0,2,1:T(8,128)(2,1)} %bitcast.47, bf16[128,5,128]{0,2,1:T(8,128)(2,1)} %bitcast.49, bf16[128,5,128]{0,2,1:T(8,128)(2,1)S(1)} %bitcast.45, f32[128,128]{1,0:T(8,128)S(1)} %fusion.59), kind=kOutput, calls=%fused_computation.28 | convolution fusion | flops 42106880 | bytes 884736 | tf_op jit(solution)/shard_map/hts,shd->thd/dot_general | solution.py:79
  60.0 0.4 collective-permute-done.9
  60.4 1.9 %multiply_reduce_fusion = (f32[128,5]{0,1:T(8,128)S(1)}, f32[128,5,128]{0,2,1:T(8,128)S(1)}) fusion(f32[5,128,128]{2,1,0:T(8,128)} %fusion.18, bf16[128,5,128]{0,2,1:T(8,128)(2,1)} %bitcast.50, bf16[5,128,128]{2,1,0:T(8,128)(2,1)} %copy-done.7, bf16[5,128,128]{2,1,0:T(8,128)(2,1)} %copy-done.8, bf16[5,128,128]{2,1,0:T(8,128)(2,1)} %copy-done.9, ...), kind=kOutput, calls=%fused_computation.83 | convolution fusion | flops 22855040 | bytes 1968646 | tf_op jit(solution)/shard_map/thd,hde->the/dot_general | solution.py:80
  62.4 0.0 collective-permute-done.10
  62.4 5.5 %fusion.11 = (bf16[640,1280]{1,0:T(8,128)(2,1)}, bf16[640,1280]{1,0:T(8,128)(2,1)}, bf16[640,1280]{1,0:T(8,128)(2,1)S(1)}, bf16[640,1280]{1,0:T(8,128)(2,1)S(1)}) fusion(s32[]{:T(128)S(6)} %select_n.200, s32[]{:T(128)S(6)} %select_n.202, bf16[1,640,2560]{2,1,0:T(8,128)(2,1)} %bitcast.7, bf16[1,640,2560]{2,1,0:T(8,128)(2,1)} %bitcast.8, s32[]{:T(128)S(6)} %select_n.205, ...), kind=kLoop, calls=%fused_computation.19 | loop fusion | flops 13107200 | bytes 13107232 | tf_op jit(solution)/shard_map/squeeze | solution.py:98
  67.9 0.7 fusion.4
  68.6 1.1 copy-done.2
  69.6 0.1 fusion.74
  69.7 0.8 broadcast_select_fusion
  70.5 7.1 %collective-permute-start.11 = (bf16[128,1280]{1,0:T(8,128)(2,1)}, bf16[128,1280]{1,0:T(8,128)(2,1)}, u32[]{:S(2)}, u32[]{:S(2)}) collective-permute-start(bf16[128,1280]{1,0:T(8,128)(2,1)} %broadcast_select_fusion), channel_id=1, source_target_pairs={{0,1},{3,2},{4,5},{7,6},{8,9},{11,10},{12,13},{15,14},{16,17},{19,... | collective-permute-start | bytes 983048 | tf_op jit(solution)/shard_map/ppermute | solution.py:116
  77.6 2.7 %fusion = f32[128,2560]{1,0:T(8,128)S(1)} fusion(bf16[128,640]{0,1:T(8,128)(2,1)S(1)} %bitcast.52, bf16[640,1280]{1,0:T(8,128)(2,1)} %get-tuple-element.18, bf16[640,1280]{1,0:T(8,128)(2,1)} %get-tuple-element.17), kind=kOutput, calls=%fused_computation.8 | convolution fusion | flops 425984000 | bytes 4751360 | tf_op jit(solution)/shard_map/dot_general | solution.py:100
  80.3 3.1 %collective-permute-done.11 = bf16[128,1280]{1,0:T(8,128)(2,1)} collective-permute-done((bf16[128,1280]{1,0:T(8,128)(2,1)}, bf16[128,1280]{1,0:T(8,128)(2,1)}, u32[]{:S(2)}, u32[]{:S(2)}) %collective-permute-start.11) | collective-permute-done | bytes 327712 | tf_op jit(solution)/shard_map/ppermute | solution.py:116
  83.5 1.1 fusion.22
  84.6 4.4 %collective-permute-start.12 = (bf16[128,1280]{1,0:T(8,128)(2,1)S(1)}, bf16[128,1280]{1,0:T(8,128)(2,1)S(1)}, u32[]{:S(2)}, u32[]{:S(2)}) collective-permute-start(bf16[128,1280]{1,0:T(8,128)(2,1)S(1)} %get-tuple-element.13), channel_id=1, source_target_pairs={{0,1},{1,2},{4,5},{5,6},{8,9},{9,10},{12,13},{13,14},{16,17},{17,1... | collective-permute-start | bytes 983048 | tf_op jit(solution)/shard_map/ppermute | solution.py:120
  89.0 0.7 collective-permute-start.13
  89.7 4.7 %collective-permute-done.12 = bf16[128,1280]{1,0:T(8,128)(2,1)S(1)} collective-permute-done((bf16[128,1280]{1,0:T(8,128)(2,1)S(1)}, bf16[128,1280]{1,0:T(8,128)(2,1)S(1)}, u32[]{:S(2)}, u32[]{:S(2)}) %collective-permute-start.12) | collective-permute-done | bytes 327712 | tf_op jit(solution)/shard_map/ppermute | solution.py:120
  94.4 0.0 collective-permute-done.13
  94.4 0.0 copy-done.3
  94.4 0.1 add_convert_fusion
  94.5 7.0 %collective-permute-start.14 = (bf16[128,1280]{1,0:T(8,128)(2,1)S(1)}, bf16[128,1280]{1,0:T(8,128)(2,1)S(1)}, u32[]{:S(2)}, u32[]{:S(2)}) collective-permute-start(bf16[128,1280]{1,0:T(8,128)(2,1)S(1)} %get-tuple-element.15), channel_id=1, source_target_pairs={{0,1},{1,2},{2,3},{4,5},{5,6},{6,7},{8,9},{9,10},{10,11},{12,13},{... | collective-permute-start | bytes 983048 | tf_op jit(solution)/shard_map/ppermute | solution.py:120
  101.5 1.3 %collective-permute-start.15 = (bf16[128,1280]{1,0:T(8,128)(2,1)S(1)}, bf16[128,1280]{1,0:T(8,128)(2,1)S(1)}, u32[]{:S(2)}, u32[]{:S(2)}) collective-permute-start(bf16[128,1280]{1,0:T(8,128)(2,1)S(1)} %get-tuple-element.16), channel_id=1, source_target_pairs={{1,0},{2,1},{3,2},{5,4},{6,5},{7,6},{9,8},{10,9},{11,10},{13,12},{... | collective-permute-start | bytes 983048 | tf_op jit(solution)/shard_map/ppermute | solution.py:121
  102.8 3.3 %collective-permute-done.14 = bf16[128,1280]{1,0:T(8,128)(2,1)S(1)} collective-permute-done((bf16[128,1280]{1,0:T(8,128)(2,1)S(1)}, bf16[128,1280]{1,0:T(8,128)(2,1)S(1)}, u32[]{:S(2)}, u32[]{:S(2)}) %collective-permute-start.14) | collective-permute-done | bytes 327712 | tf_op jit(solution)/shard_map/ppermute | solution.py:120
  106.0 4.4 %collective-permute-done.15 = bf16[128,1280]{1,0:T(8,128)(2,1)S(1)} collective-permute-done((bf16[128,1280]{1,0:T(8,128)(2,1)S(1)}, bf16[128,1280]{1,0:T(8,128)(2,1)S(1)}, u32[]{:S(2)}, u32[]{:S(2)}) %collective-permute-start.15) | collective-permute-done | bytes 327712 | tf_op jit(solution)/shard_map/ppermute | solution.py:121
  110.4 0.8 fusion.48
  (15 shorter events, 0.1 us)
Async XLA Ops:
  0.0 3.4 %copy-start = (bf16[2560,640]{1,0:T(8,128)(2,1)S(1)}, bf16[2560,640]{1,0:T(8,128)(2,1)}, u32[]{:S(2)}) copy-start(bf16[2560,640]{1,0:T(8,128)(2,1)} %param.7) | copy-start | bytes 9830404
  0.0 3.4 %collective-permute-start = (bf16[128,5120]{1,0:T(8,128)(2,1)}, bf16[128,5120]{1,0:T(8,128)(2,1)}, u32[]{:S(2)}, u32[]{:S(2)}) collective-permute-start(bf16[128,5120]{1,0:T(8,128)(2,1)} %bitcast.48), channel_id=1, source_target_pairs={{0,4},{4,0},{1,5},{5,1},{2,6},{6,2},{3,7},{7,3},{8,12},{12,8},{9,1... | collective-permute-start | bytes 3932168 | tf_op jit(solution)/shard_map/ppermute | solution.py:12
  0.0 5.1 %copy-start.1 = (bf16[2560,640]{1,0:T(8,128)(2,1)S(1)}, bf16[2560,640]{1,0:T(8,128)(2,1)}, u32[]{:S(2)}) copy-start(bf16[2560,640]{1,0:T(8,128)(2,1)} %param.8) | copy-start | bytes 9830404
  7.8 4.2 %collective-permute-start.1 = (f32[128,1280]{1,0:T(8,128)}, f32[128,1280]{1,0:T(8,128)}, u32[]{:S(2)}, u32[]{:S(2)}) collective-permute-start(f32[128,1280]{1,0:T(8,128)} %pad_maximum_fusion), channel_id=1, source_target_pairs={{0,4},{4,0},{1,5},{5,1},{2,6},{6,2},{3,7},{7,3},{8,12},{12,8},{9,1... | collective-permute-start | bytes 1966088 | tf_op jit(solution)/shard_map/ppermute | solution.py:12
  8.0 54.4 %collective-permute-start.10 = (bf16[640,2560]{1,0:T(8,128)(2,1)}, bf16[640,2560]{1,0:T(8,128)(2,1)}, u32[]{:S(2)}, u32[]{:S(2)}) collective-permute-start(bf16[640,2560]{1,0:T(8,128)(2,1)} %param.9), channel_id=1, source_target_pairs={{0,4},{4,0},{1,5},{5,1},{2,6},{6,2},{3,7},{7,3},{8,12},{12,8},{9,1... | collective-permute-start | bytes 9830408 | tf_op jit(solution)/shard_map/ppermute | solution.py:12
  8.3 3.6 %copy-start.6 = (bf16[1,128,5120]{2,1,0:T(8,128)(2,1)S(1)}, bf16[1,128,5120]{2,1,0:T(8,128)(2,1)}, u32[]{:S(2)}) copy-start(bf16[1,128,5120]{2,1,0:T(8,128)(2,1)} %param.5) | copy-start | bytes 3932164
  20.6 18.8 %copy-start.5 = (f32[128,640]{1,0:T(8,128)S(1)}, f32[128,640]{1,0:T(8,128)}, u32[]{:S(2)}) copy-start(f32[128,640]{1,0:T(8,128)} %fusion.27) | copy-start | bytes 983044
  21.8 11.9 %copy-start.4 = (f32[5,128,128]{2,1,0:T(8,128)}, f32[5,128,128]{2,1,0:T(8,128)S(1)}, u32[]{:S(2)}) copy-start(f32[5,128,128]{2,1,0:T(8,128)S(1)} %get-tuple-element.28) | copy-start | bytes 983044
  21.9 7.8 %collective-permute-start.3 = (bf16[5,128,128]{2,1,0:T(8,128)(2,1)S(1)}, bf16[5,128,128]{2,1,0:T(8,128)(2,1)S(1)}, u32[]{:S(2)}, u32[]{:S(2)}) collective-permute-start(bf16[5,128,128]{2,1,0:T(8,128)(2,1)S(1)} %get-tuple-element.27), channel_id=1, source_target_pairs={{0,8},{8,16},{16,24},{24,0},{32,40},{40,48},{48,56},{56,32},{64,72... | collective-permute-start | bytes 491528 | tf_op jit(solution)/shard_map/ppermute | solution.py:16
  23.4 8.6 %collective-permute-start.4 = (bf16[5,128,128]{2,1,0:T(8,128)(2,1)S(1)}, bf16[5,128,128]{2,1,0:T(8,128)(2,1)S(1)}, u32[]{:S(2)}, u32[]{:S(2)}) collective-permute-start(bf16[5,128,128]{2,1,0:T(8,128)(2,1)S(1)} %get-tuple-element.27), channel_id=1, source_target_pairs={{0,16},{8,24},{16,0},{24,8},{32,48},{40,56},{48,32},{56,40},{64,80... | collective-permute-start | bytes 491528 | tf_op jit(solution)/shard_map/ppermute | solution.py:16
  24.5 9.2 %collective-permute-start.5 = (bf16[5,128,128]{2,1,0:T(8,128)(2,1)S(1)}, bf16[5,128,128]{2,1,0:T(8,128)(2,1)S(1)}, u32[]{:S(2)}, u32[]{:S(2)}) collective-permute-start(bf16[5,128,128]{2,1,0:T(8,128)(2,1)S(1)} %get-tuple-element.27), channel_id=1, source_target_pairs={{0,24},{8,0},{16,8},{24,16},{32,56},{40,32},{48,40},{56,48},{64,88... | collective-permute-start | bytes 491528 | tf_op jit(solution)/shard_map/ppermute | solution.py:16
  29.5 9.9 %collective-permute-start.2 = (f32[128,640]{1,0:T(8,128)S(1)}, f32[128,640]{1,0:T(8,128)S(1)}, u32[]{:S(2)}, u32[]{:S(2)}) collective-permute-start(f32[128,640]{1,0:T(8,128)S(1)} %fusion.31), channel_id=1, source_target_pairs={{0,4},{4,0},{1,5},{5,1},{2,6},{6,2},{3,7},{7,3},{8,12},{12,8},{9,1... | collective-permute-start | bytes 983048 | tf_op jit(solution)/shard_map/ppermute | solution.py:12
  29.6 4.9 %copy-start.7 = (bf16[5,128,128]{2,1,0:T(8,128)(2,1)}, bf16[5,128,128]{2,1,0:T(8,128)(2,1)S(1)}, u32[]{:S(2)}) copy-start(bf16[5,128,128]{2,1,0:T(8,128)(2,1)S(1)} %collective-permute-done.3) | copy-start | bytes 491524
  32.0 4.1 %copy-start.8 = (bf16[5,128,128]{2,1,0:T(8,128)(2,1)}, bf16[5,128,128]{2,1,0:T(8,128)(2,1)S(1)}, u32[]{:S(2)}) copy-start(bf16[5,128,128]{2,1,0:T(8,128)(2,1)S(1)} %collective-permute-done.4) | copy-start | bytes 491524
  33.7 3.9 %copy-start.9 = (bf16[5,128,128]{2,1,0:T(8,128)(2,1)}, bf16[5,128,128]{2,1,0:T(8,128)(2,1)S(1)}, u32[]{:S(2)}) copy-start(bf16[5,128,128]{2,1,0:T(8,128)(2,1)S(1)} %collective-permute-done.5) | copy-start | bytes 491524
  34.5 7.4 %collective-permute-start.6 = (bf16[5,128,128]{2,1,0:T(8,128)(2,1)}, bf16[5,128,128]{2,1,0:T(8,128)(2,1)}, u32[]{:S(2)}, u32[]{:S(2)}) collective-permute-start(bf16[5,128,128]{2,1,0:T(8,128)(2,1)} %fusion.60), channel_id=1, source_target_pairs={{0,32},{8,40},{16,48},{24,56},{32,64},{40,72},{48,80},{56,88},{64,... | collective-permute-start | bytes 491528 | tf_op jit(solution)/shard_map/ppermute | solution.py:16
  36.1 8.8 %collective-permute-start.7 = (bf16[5,128,128]{2,1,0:T(8,128)(2,1)}, bf16[5,128,128]{2,1,0:T(8,128)(2,1)}, u32[]{:S(2)}, u32[]{:S(2)}) collective-permute-start(bf16[5,128,128]{2,1,0:T(8,128)(2,1)} %fusion.60), channel_id=1, source_target_pairs={{0,64},{8,72},{16,80},{24,88},{32,96},{40,104},{48,112},{56,120},{... | collective-permute-start | bytes 491528 | tf_op jit(solution)/shard_map/ppermute | solution.py:16
  37.7 8.9 %collective-permute-start.8 = (bf16[5,128,128]{2,1,0:T(8,128)(2,1)}, bf16[5,128,128]{2,1,0:T(8,128)(2,1)}, u32[]{:S(2)}, u32[]{:S(2)}) collective-permute-start(bf16[5,128,128]{2,1,0:T(8,128)(2,1)} %fusion.60), channel_id=1, source_target_pairs={{0,96},{8,104},{16,112},{24,120},{32,0},{40,8},{48,16},{56,24},{64... | collective-permute-start | bytes 491528 | tf_op jit(solution)/shard_map/ppermute | solution.py:16
  48.7 11.7 %collective-permute-start.9 = (bf16[5,128,128]{2,1,0:T(8,128)(2,1)}, bf16[5,128,128]{2,1,0:T(8,128)(2,1)}, u32[]{:S(2)}, u32[]{:S(2)}) collective-permute-start(bf16[5,128,128]{2,1,0:T(8,128)(2,1)} %fusion.47), channel_id=1, source_target_pairs={{0,128},{8,136},{16,144},{24,152},{32,160},{40,168},{48,176},{56,1... | collective-permute-start | bytes 491528 | tf_op jit(solution)/shard_map/ppermute | solution.py:16
  68.6 1.1 copy-start.2
  70.5 13.0 %collective-permute-start.11 = (bf16[128,1280]{1,0:T(8,128)(2,1)}, bf16[128,1280]{1,0:T(8,128)(2,1)}, u32[]{:S(2)}, u32[]{:S(2)}) collective-permute-start(bf16[128,1280]{1,0:T(8,128)(2,1)} %broadcast_select_fusion), channel_id=1, source_target_pairs={{0,1},{3,2},{4,5},{7,6},{8,9},{11,10},{12,13},{15,14},{16,17},{19,... | collective-permute-start | bytes 983048 | tf_op jit(solution)/shard_map/ppermute | solution.py:116
  77.6 16.7 %copy-start.3 = (f32[128,2560]{1,0:T(8,128)S(1)}, f32[128,2560]{1,0:T(8,128)}, u32[]{:S(2)}) copy-start(f32[128,2560]{1,0:T(8,128)} %copy-done.2) | copy-start | bytes 3932164
  84.6 9.8 %collective-permute-start.12 = (bf16[128,1280]{1,0:T(8,128)(2,1)S(1)}, bf16[128,1280]{1,0:T(8,128)(2,1)S(1)}, u32[]{:S(2)}, u32[]{:S(2)}) collective-permute-start(bf16[128,1280]{1,0:T(8,128)(2,1)S(1)} %get-tuple-element.13), channel_id=1, source_target_pairs={{0,1},{1,2},{4,5},{5,6},{8,9},{9,10},{12,13},{13,14},{16,17},{17,1... | collective-permute-start | bytes 983048 | tf_op jit(solution)/shard_map/ppermute | solution.py:120
  89.0 5.4 %collective-permute-start.13 = (bf16[128,1280]{1,0:T(8,128)(2,1)S(1)}, bf16[128,1280]{1,0:T(8,128)(2,1)S(1)}, u32[]{:S(2)}, u32[]{:S(2)}) collective-permute-start(bf16[128,1280]{1,0:T(8,128)(2,1)S(1)} %get-tuple-element.14), channel_id=1, source_target_pairs={{2,1},{3,2},{6,5},{7,6},{10,9},{11,10},{14,13},{15,14},{18,17},{19... | collective-permute-start | bytes 983048 | tf_op jit(solution)/shard_map/ppermute | solution.py:121
  94.5 11.5 %collective-permute-start.14 = (bf16[128,1280]{1,0:T(8,128)(2,1)S(1)}, bf16[128,1280]{1,0:T(8,128)(2,1)S(1)}, u32[]{:S(2)}, u32[]{:S(2)}) collective-permute-start(bf16[128,1280]{1,0:T(8,128)(2,1)S(1)} %get-tuple-element.15), channel_id=1, source_target_pairs={{0,1},{1,2},{2,3},{4,5},{5,6},{6,7},{8,9},{9,10},{10,11},{12,13},{... | collective-permute-start | bytes 983048 | tf_op jit(solution)/shard_map/ppermute | solution.py:120
  101.5 9.0 %collective-permute-start.15 = (bf16[128,1280]{1,0:T(8,128)(2,1)S(1)}, bf16[128,1280]{1,0:T(8,128)(2,1)S(1)}, u32[]{:S(2)}, u32[]{:S(2)}) collective-permute-start(bf16[128,1280]{1,0:T(8,128)(2,1)S(1)} %get-tuple-element.16), channel_id=1, source_target_pairs={{1,0},{2,1},{3,2},{5,4},{6,5},{7,6},{9,8},{10,9},{11,10},{13,12},{... | collective-permute-start | bytes 983048 | tf_op jit(solution)/shard_map/ppermute | solution.py:121

commit v14 on v12

--- a/solution.py
+++ b/solution.py
@@ -110,6 +110,11 @@
         send_r, send_l = lax.optimization_barrier((send_r, send_l))
         rpairs = [(j, j + 1) for j in range(s) if j + 1 < n]
         lpairs = [(j, j - 1) for j in range(n - s, n) if j - 1 >= 0]
+        if s == 1:
+            got = lax.ppermute(jnp.where(h == 0, send_r, send_l), "head", rpairs + lpairs).astype(F32)
+            right = jnp.where(h == 1, got, 0.0)
+            left = jnp.where(h == n - 2, got, 0.0)
+            continue
         right = lax.ppermute(send_r, "head", rpairs).astype(F32)
         left = lax.ppermute(send_l, "head", lpairs).astype(F32)
     mixed = (block(0) + right + left).astype(BF16)

time: 107 us -> 111 us (1.037)
  other arithmetic: 11.7 us -> 14.7 us
  matrix products: 21.3 us -> 23.3 us
  waiting for transfers between devices: 26.2 us -> 24.4 us
    ppermute x0 -> x1, starting transfers between devices: none -> 7.15 us  [shards(): lax.ppermute(jnp.where(h == 0, send_r, send_l), 'head', rpairs + lpairs)]
    ppermute x3 -> x2, starting transfers between devices: 18.7 us -> 11.7 us  [shards(): right = lax.ppermute(send_r, 'head', rpairs).astype(F32)]
    ppermute x3 -> x2, waiting for transfers between devices: 12.7 us -> 7.88 us  [shards(): right = lax.ppermute(send_r, 'head', rpairs).astype(F32)]
    ppermute x0 -> x1, waiting for transfers between devices: none -> 3.05 us  [shards(): lax.ppermute(jnp.where(h == 0, send_r, send_l), 'head', rpairs + lpairs)]
    dot_general x1, matrix products: 0.71 us -> 2.73 us  [shards(): jnp.dot(normed, jnp.concatenate([pieces[2], pieces[0]], axis=1), preferre...]
    squeeze x1, other arithmetic: 4.34 us -> 5.49 us  [shards(): pieces.append(piece[0])]
    unnamed x20 -> x24, local copies, waits for them, and re-layouts: 1.45 us -> 2.53 us
    ppermute x3 -> x2, starting transfers between devices: 2.66 us -> 1.97 us  [shards(): left = lax.ppermute(send_l, 'head', lpairs).astype(F32)]
  transfers between devices with their start and end apart: 18 -> 17, of which waited for: 9 -> 9; matrix products, arithmetic and copies ran while one was open for 29% -> 30% of each run, Pallas kernels for 0% -> 0%
where the time goes in v14:
time: 111 us; the launch traced here: 110 us
  starting transfers between devices  40.8 us (37%)
  waiting for transfers between devices  24.4 us (22%)
  matrix products  23.3 us (21%)
  other arithmetic  14.7 us (13%)
  local copies, waits for them, and re-layouts  7.09 us (6%)
    ppermute x7, starting transfers between devices, shifted(): return lax.ppermute(x, axis, pairs)  18.9 us
    ppermute x2, starting transfers between devices, shards(): right = lax.ppermute(send_r, 'head', rpairs).astype(F32)  11.7 us
    ppermute x7, waiting for transfers between devices, shifted(): return lax.ppermute(x, axis, pairs)  9.08 us
    ppermute x2, waiting for transfers between devices, shards(): right = lax.ppermute(send_r, 'head', rpairs).astype(F32)  7.88 us
    ppermute x1, starting transfers between devices, shards(): lax.ppermute(jnp.where(h == 0, send_r, send_l), 'head', rpairs + lpairs)  7.15 us
    dot_general x3, matrix products, shards(): own = jnp.dot(mine_cols, w, preferred_element_type=F32)  6.89 us
    dot_general x3, matrix products, shards(): lent = swap_cores(jnp.dot(got_cols, w, preferred_element_type=F32))  6.87 us
    squeeze x1, other arithmetic, shards(): pieces.append(piece[0])  5.49 us
  transfers between devices with their start and end apart: 17, of which 9 were waited for; matrix products, arithmetic and copies ran while one was open for 30% of the time, Pallas kernels for 0%

profile of v14, /device:TPU:10, one launch (start us, length us, event | category | flops | bytes accessed | tf_op | source)
XLA Modules:
  0.0 110.5 jit_solution(10326250802977412886)
XLA Ops:
  0.0 0.0 collective-permute-start
  0.0 0.5 collective-permute-start.11
  0.5 1.4 %copy-done = bf16[2560,640]{1,0:T(8,128)(2,1)S(1)} copy-done((bf16[2560,640]{1,0:T(8,128)(2,1)S(1)}, bf16[2560,640]{1,0:T(8,128)(2,1)}, u32[]{:S(2)}) %copy-start) | copy-done | bytes 3276824
  1.9 2.7 %fusion.28 = f32[128,640]{1,0:T(8,128)} fusion(bf16[2560,640]{1,0:T(8,128)(2,1)S(1)} %copy-done, bf16[1,128,5120]{2,1,0:T(8,128)(2,1)} %param.5, s32[]{:T(128)S(6)} %select_n.176), kind=kOutput, calls=%fused_computation.41 | convolution fusion | flops 419430400 | bytes 4259844 | tf_op jit(solution)/shard_map/dot_general | solution.py:63
  4.6 0.0 collective-permute-done
  4.6 2.6 %fusion.34 = f32[128,640]{1,0:T(8,128)} fusion(bf16[2560,640]{1,0:T(8,128)(2,1)S(1)} %copy-done, bf16[128,5120]{1,0:T(8,128)(2,1)} %collective-permute-done, s32[]{:T(128)S(6)} %select_n.176), kind=kOutput, calls=%fused_computation.51 | convolution fusion | flops 419430400 | bytes 4259844 | tf_op jit(solution)/shard_map/dot_general | solution.py:62
  7.2 0.0 collective-permute-start.1
  7.2 0.0 copy-done.1
  7.2 2.5 %fusion.30 = f32[128,640]{1,0:T(8,128)} fusion(bf16[2560,640]{1,0:T(8,128)(2,1)S(1)} %copy-done.1, bf16[128,5120]{1,0:T(8,128)(2,1)} %collective-permute-done, s32[]{:T(128)S(6)} %select_n.176), kind=kOutput, calls=%fused_computation.47 | convolution fusion | flops 419430400 | bytes 4259844 | tf_op jit(solution)/shard_map/dot_general | solution.py:62
  9.7 0.5 collective-permute-start.3
  10.2 0.0 copy-done.3
  10.2 1.4 %fusion.24 = f32[128,640]{1,0:T(8,128)} fusion(bf16[2560,640]{1,0:T(8,128)(2,1)S(1)} %copy-done.1, bf16[1,128,5120]{2,1,0:T(8,128)(2,1)S(1)} %copy-done.3, s32[]{:T(128)S(6)} %select_n.176), kind=kOutput, calls=%fused_computation.37 | convolution fusion | flops 419430400 | bytes 4259844 | tf_op jit(solution)/shard_map/dot_general | solution.py:63
  11.6 0.0 collective-permute-done.1
  11.6 1.8 %add_convert_fusion.2 = bf16[128,640]{1,0:T(8,128)(2,1)} fusion(f32[128,640]{1,0:T(8,128)} %fusion.28, f32[128,640]{1,0:T(8,128)} %collective-permute-done.1), kind=kLoop, calls=%fused_computation.81 | loop fusion | flops 163840 | bytes 819200 | tf_op jit(solution)/shard_map/convert_element_type | solution.py:69
  13.4 1.1 copy.11
  14.5 0.0 collective-permute-done.3
  14.5 1.9 %multiply_convert_fusion.1 = bf16[128,640]{1,0:T(8,128)(2,1)} fusion(f32[128,640]{1,0:T(8,128)} %fusion.24, f32[128,640]{1,0:T(8,128)} %collective-permute-done.3), kind=kLoop, calls=%fused_computation.79 | loop fusion | flops 491520 | bytes 819200 | tf_op jit(solution)/shard_map/convert_element_type | solution.py:68
  16.3 1.7 %copy.13 = bf16[128,640]{0,1:T(8,128)(2,1)} copy(bf16[128,640]{1,0:T(8,128)(2,1)} %multiply_convert_fusion.1) | data formatting | bytes 327680 | tf_op jit(solution)/shard_map/convert_element_type | solution.py:68
  18.1 1.3 %fusion.69 = (bf16[5,128,128]{2,1,0:T(8,128)(2,1)S(1)}, f32[5,128,128]{2,1,0:T(8,128)S(1)}) fusion(bf16[128,5,128]{0,2,1:T(8,128)(2,1)} %bitcast.44, bf16[128,5,128]{0,2,1:T(8,128)(2,1)S(1)} %bitcast.42), kind=kOutput, calls=%fused_computation.105 | convolution fusion | flops 21053440 | bytes 819200 | tf_op jit(solution)/shard_map/thd,the->hde/dot_general | solution.py:70
  19.4 1.6 %collective-permute-start.4 = (bf16[5,128,128]{2,1,0:T(8,128)(2,1)S(1)}, bf16[5,128,128]{2,1,0:T(8,128)(2,1)S(1)}, u32[]{:S(2)}, u32[]{:S(2)}) collective-permute-start(bf16[5,128,128]{2,1,0:T(8,128)(2,1)S(1)} %get-tuple-element.27), channel_id=1, source_target_pairs={{0,8},{8,16},{16,24},{24,0},{32,40},{40,48},{48,56},{56,32},{64,72... | collective-permute-start | bytes 491528 | tf_op jit(solution)/shard_map/ppermute | solution.py:16
  20.9 1.1 %collective-permute-start.5 = (bf16[5,128,128]{2,1,0:T(8,128)(2,1)S(1)}, bf16[5,128,128]{2,1,0:T(8,128)(2,1)S(1)}, u32[]{:S(2)}, u32[]{:S(2)}) collective-permute-start(bf16[5,128,128]{2,1,0:T(8,128)(2,1)S(1)} %get-tuple-element.27), channel_id=1, source_target_pairs={{0,16},{8,24},{16,0},{24,8},{32,48},{40,56},{48,32},{56,40},{64,80... | collective-permute-start | bytes 491528 | tf_op jit(solution)/shard_map/ppermute | solution.py:16
  22.0 2.1 %collective-permute-start.6 = (bf16[5,128,128]{2,1,0:T(8,128)(2,1)S(1)}, bf16[5,128,128]{2,1,0:T(8,128)(2,1)S(1)}, u32[]{:S(2)}, u32[]{:S(2)}) collective-permute-start(bf16[5,128,128]{2,1,0:T(8,128)(2,1)S(1)} %get-tuple-element.27), channel_id=1, source_target_pairs={{0,24},{8,0},{16,8},{24,16},{32,56},{40,32},{48,40},{56,48},{64,88... | collective-permute-start | bytes 491528 | tf_op jit(solution)/shard_map/ppermute | solution.py:16
  24.2 2.8 %fusion.26 = f32[128,640]{1,0:T(8,128)S(1)} fusion(bf16[2560,640]{1,0:T(8,128)(2,1)} %param.6, bf16[1,128,5120]{2,1,0:T(8,128)(2,1)} %param.5, s32[]{:T(128)S(6)} %select_n.176), kind=kOutput, calls=%fused_computation.39 | convolution fusion | flops 419430400 | bytes 4259844 | tf_op jit(solution)/shard_map/dot_general | solution.py:63
  27.0 0.0 collective-permute-done.4
  27.0 2.5 %collective-permute-done.5 = bf16[5,128,128]{2,1,0:T(8,128)(2,1)S(1)} collective-permute-done((bf16[5,128,128]{2,1,0:T(8,128)(2,1)S(1)}, bf16[5,128,128]{2,1,0:T(8,128)(2,1)S(1)}, u32[]{:S(2)}, u32[]{:S(2)}) %collective-permute-start.5) | collective-permute-done | bytes 163872 | tf_op jit(solution)/shard_map/ppermute | solution.py:16
  29.5 1.6 %collective-permute-done.6 = bf16[5,128,128]{2,1,0:T(8,128)(2,1)S(1)} collective-permute-done((bf16[5,128,128]{2,1,0:T(8,128)(2,1)S(1)}, bf16[5,128,128]{2,1,0:T(8,128)(2,1)S(1)}, u32[]{:S(2)}, u32[]{:S(2)}) %collective-permute-start.6) | collective-permute-done | bytes 163872 | tf_op jit(solution)/shard_map/ppermute | solution.py:16
  31.1 0.1 fusion.58
  31.2 1.6 %collective-permute-start.7 = (bf16[5,128,128]{2,1,0:T(8,128)(2,1)S(1)}, bf16[5,128,128]{2,1,0:T(8,128)(2,1)S(1)}, u32[]{:S(2)}, u32[]{:S(2)}) collective-permute-start(bf16[5,128,128]{2,1,0:T(8,128)(2,1)S(1)} %fusion.58), channel_id=1, source_target_pairs={{0,32},{8,40},{16,48},{24,56},{32,64},{40,72},{48,80},{56,88},{64,... | collective-permute-start | bytes 491528 | tf_op jit(solution)/shard_map/ppermute | solution.py:16
  32.8 1.6 %collective-permute-start.8 = (bf16[5,128,128]{2,1,0:T(8,128)(2,1)S(1)}, bf16[5,128,128]{2,1,0:T(8,128)(2,1)S(1)}, u32[]{:S(2)}, u32[]{:S(2)}) collective-permute-start(bf16[5,128,128]{2,1,0:T(8,128)(2,1)S(1)} %fusion.58), channel_id=1, source_target_pairs={{0,64},{8,72},{16,80},{24,88},{32,96},{40,104},{48,112},{56,120},{... | collective-permute-start | bytes 491528 | tf_op jit(solution)/shard_map/ppermute | solution.py:16
  34.5 1.7 %collective-permute-start.9 = (bf16[5,128,128]{2,1,0:T(8,128)(2,1)S(1)}, bf16[5,128,128]{2,1,0:T(8,128)(2,1)S(1)}, u32[]{:S(2)}, u32[]{:S(2)}) collective-permute-start(bf16[5,128,128]{2,1,0:T(8,128)(2,1)S(1)} %fusion.58), channel_id=1, source_target_pairs={{0,96},{8,104},{16,112},{24,120},{32,0},{40,8},{48,16},{56,24},{64... | collective-permute-start | bytes 491528 | tf_op jit(solution)/shard_map/ppermute | solution.py:16
  36.2 1.8 %fusion.32 = f32[128,640]{1,0:T(8,128)S(1)} fusion(bf16[2560,640]{1,0:T(8,128)(2,1)S(1)} %copy-done.2, bf16[128,5120]{1,0:T(8,128)(2,1)} %collective-permute-done, s32[]{:T(128)S(6)} %select_n.176), kind=kOutput, calls=%fused_computation.49 | convolution fusion | flops 419430400 | bytes 4259844 | tf_op jit(solution)/shard_map/dot_general | solution.py:62
  38.0 0.1 collective-permute-start.2
  38.1 0.0 collective-permute-done.7
  38.1 3.2 %collective-permute-done.8 = bf16[5,128,128]{2,1,0:T(8,128)(2,1)S(1)} collective-permute-done((bf16[5,128,128]{2,1,0:T(8,128)(2,1)S(1)}, bf16[5,128,128]{2,1,0:T(8,128)(2,1)S(1)}, u32[]{:S(2)}, u32[]{:S(2)}) %collective-permute-start.8) | collective-permute-done | bytes 163872 | tf_op jit(solution)/shard_map/ppermute | solution.py:16
  41.3 1.8 %collective-permute-done.9 = bf16[5,128,128]{2,1,0:T(8,128)(2,1)S(1)} collective-permute-done((bf16[5,128,128]{2,1,0:T(8,128)(2,1)S(1)}, bf16[5,128,128]{2,1,0:T(8,128)(2,1)S(1)}, u32[]{:S(2)}, u32[]{:S(2)}) %collective-permute-start.9) | collective-permute-done | bytes 163872 | tf_op jit(solution)/shard_map/ppermute | solution.py:16
  43.0 0.8 fusion.46
  43.9 9.1 %collective-permute-start.10 = (bf16[5,128,128]{2,1,0:T(8,128)(2,1)}, bf16[5,128,128]{2,1,0:T(8,128)(2,1)}, u32[]{:S(2)}, u32[]{:S(2)}) collective-permute-start(bf16[5,128,128]{2,1,0:T(8,128)(2,1)} %fusion.46), channel_id=1, source_target_pairs={{0,128},{8,136},{16,144},{24,152},{32,160},{40,168},{48,176},{56,1... | collective-permute-start | bytes 491528 | tf_op jit(solution)/shard_map/ppermute | solution.py:16
  52.9 0.0 collective-permute-done.2
  53.0 0.8 multiply_convert_fusion.2
  53.7 1.7 %copy.12 = bf16[128,640]{0,1:T(8,128)(2,1)} copy(bf16[128,640]{1,0:T(8,128)(2,1)} %multiply_convert_fusion.2) | data formatting | bytes 327680 | tf_op jit(solution)/shard_map/convert_element_type | solution.py:67
  55.5 0.1 collective-permute-done.10
  55.5 2.5 %fusion.49 = f32[5,128,128]{2,1,0:T(8,128)} fusion(bf16[128,5,128]{0,2,1:T(8,128)(2,1)} %bitcast.46, bf16[5,128,128]{2,1,0:T(8,128)(2,1)} %copy-done.6, bf16[5,128,128]{2,1,0:T(8,128)(2,1)} %copy-done.7, bf16[5,128,128]{2,1,0:T(8,128)(2,1)} %copy-done.8, bf16[5,128,128]{2,1,0:T(8,128)(2,1)} %copy-done.9, bf16[5,128,128]{2,1,0:T(8,128)(2,1)} %copy-done.10, ...), kind=kOutput, calls=%fused_computation.84 | convolution fusion | flops 22609920 | bytes 1638406 | tf_op jit(solution)/shard_map/thd,hde->the/dot_general | solution.py:78
  58.0 2.3 %multiply_reduce_fusion = (f32[128,5]{0,1:T(8,128)S(1)}, f32[128,5,128]{0,2,1:T(8,128)}) fusion(f32[5,128,128]{2,1,0:T(8,128)} %fusion.49, bf16[128,5,128]{0,2,1:T(8,128)(2,1)S(1)} %bitcast.43, bf16[128,5,128]{0,2,1:T(8,128)(2,1)} %bitcast.47, bf16[128,5,128]{0,2,1:T(8,128)(2,1)} %bitcast.45, f32[128,128]{1,0:T(8,128)S(1)} %fusion.57), kind=kOutput, calls=%fused_computation.78 | convolution fusion | flops 42352000 | bytes 1214976 | tf_op jit(solution)/shard_map/hts,shd->thd/dot_general | solution.py:77
  60.4 1.0 multiply_convert_fusion
  61.4 0.0 collective-permute-done.11
  61.4 5.5 %fusion.11 = (bf16[640,1280]{1,0:T(8,128)(2,1)}, bf16[640,1280]{1,0:T(8,128)(2,1)}, bf16[640,1280]{1,0:T(8,128)(2,1)S(1)}, bf16[640,1280]{1,0:T(8,128)(2,1)S(1)}) fusion(s32[]{:T(128)S(6)} %select_n.200, s32[]{:T(128)S(6)} %select_n.202, bf16[1,640,2560]{2,1,0:T(8,128)(2,1)} %bitcast.40, bf16[1,640,2560]{2,1,0:T(8,128)(2,1)} %bitcast.8, s32[]{:T(128)S(6)} %select_n.205, ...), kind=kLoop, calls=%fused_computation.19 | loop fusion | flops 13107200 | bytes 13107232 | tf_op jit(solution)/shard_map/squeeze | solution.py:96
  66.9 0.7 fusion.4
  67.6 1.1 copy-done.4
  68.7 0.1 fusion.68
  68.7 0.8 broadcast_select_fusion
  69.5 7.2 %collective-permute-start.12 = (bf16[128,1280]{1,0:T(8,128)(2,1)}, bf16[128,1280]{1,0:T(8,128)(2,1)}, u32[]{:S(2)}, u32[]{:S(2)}) collective-permute-start(bf16[128,1280]{1,0:T(8,128)(2,1)} %broadcast_select_fusion), channel_id=1, source_target_pairs={{0,1},{3,2},{4,5},{7,6},{8,9},{11,10},{12,13},{15,14},{16,17},{19,... | collective-permute-start | bytes 983048 | tf_op jit(solution)/shard_map/ppermute | solution.py:114
  76.6 2.7 %fusion = f32[128,2560]{1,0:T(8,128)S(1)} fusion(bf16[128,640]{0,1:T(8,128)(2,1)S(1)} %bitcast.49, bf16[640,1280]{1,0:T(8,128)(2,1)} %get-tuple-element.18, bf16[640,1280]{1,0:T(8,128)(2,1)} %get-tuple-element.17), kind=kOutput, calls=%fused_computation.8 | convolution fusion | flops 425984000 | bytes 4751360 | tf_op jit(solution)/shard_map/dot_general | solution.py:98
  79.4 3.0 %collective-permute-done.12 = bf16[128,1280]{1,0:T(8,128)(2,1)} collective-permute-done((bf16[128,1280]{1,0:T(8,128)(2,1)}, bf16[128,1280]{1,0:T(8,128)(2,1)}, u32[]{:S(2)}, u32[]{:S(2)}) %collective-permute-start.12) | collective-permute-done | bytes 327712 | tf_op jit(solution)/shard_map/ppermute | solution.py:114
  82.4 1.1 %fusion.21 = (bf16[128,1280]{1,0:T(8,128)(2,1)S(1)}, bf16[128,1280]{1,0:T(8,128)(2,1)S(1)}) fusion(bf16[128,1280]{1,0:T(8,128)(2,1)} %collective-permute-done.12, f32[128,2560]{1,0:T(8,128)S(1)} %fusion, pred[]{:T(512)S(6)} %eq.44, pred[]{:T(512)S(6)} %eq.42), kind=kLoop, calls=%fused_computation.33 | loop fusion | flops 1146880 | bytes 1638402 | tf_op jit(solution)/shard_map/convert_element_type | solution.py:109
  83.5 4.4 %collective-permute-start.13 = (bf16[128,1280]{1,0:T(8,128)(2,1)S(1)}, bf16[128,1280]{1,0:T(8,128)(2,1)S(1)}, u32[]{:S(2)}, u32[]{:S(2)}) collective-permute-start(bf16[128,1280]{1,0:T(8,128)(2,1)S(1)} %get-tuple-element.13), channel_id=1, source_target_pairs={{0,1},{1,2},{4,5},{5,6},{8,9},{9,10},{12,13},{13,14},{16,17},{17,1... | collective-permute-start | bytes 983048 | tf_op jit(solution)/shard_map/ppermute | solution.py:118
  87.9 0.7 collective-permute-start.14
  88.6 4.6 %collective-permute-done.13 = bf16[128,1280]{1,0:T(8,128)(2,1)S(1)} collective-permute-done((bf16[128,1280]{1,0:T(8,128)(2,1)S(1)}, bf16[128,1280]{1,0:T(8,128)(2,1)S(1)}, u32[]{:S(2)}, u32[]{:S(2)}) %collective-permute-start.13) | collective-permute-done | bytes 327712 | tf_op jit(solution)/shard_map/ppermute | solution.py:118
  93.3 0.0 collective-permute-done.14
  93.3 0.1 add_convert_fusion
  93.4 7.3 %collective-permute-start.15 = (bf16[128,1280]{1,0:T(8,128)(2,1)S(1)}, bf16[128,1280]{1,0:T(8,128)(2,1)S(1)}, u32[]{:S(2)}, u32[]{:S(2)}) collective-permute-start(bf16[128,1280]{1,0:T(8,128)(2,1)S(1)} %get-tuple-element.15), channel_id=1, source_target_pairs={{0,1},{1,2},{2,3},{4,5},{5,6},{6,7},{8,9},{9,10},{10,11},{12,13},{... | collective-permute-start | bytes 983048 | tf_op jit(solution)/shard_map/ppermute | solution.py:118
  100.7 1.3 %collective-permute-start.16 = (bf16[128,1280]{1,0:T(8,128)(2,1)S(1)}, bf16[128,1280]{1,0:T(8,128)(2,1)S(1)}, u32[]{:S(2)}, u32[]{:S(2)}) collective-permute-start(bf16[128,1280]{1,0:T(8,128)(2,1)S(1)} %get-tuple-element.16), channel_id=1, source_target_pairs={{1,0},{2,1},{3,2},{5,4},{6,5},{7,6},{9,8},{10,9},{11,10},{13,12},{... | collective-permute-start | bytes 983048 | tf_op jit(solution)/shard_map/ppermute | solution.py:119
  102.0 3.3 %collective-permute-done.15 = bf16[128,1280]{1,0:T(8,128)(2,1)S(1)} collective-permute-done((bf16[128,1280]{1,0:T(8,128)(2,1)S(1)}, bf16[128,1280]{1,0:T(8,128)(2,1)S(1)}, u32[]{:S(2)}, u32[]{:S(2)}) %collective-permute-start.15) | collective-permute-done | bytes 327712 | tf_op jit(solution)/shard_map/ppermute | solution.py:118
  105.2 4.4 %collective-permute-done.16 = bf16[128,1280]{1,0:T(8,128)(2,1)S(1)} collective-permute-done((bf16[128,1280]{1,0:T(8,128)(2,1)S(1)}, bf16[128,1280]{1,0:T(8,128)(2,1)S(1)}, u32[]{:S(2)}, u32[]{:S(2)}) %collective-permute-start.16) | collective-permute-done | bytes 327712 | tf_op jit(solution)/shard_map/ppermute | solution.py:119
  109.7 0.8 fusion.47
  (22 shorter events, 0.1 us)
Async XLA Ops:
  0.0 1.9 %copy-start = (bf16[2560,640]{1,0:T(8,128)(2,1)S(1)}, bf16[2560,640]{1,0:T(8,128)(2,1)}, u32[]{:S(2)}) copy-start(bf16[2560,640]{1,0:T(8,128)(2,1)} %param.8) | copy-start | bytes 9830404
  0.0 4.6 %collective-permute-start = (bf16[128,5120]{1,0:T(8,128)(2,1)}, bf16[128,5120]{1,0:T(8,128)(2,1)}, u32[]{:S(2)}, u32[]{:S(2)}) collective-permute-start(bf16[128,5120]{1,0:T(8,128)(2,1)} %bitcast.41), channel_id=1, source_target_pairs={{0,4},{4,0},{1,5},{5,1},{2,6},{6,2},{3,7},{7,3},{8,12},{12,8},{9,1... | collective-permute-start | bytes 3932168 | tf_op jit(solution)/shard_map/ppermute | solution.py:12
  0.0 61.4 %collective-permute-start.11 = (bf16[640,2560]{1,0:T(8,128)(2,1)}, bf16[640,2560]{1,0:T(8,128)(2,1)}, u32[]{:S(2)}, u32[]{:S(2)}) collective-permute-start(bf16[640,2560]{1,0:T(8,128)(2,1)} %param.9), channel_id=1, source_target_pairs={{0,4},{4,0},{1,5},{5,1},{2,6},{6,2},{3,7},{7,3},{8,12},{12,8},{9,1... | collective-permute-start | bytes 9830408 | tf_op jit(solution)/shard_map/ppermute | solution.py:12
  1.9 5.3 %copy-start.1 = (bf16[2560,640]{1,0:T(8,128)(2,1)S(1)}, bf16[2560,640]{1,0:T(8,128)(2,1)}, u32[]{:S(2)}) copy-start(bf16[2560,640]{1,0:T(8,128)(2,1)} %param.7) | copy-start | bytes 9830404
  4.6 5.6 %copy-start.3 = (bf16[1,128,5120]{2,1,0:T(8,128)(2,1)S(1)}, bf16[1,128,5120]{2,1,0:T(8,128)(2,1)}, u32[]{:S(2)}) copy-start(bf16[1,128,5120]{2,1,0:T(8,128)(2,1)} %param.5) | copy-start | bytes 3932164
  7.2 4.4 %collective-permute-start.1 = (f32[128,640]{1,0:T(8,128)}, f32[128,640]{1,0:T(8,128)}, u32[]{:S(2)}, u32[]{:S(2)}) collective-permute-start(f32[128,640]{1,0:T(8,128)} %fusion.34), channel_id=1, source_target_pairs={{0,4},{4,0},{1,5},{5,1},{2,6},{6,2},{3,7},{7,3},{8,12},{12,8},{9,1... | collective-permute-start | bytes 983048 | tf_op jit(solution)/shard_map/ppermute | solution.py:12
  9.7 4.8 %collective-permute-start.3 = (f32[128,640]{1,0:T(8,128)}, f32[128,640]{1,0:T(8,128)}, u32[]{:S(2)}, u32[]{:S(2)}) collective-permute-start(f32[128,640]{1,0:T(8,128)} %fusion.30), channel_id=1, source_target_pairs={{0,4},{4,0},{1,5},{5,1},{2,6},{6,2},{3,7},{7,3},{8,12},{12,8},{9,1... | collective-permute-start | bytes 983048 | tf_op jit(solution)/shard_map/ppermute | solution.py:12
  18.1 18.1 %copy-start.2 = (bf16[2560,640]{1,0:T(8,128)(2,1)S(1)}, bf16[2560,640]{1,0:T(8,128)(2,1)}, u32[]{:S(2)}) copy-start(bf16[2560,640]{1,0:T(8,128)(2,1)} %param.6) | copy-start | bytes 9830404
  19.4 7.7 %collective-permute-start.4 = (bf16[5,128,128]{2,1,0:T(8,128)(2,1)S(1)}, bf16[5,128,128]{2,1,0:T(8,128)(2,1)S(1)}, u32[]{:S(2)}, u32[]{:S(2)}) collective-permute-start(bf16[5,128,128]{2,1,0:T(8,128)(2,1)S(1)} %get-tuple-element.27), channel_id=1, source_target_pairs={{0,8},{8,16},{16,24},{24,0},{32,40},{40,48},{48,56},{56,32},{64,72... | collective-permute-start | bytes 491528 | tf_op jit(solution)/shard_map/ppermute | solution.py:16
  20.9 8.6 %collective-permute-start.5 = (bf16[5,128,128]{2,1,0:T(8,128)(2,1)S(1)}, bf16[5,128,128]{2,1,0:T(8,128)(2,1)S(1)}, u32[]{:S(2)}, u32[]{:S(2)}) collective-permute-start(bf16[5,128,128]{2,1,0:T(8,128)(2,1)S(1)} %get-tuple-element.27), channel_id=1, source_target_pairs={{0,16},{8,24},{16,0},{24,8},{32,48},{40,56},{48,32},{56,40},{64,80... | collective-permute-start | bytes 491528 | tf_op jit(solution)/shard_map/ppermute | solution.py:16
  22.0 9.1 %collective-permute-start.6 = (bf16[5,128,128]{2,1,0:T(8,128)(2,1)S(1)}, bf16[5,128,128]{2,1,0:T(8,128)(2,1)S(1)}, u32[]{:S(2)}, u32[]{:S(2)}) collective-permute-start(bf16[5,128,128]{2,1,0:T(8,128)(2,1)S(1)} %get-tuple-element.27), channel_id=1, source_target_pairs={{0,24},{8,0},{16,8},{24,16},{32,56},{40,32},{48,40},{56,48},{64,88... | collective-permute-start | bytes 491528 | tf_op jit(solution)/shard_map/ppermute | solution.py:16
  27.0 16.8 %copy-start.6 = (bf16[5,128,128]{2,1,0:T(8,128)(2,1)}, bf16[5,128,128]{2,1,0:T(8,128)(2,1)S(1)}, u32[]{:S(2)}) copy-start(bf16[5,128,128]{2,1,0:T(8,128)(2,1)S(1)} %collective-permute-done.4) | copy-start | bytes 491524
  29.5 14.4 %copy-start.7 = (bf16[5,128,128]{2,1,0:T(8,128)(2,1)}, bf16[5,128,128]{2,1,0:T(8,128)(2,1)S(1)}, u32[]{:S(2)}) copy-start(bf16[5,128,128]{2,1,0:T(8,128)(2,1)S(1)} %collective-permute-done.5) | copy-start | bytes 491524
  31.1 12.7 %copy-start.8 = (bf16[5,128,128]{2,1,0:T(8,128)(2,1)}, bf16[5,128,128]{2,1,0:T(8,128)(2,1)S(1)}, u32[]{:S(2)}) copy-start(bf16[5,128,128]{2,1,0:T(8,128)(2,1)S(1)} %collective-permute-done.6) | copy-start | bytes 491524
  31.2 6.9 %collective-permute-start.7 = (bf16[5,128,128]{2,1,0:T(8,128)(2,1)S(1)}, bf16[5,128,128]{2,1,0:T(8,128)(2,1)S(1)}, u32[]{:S(2)}, u32[]{:S(2)}) collective-permute-start(bf16[5,128,128]{2,1,0:T(8,128)(2,1)S(1)} %fusion.58), channel_id=1, source_target_pairs={{0,32},{8,40},{16,48},{24,56},{32,64},{40,72},{48,80},{56,88},{64,... | collective-permute-start | bytes 491528 | tf_op jit(solution)/shard_map/ppermute | solution.py:16
  32.8 8.4 %collective-permute-start.8 = (bf16[5,128,128]{2,1,0:T(8,128)(2,1)S(1)}, bf16[5,128,128]{2,1,0:T(8,128)(2,1)S(1)}, u32[]{:S(2)}, u32[]{:S(2)}) collective-permute-start(bf16[5,128,128]{2,1,0:T(8,128)(2,1)S(1)} %fusion.58), channel_id=1, source_target_pairs={{0,64},{8,72},{16,80},{24,88},{32,96},{40,104},{48,112},{56,120},{... | collective-permute-start | bytes 491528 | tf_op jit(solution)/shard_map/ppermute | solution.py:16
  34.5 8.6 %collective-permute-start.9 = (bf16[5,128,128]{2,1,0:T(8,128)(2,1)S(1)}, bf16[5,128,128]{2,1,0:T(8,128)(2,1)S(1)}, u32[]{:S(2)}, u32[]{:S(2)}) collective-permute-start(bf16[5,128,128]{2,1,0:T(8,128)(2,1)S(1)} %fusion.58), channel_id=1, source_target_pairs={{0,96},{8,104},{16,112},{24,120},{32,0},{40,8},{48,16},{56,24},{64... | collective-permute-start | bytes 491528 | tf_op jit(solution)/shard_map/ppermute | solution.py:16
  38.0 15.0 %collective-permute-start.2 = (f32[128,640]{1,0:T(8,128)S(1)}, f32[128,640]{1,0:T(8,128)S(1)}, u32[]{:S(2)}, u32[]{:S(2)}) collective-permute-start(f32[128,640]{1,0:T(8,128)S(1)} %fusion.32), channel_id=1, source_target_pairs={{0,4},{4,0},{1,5},{5,1},{2,6},{6,2},{3,7},{7,3},{8,12},{12,8},{9,1... | collective-permute-start | bytes 983048 | tf_op jit(solution)/shard_map/ppermute | solution.py:12
  38.1 14.9 %copy-start.9 = (bf16[5,128,128]{2,1,0:T(8,128)(2,1)}, bf16[5,128,128]{2,1,0:T(8,128)(2,1)S(1)}, u32[]{:S(2)}) copy-start(bf16[5,128,128]{2,1,0:T(8,128)(2,1)S(1)} %collective-permute-done.7) | copy-start | bytes 491524
  41.3 11.7 %copy-start.10 = (bf16[5,128,128]{2,1,0:T(8,128)(2,1)}, bf16[5,128,128]{2,1,0:T(8,128)(2,1)S(1)}, u32[]{:S(2)}) copy-start(bf16[5,128,128]{2,1,0:T(8,128)(2,1)S(1)} %collective-permute-done.8) | copy-start | bytes 491524
  43.0 9.9 %copy-start.11 = (bf16[5,128,128]{2,1,0:T(8,128)(2,1)}, bf16[5,128,128]{2,1,0:T(8,128)(2,1)S(1)}, u32[]{:S(2)}) copy-start(bf16[5,128,128]{2,1,0:T(8,128)(2,1)S(1)} %collective-permute-done.9) | copy-start | bytes 491524
  43.9 11.7 %collective-permute-start.10 = (bf16[5,128,128]{2,1,0:T(8,128)(2,1)}, bf16[5,128,128]{2,1,0:T(8,128)(2,1)}, u32[]{:S(2)}, u32[]{:S(2)}) collective-permute-start(bf16[5,128,128]{2,1,0:T(8,128)(2,1)} %fusion.46), channel_id=1, source_target_pairs={{0,128},{8,136},{16,144},{24,152},{32,160},{40,168},{48,176},{56,1... | collective-permute-start | bytes 491528 | tf_op jit(solution)/shard_map/ppermute | solution.py:16
  67.6 1.1 copy-start.4
  69.5 12.9 %collective-permute-start.12 = (bf16[128,1280]{1,0:T(8,128)(2,1)}, bf16[128,1280]{1,0:T(8,128)(2,1)}, u32[]{:S(2)}, u32[]{:S(2)}) collective-permute-start(bf16[128,1280]{1,0:T(8,128)(2,1)} %broadcast_select_fusion), channel_id=1, source_target_pairs={{0,1},{3,2},{4,5},{7,6},{8,9},{11,10},{12,13},{15,14},{16,17},{19,... | collective-permute-start | bytes 983048 | tf_op jit(solution)/shard_map/ppermute | solution.py:114
  76.6 16.6 %copy-start.5 = (f32[128,2560]{1,0:T(8,128)S(1)}, f32[128,2560]{1,0:T(8,128)}, u32[]{:S(2)}) copy-start(f32[128,2560]{1,0:T(8,128)} %copy-done.4) | copy-start | bytes 3932164
  83.5 9.7 %collective-permute-start.13 = (bf16[128,1280]{1,0:T(8,128)(2,1)S(1)}, bf16[128,1280]{1,0:T(8,128)(2,1)S(1)}, u32[]{:S(2)}, u32[]{:S(2)}) collective-permute-start(bf16[128,1280]{1,0:T(8,128)(2,1)S(1)} %get-tuple-element.13), channel_id=1, source_target_pairs={{0,1},{1,2},{4,5},{5,6},{8,9},{9,10},{12,13},{13,14},{16,17},{17,1... | collective-permute-start | bytes 983048 | tf_op jit(solution)/shard_map/ppermute | solution.py:118
  87.9 5.3 %collective-permute-start.14 = (bf16[128,1280]{1,0:T(8,128)(2,1)S(1)}, bf16[128,1280]{1,0:T(8,128)(2,1)S(1)}, u32[]{:S(2)}, u32[]{:S(2)}) collective-permute-start(bf16[128,1280]{1,0:T(8,128)(2,1)S(1)} %get-tuple-element.14), channel_id=1, source_target_pairs={{2,1},{3,2},{6,5},{7,6},{10,9},{11,10},{14,13},{15,14},{18,17},{19... | collective-permute-start | bytes 983048 | tf_op jit(solution)/shard_map/ppermute | solution.py:119
  93.4 11.8 %collective-permute-start.15 = (bf16[128,1280]{1,0:T(8,128)(2,1)S(1)}, bf16[128,1280]{1,0:T(8,128)(2,1)S(1)}, u32[]{:S(2)}, u32[]{:S(2)}) collective-permute-start(bf16[128,1280]{1,0:T(8,128)(2,1)S(1)} %get-tuple-element.15), channel_id=1, source_target_pairs={{0,1},{1,2},{2,3},{4,5},{5,6},{6,7},{8,9},{9,10},{10,11},{12,13},{... | collective-permute-start | bytes 983048 | tf_op jit(solution)/shard_map/ppermute | solution.py:118
  100.7 9.0 %collective-permute-start.16 = (bf16[128,1280]{1,0:T(8,128)(2,1)S(1)}, bf16[128,1280]{1,0:T(8,128)(2,1)S(1)}, u32[]{:S(2)}, u32[]{:S(2)}) collective-permute-start(bf16[128,1280]{1,0:T(8,128)(2,1)S(1)} %get-tuple-element.16), channel_id=1, source_target_pairs={{1,0},{2,1},{3,2},{5,4},{6,5},{7,6},{9,8},{10,9},{11,10},{13,12},{... | collective-permute-start | bytes 983048 | tf_op jit(solution)/shard_map/ppermute | solution.py:119

commit v15 on v8

--- a/solution.py
+++ b/solution.py
@@ -82,7 +82,8 @@
     scale = lax.rsqrt(jnp.mean(attended * attended, axis=2, keepdims=True) + 1e-06)
     normed = (attended * scale).reshape(tok_count, width_local).astype(BF16)
 
-    w_other = swap_cores(w_output)
+    w_late, _ = lax.optimization_barrier((w_output, value_sum))
+    w_other = swap_cores(w_late)
     quarter = w_output.shape[1] // 2
     n = 4
     h = lax.axis_index("head")

time: 108 us -> 116 us (1.074)
  the two profiles are of different devices: /device:TPU:10 before, /device:TPU:128 now
where the time goes in v15:
time: 116 us; the launch traced here: 115 us
  waiting for transfers between devices  40.5 us (35%)
  starting transfers between devices  32.4 us (28%)
  matrix products  24 us (21%)
  other arithmetic  11.8 us (10%)
  local copies, waits for them, and re-layouts  6.51 us (6%)
    ppermute x7, waiting for transfers between devices, shifted(): return lax.ppermute(x, axis, pairs)  22.5 us
    ppermute x3, starting transfers between devices, shards(): right = lax.ppermute(send_r, 'head', rpairs).astype(F32)  18.5 us
    ppermute x3, waiting for transfers between devices, shards(): right = lax.ppermute(send_r, 'head', rpairs).astype(F32)  13.6 us
    ppermute x7, starting transfers between devices, shifted(): return lax.ppermute(x, axis, pairs)  10.7 us
    dot_general x3, matrix products, shards(): own = jnp.dot(mine_cols, w, preferred_element_type=F32)  8.86 us
    dot_general x3, matrix products, shards(): lent = swap_cores(jnp.dot(got_cols, w, preferred_element_type=F32))  7.81 us
    ppermute x3, waiting for transfers between devices, shards(): left = lax.ppermute(send_l, 'head', lpairs).astype(F32)  4.42 us
    squeeze x1, other arithmetic, shards(): pieces.append(piece[0])  4.33 us
  transfers between devices with their start and end apart: 18, of which 11 were waited for; matrix products, arithmetic and copies ran while one was open for 27% of the time, Pallas kernels for 0%

profile of v15, /device:TPU:128, one launch (start us, length us, event | category | flops | bytes accessed | tf_op | source)
XLA Modules:
  0.0 115.4 jit_solution(18138153068169751580)
XLA Ops:
  0.0 0.0 copy-start
  0.0 0.0 collective-permute-start
  0.0 1.9 %copy-done = bf16[2560,640]{1,0:T(8,128)(2,1)S(1)} copy-done((bf16[2560,640]{1,0:T(8,128)(2,1)S(1)}, bf16[2560,640]{1,0:T(8,128)(2,1)}, u32[]{:S(2)}) %copy-start) | copy-done | bytes 3276824
  1.9 2.5 %fusion.24 = f32[128,640]{1,0:T(8,128)} fusion(bf16[2560,640]{1,0:T(8,128)(2,1)S(1)} %copy-done, bf16[1,128,5120]{2,1,0:T(8,128)(2,1)} %param.5, s32[]{:T(128)S(6)} %select_n.154), kind=kOutput, calls=%fused_computation.35 | convolution fusion | flops 419430400 | bytes 4259844 | tf_op jit(solution)/shard_map/dot_general | solution.py:63
  4.4 0.0 collective-permute-done
  4.4 2.5 %fusion.30 = f32[128,640]{1,0:T(8,128)} fusion(bf16[2560,640]{1,0:T(8,128)(2,1)S(1)} %copy-done, bf16[128,5120]{1,0:T(8,128)(2,1)} %collective-permute-done, s32[]{:T(128)S(6)} %select_n.154), kind=kOutput, calls=%fused_computation.47 | convolution fusion | flops 419430400 | bytes 4259844 | tf_op jit(solution)/shard_map/dot_general | solution.py:62
  6.9 0.0 collective-permute-start.1
  6.9 3.6 %fusion.26 = f32[128,640]{1,0:T(8,128)} fusion(bf16[2560,640]{1,0:T(8,128)(2,1)} %param.7, bf16[128,5120]{1,0:T(8,128)(2,1)} %collective-permute-done, s32[]{:T(128)S(6)} %select_n.154), kind=kOutput, calls=%fused_computation.43 | convolution fusion | flops 419430400 | bytes 4259844 | tf_op jit(solution)/shard_map/dot_general | solution.py:62
  10.5 0.5 collective-permute-start.3
  11.0 0.0 collective-permute-done.1
  11.0 1.8 %add.177 = bf16[128,640]{1,0:T(8,128)(2,1)} add(f32[128,640]{1,0:T(8,128)} %fusion.24, f32[128,640]{1,0:T(8,128)} %collective-permute-done.1) | non-fusion elementwise | flops 81920 | bytes 819200 | tf_op jit(solution)/shard_map/add | solution.py:64
  12.8 0.0 collective-permute-start.11
  12.8 3.5 %fusion.20 = f32[128,640]{1,0:T(8,128)} fusion(bf16[2560,640]{1,0:T(8,128)(2,1)} %param.7, bf16[1,128,5120]{2,1,0:T(8,128)(2,1)} %param.5, s32[]{:T(128)S(6)} %select_n.154), kind=kOutput, calls=%fused_computation.31 | convolution fusion | flops 419430400 | bytes 4259844 | tf_op jit(solution)/shard_map/dot_general | solution.py:63
  16.3 1.1 copy.11
  17.4 0.0 collective-permute-done.3
  17.4 1.8 %multiply_convert_fusion.1 = bf16[128,640]{1,0:T(8,128)(2,1)} fusion(f32[128,640]{1,0:T(8,128)} %fusion.20, f32[128,640]{1,0:T(8,128)} %collective-permute-done.3), kind=kLoop, calls=%fused_computation.75 | loop fusion | flops 491520 | bytes 819200 | tf_op jit(solution)/shard_map/convert_element_type | solution.py:68
  19.2 1.7 %copy.13 = bf16[128,640]{0,1:T(8,128)(2,1)} copy(bf16[128,640]{1,0:T(8,128)(2,1)} %multiply_convert_fusion.1) | data formatting | bytes 327680 | tf_op jit(solution)/shard_map/convert_element_type | solution.py:68
  21.0 1.3 %fusion.64 = (bf16[5,128,128]{2,1,0:T(8,128)(2,1)S(1)}, f32[5,128,128]{2,1,0:T(8,128)S(1)}) fusion(bf16[128,5,128]{0,2,1:T(8,128)(2,1)} %bitcast.43, bf16[128,5,128]{0,2,1:T(8,128)(2,1)S(1)} %bitcast.41), kind=kOutput, calls=%fused_computation.98 | convolution fusion | flops 21053440 | bytes 819200 | tf_op jit(solution)/shard_map/thd,the->hde/dot_general | solution.py:70
  22.3 2.8 %collective-permute-start.6 = (bf16[5,128,128]{2,1,0:T(8,128)(2,1)S(1)}, bf16[5,128,128]{2,1,0:T(8,128)(2,1)S(1)}, u32[]{:S(2)}, u32[]{:S(2)}) collective-permute-start(bf16[5,128,128]{2,1,0:T(8,128)(2,1)S(1)} %get-tuple-element.29), channel_id=1, source_target_pairs={{0,24},{8,0},{16,8},{24,16},{32,56},{40,32},{48,40},{56,48},{64,88... | collective-permute-start | bytes 491528 | tf_op jit(solution)/shard_map/ppermute | solution.py:16
  25.1 0.8 collective-permute-start.5
  25.9 0.9 collective-permute-start.4
  26.8 2.8 %fusion.22 = f32[128,640]{1,0:T(8,128)S(1)} fusion(bf16[2560,640]{1,0:T(8,128)(2,1)} %param.6, bf16[1,128,5120]{2,1,0:T(8,128)(2,1)} %param.5, s32[]{:T(128)S(6)} %select_n.154), kind=kOutput, calls=%fused_computation.33 | convolution fusion | flops 419430400 | bytes 4259844 | tf_op jit(solution)/shard_map/dot_general | solution.py:63
  29.6 3.2 %collective-permute-done.6 = bf16[5,128,128]{2,1,0:T(8,128)(2,1)S(1)} collective-permute-done((bf16[5,128,128]{2,1,0:T(8,128)(2,1)S(1)}, bf16[5,128,128]{2,1,0:T(8,128)(2,1)S(1)}, u32[]{:S(2)}, u32[]{:S(2)}) %collective-permute-start.6) | collective-permute-done | bytes 163872 | tf_op jit(solution)/shard_map/ppermute | solution.py:16
  32.8 1.0 collective-permute-done.5
  33.7 2.7 %collective-permute-done.4 = bf16[5,128,128]{2,1,0:T(8,128)(2,1)S(1)} collective-permute-done((bf16[5,128,128]{2,1,0:T(8,128)(2,1)S(1)}, bf16[5,128,128]{2,1,0:T(8,128)(2,1)S(1)}, u32[]{:S(2)}, u32[]{:S(2)}) %collective-permute-start.4) | collective-permute-done | bytes 163872 | tf_op jit(solution)/shard_map/ppermute | solution.py:16
  36.4 0.1 fusion.54
  36.5 3.1 %collective-permute-start.9 = (bf16[5,128,128]{2,1,0:T(8,128)(2,1)S(1)}, bf16[5,128,128]{2,1,0:T(8,128)(2,1)S(1)}, u32[]{:S(2)}, u32[]{:S(2)}) collective-permute-start(bf16[5,128,128]{2,1,0:T(8,128)(2,1)S(1)} %fusion.54), channel_id=1, source_target_pairs={{0,96},{8,104},{16,112},{24,120},{32,0},{40,8},{48,16},{56,24},{64... | collective-permute-start | bytes 491528 | tf_op jit(solution)/shard_map/ppermute | solution.py:16
  39.6 0.6 collective-permute-start.8
  40.2 1.0 collective-permute-start.7
  41.2 0.0 copy-done.1
  41.2 1.8 %fusion.28 = f32[128,640]{1,0:T(8,128)S(1)} fusion(bf16[2560,640]{1,0:T(8,128)(2,1)S(1)} %copy-done.1, bf16[128,5120]{1,0:T(8,128)(2,1)} %collective-permute-done, s32[]{:T(128)S(6)} %select_n.154), kind=kOutput, calls=%fused_computation.45 | convolution fusion | flops 419430400 | bytes 4259844 | tf_op jit(solution)/shard_map/dot_general | solution.py:62
  43.0 0.1 collective-permute-start.2
  43.1 3.7 %collective-permute-done.9 = bf16[5,128,128]{2,1,0:T(8,128)(2,1)S(1)} collective-permute-done((bf16[5,128,128]{2,1,0:T(8,128)(2,1)S(1)}, bf16[5,128,128]{2,1,0:T(8,128)(2,1)S(1)}, u32[]{:S(2)}, u32[]{:S(2)}) %collective-permute-start.9) | collective-permute-done | bytes 163872 | tf_op jit(solution)/shard_map/ppermute | solution.py:16
  46.8 1.5 %collective-permute-done.8 = bf16[5,128,128]{2,1,0:T(8,128)(2,1)S(1)} collective-permute-done((bf16[5,128,128]{2,1,0:T(8,128)(2,1)S(1)}, bf16[5,128,128]{2,1,0:T(8,128)(2,1)S(1)}, u32[]{:S(2)}, u32[]{:S(2)}) %collective-permute-start.8) | collective-permute-done | bytes 163872 | tf_op jit(solution)/shard_map/ppermute | solution.py:16
  48.2 2.2 %collective-permute-done.7 = bf16[5,128,128]{2,1,0:T(8,128)(2,1)S(1)} collective-permute-done((bf16[5,128,128]{2,1,0:T(8,128)(2,1)S(1)}, bf16[5,128,128]{2,1,0:T(8,128)(2,1)S(1)}, u32[]{:S(2)}, u32[]{:S(2)}) %collective-permute-start.7) | collective-permute-done | bytes 163872 | tf_op jit(solution)/shard_map/ppermute | solution.py:16
  50.5 0.8 fusion.42
  51.3 0.0 copy-done.2
  51.3 1.5 %collective-permute-start.10 = (bf16[5,128,128]{2,1,0:T(8,128)(2,1)}, bf16[5,128,128]{2,1,0:T(8,128)(2,1)}, u32[]{:S(2)}, u32[]{:S(2)}) collective-permute-start(bf16[5,128,128]{2,1,0:T(8,128)(2,1)} %fusion.42), channel_id=1, source_target_pairs={{0,128},{8,136},{16,144},{24,152},{32,160},{40,168},{48,176},{56,1... | collective-permute-start | bytes 491528 | tf_op jit(solution)/shard_map/ppermute | solution.py:16
  52.8 0.0 collective-permute-done.2
  52.8 0.8 multiply_convert_fusion.2
  53.6 1.7 %copy.12 = bf16[128,640]{0,1:T(8,128)(2,1)} copy(bf16[128,640]{1,0:T(8,128)(2,1)} %multiply_convert_fusion.2) | data formatting | bytes 327680 | tf_op jit(solution)/shard_map/convert_element_type | solution.py:67
  55.3 8.3 %collective-permute-done.10 = bf16[5,128,128]{2,1,0:T(8,128)(2,1)} collective-permute-done((bf16[5,128,128]{2,1,0:T(8,128)(2,1)}, bf16[5,128,128]{2,1,0:T(8,128)(2,1)}, u32[]{:S(2)}, u32[]{:S(2)}) %collective-permute-start.10) | collective-permute-done | bytes 163872 | tf_op jit(solution)/shard_map/ppermute | solution.py:16
  63.6 2.5 %fusion.45 = f32[5,128,128]{2,1,0:T(8,128)} fusion(bf16[128,5,128]{0,2,1:T(8,128)(2,1)} %bitcast.45, bf16[5,128,128]{2,1,0:T(8,128)(2,1)} %copy-done.4, bf16[5,128,128]{2,1,0:T(8,128)(2,1)} %copy-done.3, bf16[5,128,128]{2,1,0:T(8,128)(2,1)} %copy-done.2, bf16[5,128,128]{2,1,0:T(8,128)(2,1)} %copy-done.7, bf16[5,128,128]{2,1,0:T(8,128)(2,1)} %copy-done.6, ...), kind=kOutput, calls=%fused_computation.78 | convolution fusion | flops 22609920 | bytes 1638406 | tf_op jit(solution)/shard_map/thd,hde->the/dot_general | solution.py:78
  66.1 2.3 %multiply_reduce_fusion = (f32[128,5]{0,1:T(8,128)S(1)}, f32[128,5,128]{0,2,1:T(8,128)}) fusion(f32[5,128,128]{2,1,0:T(8,128)} %fusion.45, bf16[128,5,128]{0,2,1:T(8,128)(2,1)S(1)} %bitcast.42, bf16[128,5,128]{0,2,1:T(8,128)(2,1)} %bitcast.46, bf16[128,5,128]{0,2,1:T(8,128)(2,1)} %bitcast.44, f32[128,128]{1,0:T(8,128)S(1)} %fusion.53), kind=kOutput, calls=%fused_computation.74 | convolution fusion | flops 42352000 | bytes 1214976 | tf_op jit(solution)/shard_map/hts,shd->thd/dot_general | solution.py:77
  68.4 1.0 multiply_convert_fusion
  69.4 0.0 collective-permute-done.11
  69.5 4.3 %fusion.11 = (bf16[640,1280]{1,0:T(8,128)(2,1)S(1)}, bf16[640,1280]{1,0:T(8,128)(2,1)S(1)}, bf16[640,1280]{1,0:T(8,128)(2,1)S(1)}, bf16[640,1280]{1,0:T(8,128)(2,1)S(1)}) fusion(s32[]{:T(128)S(6)} %select_n.178, s32[]{:T(128)S(6)} %select_n.180, bf16[1,640,2560]{2,1,0:T(8,128)(2,1)} %bitcast.39, bf16[1,640,2560]{2,1,0:T(8,128)(2,1)} %bitcast.8, ...), kind=kLoop, calls=%fused_computation.19 | loop fusion | flops 13107200 | bytes 13107232 | tf_op jit(solution)/shard_map/squeeze | solution.py:97
  73.8 1.2 %fusion = f32[128,5120]{1,0:T(8,128)S(1)} fusion(bf16[128,640]{0,1:T(8,128)(2,1)S(1)} %bitcast.47, bf16[640,1280]{1,0:T(8,128)(2,1)S(1)} %get-tuple-element.22, bf16[640,1280]{1,0:T(8,128)(2,1)S(1)} %get-tuple-element.21, bf16[640,1280]{1,0:T(8,128)(2,1)S(1)} %get-tuple-element.20, bf16[640,1280]{1,0:T(8,128)(2,1)S(1)} %get-tuple-element.19), kind=kOutput, calls=%fused_computation.8 | convolution fusion | flops 865075200 | bytes 9338880 | tf_op jit(solution)/shard_map/dot_general | solution.py:99
  75.0 0.1 fusion.63
  75.1 6.3 %collective-permute-start.12 = (bf16[128,1280]{1,0:T(8,128)(2,1)S(1)}, bf16[128,1280]{1,0:T(8,128)(2,1)S(1)}, u32[]{:S(2)}, u32[]{:S(2)}) collective-permute-start(bf16[128,1280]{1,0:T(8,128)(2,1)S(1)} %get-tuple-element.13), channel_id=1, source_target_pairs={{0,1},{4,5},{8,9},{12,13},{16,17},{20,21},{24,25},{28,29},{32,33},... | collective-permute-start | bytes 983048 | tf_op jit(solution)/shard_map/ppermute | solution.py:112
  81.5 0.7 collective-permute-start.13
  82.2 5.6 %collective-permute-done.12 = bf16[128,1280]{1,0:T(8,128)(2,1)S(1)} collective-permute-done((bf16[128,1280]{1,0:T(8,128)(2,1)S(1)}, bf16[128,1280]{1,0:T(8,128)(2,1)S(1)}, u32[]{:S(2)}, u32[]{:S(2)}) %collective-permute-start.12) | collective-permute-done | bytes 327712 | tf_op jit(solution)/shard_map/ppermute | solution.py:112
  87.7 0.0 collective-permute-done.13
  87.7 0.1 add_convert_fusion.2
  87.9 4.4 %collective-permute-start.14 = (bf16[128,1280]{1,0:T(8,128)(2,1)S(1)}, bf16[128,1280]{1,0:T(8,128)(2,1)S(1)}, u32[]{:S(2)}, u32[]{:S(2)}) collective-permute-start(bf16[128,1280]{1,0:T(8,128)(2,1)S(1)} %get-tuple-element.15), channel_id=1, source_target_pairs={{0,1},{1,2},{4,5},{5,6},{8,9},{9,10},{12,13},{13,14},{16,17},{17,1... | collective-permute-start | bytes 983048 | tf_op jit(solution)/shard_map/ppermute | solution.py:112
  92.3 0.7 collective-permute-start.15
  93.0 4.7 %collective-permute-done.14 = bf16[128,1280]{1,0:T(8,128)(2,1)S(1)} collective-permute-done((bf16[128,1280]{1,0:T(8,128)(2,1)S(1)}, bf16[128,1280]{1,0:T(8,128)(2,1)S(1)}, u32[]{:S(2)}, u32[]{:S(2)}) %collective-permute-start.14) | collective-permute-done | bytes 327712 | tf_op jit(solution)/shard_map/ppermute | solution.py:112
  97.7 0.0 collective-permute-done.15
  97.7 0.2 add_convert_fusion
  97.9 7.7 %collective-permute-start.16 = (bf16[128,1280]{1,0:T(8,128)(2,1)S(1)}, bf16[128,1280]{1,0:T(8,128)(2,1)S(1)}, u32[]{:S(2)}, u32[]{:S(2)}) collective-permute-start(bf16[128,1280]{1,0:T(8,128)(2,1)S(1)} %get-tuple-element.17), channel_id=1, source_target_pairs={{0,1},{1,2},{2,3},{4,5},{5,6},{6,7},{8,9},{9,10},{10,11},{12,13},{... | collective-permute-start | bytes 983048 | tf_op jit(solution)/shard_map/ppermute | solution.py:112
  105.6 1.3 %collective-permute-start.17 = (bf16[128,1280]{1,0:T(8,128)(2,1)S(1)}, bf16[128,1280]{1,0:T(8,128)(2,1)S(1)}, u32[]{:S(2)}, u32[]{:S(2)}) collective-permute-start(bf16[128,1280]{1,0:T(8,128)(2,1)S(1)} %get-tuple-element.18), channel_id=1, source_target_pairs={{1,0},{2,1},{3,2},{5,4},{6,5},{7,6},{9,8},{10,9},{11,10},{13,12},{... | collective-permute-start | bytes 983048 | tf_op jit(solution)/shard_map/ppermute | solution.py:113
  106.9 3.3 %collective-permute-done.16 = bf16[128,1280]{1,0:T(8,128)(2,1)S(1)} collective-permute-done((bf16[128,1280]{1,0:T(8,128)(2,1)S(1)}, bf16[128,1280]{1,0:T(8,128)(2,1)S(1)}, u32[]{:S(2)}, u32[]{:S(2)}) %collective-permute-start.16) | collective-permute-done | bytes 327712 | tf_op jit(solution)/shard_map/ppermute | solution.py:112
  110.2 4.4 %collective-permute-done.17 = bf16[128,1280]{1,0:T(8,128)(2,1)S(1)} collective-permute-done((bf16[128,1280]{1,0:T(8,128)(2,1)S(1)}, bf16[128,1280]{1,0:T(8,128)(2,1)S(1)}, u32[]{:S(2)}, u32[]{:S(2)}) %collective-permute-start.17) | collective-permute-done | bytes 327712 | tf_op jit(solution)/shard_map/ppermute | solution.py:113
  114.6 0.8 fusion.43
  (14 shorter events, 0.0 us)
Async XLA Ops:
  0.0 1.9 %copy-start = (bf16[2560,640]{1,0:T(8,128)(2,1)S(1)}, bf16[2560,640]{1,0:T(8,128)(2,1)}, u32[]{:S(2)}) copy-start(bf16[2560,640]{1,0:T(8,128)(2,1)} %param.8) | copy-start | bytes 9830404
  0.0 4.4 %collective-permute-start = (bf16[128,5120]{1,0:T(8,128)(2,1)}, bf16[128,5120]{1,0:T(8,128)(2,1)}, u32[]{:S(2)}, u32[]{:S(2)}) collective-permute-start(bf16[128,5120]{1,0:T(8,128)(2,1)} %bitcast.40), channel_id=1, source_target_pairs={{0,4},{4,0},{1,5},{5,1},{2,6},{6,2},{3,7},{7,3},{8,12},{12,8},{9,1... | collective-permute-start | bytes 3932168 | tf_op jit(solution)/shard_map/ppermute | solution.py:12
  6.9 4.1 %collective-permute-start.1 = (f32[128,640]{1,0:T(8,128)}, f32[128,640]{1,0:T(8,128)}, u32[]{:S(2)}, u32[]{:S(2)}) collective-permute-start(f32[128,640]{1,0:T(8,128)} %fusion.30), channel_id=1, source_target_pairs={{0,4},{4,0},{1,5},{5,1},{2,6},{6,2},{3,7},{7,3},{8,12},{12,8},{9,1... | collective-permute-start | bytes 983048 | tf_op jit(solution)/shard_map/ppermute | solution.py:12
  10.5 6.9 %collective-permute-start.3 = (f32[128,640]{1,0:T(8,128)}, f32[128,640]{1,0:T(8,128)}, u32[]{:S(2)}, u32[]{:S(2)}) collective-permute-start(f32[128,640]{1,0:T(8,128)} %fusion.26), channel_id=1, source_target_pairs={{0,4},{4,0},{1,5},{5,1},{2,6},{6,2},{3,7},{7,3},{8,12},{12,8},{9,1... | collective-permute-start | bytes 983048 | tf_op jit(solution)/shard_map/ppermute | solution.py:12
  12.8 56.7 %collective-permute-start.11 = (bf16[640,2560]{1,0:T(8,128)(2,1)}, bf16[640,2560]{1,0:T(8,128)(2,1)}, u32[]{:S(2)}, u32[]{:S(2)}) collective-permute-start(bf16[640,2560]{1,0:T(8,128)(2,1)} %param.9), channel_id=1, source_target_pairs={{0,4},{4,0},{1,5},{5,1},{2,6},{6,2},{3,7},{7,3},{8,12},{12,8},{9,1... | collective-permute-start | bytes 9830408 | tf_op jit(solution)/shard_map/ppermute | solution.py:12
  21.0 20.2 %copy-start.1 = (bf16[2560,640]{1,0:T(8,128)(2,1)S(1)}, bf16[2560,640]{1,0:T(8,128)(2,1)}, u32[]{:S(2)}) copy-start(bf16[2560,640]{1,0:T(8,128)(2,1)} %param.6) | copy-start | bytes 9830404
  22.3 10.5 %collective-permute-start.6 = (bf16[5,128,128]{2,1,0:T(8,128)(2,1)S(1)}, bf16[5,128,128]{2,1,0:T(8,128)(2,1)S(1)}, u32[]{:S(2)}, u32[]{:S(2)}) collective-permute-start(bf16[5,128,128]{2,1,0:T(8,128)(2,1)S(1)} %get-tuple-element.29), channel_id=1, source_target_pairs={{0,24},{8,0},{16,8},{24,16},{32,56},{40,32},{48,40},{56,48},{64,88... | collective-permute-start | bytes 491528 | tf_op jit(solution)/shard_map/ppermute | solution.py:16
  25.1 8.6 %collective-permute-start.5 = (bf16[5,128,128]{2,1,0:T(8,128)(2,1)S(1)}, bf16[5,128,128]{2,1,0:T(8,128)(2,1)S(1)}, u32[]{:S(2)}, u32[]{:S(2)}) collective-permute-start(bf16[5,128,128]{2,1,0:T(8,128)(2,1)S(1)} %get-tuple-element.29), channel_id=1, source_target_pairs={{0,16},{8,24},{16,0},{24,8},{32,48},{40,56},{48,32},{56,40},{64,80... | collective-permute-start | bytes 491528 | tf_op jit(solution)/shard_map/ppermute | solution.py:16
  25.9 10.6 %collective-permute-start.4 = (bf16[5,128,128]{2,1,0:T(8,128)(2,1)S(1)}, bf16[5,128,128]{2,1,0:T(8,128)(2,1)S(1)}, u32[]{:S(2)}, u32[]{:S(2)}) collective-permute-start(bf16[5,128,128]{2,1,0:T(8,128)(2,1)S(1)} %get-tuple-element.29), channel_id=1, source_target_pairs={{0,8},{8,16},{16,24},{24,0},{32,40},{40,48},{48,56},{56,32},{64,72... | collective-permute-start | bytes 491528 | tf_op jit(solution)/shard_map/ppermute | solution.py:16
  32.8 18.5 %copy-start.2 = (bf16[5,128,128]{2,1,0:T(8,128)(2,1)}, bf16[5,128,128]{2,1,0:T(8,128)(2,1)S(1)}, u32[]{:S(2)}) copy-start(bf16[5,128,128]{2,1,0:T(8,128)(2,1)S(1)} %collective-permute-done.6) | copy-start | bytes 491524
  33.7 17.6 %copy-start.3 = (bf16[5,128,128]{2,1,0:T(8,128)(2,1)}, bf16[5,128,128]{2,1,0:T(8,128)(2,1)S(1)}, u32[]{:S(2)}) copy-start(bf16[5,128,128]{2,1,0:T(8,128)(2,1)S(1)} %collective-permute-done.5) | copy-start | bytes 491524
  36.4 14.9 %copy-start.4 = (bf16[5,128,128]{2,1,0:T(8,128)(2,1)}, bf16[5,128,128]{2,1,0:T(8,128)(2,1)S(1)}, u32[]{:S(2)}) copy-start(bf16[5,128,128]{2,1,0:T(8,128)(2,1)S(1)} %collective-permute-done.4) | copy-start | bytes 491524
  36.5 10.2 %collective-permute-start.9 = (bf16[5,128,128]{2,1,0:T(8,128)(2,1)S(1)}, bf16[5,128,128]{2,1,0:T(8,128)(2,1)S(1)}, u32[]{:S(2)}, u32[]{:S(2)}) collective-permute-start(bf16[5,128,128]{2,1,0:T(8,128)(2,1)S(1)} %fusion.54), channel_id=1, source_target_pairs={{0,96},{8,104},{16,112},{24,120},{32,0},{40,8},{48,16},{56,24},{64... | collective-permute-start | bytes 491528 | tf_op jit(solution)/shard_map/ppermute | solution.py:16
  39.6 8.6 %collective-permute-start.8 = (bf16[5,128,128]{2,1,0:T(8,128)(2,1)S(1)}, bf16[5,128,128]{2,1,0:T(8,128)(2,1)S(1)}, u32[]{:S(2)}, u32[]{:S(2)}) collective-permute-start(bf16[5,128,128]{2,1,0:T(8,128)(2,1)S(1)} %fusion.54), channel_id=1, source_target_pairs={{0,64},{8,72},{16,80},{24,88},{32,96},{40,104},{48,112},{56,120},{... | collective-permute-start | bytes 491528 | tf_op jit(solution)/shard_map/ppermute | solution.py:16
  40.2 10.2 %collective-permute-start.7 = (bf16[5,128,128]{2,1,0:T(8,128)(2,1)S(1)}, bf16[5,128,128]{2,1,0:T(8,128)(2,1)S(1)}, u32[]{:S(2)}, u32[]{:S(2)}) collective-permute-start(bf16[5,128,128]{2,1,0:T(8,128)(2,1)S(1)} %fusion.54), channel_id=1, source_target_pairs={{0,32},{8,40},{16,48},{24,56},{32,64},{40,72},{48,80},{56,88},{64,... | collective-permute-start | bytes 491528 | tf_op jit(solution)/shard_map/ppermute | solution.py:16
  43.0 9.8 %collective-permute-start.2 = (f32[128,640]{1,0:T(8,128)S(1)}, f32[128,640]{1,0:T(8,128)S(1)}, u32[]{:S(2)}, u32[]{:S(2)}) collective-permute-start(f32[128,640]{1,0:T(8,128)S(1)} %fusion.28), channel_id=1, source_target_pairs={{0,4},{4,0},{1,5},{5,1},{2,6},{6,2},{3,7},{7,3},{8,12},{12,8},{9,1... | collective-permute-start | bytes 983048 | tf_op jit(solution)/shard_map/ppermute | solution.py:12
  46.8 6.0 %copy-start.5 = (bf16[5,128,128]{2,1,0:T(8,128)(2,1)}, bf16[5,128,128]{2,1,0:T(8,128)(2,1)S(1)}, u32[]{:S(2)}) copy-start(bf16[5,128,128]{2,1,0:T(8,128)(2,1)S(1)} %collective-permute-done.9) | copy-start | bytes 491524
  48.2 4.6 %copy-start.6 = (bf16[5,128,128]{2,1,0:T(8,128)(2,1)}, bf16[5,128,128]{2,1,0:T(8,128)(2,1)S(1)}, u32[]{:S(2)}) copy-start(bf16[5,128,128]{2,1,0:T(8,128)(2,1)S(1)} %collective-permute-done.8) | copy-start | bytes 491524
  50.5 2.3 %copy-start.7 = (bf16[5,128,128]{2,1,0:T(8,128)(2,1)}, bf16[5,128,128]{2,1,0:T(8,128)(2,1)S(1)}, u32[]{:S(2)}) copy-start(bf16[5,128,128]{2,1,0:T(8,128)(2,1)S(1)} %collective-permute-done.7) | copy-start | bytes 491524
  51.3 12.3 %collective-permute-start.10 = (bf16[5,128,128]{2,1,0:T(8,128)(2,1)}, bf16[5,128,128]{2,1,0:T(8,128)(2,1)}, u32[]{:S(2)}, u32[]{:S(2)}) collective-permute-start(bf16[5,128,128]{2,1,0:T(8,128)(2,1)} %fusion.42), channel_id=1, source_target_pairs={{0,128},{8,136},{16,144},{24,152},{32,160},{40,168},{48,176},{56,1... | collective-permute-start | bytes 491528 | tf_op jit(solution)/shard_map/ppermute | solution.py:16
  75.1 12.6 %collective-permute-start.12 = (bf16[128,1280]{1,0:T(8,128)(2,1)S(1)}, bf16[128,1280]{1,0:T(8,128)(2,1)S(1)}, u32[]{:S(2)}, u32[]{:S(2)}) collective-permute-start(bf16[128,1280]{1,0:T(8,128)(2,1)S(1)} %get-tuple-element.13), channel_id=1, source_target_pairs={{0,1},{4,5},{8,9},{12,13},{16,17},{20,21},{24,25},{28,29},{32,33},... | collective-permute-start | bytes 983048 | tf_op jit(solution)/shard_map/ppermute | solution.py:112
  81.5 6.3 %collective-permute-start.13 = (bf16[128,1280]{1,0:T(8,128)(2,1)S(1)}, bf16[128,1280]{1,0:T(8,128)(2,1)S(1)}, u32[]{:S(2)}, u32[]{:S(2)}) collective-permute-start(bf16[128,1280]{1,0:T(8,128)(2,1)S(1)} %get-tuple-element.14), channel_id=1, source_target_pairs={{3,2},{7,6},{11,10},{15,14},{19,18},{23,22},{27,26},{31,30},{35,34... | collective-permute-start | bytes 983048 | tf_op jit(solution)/shard_map/ppermute | solution.py:113
  87.9 9.8 %collective-permute-start.14 = (bf16[128,1280]{1,0:T(8,128)(2,1)S(1)}, bf16[128,1280]{1,0:T(8,128)(2,1)S(1)}, u32[]{:S(2)}, u32[]{:S(2)}) collective-permute-start(bf16[128,1280]{1,0:T(8,128)(2,1)S(1)} %get-tuple-element.15), channel_id=1, source_target_pairs={{0,1},{1,2},{4,5},{5,6},{8,9},{9,10},{12,13},{13,14},{16,17},{17,1... | collective-permute-start | bytes 983048 | tf_op jit(solution)/shard_map/ppermute | solution.py:112
  92.3 5.4 %collective-permute-start.15 = (bf16[128,1280]{1,0:T(8,128)(2,1)S(1)}, bf16[128,1280]{1,0:T(8,128)(2,1)S(1)}, u32[]{:S(2)}, u32[]{:S(2)}) collective-permute-start(bf16[128,1280]{1,0:T(8,128)(2,1)S(1)} %get-tuple-element.16), channel_id=1, source_target_pairs={{2,1},{3,2},{6,5},{7,6},{10,9},{11,10},{14,13},{15,14},{18,17},{19... | collective-permute-start | bytes 983048 | tf_op jit(solution)/shard_map/ppermute | solution.py:113
  97.9 12.3 %collective-permute-start.16 = (bf16[128,1280]{1,0:T(8,128)(2,1)S(1)}, bf16[128,1280]{1,0:T(8,128)(2,1)S(1)}, u32[]{:S(2)}, u32[]{:S(2)}) collective-permute-start(bf16[128,1280]{1,0:T(8,128)(2,1)S(1)} %get-tuple-element.17), channel_id=1, source_target_pairs={{0,1},{1,2},{2,3},{4,5},{5,6},{6,7},{8,9},{9,10},{10,11},{12,13},{... | collective-permute-start | bytes 983048 | tf_op jit(solution)/shard_map/ppermute | solution.py:112
  105.6 9.0 %collective-permute-start.17 = (bf16[128,1280]{1,0:T(8,128)(2,1)S(1)}, bf16[128,1280]{1,0:T(8,128)(2,1)S(1)}, u32[]{:S(2)}, u32[]{:S(2)}) collective-permute-start(bf16[128,1280]{1,0:T(8,128)(2,1)S(1)} %get-tuple-element.18), channel_id=1, source_target_pairs={{1,0},{2,1},{3,2},{5,4},{6,5},{7,6},{9,8},{10,9},{11,10},{13,12},{... | collective-permute-start | bytes 983048 | tf_op jit(solution)/shard_map/ppermute | solution.py:113

commit v16 on v8

--- a/solution.py
+++ b/solution.py
@@ -27,7 +27,7 @@
         sent = value.astype(BF16)
         before = jnp.zeros_like(value)
         total = value
-        for d in range(1, size):
+        for d in sorted(range(1, size), key=lambda d: -min(d, size - d)):
             pairs = []
             for j in range(seq_size):
                 jp = (j // stride) % size

time: 108 us -> 108 us (level)
  no operation moved by 1% of the time
where the time goes in v16:
time: 108 us
  starting transfers between devices  40.8 us (38%)
  waiting for transfers between devices  27.7 us (26%)
  matrix products  21.1 us (20%)
  other arithmetic  11.8 us (11%)
  local copies, waits for them, and re-layouts  6 us (6%)
    ppermute x3, starting transfers between devices, shards(): right = lax.ppermute(send_r, 'head', rpairs).astype(F32)  18.6 us
    ppermute x7, starting transfers between devices, shifted(): return lax.ppermute(x, axis, pairs)  18.4 us
    ppermute x3, waiting for transfers between devices, shards(): right = lax.ppermute(send_r, 'head', rpairs).astype(F32)  13.4 us
    ppermute x7, waiting for transfers between devices, shifted(): return lax.ppermute(x, axis, pairs)  9.84 us
    dot_general x3, matrix products, shards(): own = jnp.dot(mine_cols, w, preferred_element_type=F32)  6.89 us
    dot_general x3, matrix products, shards(): lent = swap_cores(jnp.dot(got_cols, w, preferred_element_type=F32))  6.87 us
    ppermute x3, waiting for transfers between devices, shards(): left = lax.ppermute(send_l, 'head', lpairs).astype(F32)  4.42 us
    squeeze x1, other arithmetic, shards(): pieces.append(piece[0])  4.33 us
  transfers between devices with their start and end apart: 18, of which 9 were waited for; matrix products, arithmetic and copies ran while one was open for 29% of the time, Pallas kernels for 0%

profile of v16, /device:TPU:10, one launch (start us, length us, event | category | flops | bytes accessed | tf_op | source)
XLA Modules:
  0.0 107.5 jit_solution(15521909156135660507)
XLA Ops:
  0.0 0.0 copy-start
  0.0 0.0 collective-permute-start
  0.0 0.5 collective-permute-start.11
  0.5 1.4 %copy-done = bf16[2560,640]{1,0:T(8,128)(2,1)S(1)} copy-done((bf16[2560,640]{1,0:T(8,128)(2,1)S(1)}, bf16[2560,640]{1,0:T(8,128)(2,1)}, u32[]{:S(2)}) %copy-start) | copy-done | bytes 3276824
  1.9 2.7 %fusion.24 = f32[128,640]{1,0:T(8,128)} fusion(bf16[2560,640]{1,0:T(8,128)(2,1)S(1)} %copy-done, bf16[1,128,5120]{2,1,0:T(8,128)(2,1)} %param.5, s32[]{:T(128)S(6)} %select_n.154), kind=kOutput, calls=%fused_computation.35 | convolution fusion | flops 419430400 | bytes 4259844 | tf_op jit(solution)/shard_map/dot_general | solution.py:63
  4.6 0.0 collective-permute-done
  4.6 2.6 %fusion.30 = f32[128,640]{1,0:T(8,128)} fusion(bf16[2560,640]{1,0:T(8,128)(2,1)S(1)} %copy-done, bf16[128,5120]{1,0:T(8,128)(2,1)} %collective-permute-done, s32[]{:T(128)S(6)} %select_n.154), kind=kOutput, calls=%fused_computation.47 | convolution fusion | flops 419430400 | bytes 4259844 | tf_op jit(solution)/shard_map/dot_general | solution.py:62
  7.2 0.0 collective-permute-start.1
  7.2 2.5 %fusion.26 = f32[128,640]{1,0:T(8,128)} fusion(bf16[2560,640]{1,0:T(8,128)(2,1)S(1)} %copy-done.1, bf16[128,5120]{1,0:T(8,128)(2,1)} %collective-permute-done, s32[]{:T(128)S(6)} %select_n.154), kind=kOutput, calls=%fused_computation.43 | convolution fusion | flops 419430400 | bytes 4259844 | tf_op jit(solution)/shard_map/dot_general | solution.py:62
  9.7 0.5 collective-permute-start.3
  10.2 0.0 copy-done.3
  10.2 1.4 %fusion.20 = f32[128,640]{1,0:T(8,128)} fusion(bf16[2560,640]{1,0:T(8,128)(2,1)S(1)} %copy-done.1, bf16[1,128,5120]{2,1,0:T(8,128)(2,1)S(1)} %copy-done.3, s32[]{:T(128)S(6)} %select_n.154), kind=kOutput, calls=%fused_computation.31 | convolution fusion | flops 419430400 | bytes 4259844 | tf_op jit(solution)/shard_map/dot_general | solution.py:63
  11.6 0.0 collective-permute-done.1
  11.6 1.8 %add_convert_fusion.4 = bf16[128,640]{1,0:T(8,128)(2,1)} fusion(f32[128,640]{1,0:T(8,128)} %fusion.24, f32[128,640]{1,0:T(8,128)} %collective-permute-done.1), kind=kLoop, calls=%fused_computation.77 | loop fusion | flops 163840 | bytes 819200 | tf_op jit(solution)/shard_map/convert_element_type | solution.py:69
  13.4 1.1 copy.11
  14.5 0.0 collective-permute-done.3
  14.5 1.8 %multiply_convert_fusion.1 = bf16[128,640]{1,0:T(8,128)(2,1)} fusion(f32[128,640]{1,0:T(8,128)} %fusion.20, f32[128,640]{1,0:T(8,128)} %collective-permute-done.3), kind=kLoop, calls=%fused_computation.75 | loop fusion | flops 491520 | bytes 819200 | tf_op jit(solution)/shard_map/convert_element_type | solution.py:68
  16.3 1.7 %copy.13 = bf16[128,640]{0,1:T(8,128)(2,1)} copy(bf16[128,640]{1,0:T(8,128)(2,1)} %multiply_convert_fusion.1) | data formatting | bytes 327680 | tf_op jit(solution)/shard_map/convert_element_type | solution.py:68
  18.0 1.3 %fusion.64 = (bf16[5,128,128]{2,1,0:T(8,128)(2,1)S(1)}, f32[5,128,128]{2,1,0:T(8,128)S(1)}) fusion(bf16[128,5,128]{0,2,1:T(8,128)(2,1)} %bitcast.43, bf16[128,5,128]{0,2,1:T(8,128)(2,1)S(1)} %bitcast.41), kind=kOutput, calls=%fused_computation.99 | convolution fusion | flops 21053440 | bytes 819200 | tf_op jit(solution)/shard_map/thd,the->hde/dot_general | solution.py:70
  19.3 2.2 %collective-permute-start.4 = (bf16[5,128,128]{2,1,0:T(8,128)(2,1)S(1)}, bf16[5,128,128]{2,1,0:T(8,128)(2,1)S(1)}, u32[]{:S(2)}, u32[]{:S(2)}) collective-permute-start(bf16[5,128,128]{2,1,0:T(8,128)(2,1)S(1)} %get-tuple-element.27), channel_id=1, source_target_pairs={{0,16},{8,24},{16,0},{24,8},{32,48},{40,56},{48,32},{56,40},{64,80... | collective-permute-start | bytes 491528 | tf_op jit(solution)/shard_map/ppermute | solution.py:16
  21.5 0.0 collective-permute-start.5
  21.5 2.0 %collective-permute-start.6 = (bf16[5,128,128]{2,1,0:T(8,128)(2,1)S(1)}, bf16[5,128,128]{2,1,0:T(8,128)(2,1)S(1)}, u32[]{:S(2)}, u32[]{:S(2)}) collective-permute-start(bf16[5,128,128]{2,1,0:T(8,128)(2,1)S(1)} %get-tuple-element.27), channel_id=1, source_target_pairs={{0,24},{8,0},{16,8},{24,16},{32,56},{40,32},{48,40},{56,48},{64,88... | collective-permute-start | bytes 491528 | tf_op jit(solution)/shard_map/ppermute | solution.py:16
  23.6 2.8 %fusion.22 = f32[128,640]{1,0:T(8,128)S(1)} fusion(bf16[2560,640]{1,0:T(8,128)(2,1)} %param.6, bf16[1,128,5120]{2,1,0:T(8,128)(2,1)} %param.5, s32[]{:T(128)S(6)} %select_n.154), kind=kOutput, calls=%fused_computation.33 | convolution fusion | flops 419430400 | bytes 4259844 | tf_op jit(solution)/shard_map/dot_general | solution.py:63
  26.4 1.6 %collective-permute-done.4 = bf16[5,128,128]{2,1,0:T(8,128)(2,1)S(1)} collective-permute-done((bf16[5,128,128]{2,1,0:T(8,128)(2,1)S(1)}, bf16[5,128,128]{2,1,0:T(8,128)(2,1)S(1)}, u32[]{:S(2)}, u32[]{:S(2)}) %collective-permute-start.4) | collective-permute-done | bytes 163872 | tf_op jit(solution)/shard_map/ppermute | solution.py:16
  28.0 2.6 %collective-permute-done.5 = bf16[5,128,128]{2,1,0:T(8,128)(2,1)S(1)} collective-permute-done((bf16[5,128,128]{2,1,0:T(8,128)(2,1)S(1)}, bf16[5,128,128]{2,1,0:T(8,128)(2,1)S(1)}, u32[]{:S(2)}, u32[]{:S(2)}) %collective-permute-start.5) | collective-permute-done | bytes 163872 | tf_op jit(solution)/shard_map/ppermute | solution.py:16
  30.6 0.0 collective-permute-done.6
  30.6 0.1 fusion.54
  30.7 2.4 %collective-permute-start.7 = (bf16[5,128,128]{2,1,0:T(8,128)(2,1)S(1)}, bf16[5,128,128]{2,1,0:T(8,128)(2,1)S(1)}, u32[]{:S(2)}, u32[]{:S(2)}) collective-permute-start(bf16[5,128,128]{2,1,0:T(8,128)(2,1)S(1)} %fusion.54), channel_id=1, source_target_pairs={{0,64},{8,72},{16,80},{24,88},{32,96},{40,104},{48,112},{56,120},{... | collective-permute-start | bytes 491528 | tf_op jit(solution)/shard_map/ppermute | solution.py:16
  33.1 0.0 collective-permute-start.8
  33.1 2.0 %collective-permute-start.9 = (bf16[5,128,128]{2,1,0:T(8,128)(2,1)S(1)}, bf16[5,128,128]{2,1,0:T(8,128)(2,1)S(1)}, u32[]{:S(2)}, u32[]{:S(2)}) collective-permute-start(bf16[5,128,128]{2,1,0:T(8,128)(2,1)S(1)} %fusion.54), channel_id=1, source_target_pairs={{0,96},{8,104},{16,112},{24,120},{32,0},{40,8},{48,16},{56,24},{64... | collective-permute-start | bytes 491528 | tf_op jit(solution)/shard_map/ppermute | solution.py:16
  35.1 1.8 %fusion.28 = f32[128,640]{1,0:T(8,128)S(1)} fusion(bf16[2560,640]{1,0:T(8,128)(2,1)S(1)} %copy-done.2, bf16[128,5120]{1,0:T(8,128)(2,1)} %collective-permute-done, s32[]{:T(128)S(6)} %select_n.154), kind=kOutput, calls=%fused_computation.45 | convolution fusion | flops 419430400 | bytes 4259844 | tf_op jit(solution)/shard_map/dot_general | solution.py:62
  36.9 0.1 collective-permute-start.2
  37.0 2.4 %collective-permute-done.7 = bf16[5,128,128]{2,1,0:T(8,128)(2,1)S(1)} collective-permute-done((bf16[5,128,128]{2,1,0:T(8,128)(2,1)S(1)}, bf16[5,128,128]{2,1,0:T(8,128)(2,1)S(1)}, u32[]{:S(2)}, u32[]{:S(2)}) %collective-permute-start.7) | collective-permute-done | bytes 163872 | tf_op jit(solution)/shard_map/ppermute | solution.py:16
  39.4 2.6 %collective-permute-done.8 = bf16[5,128,128]{2,1,0:T(8,128)(2,1)S(1)} collective-permute-done((bf16[5,128,128]{2,1,0:T(8,128)(2,1)S(1)}, bf16[5,128,128]{2,1,0:T(8,128)(2,1)S(1)}, u32[]{:S(2)}, u32[]{:S(2)}) %collective-permute-start.8) | collective-permute-done | bytes 163872 | tf_op jit(solution)/shard_map/ppermute | solution.py:16
  42.0 0.0 collective-permute-done.9
  42.0 0.8 fusion.42
  42.9 0.0 copy-done.5
  42.9 9.8 %collective-permute-start.10 = (bf16[5,128,128]{2,1,0:T(8,128)(2,1)}, bf16[5,128,128]{2,1,0:T(8,128)(2,1)}, u32[]{:S(2)}, u32[]{:S(2)}) collective-permute-start(bf16[5,128,128]{2,1,0:T(8,128)(2,1)} %fusion.42), channel_id=1, source_target_pairs={{0,128},{8,136},{16,144},{24,152},{32,160},{40,168},{48,176},{56,1... | collective-permute-start | bytes 491528 | tf_op jit(solution)/shard_map/ppermute | solution.py:16
  52.6 0.0 collective-permute-done.2
  52.6 0.8 multiply_convert_fusion.2
  53.4 1.7 %copy.12 = bf16[128,640]{0,1:T(8,128)(2,1)} copy(bf16[128,640]{1,0:T(8,128)(2,1)} %multiply_convert_fusion.2) | data formatting | bytes 327680 | tf_op jit(solution)/shard_map/convert_element_type | solution.py:67
  55.1 0.6 collective-permute-done.10
  55.7 2.5 %fusion.45 = f32[5,128,128]{2,1,0:T(8,128)} fusion(bf16[128,5,128]{0,2,1:T(8,128)(2,1)} %bitcast.45, bf16[5,128,128]{2,1,0:T(8,128)(2,1)} %copy-done.4, bf16[5,128,128]{2,1,0:T(8,128)(2,1)} %copy-done.5, bf16[5,128,128]{2,1,0:T(8,128)(2,1)} %copy-done.6, bf16[5,128,128]{2,1,0:T(8,128)(2,1)} %copy-done.7, bf16[5,128,128]{2,1,0:T(8,128)(2,1)} %copy-done.8, ...), kind=kOutput, calls=%fused_computation.79 | convolution fusion | flops 22609920 | bytes 1638406 | tf_op jit(solution)/shard_map/thd,hde->the/dot_general | solution.py:78
  58.2 2.3 %multiply_reduce_fusion = (f32[128,5]{0,1:T(8,128)S(1)}, f32[128,5,128]{0,2,1:T(8,128)}) fusion(f32[5,128,128]{2,1,0:T(8,128)} %fusion.45, bf16[128,5,128]{0,2,1:T(8,128)(2,1)S(1)} %bitcast.42, bf16[128,5,128]{0,2,1:T(8,128)(2,1)} %bitcast.46, bf16[128,5,128]{0,2,1:T(8,128)(2,1)} %bitcast.44, f32[128,128]{1,0:T(8,128)S(1)} %fusion.53), kind=kOutput, calls=%fused_computation.74 | convolution fusion | flops 42352000 | bytes 1214976 | tf_op jit(solution)/shard_map/hts,shd->thd/dot_general | solution.py:77
  60.6 1.0 multiply_convert_fusion
  61.6 0.0 collective-permute-done.11
  61.6 4.3 %fusion.11 = (bf16[640,1280]{1,0:T(8,128)(2,1)S(1)}, bf16[640,1280]{1,0:T(8,128)(2,1)S(1)}, bf16[640,1280]{1,0:T(8,128)(2,1)S(1)}, bf16[640,1280]{1,0:T(8,128)(2,1)S(1)}) fusion(s32[]{:T(128)S(6)} %select_n.178, s32[]{:T(128)S(6)} %select_n.180, bf16[1,640,2560]{2,1,0:T(8,128)(2,1)} %bitcast.39, bf16[1,640,2560]{2,1,0:T(8,128)(2,1)} %bitcast.8, ...), kind=kLoop, calls=%fused_computation.19 | loop fusion | flops 13107200 | bytes 13107232 | tf_op jit(solution)/shard_map/squeeze | solution.py:96
  65.9 1.2 %fusion = f32[128,5120]{1,0:T(8,128)S(1)} fusion(bf16[128,640]{0,1:T(8,128)(2,1)S(1)} %bitcast.47, bf16[640,1280]{1,0:T(8,128)(2,1)S(1)} %get-tuple-element.20, bf16[640,1280]{1,0:T(8,128)(2,1)S(1)} %get-tuple-element.19, bf16[640,1280]{1,0:T(8,128)(2,1)S(1)} %get-tuple-element.18, bf16[640,1280]{1,0:T(8,128)(2,1)S(1)} %get-tuple-element.17), kind=kOutput, calls=%fused_computation.8 | convolution fusion | flops 865075200 | bytes 9338880 | tf_op jit(solution)/shard_map/dot_general | solution.py:98
  67.1 0.1 fusion.63
  67.2 6.4 %collective-permute-start.12 = (bf16[128,1280]{1,0:T(8,128)(2,1)S(1)}, bf16[128,1280]{1,0:T(8,128)(2,1)S(1)}, u32[]{:S(2)}, u32[]{:S(2)}) collective-permute-start(bf16[128,1280]{1,0:T(8,128)(2,1)S(1)} %get-tuple-element.11), channel_id=1, source_target_pairs={{0,1},{4,5},{8,9},{12,13},{16,17},{20,21},{24,25},{28,29},{32,33},... | collective-permute-start | bytes 983048 | tf_op jit(solution)/shard_map/ppermute | solution.py:111
  73.7 0.7 collective-permute-start.13
  74.4 5.5 %collective-permute-done.12 = bf16[128,1280]{1,0:T(8,128)(2,1)S(1)} collective-permute-done((bf16[128,1280]{1,0:T(8,128)(2,1)S(1)}, bf16[128,1280]{1,0:T(8,128)(2,1)S(1)}, u32[]{:S(2)}, u32[]{:S(2)}) %collective-permute-start.12) | collective-permute-done | bytes 327712 | tf_op jit(solution)/shard_map/ppermute | solution.py:111
  79.9 0.0 collective-permute-done.13
  79.9 0.1 add_convert_fusion.2
  80.0 4.4 %collective-permute-start.14 = (bf16[128,1280]{1,0:T(8,128)(2,1)S(1)}, bf16[128,1280]{1,0:T(8,128)(2,1)S(1)}, u32[]{:S(2)}, u32[]{:S(2)}) collective-permute-start(bf16[128,1280]{1,0:T(8,128)(2,1)S(1)} %get-tuple-element.13), channel_id=1, source_target_pairs={{0,1},{1,2},{4,5},{5,6},{8,9},{9,10},{12,13},{13,14},{16,17},{17,1... | collective-permute-start | bytes 983048 | tf_op jit(solution)/shard_map/ppermute | solution.py:111
  84.4 0.7 collective-permute-start.15
  85.1 4.7 %collective-permute-done.14 = bf16[128,1280]{1,0:T(8,128)(2,1)S(1)} collective-permute-done((bf16[128,1280]{1,0:T(8,128)(2,1)S(1)}, bf16[128,1280]{1,0:T(8,128)(2,1)S(1)}, u32[]{:S(2)}, u32[]{:S(2)}) %collective-permute-start.14) | collective-permute-done | bytes 327712 | tf_op jit(solution)/shard_map/ppermute | solution.py:111
  89.8 0.0 collective-permute-done.15
  89.8 0.2 add_convert_fusion
  90.0 7.7 %collective-permute-start.16 = (bf16[128,1280]{1,0:T(8,128)(2,1)S(1)}, bf16[128,1280]{1,0:T(8,128)(2,1)S(1)}, u32[]{:S(2)}, u32[]{:S(2)}) collective-permute-start(bf16[128,1280]{1,0:T(8,128)(2,1)S(1)} %get-tuple-element.15), channel_id=1, source_target_pairs={{0,1},{1,2},{2,3},{4,5},{5,6},{6,7},{8,9},{9,10},{10,11},{12,13},{... | collective-permute-start | bytes 983048 | tf_op jit(solution)/shard_map/ppermute | solution.py:111
  97.7 1.3 %collective-permute-start.17 = (bf16[128,1280]{1,0:T(8,128)(2,1)S(1)}, bf16[128,1280]{1,0:T(8,128)(2,1)S(1)}, u32[]{:S(2)}, u32[]{:S(2)}) collective-permute-start(bf16[128,1280]{1,0:T(8,128)(2,1)S(1)} %get-tuple-element.16), channel_id=1, source_target_pairs={{1,0},{2,1},{3,2},{5,4},{6,5},{7,6},{9,8},{10,9},{11,10},{13,12},{... | collective-permute-start | bytes 983048 | tf_op jit(solution)/shard_map/ppermute | solution.py:112
  99.0 3.3 %collective-permute-done.16 = bf16[128,1280]{1,0:T(8,128)(2,1)S(1)} collective-permute-done((bf16[128,1280]{1,0:T(8,128)(2,1)S(1)}, bf16[128,1280]{1,0:T(8,128)(2,1)S(1)}, u32[]{:S(2)}, u32[]{:S(2)}) %collective-permute-start.16) | collective-permute-done | bytes 327712 | tf_op jit(solution)/shard_map/ppermute | solution.py:111
  102.3 4.4 %collective-permute-done.17 = bf16[128,1280]{1,0:T(8,128)(2,1)S(1)} collective-permute-done((bf16[128,1280]{1,0:T(8,128)(2,1)S(1)}, bf16[128,1280]{1,0:T(8,128)(2,1)S(1)}, u32[]{:S(2)}, u32[]{:S(2)}) %collective-permute-start.17) | collective-permute-done | bytes 327712 | tf_op jit(solution)/shard_map/ppermute | solution.py:112
  106.7 0.8 fusion.43
  (18 shorter events, 0.0 us)
Async XLA Ops:
  0.0 1.9 %copy-start = (bf16[2560,640]{1,0:T(8,128)(2,1)S(1)}, bf16[2560,640]{1,0:T(8,128)(2,1)}, u32[]{:S(2)}) copy-start(bf16[2560,640]{1,0:T(8,128)(2,1)} %param.8) | copy-start | bytes 9830404
  0.0 4.6 %collective-permute-start = (bf16[128,5120]{1,0:T(8,128)(2,1)}, bf16[128,5120]{1,0:T(8,128)(2,1)}, u32[]{:S(2)}, u32[]{:S(2)}) collective-permute-start(bf16[128,5120]{1,0:T(8,128)(2,1)} %bitcast.40), channel_id=1, source_target_pairs={{0,4},{4,0},{1,5},{5,1},{2,6},{6,2},{3,7},{7,3},{8,12},{12,8},{9,1... | collective-permute-start | bytes 3932168 | tf_op jit(solution)/shard_map/ppermute | solution.py:12
  0.0 61.6 %collective-permute-start.11 = (bf16[640,2560]{1,0:T(8,128)(2,1)}, bf16[640,2560]{1,0:T(8,128)(2,1)}, u32[]{:S(2)}, u32[]{:S(2)}) collective-permute-start(bf16[640,2560]{1,0:T(8,128)(2,1)} %param.9), channel_id=1, source_target_pairs={{0,4},{4,0},{1,5},{5,1},{2,6},{6,2},{3,7},{7,3},{8,12},{12,8},{9,1... | collective-permute-start | bytes 9830408 | tf_op jit(solution)/shard_map/ppermute | solution.py:12
  1.9 5.3 %copy-start.1 = (bf16[2560,640]{1,0:T(8,128)(2,1)S(1)}, bf16[2560,640]{1,0:T(8,128)(2,1)}, u32[]{:S(2)}) copy-start(bf16[2560,640]{1,0:T(8,128)(2,1)} %param.7) | copy-start | bytes 9830404
  4.6 5.6 %copy-start.3 = (bf16[1,128,5120]{2,1,0:T(8,128)(2,1)S(1)}, bf16[1,128,5120]{2,1,0:T(8,128)(2,1)}, u32[]{:S(2)}) copy-start(bf16[1,128,5120]{2,1,0:T(8,128)(2,1)} %param.5) | copy-start | bytes 3932164
  7.2 4.4 %collective-permute-start.1 = (f32[128,640]{1,0:T(8,128)}, f32[128,640]{1,0:T(8,128)}, u32[]{:S(2)}, u32[]{:S(2)}) collective-permute-start(f32[128,640]{1,0:T(8,128)} %fusion.30), channel_id=1, source_target_pairs={{0,4},{4,0},{1,5},{5,1},{2,6},{6,2},{3,7},{7,3},{8,12},{12,8},{9,1... | collective-permute-start | bytes 983048 | tf_op jit(solution)/shard_map/ppermute | solution.py:12
  9.7 4.8 %collective-permute-start.3 = (f32[128,640]{1,0:T(8,128)}, f32[128,640]{1,0:T(8,128)}, u32[]{:S(2)}, u32[]{:S(2)}) collective-permute-start(f32[128,640]{1,0:T(8,128)} %fusion.26), channel_id=1, source_target_pairs={{0,4},{4,0},{1,5},{5,1},{2,6},{6,2},{3,7},{7,3},{8,12},{12,8},{9,1... | collective-permute-start | bytes 983048 | tf_op jit(solution)/shard_map/ppermute | solution.py:12
  18.0 17.1 %copy-start.2 = (bf16[2560,640]{1,0:T(8,128)(2,1)S(1)}, bf16[2560,640]{1,0:T(8,128)(2,1)}, u32[]{:S(2)}) copy-start(bf16[2560,640]{1,0:T(8,128)(2,1)} %param.6) | copy-start | bytes 9830404
  19.3 8.7 %collective-permute-start.4 = (bf16[5,128,128]{2,1,0:T(8,128)(2,1)S(1)}, bf16[5,128,128]{2,1,0:T(8,128)(2,1)S(1)}, u32[]{:S(2)}, u32[]{:S(2)}) collective-permute-start(bf16[5,128,128]{2,1,0:T(8,128)(2,1)S(1)} %get-tuple-element.27), channel_id=1, source_target_pairs={{0,16},{8,24},{16,0},{24,8},{32,48},{40,56},{48,32},{56,40},{64,80... | collective-permute-start | bytes 491528 | tf_op jit(solution)/shard_map/ppermute | solution.py:16
  21.5 9.1 %collective-permute-start.5 = (bf16[5,128,128]{2,1,0:T(8,128)(2,1)S(1)}, bf16[5,128,128]{2,1,0:T(8,128)(2,1)S(1)}, u32[]{:S(2)}, u32[]{:S(2)}) collective-permute-start(bf16[5,128,128]{2,1,0:T(8,128)(2,1)S(1)} %get-tuple-element.27), channel_id=1, source_target_pairs={{0,8},{8,16},{16,24},{24,0},{32,40},{40,48},{48,56},{56,32},{64,72... | collective-permute-start | bytes 491528 | tf_op jit(solution)/shard_map/ppermute | solution.py:16
  21.5 9.1 %collective-permute-start.6 = (bf16[5,128,128]{2,1,0:T(8,128)(2,1)S(1)}, bf16[5,128,128]{2,1,0:T(8,128)(2,1)S(1)}, u32[]{:S(2)}, u32[]{:S(2)}) collective-permute-start(bf16[5,128,128]{2,1,0:T(8,128)(2,1)S(1)} %get-tuple-element.27), channel_id=1, source_target_pairs={{0,24},{8,0},{16,8},{24,16},{32,56},{40,32},{48,40},{56,48},{64,88... | collective-permute-start | bytes 491528 | tf_op jit(solution)/shard_map/ppermute | solution.py:16
  28.0 14.8 %copy-start.4 = (bf16[5,128,128]{2,1,0:T(8,128)(2,1)}, bf16[5,128,128]{2,1,0:T(8,128)(2,1)S(1)}, u32[]{:S(2)}) copy-start(bf16[5,128,128]{2,1,0:T(8,128)(2,1)S(1)} %collective-permute-done.4) | copy-start | bytes 491524
  30.6 12.2 %copy-start.5 = (bf16[5,128,128]{2,1,0:T(8,128)(2,1)}, bf16[5,128,128]{2,1,0:T(8,128)(2,1)S(1)}, u32[]{:S(2)}) copy-start(bf16[5,128,128]{2,1,0:T(8,128)(2,1)S(1)} %collective-permute-done.5) | copy-start | bytes 491524
  30.6 12.2 %copy-start.6 = (bf16[5,128,128]{2,1,0:T(8,128)(2,1)}, bf16[5,128,128]{2,1,0:T(8,128)(2,1)S(1)}, u32[]{:S(2)}) copy-start(bf16[5,128,128]{2,1,0:T(8,128)(2,1)S(1)} %collective-permute-done.6) | copy-start | bytes 491524
  30.7 8.7 %collective-permute-start.7 = (bf16[5,128,128]{2,1,0:T(8,128)(2,1)S(1)}, bf16[5,128,128]{2,1,0:T(8,128)(2,1)S(1)}, u32[]{:S(2)}, u32[]{:S(2)}) collective-permute-start(bf16[5,128,128]{2,1,0:T(8,128)(2,1)S(1)} %fusion.54), channel_id=1, source_target_pairs={{0,64},{8,72},{16,80},{24,88},{32,96},{40,104},{48,112},{56,120},{... | collective-permute-start | bytes 491528 | tf_op jit(solution)/shard_map/ppermute | solution.py:16
  33.1 8.9 %collective-permute-start.8 = (bf16[5,128,128]{2,1,0:T(8,128)(2,1)S(1)}, bf16[5,128,128]{2,1,0:T(8,128)(2,1)S(1)}, u32[]{:S(2)}, u32[]{:S(2)}) collective-permute-start(bf16[5,128,128]{2,1,0:T(8,128)(2,1)S(1)} %fusion.54), channel_id=1, source_target_pairs={{0,32},{8,40},{16,48},{24,56},{32,64},{40,72},{48,80},{56,88},{64,... | collective-permute-start | bytes 491528 | tf_op jit(solution)/shard_map/ppermute | solution.py:16
  33.1 8.9 %collective-permute-start.9 = (bf16[5,128,128]{2,1,0:T(8,128)(2,1)S(1)}, bf16[5,128,128]{2,1,0:T(8,128)(2,1)S(1)}, u32[]{:S(2)}, u32[]{:S(2)}) collective-permute-start(bf16[5,128,128]{2,1,0:T(8,128)(2,1)S(1)} %fusion.54), channel_id=1, source_target_pairs={{0,96},{8,104},{16,112},{24,120},{32,0},{40,8},{48,16},{56,24},{64... | collective-permute-start | bytes 491528 | tf_op jit(solution)/shard_map/ppermute | solution.py:16
  36.9 15.7 %collective-permute-start.2 = (f32[128,640]{1,0:T(8,128)S(1)}, f32[128,640]{1,0:T(8,128)S(1)}, u32[]{:S(2)}, u32[]{:S(2)}) collective-permute-start(f32[128,640]{1,0:T(8,128)S(1)} %fusion.28), channel_id=1, source_target_pairs={{0,4},{4,0},{1,5},{5,1},{2,6},{6,2},{3,7},{7,3},{8,12},{12,8},{9,1... | collective-permute-start | bytes 983048 | tf_op jit(solution)/shard_map/ppermute | solution.py:12
  39.4 13.2 %copy-start.7 = (bf16[5,128,128]{2,1,0:T(8,128)(2,1)}, bf16[5,128,128]{2,1,0:T(8,128)(2,1)S(1)}, u32[]{:S(2)}) copy-start(bf16[5,128,128]{2,1,0:T(8,128)(2,1)S(1)} %collective-permute-done.7) | copy-start | bytes 491524
  42.0 10.6 %copy-start.8 = (bf16[5,128,128]{2,1,0:T(8,128)(2,1)}, bf16[5,128,128]{2,1,0:T(8,128)(2,1)S(1)}, u32[]{:S(2)}) copy-start(bf16[5,128,128]{2,1,0:T(8,128)(2,1)S(1)} %collective-permute-done.8) | copy-start | bytes 491524
  42.0 10.6 %copy-start.9 = (bf16[5,128,128]{2,1,0:T(8,128)(2,1)}, bf16[5,128,128]{2,1,0:T(8,128)(2,1)S(1)}, u32[]{:S(2)}) copy-start(bf16[5,128,128]{2,1,0:T(8,128)(2,1)S(1)} %collective-permute-done.9) | copy-start | bytes 491524
  42.9 12.9 %collective-permute-start.10 = (bf16[5,128,128]{2,1,0:T(8,128)(2,1)}, bf16[5,128,128]{2,1,0:T(8,128)(2,1)}, u32[]{:S(2)}, u32[]{:S(2)}) collective-permute-start(bf16[5,128,128]{2,1,0:T(8,128)(2,1)} %fusion.42), channel_id=1, source_target_pairs={{0,128},{8,136},{16,144},{24,152},{32,160},{40,168},{48,176},{56,1... | collective-permute-start | bytes 491528 | tf_op jit(solution)/shard_map/ppermute | solution.py:16
  67.2 12.7 %collective-permute-start.12 = (bf16[128,1280]{1,0:T(8,128)(2,1)S(1)}, bf16[128,1280]{1,0:T(8,128)(2,1)S(1)}, u32[]{:S(2)}, u32[]{:S(2)}) collective-permute-start(bf16[128,1280]{1,0:T(8,128)(2,1)S(1)} %get-tuple-element.11), channel_id=1, source_target_pairs={{0,1},{4,5},{8,9},{12,13},{16,17},{20,21},{24,25},{28,29},{32,33},... | collective-permute-start | bytes 983048 | tf_op jit(solution)/shard_map/ppermute | solution.py:111
  73.7 6.2 %collective-permute-start.13 = (bf16[128,1280]{1,0:T(8,128)(2,1)S(1)}, bf16[128,1280]{1,0:T(8,128)(2,1)S(1)}, u32[]{:S(2)}, u32[]{:S(2)}) collective-permute-start(bf16[128,1280]{1,0:T(8,128)(2,1)S(1)} %get-tuple-element.12), channel_id=1, source_target_pairs={{3,2},{7,6},{11,10},{15,14},{19,18},{23,22},{27,26},{31,30},{35,34... | collective-permute-start | bytes 983048 | tf_op jit(solution)/shard_map/ppermute | solution.py:112
  80.0 9.8 %collective-permute-start.14 = (bf16[128,1280]{1,0:T(8,128)(2,1)S(1)}, bf16[128,1280]{1,0:T(8,128)(2,1)S(1)}, u32[]{:S(2)}, u32[]{:S(2)}) collective-permute-start(bf16[128,1280]{1,0:T(8,128)(2,1)S(1)} %get-tuple-element.13), channel_id=1, source_target_pairs={{0,1},{1,2},{4,5},{5,6},{8,9},{9,10},{12,13},{13,14},{16,17},{17,1... | collective-permute-start | bytes 983048 | tf_op jit(solution)/shard_map/ppermute | solution.py:111
  84.4 5.4 %collective-permute-start.15 = (bf16[128,1280]{1,0:T(8,128)(2,1)S(1)}, bf16[128,1280]{1,0:T(8,128)(2,1)S(1)}, u32[]{:S(2)}, u32[]{:S(2)}) collective-permute-start(bf16[128,1280]{1,0:T(8,128)(2,1)S(1)} %get-tuple-element.14), channel_id=1, source_target_pairs={{2,1},{3,2},{6,5},{7,6},{10,9},{11,10},{14,13},{15,14},{18,17},{19... | collective-permute-start | bytes 983048 | tf_op jit(solution)/shard_map/ppermute | solution.py:112
  90.0 12.3 %collective-permute-start.16 = (bf16[128,1280]{1,0:T(8,128)(2,1)S(1)}, bf16[128,1280]{1,0:T(8,128)(2,1)S(1)}, u32[]{:S(2)}, u32[]{:S(2)}) collective-permute-start(bf16[128,1280]{1,0:T(8,128)(2,1)S(1)} %get-tuple-element.15), channel_id=1, source_target_pairs={{0,1},{1,2},{2,3},{4,5},{5,6},{6,7},{8,9},{9,10},{10,11},{12,13},{... | collective-permute-start | bytes 983048 | tf_op jit(solution)/shard_map/ppermute | solution.py:111
  97.7 9.0 %collective-permute-start.17 = (bf16[128,1280]{1,0:T(8,128)(2,1)S(1)}, bf16[128,1280]{1,0:T(8,128)(2,1)S(1)}, u32[]{:S(2)}, u32[]{:S(2)}) collective-permute-start(bf16[128,1280]{1,0:T(8,128)(2,1)S(1)} %get-tuple-element.16), channel_id=1, source_target_pairs={{1,0},{2,1},{3,2},{5,4},{6,5},{7,6},{9,8},{10,9},{11,10},{13,12},{... | collective-permute-start | bytes 983048 | tf_op jit(solution)/shard_map/ppermute | solution.py:112
